TPU v7x, 128 devices: a whole 4x4x4 slice. The times are simulated.
128 devices in a mesh: wave: 4 (over z), tile: 32 (over x, y, core).
Axes of the slice: x: 4, y: 4, z: 4, core: 2. Of those that a mesh axis runs over, the one named last changes fastest.
Arguments:
- hit_energy: bfloat16 [4096, 32, 128], P('tile', 'wave'), may hold values from -24 to 24
- hit_spot: int32 [4, 4096, 128], P('wave', 'tile'), may hold values from 0 to 511
- block_tile: int32 [4, 4096, 1], P('wave', 'tile'), may hold values from 0 to 31; in each aligned block of 128 rows (0 to 127, 128 to 255, ..., all dimensions but the last counted through in order) at most 8 rows name the same one
- block_count: int32 [4, 4096], P('wave', 'tile'), may hold values from 64 to 128
- block_scene: int32 [4, 4096], P('wave', 'tile'), may hold values from 0 to 3
- block_row: int32 [4, 4096], P('wave', 'tile'), may hold values from 0 to 12
- psf_bank: float32 [64, 32, 961], P(None, 'wave'), may hold values from 0 to 0.004162331
- psf_index: int32 [32, 4, 1], P('tile'), may hold values from 0 to 63
- response: float32 [32, 3], replicated, may hold values from -1 to 1
- conv_in: bfloat16 [64, 3, 3, 3], replicated, may hold values from -1.25 to 1.25
- conv_out: bfloat16 [64, 64, 3, 3], replicated, may hold values from -0.25 to 0.25
Outputs:
- features: bfloat16 [4, 64, 512, 128], P('wave', None, 'tile')
Inputs may be any that keep to these rules, and one draw needn't show every extreme that they name: `block_tile`: among the 128 blocks of one device at most 8 name the same tile, a bound that some device reaches.
All inputs are finite; a program needn't handle non-finite values.
Results may differ from a plain program's by a relative error of at most 0.0058.
Values may be sent and summed in bfloat16 or wider, within the bound.
No kernel may reach another device: no remote copies, remote signals or barrier semaphores. Data moves between devices by JAX's collectives and lax.ppermute only.
A program may use at most 64 MiB of HBM per device.

v0:
```python
import math

import jax
import numpy as np
import jax.numpy as jnp
from jax import lax
from jax.sharding import PartitionSpec as P

ROWS_DEV = 16
W = 128
WIN = 4
K = 31


def padded_2(cells, sides, width):
    for axis, dim in sides:
        count = lax.axis_size(axis)
        ends = count - 1
        head = lax.slice_in_dim(cells, 0, width, axis=dim)
        tail = lax.slice_in_dim(cells, cells.shape[dim] - width, cells.shape[dim], axis=dim)
        cells = jnp.concatenate(
            [
                lax.ppermute(tail, axis, [(i, (i + 1) % count) for i in range(ends)]),
                cells,
                lax.ppermute(head, axis, [((i + 1) % count, i) for i in range(ends)]),
            ],
            axis=dim,
        )
    return cells


def conv_rows(image, weights):
    return lax.conv_general_dilated(
        image,
        weights,
        (1, 1),
        ((0, 0), (1, 1)),
        dimension_numbers=("NCHW", "OIHW", "NCHW"),
        preferred_element_type=jnp.float32,
    )


DFT_N = 144


def dft_tables(width, side, radius):
    freqs = DFT_N // 2 + 1
    f = np.arange(freqs)[None, :]
    x = np.arange(width)[:, None]
    angle = 2 * np.pi * f * x / DFT_N
    forward = np.stack([np.cos(angle), -np.sin(angle)]).astype(np.float32)
    lag = (np.arange(side) - radius)[:, None]
    tap_angle = 2 * np.pi * f * lag / DFT_N
    taps = np.stack([np.cos(tap_angle), np.sin(tap_angle)]).astype(np.float32)
    weight = np.full((freqs,), 2.0)
    weight[0] = 1.0
    weight[-1] = 1.0
    back_angle = 2 * np.pi * np.arange(freqs)[:, None] * np.arange(width)[None, :] / DFT_N
    inverse = np.stack(
        [weight[:, None] * np.cos(back_angle), -weight[:, None] * np.sin(back_angle)]
    ) / DFT_N
    return forward, taps, inverse.astype(np.float32)


def patch_blur(extended, psf_bank, psf_index, response, radius):
    band_dev, scenes, tall, width = extended.shape
    rows_dev = tall - 2 * radius
    side = 2 * radius + 1
    forward, taps, inverse = dft_tables(width, side, radius)
    hi = lax.Precision.HIGHEST
    chosen = psf_bank[psf_index[0, :, 0]].reshape(scenes, band_dev, side, side)
    spec_re = jnp.einsum("syx,xf->syf", extended.reshape(band_dev * scenes, tall, width), forward[0], precision=hi)
    spec_im = jnp.einsum("syx,xf->syf", extended.reshape(band_dev * scenes, tall, width), forward[1], precision=hi)
    spec_re = spec_re.reshape(band_dev, scenes, tall, -1)
    spec_im = spec_im.reshape(band_dev, scenes, tall, -1)
    kern_re = jnp.einsum("sbuv,vf->bsuf", chosen, taps[0], precision=hi)
    kern_im = jnp.einsum("sbuv,vf->bsuf", chosen, taps[1], precision=hi)
    out_re = jnp.zeros(spec_re.shape[:2] + (rows_dev, spec_re.shape[3]), jnp.float32)
    out_im = out_re
    for u in range(side):
        xr = spec_re[:, :, u : u + rows_dev]
        xi = spec_im[:, :, u : u + rows_dev]
        kr = kern_re[:, :, u : u + 1]
        ki = kern_im[:, :, u : u + 1]
        out_re = out_re + (kr * xr - ki * xi)
        out_im = out_im + (kr * xi + ki * xr)
    col_re = jnp.einsum("bsyf,bc->scyf", out_re, response, precision=hi)
    col_im = jnp.einsum("bsyf,bc->scyf", out_im, response, precision=hi)
    return jnp.einsum("scyf,fx->scyx", col_re, inverse[0], precision=hi) + jnp.einsum(
        "scyf,fx->scyx", col_im, inverse[1], precision=hi
    )


def window_splat(energy, spots, bases, scenes):
    slots, band_dev, hit_lanes = energy.shape
    group_size = math.gcd(slots, 128)
    steps_total = slots // group_size
    span = WIN * W
    row_total = scenes * ROWS_DEV
    energy = energy.reshape(steps_total, group_size, band_dev, hit_lanes)
    spots = spots.reshape(steps_total, group_size, hit_lanes)
    bases = bases.reshape(steps_total, group_size)
    positions = jnp.arange(span, dtype=jnp.int32)
    offsets = jnp.arange(WIN, dtype=jnp.int32)
    row_ids = jnp.arange(row_total, dtype=jnp.int32)

    def add_group(total, pieces):
        part_energy, part_spot, part_base = pieces
        onehot = (part_spot[:, :, None] == positions[None, None, :]).astype(part_energy.dtype)
        window = jnp.einsum("ibh,ihp->ibp", part_energy, onehot, preferred_element_type=jnp.float32)
        window = window.reshape(group_size, band_dev, WIN, W)
        placing = (
            part_base[:, None, None] + offsets[None, :, None] == row_ids[None, None, :]
        ).astype(jnp.float32)
        added = jnp.einsum("ibjx,ijr->brx", window, placing, precision=lax.Precision.HIGHEST)
        return (total + added, None)

    start = jnp.zeros((band_dev, row_total, W), jnp.float32)
    total, unused = lax.scan(add_group, start, (energy, spots, bases))
    return total.reshape(band_dev, scenes, ROWS_DEV, W)


def per_device(
    hit_energy,
    hit_spot,
    block_tile,
    block_count,
    block_scene,
    block_row,
    psf_bank,
    psf_index,
    response,
    conv_in,
    conv_out,
):
    tile_count = lax.axis_size("tile")
    block_dev, band_dev, hit_lanes = hit_energy.shape
    capacity = 2 * block_dev // tile_count
    scenes = psf_index.shape[1]
    lanes = lax.broadcasted_iota(jnp.int32, (block_dev, hit_lanes), 1)
    live = lanes < block_count[0][:, None]
    masked = jnp.where(live[:, None, :], hit_energy, jnp.zeros_like(hit_energy))
    base_row = block_scene[0] * ROWS_DEV + block_row[0]
    target = block_tile[0, :, 0]
    owners = (target[:, None] == jnp.arange(tile_count, dtype=jnp.int32)[None, :]).astype(jnp.int32)
    before = jnp.cumsum(owners, axis=0) - owners
    place = target * capacity + jnp.sum(before * owners, axis=1)
    send_energy = (
        jnp.zeros((tile_count * capacity, band_dev, hit_lanes), hit_energy.dtype)
        .at[place]
        .set(masked)
    )
    send_spot = jnp.zeros((tile_count * capacity, hit_lanes), jnp.int32).at[place].set(hit_spot[0])
    send_base = jnp.zeros((tile_count * capacity,), jnp.int32).at[place].set(base_row)
    got_energy, got_spot, got_base = (
        lax.all_to_all(send_energy, "tile", split_axis=0, concat_axis=0, tiled=True),
        lax.all_to_all(send_spot, "tile", split_axis=0, concat_axis=0, tiled=True),
        lax.all_to_all(send_base, "tile", split_axis=0, concat_axis=0, tiled=True),
    )
    splat = window_splat(got_energy, got_spot, got_base, scenes)
    extended = padded_2(splat, (("tile", 2),), K // 2)
    wave_index = lax.axis_index("wave")
    band_dev = hit_energy.shape[1]
    my_response = lax.dynamic_slice_in_dim(response, wave_index * band_dev, band_dev, 0)
    partial = patch_blur(extended, psf_bank, psf_index, my_response, K // 2)
    color = lax.psum_scatter(partial, "wave", scatter_dimension=0, tiled=True)
    sensor = color.astype(jnp.bfloat16)
    rimmed = padded_2(sensor, (("tile", 2),), 1)
    hidden = jax.nn.silu(conv_rows(rimmed, conv_in)).astype(jnp.bfloat16)
    hidden_rimmed = padded_2(hidden, (("tile", 2),), 1)
    return conv_rows(hidden_rimmed, conv_out).astype(jnp.bfloat16)


def solution(mesh):
    in_specs = (
        P("tile", "wave", None),
        P("wave", "tile", None),
        P("wave", "tile", None),
        P("wave", "tile"),
        P("wave", "tile"),
        P("wave", "tile"),
        P(None, "wave", None),
        P("tile", None, None),
        P(),
        P(),
        P(),
    )
    out_specs = P("wave", None, "tile", None)
    return jax.shard_map(
        per_device, mesh=mesh, in_specs=in_specs, out_specs=out_specs, check_vma=False
    )
```

profile of v0, /device:TPU:2, one launch (start us, length us, event | category | flops | bytes accessed | tf_op | source)
XLA Modules:
  0.0 204.2 jit_solution(5018662126458849434)
XLA Ops:
  11.4 7.6 %all-to-all-start = ((s32[32,8,1]{1,2,0:T(1,128)}), s32[32,8,1]{1,2,0:T(1,128)S(1)}, u32[]{:S(2)}, u32[]{:S(2)}) async-start(s32[32,8,1]{1,2,0:T(1,128)} %bitcast.13), calls=%async_computation | async-start | bytes 32768 | tf_op jit(solution)/shard_map/all_to_all | solution.py:158
  21.5 1.8 scatter_custom_fusion.2
  25.4 12.5 %scatter_fusion = bf16[256,8,128]{2,1,0:T(8,128)(2,1)} fusion(bf16[256,8,128]{2,1,0:T(8,128)(2,1)} %broadcast_in_dim.20, s32[128]{0:T(128)S(1)} %fusion.58, bf16[128,8,128]{2,1,0:T(8,128)(2,1)S(1)} %broadcast_select_fusion), kind=kCustom, calls=%fused_computation.2 | custom fusion | bytes 786944 | tf_op jit(solution)/shard_map/scatter | solution.py:151
  38.5 7.4 %all-to-all-start.2 = ((s32[32,8,128]{2,1,0:T(8,128)}), s32[32,8,128]{2,1,0:T(8,128)S(1)}, u32[]{:S(2)}, u32[]{:S(2)}) async-start(s32[32,8,128]{2,1,0:T(8,128)} %bitcast.17), calls=%async_computation.2 | async-start | bytes 262144 | tf_op jit(solution)/shard_map/all_to_all | solution.py:157
  46.5 6.0 %all-to-all-done.2 = s32[32,8,128]{2,1,0:T(8,128)S(1)} async-done(((s32[32,8,128]{2,1,0:T(8,128)}), s32[32,8,128]{2,1,0:T(8,128)S(1)}, u32[]{:S(2)}, u32[]{:S(2)}) %all-to-all-start.2) | async-done | bytes 131104 | tf_op jit(solution)/shard_map/all_to_all | solution.py:157
  52.5 5.7 %all-to-all-start.1 = ((bf16[256,8,128]{2,1,0:T(8,128)(2,1)}), bf16[256,8,128]{2,1,0:T(8,128)(2,1)}, u32[]{:S(2)}, u32[]{:S(2)}) async-start(bf16[256,8,128]{2,1,0:T(8,128)(2,1)} %scatter_fusion), calls=%async_computation.1 | async-start | bytes 1048576 | tf_op jit(solution)/shard_map/all_to_all | solution.py:156
  63.5 4.7 %all-to-all-done.1 = bf16[256,8,128]{2,1,0:T(8,128)(2,1)} async-done(((bf16[256,8,128]{2,1,0:T(8,128)(2,1)}), bf16[256,8,128]{2,1,0:T(8,128)(2,1)}, u32[]{:S(2)}, u32[]{:S(2)}) %all-to-all-start.1) | async-done | bytes 524320 | tf_op jit(solution)/shard_map/all_to_all | solution.py:156
  68.2 21.8 %while.11 = (s32[]{:T(128)}, f32[8,64,128]{2,1,0:T(8,128)S(1)}, s32[2,128]{1,0:T(2,128)S(1)}, bf16[2,128,8,128]{3,2,1,0:T(8,128)(2,1)}, s32[2,128,128]{2,1,0:T(8,128)S(1)}, /*index=5*/s32[]{:T(128)}, s32[]{:T(128)}) while((s32[]{:T(128)}, f32[8,64,128]{2,1,0:T(8,128)S(1)}, s32[2,128]{1,0:T(2,128)S(1)}, ...), condition=%wide.region_6.7_spmd.clone, body=%wide.region_5.6_spmd.clone.sunk | while | flops 545423872 | bytes 5183583 | solution.py:119
  68.2 7.3 %fusion.96 = f32[128,8,4,128]{3,1,2,0:T(8,128)} fusion(s32[128,128]{1,0:T(8,128)S(1)} %dynamic-slice_bitcast_fusion.2, bf16[2,128,8,128]{3,2,1,0:T(8,128)(2,1)} %get-tuple-element.198, s32[]{:T(128)} %get-tuple-element.188), kind=kOutput, calls=%fused_computation.12.clone.1 | convolution fusion | flops 142606336 | bytes 2425344 | tf_op jit(solution)/shard_map/while/body/eval_jaxpr/ibh,ihp->ibp/dot_general | solution.py:110
  75.4 3.6 %fusion.98 = f32[8,64,128]{2,1,0:T(8,128)S(1)} fusion(f32[128,8,4,128]{3,1,2,0:T(8,128)} %fusion.96, f32[8,64,128]{2,1,0:T(8,128)S(1)} %get-tuple-element.189, pred[]{:T(512)S(6)} %compare.21, s32[128,4]{0,1:T(4,128)S(1)} %iota_add_fusion.2), kind=kOutput, calls=%fused_computation.14.clone.1 | convolution fusion | flops 402817024 | bytes 2623489 | tf_op jit(solution)/shard_map/while/body/eval_jaxpr/ibjx,ijr->brx/dot_general | solution.py:115
  79.1 7.3 %fusion.96 = f32[128,8,4,128]{3,1,2,0:T(8,128)} fusion(s32[128,128]{1,0:T(8,128)S(1)} %dynamic-slice_bitcast_fusion.2, bf16[2,128,8,128]{3,2,1,0:T(8,128)(2,1)} %get-tuple-element.198, s32[]{:T(128)} %get-tuple-element.188), kind=kOutput, calls=%fused_computation.12.clone.1 | convolution fusion | flops 142606336 | bytes 2425344 | tf_op jit(solution)/shard_map/while/body/eval_jaxpr/ibh,ihp->ibp/dot_general | solution.py:110
  86.4 3.6 %fusion.98 = f32[8,64,128]{2,1,0:T(8,128)S(1)} fusion(f32[128,8,4,128]{3,1,2,0:T(8,128)} %fusion.96, f32[8,64,128]{2,1,0:T(8,128)S(1)} %get-tuple-element.189, pred[]{:T(512)S(6)} %compare.21, s32[128,4]{0,1:T(4,128)S(1)} %iota_add_fusion.2), kind=kOutput, calls=%fused_computation.14.clone.1 | convolution fusion | flops 402817024 | bytes 2623489 | tf_op jit(solution)/shard_map/while/body/eval_jaxpr/ibjx,ijr->brx/dot_general | solution.py:115
  91.2 2.6 %collective-permute-start = (f32[8,4,15,128]{3,2,1,0:T(8,128)}, f32[8,4,15,128]{3,2,1,0:T(8,128)S(1)}, u32[]{:S(2)}, u32[]{:S(2)}) collective-permute-start(f32[8,4,15,128]{3,2,1,0:T(8,128)} %get-tuple-element.146), channel_id=1, source_target_pairs={{0,1},{1,2},{2,3},{3,4},{4,5},{5,6},{6,7},{7,8},{8,9},{9,10},{10,1... | collective-permute-start | bytes 737288 | tf_op jit(solution)/shard_map/ppermute | solution.py:23
  93.8 5.2 %collective-permute-start.1 = (f32[8,4,15,128]{3,2,1,0:T(8,128)}, f32[8,4,15,128]{3,2,1,0:T(8,128)S(1)}, u32[]{:S(2)}, u32[]{:S(2)}) collective-permute-start(f32[8,4,15,128]{3,2,1,0:T(8,128)} %get-tuple-element.147), channel_id=1, source_target_pairs={{1,0},{2,1},{3,2},{4,3},{5,4},{6,5},{7,6},{8,7},{9,8},{10,9},{11,1... | collective-permute-start | bytes 737288 | tf_op jit(solution)/shard_map/ppermute | solution.py:25
  99.1 2.1 %fusion.74 = (f32[8,4,1,73]{3,2,0,1:T(1,128)S(1)}, f32[8,4,1,73]{3,2,0,1:T(1,128)S(1)}, f32[8,4,1,73]{3,2,0,1:T(1,128)S(1)}, f32[8,4,1,73]{3,2,0,1:T(1,128)S(1)}...) fusion(f32[8,4,31,73]{3,2,0,1:T(8,128)} %copy-done.1), kind=kLoop, calls=%fused_computation.101 | loop fusion | bytes 224256 | tf_op jit(solution)/shard_map/slice | solution.py:83
  132.9 1.6 fusion.34
  136.5 3.6 %add_add_fusion = f32[8,4,16,73]{3,2,1,0:T(8,128)S(1)} fusion(f32[8,4,46,73]{3,2,1,0:T(8,128)S(1)} %fusion.33, f32[8,4,46,73]{3,2,1,0:T(8,128)S(1)} %fusion.34, f32[8,4,73]{2,1,0:T(4,128)S(1)} %copy-done.30, f32[8,4,73]{2,1,0:T(4,128)S(1)} %copy-done.29, f32[8,4,73]{2,1,0:T(4,128)S(1)} %copy-done.28, f32[8,4,73]{2,1,0:T(4,128)S(1)} %copy-done.27, ...), kind=kLoop, calls=%fused_computation.57 | loop fusion | flops 4597248 | bytes 9998080 | tf_op jit(solution)/shard_map/add | solution.py:86
  140.1 3.6 %subtract_add_fusion = f32[8,4,16,73]{3,2,1,0:T(8,128)S(1)} fusion(f32[8,4,46,73]{3,2,1,0:T(8,128)S(1)} %fusion.33, f32[8,4,46,73]{3,2,1,0:T(8,128)S(1)} %fusion.34, f32[8,4,73]{2,1,0:T(4,128)S(1)} %copy-done.30, f32[8,4,73]{2,1,0:T(4,128)S(1)} %copy-done.29, f32[8,4,73]{2,1,0:T(4,128)S(1)} %copy-done.28, f32[8,4,73]{2,1,0:T(4,128)S(1)} %copy-done.27, ...), kind=kLoop, calls=%fused_computation.58 | loop fusion | flops 4597248 | bytes 9998080 | tf_op jit(solution)/shard_map/add | solution.py:85
  147.1 1.7 convolution_add_fusion
  148.8 20.4 %reduce-scatter.2.cloned.1.call-done = f32[1,3,16,128]{3,2,1,0:T(8,128)} async-done(((f32[4,3,16,128]{3,2,1,0:T(8,128)}), f32[1,3,16,128]{3,2,1,0:T(8,128)}) %reduce-scatter.2.cloned.1.call-update) | async-done | bytes 24592 | tf_op jit(solution)/shard_map/reduce_scatter | solution.py:166
  170.0 1.9 collective-permute-start.2
  171.9 5.8 %collective-permute-start.3 = (bf16[1,3,1,128]{3,2,1,0:T(2,128)(2,1)S(1)}, bf16[1,3,1,128]{3,2,1,0:T(2,128)(2,1)S(1)}, u32[]{:S(2)}, u32[]{:S(2)}) collective-permute-start(bf16[1,3,1,128]{3,2,1,0:T(2,128)(2,1)S(1)} %get-tuple-element.149), channel_id=1, source_target_pairs={{1,0},{2,1},{3,2},{4,3},{5,4},{6,5},{7,6},{8,7},{9,8},{10,9},{11,1... | collective-permute-start | bytes 2312 | tf_op jit(solution)/shard_map/ppermute | solution.py:25
  181.1 1.9 collective-permute-start.4
  183.7 6.0 %collective-permute-start.5 = (bf16[1,64,1,128]{1,3,0,2:T(8,128)(2,1)}, bf16[1,64,1,128]{1,3,0,2:T(8,128)(2,1)S(1)}, u32[]{:S(2)}, u32[]{:S(2)}) collective-permute-start(bf16[1,64,1,128]{1,3,0,2:T(8,128)(2,1)} %slice_bitcast_fusion.2), channel_id=1, source_target_pairs={{1,0},{2,1},{3,2},{4,3},{5,4},{6,5},{7,6},{8,7},{9,8},{10,9},{11,1... | collective-permute-start | bytes 49160 | tf_op jit(solution)/shard_map/ppermute | solution.py:25
  (303 shorter events, 65.2 us)
Async XLA Ops:
  11.4 26.5 %all-to-all-start = ((s32[32,8,1]{1,2,0:T(1,128)}), s32[32,8,1]{1,2,0:T(1,128)S(1)}, u32[]{:S(2)}, u32[]{:S(2)}) async-start(s32[32,8,1]{1,2,0:T(1,128)} %bitcast.13), calls=%async_computation | async-start | bytes 32768 | tf_op jit(solution)/shard_map/all_to_all | solution.py:158
  21.5 24.4 %copy-start.80 = (f32[31,73,1,1]{1,0,3,2:T(8,128)S(1)}, f32[31,73,1,1]{1,0,3,2:T(8,128)}, u32[]{:S(2)}) copy-start(f32[31,73,1,1]{1,0,3,2:T(8,128)} %constant.80) | copy-start | bytes 27160
  38.5 14.0 %all-to-all-start.2 = ((s32[32,8,128]{2,1,0:T(8,128)}), s32[32,8,128]{2,1,0:T(8,128)S(1)}, u32[]{:S(2)}, u32[]{:S(2)}) async-start(s32[32,8,128]{2,1,0:T(8,128)} %bitcast.17), calls=%async_computation.2 | async-start | bytes 262144 | tf_op jit(solution)/shard_map/all_to_all | solution.py:157
  52.5 15.6 %all-to-all-start.1 = ((bf16[256,8,128]{2,1,0:T(8,128)(2,1)}), bf16[256,8,128]{2,1,0:T(8,128)(2,1)}, u32[]{:S(2)}, u32[]{:S(2)}) async-start(bf16[256,8,128]{2,1,0:T(8,128)(2,1)} %scatter_fusion), calls=%async_computation.1 | async-start | bytes 1048576 | tf_op jit(solution)/shard_map/all_to_all | solution.py:156
  58.2 111.0 %reduce-scatter.2.cloned.1.call-start = ((), (), s32[]{:S(2)}) async-start(), calls=%async_computation.4 | async-start | bytes 122880 | tf_op jit(solution)/shard_map/reduce_scatter | solution.py:166
  90.3 22.1 %copy-start.60 = (f32[8,4,1,73]{3,2,0,1:T(1,128)S(1)}, f32[8,4,1,73]{3,2,0,1:T(1,128)}, u32[]{:S(2)}) copy-start(f32[8,4,1,73]{3,2,0,1:T(1,128)} %get-tuple-element.109) | copy-start | bytes 28036
  90.3 22.7 %copy-start.46 = (f32[8,4,1,73]{3,2,0,1:T(1,128)S(1)}, f32[8,4,1,73]{3,2,0,1:T(1,128)}, u32[]{:S(2)}) copy-start(f32[8,4,1,73]{3,2,0,1:T(1,128)} %get-tuple-element.89) | copy-start | bytes 28036
  90.3 23.3 %copy-start.58 = (f32[8,4,1,73]{3,2,0,1:T(1,128)S(1)}, f32[8,4,1,73]{3,2,0,1:T(1,128)}, u32[]{:S(2)}) copy-start(f32[8,4,1,73]{3,2,0,1:T(1,128)} %get-tuple-element.108) | copy-start | bytes 28036
  90.3 23.9 %copy-start.45 = (f32[8,4,1,73]{3,2,0,1:T(1,128)S(1)}, f32[8,4,1,73]{3,2,0,1:T(1,128)}, u32[]{:S(2)}) copy-start(f32[8,4,1,73]{3,2,0,1:T(1,128)} %get-tuple-element.88) | copy-start | bytes 28036
  90.3 24.5 %copy-start.56 = (f32[8,4,1,73]{3,2,0,1:T(1,128)S(1)}, f32[8,4,1,73]{3,2,0,1:T(1,128)}, u32[]{:S(2)}) copy-start(f32[8,4,1,73]{3,2,0,1:T(1,128)} %get-tuple-element.107) | copy-start | bytes 28036
  90.3 25.1 %copy-start.44 = (f32[8,4,1,73]{3,2,0,1:T(1,128)S(1)}, f32[8,4,1,73]{3,2,0,1:T(1,128)}, u32[]{:S(2)}) copy-start(f32[8,4,1,73]{3,2,0,1:T(1,128)} %get-tuple-element.87) | copy-start | bytes 28036
  90.3 25.7 %copy-start.54 = (f32[8,4,1,73]{3,2,0,1:T(1,128)S(1)}, f32[8,4,1,73]{3,2,0,1:T(1,128)}, u32[]{:S(2)}) copy-start(f32[8,4,1,73]{3,2,0,1:T(1,128)} %get-tuple-element.106) | copy-start | bytes 28036
  90.3 26.2 %copy-start.43 = (f32[8,4,1,73]{3,2,0,1:T(1,128)S(1)}, f32[8,4,1,73]{3,2,0,1:T(1,128)}, u32[]{:S(2)}) copy-start(f32[8,4,1,73]{3,2,0,1:T(1,128)} %get-tuple-element.86) | copy-start | bytes 28036
  90.4 26.8 %copy-start.52 = (f32[8,4,1,73]{3,2,0,1:T(1,128)S(1)}, f32[8,4,1,73]{3,2,0,1:T(1,128)}, u32[]{:S(2)}) copy-start(f32[8,4,1,73]{3,2,0,1:T(1,128)} %get-tuple-element.105) | copy-start | bytes 28036
  90.4 27.4 %copy-start.42 = (f32[8,4,1,73]{3,2,0,1:T(1,128)S(1)}, f32[8,4,1,73]{3,2,0,1:T(1,128)}, u32[]{:S(2)}) copy-start(f32[8,4,1,73]{3,2,0,1:T(1,128)} %get-tuple-element.85) | copy-start | bytes 28036
  90.4 28.0 %copy-start.50 = (f32[8,4,1,73]{3,2,0,1:T(1,128)S(1)}, f32[8,4,1,73]{3,2,0,1:T(1,128)}, u32[]{:S(2)}) copy-start(f32[8,4,1,73]{3,2,0,1:T(1,128)} %get-tuple-element.104) | copy-start | bytes 28036
  91.2 41.7 %collective-permute-start = (f32[8,4,15,128]{3,2,1,0:T(8,128)}, f32[8,4,15,128]{3,2,1,0:T(8,128)S(1)}, u32[]{:S(2)}, u32[]{:S(2)}) collective-permute-start(f32[8,4,15,128]{3,2,1,0:T(8,128)} %get-tuple-element.146), channel_id=1, source_target_pairs={{0,1},{1,2},{2,3},{3,4},{4,5},{5,6},{6,7},{7,8},{8,9},{9,10},{10,1... | collective-permute-start | bytes 737288 | tf_op jit(solution)/shard_map/ppermute | solution.py:23
  93.8 39.1 %collective-permute-start.1 = (f32[8,4,15,128]{3,2,1,0:T(8,128)}, f32[8,4,15,128]{3,2,1,0:T(8,128)S(1)}, u32[]{:S(2)}, u32[]{:S(2)}) collective-permute-start(f32[8,4,15,128]{3,2,1,0:T(8,128)} %get-tuple-element.147), channel_id=1, source_target_pairs={{1,0},{2,1},{3,2},{4,3},{5,4},{6,5},{7,6},{8,7},{9,8},{10,9},{11,1... | collective-permute-start | bytes 737288 | tf_op jit(solution)/shard_map/ppermute | solution.py:25
  143.7 36.1 %copy-start.82 = (bf16[64,3,3,3]{0,3,2,1:T(4,128)(2,1)S(1)}, bf16[64,3,3,3]{0,3,2,1:T(4,128)(2,1)}, u32[]{:S(2)}) copy-start(bf16[64,3,3,3]{0,3,2,1:T(4,128)(2,1)} %param.28) | copy-start | bytes 10372
  143.7 36.1 %copy-start.83 = (pred[8,17]{0,1:T(8,128)(4,1)S(1)}, pred[8,17]{0,1:T(8,128)(4,1)}, u32[]{:S(2)}) copy-start(pred[8,17]{0,1:T(8,128)(4,1)} %constant.78) | copy-start | bytes 412
  170.0 7.7 %collective-permute-start.2 = (bf16[1,3,1,128]{3,2,1,0:T(2,128)(2,1)S(1)}, bf16[1,3,1,128]{3,2,1,0:T(2,128)(2,1)S(1)}, u32[]{:S(2)}, u32[]{:S(2)}) collective-permute-start(bf16[1,3,1,128]{3,2,1,0:T(2,128)(2,1)S(1)} %get-tuple-element.148), channel_id=1, source_target_pairs={{0,1},{1,2},{2,3},{3,4},{4,5},{5,6},{6,7},{7,8},{8,9},{9,10},{10,1... | collective-permute-start | bytes 2312 | tf_op jit(solution)/shard_map/ppermute | solution.py:23
  171.9 7.0 %collective-permute-start.3 = (bf16[1,3,1,128]{3,2,1,0:T(2,128)(2,1)S(1)}, bf16[1,3,1,128]{3,2,1,0:T(2,128)(2,1)S(1)}, u32[]{:S(2)}, u32[]{:S(2)}) collective-permute-start(bf16[1,3,1,128]{3,2,1,0:T(2,128)(2,1)S(1)} %get-tuple-element.149), channel_id=1, source_target_pairs={{1,0},{2,1},{3,2},{4,3},{5,4},{6,5},{7,6},{8,7},{9,8},{10,9},{11,1... | collective-permute-start | bytes 2312 | tf_op jit(solution)/shard_map/ppermute | solution.py:25
  181.1 9.1 %collective-permute-start.4 = (bf16[1,64,1,128]{1,3,0,2:T(8,128)(2,1)S(1)}, bf16[1,64,1,128]{1,3,0,2:T(8,128)(2,1)S(1)}, u32[]{:S(2)}, u32[]{:S(2)}) collective-permute-start(bf16[1,64,1,128]{1,3,0,2:T(8,128)(2,1)S(1)} %slice_bitcast_fusion.3), channel_id=1, source_target_pairs={{0,1},{1,2},{2,3},{3,4},{4,5},{5,6},{6,7},{7,8},{8,9},{9,10},{10,1... | collective-permute-start | bytes 49160 | tf_op jit(solution)/shard_map/ppermute | solution.py:23
  183.7 7.6 %collective-permute-start.5 = (bf16[1,64,1,128]{1,3,0,2:T(8,128)(2,1)}, bf16[1,64,1,128]{1,3,0,2:T(8,128)(2,1)S(1)}, u32[]{:S(2)}, u32[]{:S(2)}) collective-permute-start(bf16[1,64,1,128]{1,3,0,2:T(8,128)(2,1)} %slice_bitcast_fusion.2), channel_id=1, source_target_pairs={{1,0},{2,1},{3,2},{4,3},{5,4},{6,5},{7,6},{8,7},{9,8},{10,9},{11,1... | collective-permute-start | bytes 49160 | tf_op jit(solution)/shard_map/ppermute | solution.py:25
  (70 other events, 560.7 us)
Sparse Core Ops, SparseCore 0:
  148.9 20.2 reduce-scatter.1
where the time goes:
time: 207 us; the launch traced here: 204 us
  local copies, waits for them, and re-layouts  62.1 us (30%)
  starting transfers between devices  44.1 us (21%)
  matrix products  34.4 us (17%)
  waiting for transfers between devices  33.5 us (16%)
  other arithmetic  15.1 us (7%)
  between operations  15 us (7%)
    mul x62, local copies, waits for them, and re-layouts, patch_blur(): out_re = out_re + (kr * xr - ki * xi)  30.8 us
    reduce_scatter x1, waiting for transfers between devices, per_device(): color = lax.psum_scatter(partial, 'wave', scatter_dimension=0, tiled=True)  20.4 us
    ppermute x3, starting transfers between devices, padded_2(): lax.ppermute(head, axis, [((i + 1) % count, i) for i in range(ends)])  16.9 us
    dot_general x2, matrix products, add_group(): jnp.einsum('ibh,ihp->ibp', part_energy, onehot, preferred_element_type=jn...  14.5 us
    scatter x1, local copies, waits for them, and re-layouts, per_device(): send_energy = jnp.zeros((tile_count * capacity, band_dev, hit_lanes), hit...  12.5 us
    all_to_all x1, starting transfers between devices, per_device(): lax.all_to_all(send_base, 'tile', split_axis=0, concat_axis=0, tiled=True)  7.62 us
    all_to_all x1, starting transfers between devices, per_device(): lax.all_to_all(send_spot, 'tile', split_axis=0, concat_axis=0, tiled=True)  7.38 us
    dot_general x2, matrix products, add_group(): jnp.einsum('ibjx,ijr->brx', window, placing, precision=lax.Precision.HIGH...  7.22 us
  transfers between devices with their start and end apart: 10, of which 5 were waited for; matrix products, arithmetic and copies ran while one was open for 29% of the time, Pallas kernels for 0%

commit v1 on v0

v1 whole, which is shorter than its diff:
```python
import functools

import jax
import jax.numpy as jnp
import numpy as np
from jax import lax
from jax.experimental import pallas as pl
from jax.sharding import PartitionSpec as P

ROWS_DEV = 16
W = 128
WIN = 4
K = 31
DFT_N = 144
LANE = 128
GROUP = 8


def padded_2(cells, sides, width):
    for axis, dim in sides:
        count = lax.axis_size(axis)
        ends = count - 1
        head = lax.slice_in_dim(cells, 0, width, axis=dim)
        tail = lax.slice_in_dim(cells, cells.shape[dim] - width, cells.shape[dim], axis=dim)
        cells = jnp.concatenate(
            [
                lax.ppermute(tail, axis, [(i, (i + 1) % count) for i in range(ends)]),
                cells,
                lax.ppermute(head, axis, [((i + 1) % count, i) for i in range(ends)]),
            ],
            axis=dim,
        )
    return cells


def conv_rows(image, weights):
    return lax.conv_general_dilated(
        image,
        weights,
        (1, 1),
        ((0, 0), (1, 1)),
        dimension_numbers=("NCHW", "OIHW", "NCHW"),
        preferred_element_type=jnp.float32,
    )


def dft_tables(width, side, radius):
    freqs = DFT_N // 2 + 1
    f = np.arange(freqs)[None, :]
    x = np.arange(width)[:, None]
    angle = 2 * np.pi * f * x / DFT_N
    forward = np.zeros((width, 2 * LANE))
    forward[:, :freqs] = np.cos(angle)
    forward[:, LANE : LANE + freqs] = -np.sin(angle)
    lag = (np.arange(side) - radius)[:, None]
    tap_angle = 2 * np.pi * f * lag / DFT_N
    taps = np.zeros((side, 2 * LANE))
    taps[:, :freqs] = np.cos(tap_angle)
    taps[:, LANE : LANE + freqs] = np.sin(tap_angle)
    weight = np.full((freqs,), 2.0)
    weight[0] = 1.0
    weight[-1] = 1.0
    back_angle = 2 * np.pi * np.arange(freqs)[:, None] * np.arange(width)[None, :] / DFT_N
    inverse = np.zeros((2 * LANE, width))
    inverse[:freqs] = weight[:, None] * np.cos(back_angle) / DFT_N
    inverse[LANE : LANE + freqs] = -weight[:, None] * np.sin(back_angle) / DFT_N
    return (
        forward.astype(np.float32),
        taps.astype(np.float32),
        inverse.astype(np.float32),
    )


def row_taps_kernel(spec_ref, kern_ref, out_ref):
    group = spec_ref.shape[0]
    side = kern_ref.shape[1]
    rows = out_ref.shape[1]

    def one(c, carry):
        acc_re = jnp.zeros((rows, LANE), jnp.float32)
        acc_im = jnp.zeros((rows, LANE), jnp.float32)
        for u in range(side):
            xr = spec_ref[c, pl.ds(u, rows), pl.ds(0, LANE)]
            xi = spec_ref[c, pl.ds(u, rows), pl.ds(LANE, LANE)]
            kr = kern_ref[c, pl.ds(u, 1), pl.ds(0, LANE)]
            ki = kern_ref[c, pl.ds(u, 1), pl.ds(LANE, LANE)]
            acc_re = acc_re + (kr * xr - ki * xi)
            acc_im = acc_im + (kr * xi + ki * xr)
        out_ref[c, :, pl.ds(0, LANE)] = acc_re
        out_ref[c, :, pl.ds(LANE, LANE)] = acc_im
        return carry

    lax.fori_loop(0, group, one, 0)


def row_taps(spec, kern, rows):
    channels, tall, both = spec.shape
    side = kern.shape[1]
    return pl.pallas_call(
        row_taps_kernel,
        out_shape=jax.ShapeDtypeStruct((channels, rows, both), jnp.float32),
        grid=(channels // GROUP,),
        in_specs=[
            pl.BlockSpec((GROUP, tall, both), lambda g: (g, 0, 0)),
            pl.BlockSpec((GROUP, side, both), lambda g: (g, 0, 0)),
        ],
        out_specs=pl.BlockSpec((GROUP, rows, both), lambda g: (g, 0, 0)),
    )(spec, kern)


def patch_blur(extended, psf_bank, psf_index, response, radius):
    band_dev, scenes, tall, width = extended.shape
    rows_dev = tall - 2 * radius
    side = 2 * radius + 1
    forward, taps, inverse = dft_tables(width, side, radius)
    hi = lax.Precision.HIGHEST
    chosen = psf_bank[psf_index[0, :, 0]].reshape(scenes, band_dev, side, side)
    chosen = chosen.transpose(1, 0, 2, 3).reshape(band_dev * scenes, side, side)
    spec = jnp.einsum(
        "cyx,xf->cyf", extended.reshape(band_dev * scenes, tall, width), forward, precision=hi
    )
    kern = jnp.einsum("cuv,vf->cuf", chosen, taps, precision=hi)
    out = row_taps(spec, kern, rows_dev).reshape(band_dev, scenes, rows_dev, -1)
    color = jnp.einsum("bsyf,bc->scyf", out, response, precision=hi)
    return jnp.einsum("scyf,fx->scyx", color, inverse, precision=hi)


def window_splat(got, scenes):
    band_dev = got.shape[1] - 2
    energy = got[:, :band_dev]
    field = got[:, band_dev].astype(jnp.int32)
    column = got[:, band_dev + 1].astype(jnp.int32)
    offset = field % WIN
    base = field[:, 0] // WIN
    rows = jnp.arange(WIN, dtype=jnp.int32)
    spread = jnp.where(
        offset[:, None, None, :] == rows[None, None, :, None],
        energy[:, :, None, :],
        jnp.zeros((), energy.dtype),
    )
    onehot = (column[:, :, None] == jnp.arange(W, dtype=jnp.int32)[None, None, :]).astype(
        energy.dtype
    )
    window = jnp.einsum("ibjh,ihc->ibjc", spread, onehot, preferred_element_type=jnp.float32)
    row_ids = jnp.arange(scenes * ROWS_DEV, dtype=jnp.int32)
    placing = (base[:, None, None] + rows[None, :, None] == row_ids[None, None, :]).astype(
        jnp.float32
    )
    total = jnp.einsum("ibjc,ijr->brc", window, placing, precision=lax.Precision.HIGHEST)
    return total.reshape(band_dev, scenes, ROWS_DEV, W)


def per_device(
    hit_energy,
    hit_spot,
    block_tile,
    block_count,
    block_scene,
    block_row,
    psf_bank,
    psf_index,
    response,
    conv_in,
    conv_out,
):
    tile_count = lax.axis_size("tile")
    wave_count = lax.axis_size("wave")
    block_dev, band_dev, hit_lanes = hit_energy.shape
    capacity = 2 * block_dev // tile_count
    scenes = psf_index.shape[1]
    lanes = lax.broadcasted_iota(jnp.int32, (block_dev, hit_lanes), 1)
    live = lanes < block_count[0][:, None]
    masked = jnp.where(live[:, None, :], hit_energy, jnp.zeros_like(hit_energy))
    base_row = block_scene[0] * ROWS_DEV + block_row[0]
    spot = hit_spot[0]
    field = base_row[:, None] * WIN + spot // W
    column = spot % W
    payload = jnp.concatenate(
        [
            masked,
            field.astype(hit_energy.dtype)[:, None, :],
            column.astype(hit_energy.dtype)[:, None, :],
        ],
        axis=1,
    )
    target = block_tile[0, :, 0]
    owners = (target[:, None] == jnp.arange(tile_count, dtype=jnp.int32)[None, :]).astype(jnp.int32)
    before = jnp.cumsum(owners, axis=0) - owners
    place = target * capacity + jnp.sum(before * owners, axis=1)
    slots = jnp.arange(tile_count * capacity, dtype=jnp.int32)
    select = (slots[:, None] == place[None, :]).astype(hit_energy.dtype)
    send = jnp.einsum(
        "pi,ibh->pbh", select, payload, preferred_element_type=jnp.float32
    ).astype(hit_energy.dtype)
    got = lax.all_to_all(send, "tile", split_axis=0, concat_axis=0, tiled=True)
    splat = window_splat(got, scenes)
    extended = padded_2(splat, (("tile", 2),), K // 2)
    wave_index = lax.axis_index("wave")
    my_response = lax.dynamic_slice_in_dim(response, wave_index * band_dev, band_dev, 0)
    partial = patch_blur(extended, psf_bank, psf_index, my_response, K // 2)
    color = lax.dynamic_index_in_dim(partial, wave_index, 0, keepdims=False)
    for step in range(1, wave_count):
        piece = lax.dynamic_index_in_dim(partial, (wave_index + step) % wave_count, 0, keepdims=False)
        color = color + lax.ppermute(
            piece, "wave", [(i, (i + step) % wave_count) for i in range(wave_count)]
        )
    sensor = color[None].astype(jnp.bfloat16)
    rimmed = padded_2(sensor, (("tile", 2),), 1)
    hidden = jax.nn.silu(conv_rows(rimmed, conv_in)).astype(jnp.bfloat16)
    hidden_rimmed = padded_2(hidden, (("tile", 2),), 1)
    return conv_rows(hidden_rimmed, conv_out).astype(jnp.bfloat16)


def solution(mesh):
    in_specs = (
        P("tile", "wave", None),
        P("wave", "tile", None),
        P("wave", "tile", None),
        P("wave", "tile"),
        P("wave", "tile"),
        P("wave", "tile"),
        P(None, "wave", None),
        P("tile", None, None),
        P(),
        P(),
        P(),
    )
    out_specs = P("wave", None, "tile", None)
    return jax.shard_map(
        per_device, mesh=mesh, in_specs=in_specs, out_specs=out_specs, check_vma=False
    )
```

time: 207 us -> 105 us (0.51); the launches traced: 204 us -> 105 us
  local copies, waits for them, and re-layouts: 62.1 us -> 11.8 us
  starting transfers between devices: 44.1 us -> 29.3 us
  between operations: 15 us -> 0.54 us
  matrix products: 34.4 us -> 21.5 us
  other arithmetic: 15.1 us -> 6.53 us
  Pallas kernels: 0 us -> 6.33 us
  waiting for transfers between devices: 33.5 us -> 28.9 us
    mul x62 -> x0, local copies, waits for them, and re-layouts: 30.8 us -> none  [patch_blur(): out_re = out_re + (kr * xr - ki * xi)]
    reduce_scatter x1 -> x0, waiting for transfers between devices: 20.4 us -> none  [per_device(): color = lax.psum_scatter(partial, 'wave', scatter_dimension=0, tiled=True)]
    scatter x3 -> x0, local copies, waits for them, and re-layouts: 15.3 us -> none  [the longest x1 12.5 us: per_device(): send_energy = jnp.zeros((tile_count * capacity, band_dev, hit_lanes), hit...]
    ppermute x3, waiting for transfers between devices: 0.01 us -> 14.6 us  [padded_2(): lax.ppermute(tail, axis, [(i, (i + 1) % count) for i in range(ends)])]
    all_to_all x3 -> x1, starting transfers between devices: 20.7 us -> 7.62 us  [per_device(): got = lax.all_to_all(send, 'tile', split_axis=0, concat_axis=0, tiled=True)]
    dot_general x12 -> x7, matrix products: 31.7 us -> 18.8 us  [the longest x1 7.54 us: window_splat(): jnp.einsum('ibjh,ihc->ibjc', spread, onehot, preferred_element_type=jnp.f...]
    ppermute x3, starting transfers between devices: 16.9 us -> 9.25 us  [padded_2(): lax.ppermute(head, axis, [((i + 1) % count, i) for i in range(ends)])]
    add x5 -> x2, other arithmetic: 7.89 us -> 0.67 us  [the longest x1 0.67 us: per_device(): place = target * capacity + jnp.sum(before * owners, axis=1)]
  transfers between devices with their start and end apart: 10 -> 10, of which waited for: 5 -> 6; matrix products, arithmetic and copies ran while one was open for 29% -> 7% of each run, Pallas kernels for 0% -> 0%
where the time goes in v1:
time: 105 us
  starting transfers between devices  29.3 us (28%)
  waiting for transfers between devices  28.9 us (28%)
  matrix products  21.5 us (20%)
  local copies, waits for them, and re-layouts  11.8 us (11%)
  other arithmetic  6.53 us (6%)
  Pallas kernels  6.33 us (6%)
    ppermute x3, waiting for transfers between devices, padded_2(): lax.ppermute(tail, axis, [(i, (i + 1) % count) for i in range(ends)])  14.6 us
    all_to_all x1, waiting for transfers between devices, per_device(): got = lax.all_to_all(send, 'tile', split_axis=0, concat_axis=0, tiled=True)  10.1 us
    ppermute x3, starting transfers between devices, padded_2(): lax.ppermute(head, axis, [((i + 1) % count, i) for i in range(ends)])  9.25 us
    all_to_all x1, starting transfers between devices, per_device(): got = lax.all_to_all(send, 'tile', split_axis=0, concat_axis=0, tiled=True)  7.62 us
    dot_general x1, matrix products, window_splat(): jnp.einsum('ibjh,ihc->ibjc', spread, onehot, preferred_element_type=jnp.f...  7.54 us
    ppermute x3, starting transfers between devices, padded_2(): lax.ppermute(tail, axis, [(i, (i + 1) % count) for i in range(ends)])  6.73 us
    pallas_call x1, Pallas kernels, row_taps(): pl.pallas_call(row_taps_kernel, out_shape=jax.ShapeDtypeStruct((channels,...  6.33 us
    ppermute x3, starting transfers between devices, per_device(): lax.ppermute(piece, 'wave', [(i, (i + step) % wave_count) for i in range(...  5.68 us
  transfers between devices with their start and end apart: 10, of which 6 were waited for; matrix products, arithmetic and copies ran while one was open for 7% of the time, Pallas kernels for 0%

profile of v1, /device:TPU:2, one launch (start us, length us, event | category | flops | bytes accessed | tf_op | source)
XLA Modules:
  0.0 104.8 jit_solution(15604020992659778524)
XLA Ops:
  6.3 1.5 %copy.79 = bf16[256,10,128]{2,1,0:T(8,128)(2,1)} copy(bf16[256,10,128]{2,0,1:T(8,128)(2,1)S(1)} %convolution_convert_fusion) | data formatting | bytes 1310720 | tf_op jit(solution)/shard_map/convert_element_type | solution.py:194
  7.7 7.6 %all-to-all-start = ((bf16[256,10,128]{2,1,0:T(8,128)(2,1)}), bf16[256,10,128]{2,1,0:T(8,128)(2,1)S(1)}, u32[]{:S(2)}, u32[]{:S(2)}) async-start(bf16[256,10,128]{2,1,0:T(8,128)(2,1)} %copy.79), calls=%async_computation | async-start | bytes 2097152 | tf_op jit(solution)/shard_map/all_to_all | solution.py:195
  16.0 1.4 %reshape.305 = f32[4,8,31,31]{3,2,1,0:T(8,128)} reshape(f32[4,8,961]{2,1,0:T(8,128)S(1)} %gather_fusion) | data formatting | bytes 246016 | tf_op jit(solution)/shard_map/reshape | solution.py:117
  17.4 2.2 %copy.81 = f32[8,4,31,31]{3,1,0,2:T(4,128)} copy(f32[8,4,31,31]{3,2,0,1:T(8,128)} %bitcast.126) | data formatting | bytes 246016 | tf_op jit(solution)/shard_map/transpose | solution.py:118
  19.6 10.1 %all-to-all-done = bf16[256,10,128]{2,1,0:T(8,128)(2,1)S(1)} async-done(((bf16[256,10,128]{2,1,0:T(8,128)(2,1)}), bf16[256,10,128]{2,1,0:T(8,128)(2,1)S(1)}, u32[]{:S(2)}, u32[]{:S(2)}) %all-to-all-start) | async-done | bytes 655392 | tf_op jit(solution)/shard_map/all_to_all | solution.py:195
  30.5 7.5 %fusion.1 = f32[256,8,4,128]{3,2,1,0:T(4,128)S(1)} fusion(s32[256,128]{1,0:T(8,128)S(1)} %bitcast.132, pred[256,4,128]{2,1,0:T(4,128)(4,1)S(1)} %iota_compare_fusion.3, bf16[256,8,128]{2,1,0:T(8,128)(2,1)S(1)} %slice.52), kind=kOutput, calls=%fused_computation.3 | convolution fusion | flops 273678336 | bytes 4980736 | tf_op jit(solution)/shard_map/ibjh,ihc->ibjc/dot_general | solution.py:144
  38.1 4.1 %fusion.4 = f32[64,8,128,1]{2,0,3,1:T(8,128)S(1)} fusion(f32[256,8,4,128]{3,2,1,0:T(4,128)S(1)} %fusion.1, s32[256,4]{0,1:T(4,128)S(1)} %iota_add_fusion), kind=kOutput, calls=%fused_computation.5 | convolution fusion | flops 805371904 | bytes 4460544 | tf_op jit(solution)/shard_map/ibjc,ijr->brc/dot_general | solution.py:149
  42.2 5.4 %collective-permute-start.1 = (f32[8,4,15,128]{3,2,1,0:T(8,128)S(1)}, f32[8,4,15,128]{3,2,1,0:T(8,128)S(1)}, u32[]{:S(2)}, u32[]{:S(2)}) collective-permute-start(f32[8,4,15,128]{3,2,1,0:T(8,128)S(1)} %get-tuple-element.10), channel_id=1, source_target_pairs={{1,0},{2,1},{3,2},{4,3},{5,4},{6,5},{7,6},{8,7},{9,8},{10,9},{11,1... | collective-permute-start | bytes 737288 | tf_op jit(solution)/shard_map/ppermute | solution.py:29
  47.6 1.9 %collective-permute-start = (f32[8,4,15,128]{3,2,1,0:T(8,128)S(1)}, f32[8,4,15,128]{3,2,1,0:T(8,128)S(1)}, u32[]{:S(2)}, u32[]{:S(2)}) collective-permute-start(f32[8,4,15,128]{3,2,1,0:T(8,128)S(1)} %get-tuple-element.9), channel_id=1, source_target_pairs={{0,1},{1,2},{2,3},{3,4},{4,5},{5,6},{6,7},{7,8},{8,9},{9,10},{10,1... | collective-permute-start | bytes 737288 | tf_op jit(solution)/shard_map/ppermute | solution.py:27
  49.6 2.1 %fusion.25.kern_ref = f32[32,31,256]{2,1,0:T(8,128)} fusion(f32[31,256,1]{1,0,2:T(8,128)S(1)} %copy-done.4, f32[32,31,31]{2,0,1:T(8,128)S(1)} %bitcast.125), kind=kOutput, calls=%fused_computation.34 | convolution fusion | flops 94470144 | bytes 1170560 | tf_op jit(solution)/shard_map/cuv,vf->cuf/dot_general | solution.py:122
  51.7 5.7 %collective-permute-done = f32[8,4,15,128]{3,2,1,0:T(8,128)S(1)} collective-permute-done((f32[8,4,15,128]{3,2,1,0:T(8,128)S(1)}, f32[8,4,15,128]{3,2,1,0:T(8,128)S(1)}, u32[]{:S(2)}, u32[]{:S(2)}) %collective-permute-start) | collective-permute-done | bytes 245792 | tf_op jit(solution)/shard_map/ppermute | solution.py:27
  57.4 2.5 %fusion.12.spec_ref = f32[32,46,256]{2,1,0:T(8,128)} fusion(f32[128,256,1]{1,0,2:T(8,128)S(1)} %copy-done.2, f32[32,15,128]{2,1,0:T(8,128)S(1)} %bitcast.130, f32[32,16,128]{2,1,0:T(8,128)S(1)} %bitcast.122, f32[32,15,128]{2,1,0:T(8,128)S(1)} %bitcast.131), kind=kOutput, calls=%fused_computation.19 | convolution fusion | flops 579190784 | bytes 2392064 | tf_op jit(solution)/shard_map/cyx,xf->cyf/dot_general | solution.py:119
  60.0 6.3 %shard_map.136 = f32[32,16,256]{2,1,0:T(8,128)} custom-call(f32[32,46,256]{2,1,0:T(8,128)} %fusion.12.spec_ref, f32[32,31,256]{2,1,0:T(8,128)} %fusion.25.kern_ref), custom_call_target="tpu_custom_call" | custom-call | tf_op jit(solution)/shard_map/pallas_call | solution.py:99
  66.3 1.9 %convolution_bitcast_fusion = f32[4,3,16,256]{3,1,2,0:T(4,128)S(1)} fusion(f32[8,4,16,256]{3,2,1,0:T(8,128)} %bitcast.127, f32[32,3]{0,1:T(4,128)S(1)} %copy-done.5, s32[]{:T(128)S(6)} %select_n.93), kind=kOutput, calls=%fused_computation.15 | convolution fusion | flops 4718592 | bytes 721284 | tf_op jit(solution)/shard_map/bsyf,bc->scyf/dot_general | solution.py:124
  68.6 4.4 %collective-permute-start.4 = (f32[3,16,128]{2,1,0:T(8,128)S(1)}, f32[3,16,128]{2,1,0:T(8,128)S(1)}, u32[]{:S(2)}, u32[]{:S(2)}) collective-permute-start(f32[3,16,128]{2,1,0:T(8,128)S(1)} %get-tuple-element.12), channel_id=1, source_target_pairs={{0,96},{32,0},{64,32},{96,64},{1,97},{33,1},{65,33},{97,65},{2,98}... | collective-permute-start | bytes 73736 | tf_op jit(solution)/shard_map/ppermute | solution.py:204
  74.5 3.8 %collective-permute-done.3 = f32[3,16,128]{2,1,0:T(8,128)S(1)} collective-permute-done((f32[3,16,128]{2,1,0:T(8,128)S(1)}, f32[3,16,128]{2,1,0:T(8,128)S(1)}, u32[]{:S(2)}, u32[]{:S(2)}) %collective-permute-start.3) | collective-permute-done | bytes 24608 | tf_op jit(solution)/shard_map/ppermute | solution.py:204
  78.3 1.9 %collective-permute-start.6 = (bf16[1,3,1,128]{3,2,1,0:T(2,128)(2,1)S(1)}, bf16[1,3,1,128]{3,2,1,0:T(2,128)(2,1)S(1)}, u32[]{:S(2)}, u32[]{:S(2)}) collective-permute-start(bf16[1,3,1,128]{3,2,1,0:T(2,128)(2,1)S(1)} %get-tuple-element.17), channel_id=1, source_target_pairs={{1,0},{2,1},{3,2},{4,3},{5,4},{6,5},{7,6},{8,7},{9,8},{10,9},{11,1... | collective-permute-start | bytes 2312 | tf_op jit(solution)/shard_map/ppermute | solution.py:29
  80.3 2.4 %collective-permute-start.5 = (bf16[1,3,1,128]{3,2,1,0:T(2,128)(2,1)S(1)}, bf16[1,3,1,128]{3,2,1,0:T(2,128)(2,1)S(1)}, u32[]{:S(2)}, u32[]{:S(2)}) collective-permute-start(bf16[1,3,1,128]{3,2,1,0:T(2,128)(2,1)S(1)} %get-tuple-element.16), channel_id=1, source_target_pairs={{0,1},{1,2},{2,3},{3,4},{4,5},{5,6},{6,7},{7,8},{8,9},{9,10},{10,1... | collective-permute-start | bytes 2312 | tf_op jit(solution)/shard_map/ppermute | solution.py:27
  82.7 4.6 %collective-permute-done.5 = bf16[1,3,1,128]{3,2,1,0:T(2,128)(2,1)S(1)} collective-permute-done((bf16[1,3,1,128]{3,2,1,0:T(2,128)(2,1)S(1)}, bf16[1,3,1,128]{3,2,1,0:T(2,128)(2,1)S(1)}, u32[]{:S(2)}, u32[]{:S(2)}) %collective-permute-start.5) | collective-permute-done | bytes 800 | tf_op jit(solution)/shard_map/ppermute | solution.py:27
  89.6 1.9 %collective-permute-start.8 = (bf16[1,64,1,128]{1,3,0,2:T(8,128)(2,1)S(1)}, bf16[1,64,1,128]{1,3,0,2:T(8,128)(2,1)S(1)}, u32[]{:S(2)}, u32[]{:S(2)}) collective-permute-start(bf16[1,64,1,128]{1,3,0,2:T(8,128)(2,1)S(1)} %slice_bitcast_fusion.2), channel_id=1, source_target_pairs={{1,0},{2,1},{3,2},{4,3},{5,4},{6,5},{7,6},{8,7},{9,8},{10,9},{11,1... | collective-permute-start | bytes 49160 | tf_op jit(solution)/shard_map/ppermute | solution.py:29
  91.5 2.4 %collective-permute-start.7 = (bf16[1,64,1,128]{1,3,0,2:T(8,128)(2,1)S(1)}, bf16[1,64,1,128]{1,3,0,2:T(8,128)(2,1)S(1)}, u32[]{:S(2)}, u32[]{:S(2)}) collective-permute-start(bf16[1,64,1,128]{1,3,0,2:T(8,128)(2,1)S(1)} %slice_bitcast_fusion.3), channel_id=1, source_target_pairs={{0,1},{1,2},{2,3},{3,4},{4,5},{5,6},{6,7},{7,8},{8,9},{9,10},{10,1... | collective-permute-start | bytes 49160 | tf_op jit(solution)/shard_map/ppermute | solution.py:27
  94.6 4.3 %collective-permute-done.7 = bf16[1,64,1,128]{1,3,0,2:T(8,128)(2,1)S(1)} collective-permute-done((bf16[1,64,1,128]{1,3,0,2:T(8,128)(2,1)S(1)}, bf16[1,64,1,128]{1,3,0,2:T(8,128)(2,1)S(1)}, u32[]{:S(2)}, u32[]{:S(2)}) %collective-permute-start.7) | collective-permute-done | bytes 16416 | tf_op jit(solution)/shard_map/ppermute | solution.py:27
  100.4 1.4 %reshape.319 = bf16[64,18,1,8,17]{0,4,3,1,2:T(8,128)(2,1)S(1)} reshape(bf16[64,18,1,136]{0,3,1,2:T(8,128)(2,1)} %pad.2.clone) | data formatting | bytes 626688 | tf_op jit(solution)/shard_map/conv_general_dilated | solution.py:37
  102.0 1.5 %fusion.9 = bf16[16,8,17,64]{3,1,2,0:T(8,128)(2,1)S(1)} fusion(bf16[64,64,3,3]{1,0,3,2:T(8,128)(2,1)S(1)} %copy-done.6, bf16[64,18,1,7,2]{0,3,4,1,2:T(8,128)(2,1)S(1)} %slice.64, bf16[64,18,1,8,17]{0,3,4,1,2:T(8,128)(2,1)S(1)} %copy.96, pred[8,17]{0,1:T(8,128)(4,1)S(1)} %copy-done.9), kind=kOutput, calls=%fused_computation.14 | convolution fusion | flops 161761280 | bytes 697992 | tf_op jit(solution)/shard_map/conv_general_dilated | solution.py:37
  (77 shorter events, 15.3 us)
Async XLA Ops:
  0.0 15.4 %copy-start = (f32[64,8,961]{2,1,0:T(8,128)S(1)}, f32[64,8,961]{2,1,0:T(8,128)}, u32[]{:S(2)}) copy-start(f32[64,8,961]{2,1,0:T(8,128)} %param.20) | copy-start | bytes 5904388
  6.2 9.1 %copy-start.8 = (s32[1,4,1]{1,2,0:T(1,128)S(1)}, s32[1,4,1]{1,2,0:T(1,128)}, u32[]{:S(2)}) copy-start(s32[1,4,1]{1,2,0:T(1,128)} %param.21) | copy-start | bytes 52
  7.7 22.0 %all-to-all-start = ((bf16[256,10,128]{2,1,0:T(8,128)(2,1)}), bf16[256,10,128]{2,1,0:T(8,128)(2,1)S(1)}, u32[]{:S(2)}, u32[]{:S(2)}) async-start(bf16[256,10,128]{2,1,0:T(8,128)(2,1)} %copy.79), calls=%async_computation | async-start | bytes 2097152 | tf_op jit(solution)/shard_map/all_to_all | solution.py:195
  38.0 11.5 %copy-start.1 = (f32[8,4,31,31]{3,1,0,2:T(4,128)S(1)}, f32[8,4,31,31]{3,1,0,2:T(4,128)}, u32[]{:S(2)}) copy-start(f32[8,4,31,31]{3,1,0,2:T(4,128)} %copy.81) | copy-start | bytes 369028
  38.1 11.5 %copy-start.4 = (f32[31,256,1]{1,0,2:T(8,128)S(1)}, f32[31,256,1]{1,0,2:T(8,128)}, u32[]{:S(2)}) copy-start(f32[31,256,1]{1,0,2:T(8,128)} %constant.134) | copy-start | bytes 95236
  42.1 15.3 %copy-start.2 = (f32[128,256,1]{1,0,2:T(8,128)S(1)}, f32[128,256,1]{1,0,2:T(8,128)}, u32[]{:S(2)}) copy-start(f32[128,256,1]{1,0,2:T(8,128)} %constant.133) | copy-start | bytes 393220
  42.2 9.5 %collective-permute-start.1 = (f32[8,4,15,128]{3,2,1,0:T(8,128)S(1)}, f32[8,4,15,128]{3,2,1,0:T(8,128)S(1)}, u32[]{:S(2)}, u32[]{:S(2)}) collective-permute-start(f32[8,4,15,128]{3,2,1,0:T(8,128)S(1)} %get-tuple-element.10), channel_id=1, source_target_pairs={{1,0},{2,1},{3,2},{4,3},{5,4},{6,5},{7,6},{8,7},{9,8},{10,9},{11,1... | collective-permute-start | bytes 737288 | tf_op jit(solution)/shard_map/ppermute | solution.py:29
  47.6 9.8 %collective-permute-start = (f32[8,4,15,128]{3,2,1,0:T(8,128)S(1)}, f32[8,4,15,128]{3,2,1,0:T(8,128)S(1)}, u32[]{:S(2)}, u32[]{:S(2)}) collective-permute-start(f32[8,4,15,128]{3,2,1,0:T(8,128)S(1)} %get-tuple-element.9), channel_id=1, source_target_pairs={{0,1},{1,2},{2,3},{3,4},{4,5},{5,6},{6,7},{7,8},{8,9},{9,10},{10,1... | collective-permute-start | bytes 737288 | tf_op jit(solution)/shard_map/ppermute | solution.py:27
  60.0 6.3 %copy-start.5 = (f32[32,3]{0,1:T(4,128)S(1)}, f32[32,3]{0,1:T(4,128)}, u32[]{:S(2)}) copy-start(f32[32,3]{0,1:T(4,128)} %param.22) | copy-start | bytes 1156
  60.0 8.2 %copy-start.3 = (f32[256,128,1,1]{1,0,3,2:T(8,128)S(1)}, f32[256,128,1,1]{1,0,3,2:T(8,128)}, u32[]{:S(2)}) copy-start(f32[256,128,1,1]{1,0,3,2:T(8,128)} %constant.135) | copy-start | bytes 393220
  66.3 21.9 %copy-start.7 = (bf16[64,3,3,3]{0,3,2,1:T(4,128)(2,1)S(1)}, bf16[64,3,3,3]{0,3,2,1:T(4,128)(2,1)}, u32[]{:S(2)}) copy-start(bf16[64,3,3,3]{0,3,2,1:T(4,128)(2,1)} %param.23) | copy-start | bytes 10372
  66.3 21.9 %copy-start.9 = (pred[8,17]{0,1:T(8,128)(4,1)S(1)}, pred[8,17]{0,1:T(8,128)(4,1)}, u32[]{:S(2)}) copy-start(pred[8,17]{0,1:T(8,128)(4,1)} %constant.131) | copy-start | bytes 412
  68.6 5.9 %collective-permute-start.4 = (f32[3,16,128]{2,1,0:T(8,128)S(1)}, f32[3,16,128]{2,1,0:T(8,128)S(1)}, u32[]{:S(2)}, u32[]{:S(2)}) collective-permute-start(f32[3,16,128]{2,1,0:T(8,128)S(1)} %get-tuple-element.12), channel_id=1, source_target_pairs={{0,96},{32,0},{64,32},{96,64},{1,97},{33,1},{65,33},{97,65},{2,98}... | collective-permute-start | bytes 73736 | tf_op jit(solution)/shard_map/ppermute | solution.py:204
  73.0 5.3 %collective-permute-start.3 = (f32[3,16,128]{2,1,0:T(8,128)S(1)}, f32[3,16,128]{2,1,0:T(8,128)S(1)}, u32[]{:S(2)}, u32[]{:S(2)}) collective-permute-start(f32[3,16,128]{2,1,0:T(8,128)S(1)} %get-tuple-element.13), channel_id=1, source_target_pairs={{0,64},{32,96},{64,0},{96,32},{1,65},{33,97},{65,1},{97,33},{2,66}... | collective-permute-start | bytes 73736 | tf_op jit(solution)/shard_map/ppermute | solution.py:204
  73.0 5.3 %collective-permute-start.2 = (f32[3,16,128]{2,1,0:T(8,128)S(1)}, f32[3,16,128]{2,1,0:T(8,128)S(1)}, u32[]{:S(2)}, u32[]{:S(2)}) collective-permute-start(f32[3,16,128]{2,1,0:T(8,128)S(1)} %get-tuple-element.11), channel_id=1, source_target_pairs={{0,32},{32,64},{64,96},{96,0},{1,33},{33,65},{65,97},{97,1},{2,34}... | collective-permute-start | bytes 73736 | tf_op jit(solution)/shard_map/ppermute | solution.py:204
  78.3 4.3 %collective-permute-start.6 = (bf16[1,3,1,128]{3,2,1,0:T(2,128)(2,1)S(1)}, bf16[1,3,1,128]{3,2,1,0:T(2,128)(2,1)S(1)}, u32[]{:S(2)}, u32[]{:S(2)}) collective-permute-start(bf16[1,3,1,128]{3,2,1,0:T(2,128)(2,1)S(1)} %get-tuple-element.17), channel_id=1, source_target_pairs={{1,0},{2,1},{3,2},{4,3},{5,4},{6,5},{7,6},{8,7},{9,8},{10,9},{11,1... | collective-permute-start | bytes 2312 | tf_op jit(solution)/shard_map/ppermute | solution.py:29
  80.3 7.0 %collective-permute-start.5 = (bf16[1,3,1,128]{3,2,1,0:T(2,128)(2,1)S(1)}, bf16[1,3,1,128]{3,2,1,0:T(2,128)(2,1)S(1)}, u32[]{:S(2)}, u32[]{:S(2)}) collective-permute-start(bf16[1,3,1,128]{3,2,1,0:T(2,128)(2,1)S(1)} %get-tuple-element.16), channel_id=1, source_target_pairs={{0,1},{1,2},{2,3},{3,4},{4,5},{5,6},{6,7},{7,8},{8,9},{9,10},{10,1... | collective-permute-start | bytes 2312 | tf_op jit(solution)/shard_map/ppermute | solution.py:27
  89.6 4.9 %collective-permute-start.8 = (bf16[1,64,1,128]{1,3,0,2:T(8,128)(2,1)S(1)}, bf16[1,64,1,128]{1,3,0,2:T(8,128)(2,1)S(1)}, u32[]{:S(2)}, u32[]{:S(2)}) collective-permute-start(bf16[1,64,1,128]{1,3,0,2:T(8,128)(2,1)S(1)} %slice_bitcast_fusion.2), channel_id=1, source_target_pairs={{1,0},{2,1},{3,2},{4,3},{5,4},{6,5},{7,6},{8,7},{9,8},{10,9},{11,1... | collective-permute-start | bytes 49160 | tf_op jit(solution)/shard_map/ppermute | solution.py:29
  91.5 7.3 %collective-permute-start.7 = (bf16[1,64,1,128]{1,3,0,2:T(8,128)(2,1)S(1)}, bf16[1,64,1,128]{1,3,0,2:T(8,128)(2,1)S(1)}, u32[]{:S(2)}, u32[]{:S(2)}) collective-permute-start(bf16[1,64,1,128]{1,3,0,2:T(8,128)(2,1)S(1)} %slice_bitcast_fusion.3), channel_id=1, source_target_pairs={{0,1},{1,2},{2,3},{3,4},{4,5},{5,6},{6,7},{7,8},{8,9},{9,10},{10,1... | collective-permute-start | bytes 49160 | tf_op jit(solution)/shard_map/ppermute | solution.py:27
  100.4 1.5 %copy-start.6 = (bf16[64,64,3,3]{1,0,3,2:T(8,128)(2,1)S(1)}, bf16[64,64,3,3]{1,0,3,2:T(8,128)(2,1)}, u32[]{:S(2)}) copy-start(bf16[64,64,3,3]{1,0,3,2:T(8,128)(2,1)} %param.24) | copy-start | bytes 221188

commit v2 on v1

--- a/solution.py
+++ b/solution.py
@@ -146,7 +146,12 @@
     placing = (base[:, None, None] + rows[None, :, None] == row_ids[None, None, :]).astype(
         jnp.float32
     )
-    total = jnp.einsum("ibjc,ijr->brc", window, placing, precision=lax.Precision.HIGHEST)
+    placing = placing.astype(jnp.bfloat16)
+    upper = window.astype(jnp.bfloat16)
+    lower = (window - upper.astype(jnp.float32)).astype(jnp.bfloat16)
+    total = jnp.einsum(
+        "ibjc,ijr->brc", upper, placing, preferred_element_type=jnp.float32
+    ) + jnp.einsum("ibjc,ijr->brc", lower, placing, preferred_element_type=jnp.float32)
     return total.reshape(band_dev, scenes, ROWS_DEV, W)
 
 
@@ -185,8 +190,11 @@
     )
     target = block_tile[0, :, 0]
     owners = (target[:, None] == jnp.arange(tile_count, dtype=jnp.int32)[None, :]).astype(jnp.int32)
-    before = jnp.cumsum(owners, axis=0) - owners
-    place = target * capacity + jnp.sum(before * owners, axis=1)
+    order = lax.broadcasted_iota(jnp.int32, (block_dev, block_dev), 0)
+    earlier = (order > order.T).astype(jnp.bfloat16)
+    before = jnp.dot(earlier, owners.astype(jnp.bfloat16), preferred_element_type=jnp.float32)
+    rank = jnp.sum(before * owners.astype(jnp.float32), axis=1).astype(jnp.int32)
+    place = target * capacity + rank
     slots = jnp.arange(tile_count * capacity, dtype=jnp.int32)
     select = (slots[:, None] == place[None, :]).astype(hit_energy.dtype)
     send = jnp.einsum(
@@ -205,10 +213,15 @@
             piece, "wave", [(i, (i + step) % wave_count) for i in range(wave_count)]
         )
     sensor = color[None].astype(jnp.bfloat16)
-    rimmed = padded_2(sensor, (("tile", 2),), 1)
+    rimmed = padded_2(sensor, (("tile", 2),), 2)
     hidden = jax.nn.silu(conv_rows(rimmed, conv_in)).astype(jnp.bfloat16)
-    hidden_rimmed = padded_2(hidden, (("tile", 2),), 1)
-    return conv_rows(hidden_rimmed, conv_out).astype(jnp.bfloat16)
+    tile_index = lax.axis_index("tile")
+    row_ids = lax.broadcasted_iota(jnp.int32, hidden.shape, 2)
+    outside = ((tile_index == 0) & (row_ids == 0)) | (
+        (tile_index == tile_count - 1) & (row_ids == hidden.shape[2] - 1)
+    )
+    hidden = jnp.where(outside, jnp.zeros_like(hidden), hidden)
+    return conv_rows(hidden, conv_out).astype(jnp.bfloat16)
 
 
 def solution(mesh):

time: 105 us -> 89.4 us (0.85)
  starting transfers between devices: 29.3 us -> 24.8 us
  waiting for transfers between devices: 28.9 us -> 24.4 us
  local copies, waits for them, and re-layouts: 11.8 us -> 8.19 us
  other arithmetic: 6.53 us -> 4.75 us
  matrix products: 21.5 us -> 20 us
    ppermute x3 -> x2, waiting for transfers between devices: 14.6 us -> 10.1 us  [padded_2(): lax.ppermute(tail, axis, [(i, (i + 1) % count) for i in range(ends)])]
    ppermute x3 -> x2, starting transfers between devices: 6.73 us -> 4.51 us  [padded_2(): lax.ppermute(tail, axis, [(i, (i + 1) % count) for i in range(ends)])]
    ppermute x3 -> x2, starting transfers between devices: 9.25 us -> 7.33 us  [padded_2(): lax.ppermute(head, axis, [((i + 1) % count, i) for i in range(ends)])]
    dot_general x1 -> x3, matrix products: 4.06 us -> 2.44 us  [the longest x1 0.89 us: per_device(): jnp.dot(earlier, owners.astype(jnp.bfloat16), preferred_element_type=jnp....]
    conv_general_dilated x6 -> x3, local copies, waits for them, and re-layouts: 2.28 us -> 0.82 us  [conv_rows(): lax.conv_general_dilated(image, weights, (1, 1), ((0, 0), (1, 1)), dimens...]
  transfers between devices with their start and end apart: 10 -> 8, of which waited for: 6 -> 5; matrix products, arithmetic and copies ran while one was open for 7% -> 7% of each run, Pallas kernels for 0% -> 0%
where the time goes in v2:
time: 89.4 us; the launch traced here: 88.8 us
  starting transfers between devices  24.8 us (28%)
  waiting for transfers between devices  24.4 us (27%)
  matrix products  20 us (22%)
  local copies, waits for them, and re-layouts  8.19 us (9%)
  Pallas kernels  6.31 us (7%)
  other arithmetic  4.75 us (5%)
    all_to_all x1, waiting for transfers between devices, per_device(): got = lax.all_to_all(send, 'tile', split_axis=0, concat_axis=0, tiled=True)  10.1 us
    ppermute x2, waiting for transfers between devices, padded_2(): lax.ppermute(tail, axis, [(i, (i + 1) % count) for i in range(ends)])  10.1 us
    all_to_all x1, starting transfers between devices, per_device(): got = lax.all_to_all(send, 'tile', split_axis=0, concat_axis=0, tiled=True)  7.62 us
    dot_general x1, matrix products, window_splat(): jnp.einsum('ibjh,ihc->ibjc', spread, onehot, preferred_element_type=jnp.f...  7.48 us
    ppermute x2, starting transfers between devices, padded_2(): lax.ppermute(head, axis, [((i + 1) % count, i) for i in range(ends)])  7.33 us
    pallas_call x1, Pallas kernels, row_taps(): pl.pallas_call(row_taps_kernel, out_shape=jax.ShapeDtypeStruct((channels,...  6.31 us
    ppermute x3, starting transfers between devices, per_device(): lax.ppermute(piece, 'wave', [(i, (i + step) % wave_count) for i in range(...  5.36 us
    ppermute x2, starting transfers between devices, padded_2(): lax.ppermute(tail, axis, [(i, (i + 1) % count) for i in range(ends)])  4.51 us
  transfers between devices with their start and end apart: 8, of which 5 were waited for; matrix products, arithmetic and copies ran while one was open for 7% of the time, Pallas kernels for 0%

profile of v2, /device:TPU:2, one launch (start us, length us, event | category | flops | bytes accessed | tf_op | source)
XLA Modules:
  0.0 88.8 jit_solution(5670247583865646948)
XLA Ops:
  3.1 0.9 %fusion.71 = (bf16[128,1,128]{2,0,1:T(8,128)(2,1)S(1)}, bf16[128,1,128]{2,0,1:T(8,128)(2,1)S(1)}) fusion(s32[1,128,128]{2,1,0:T(8,128)} %param.15, s32[128]{0:T(128)S(1)} %multiply_bitcast_fusion), kind=kLoop, calls=%fused_computation.87 | loop fusion | flops 360448 | bytes 131584 | tf_op jit(solution)/shard_map/convert_element_type | solution.py:186
  4.1 1.0 %copy_select_fusion = bf16[128,8,128]{2,0,1:T(8,128)(2,1)S(1)} fusion(bf16[128,8,128]{2,1,0:T(8,128)(2,1)} %param.14, pred[128,128]{1,0:T(8,128)(4,1)S(1)} %iota_compare_fusion.7), kind=kLoop, calls=%fused_computation.63 | loop fusion | flops 131072 | bytes 540672 | tf_op jit(solution)/shard_map/jit(_where)/select_n | solution.py:178
  5.4 1.5 %copy.60 = bf16[256,10,128]{2,1,0:T(8,128)(2,1)} copy(bf16[256,10,128]{2,0,1:T(8,128)(2,1)S(1)} %convolution_convert_fusion) | data formatting | bytes 1310720 | tf_op jit(solution)/shard_map/convert_element_type | solution.py:202
  6.9 7.6 %all-to-all-start = ((bf16[256,10,128]{2,1,0:T(8,128)(2,1)}), bf16[256,10,128]{2,1,0:T(8,128)(2,1)S(1)}, u32[]{:S(2)}, u32[]{:S(2)}) async-start(bf16[256,10,128]{2,1,0:T(8,128)(2,1)} %copy.60), calls=%async_computation | async-start | bytes 2097152 | tf_op jit(solution)/shard_map/all_to_all | solution.py:203
  15.1 1.4 %reshape.308 = f32[4,8,31,31]{3,2,1,0:T(8,128)} reshape(f32[4,8,961]{2,1,0:T(8,128)S(1)} %gather_fusion) | data formatting | bytes 246016 | tf_op jit(solution)/shard_map/reshape | solution.py:117
  16.6 2.2 %copy.63 = f32[8,4,31,31]{3,1,0,2:T(4,128)} copy(f32[8,4,31,31]{3,2,0,1:T(8,128)} %bitcast.125) | data formatting | bytes 246016 | tf_op jit(solution)/shard_map/transpose | solution.py:118
  18.8 10.1 %all-to-all-done = bf16[256,10,128]{2,1,0:T(8,128)(2,1)S(1)} async-done(((bf16[256,10,128]{2,1,0:T(8,128)(2,1)}), bf16[256,10,128]{2,1,0:T(8,128)(2,1)S(1)}, u32[]{:S(2)}, u32[]{:S(2)}) %all-to-all-start) | async-done | bytes 655392 | tf_op jit(solution)/shard_map/all_to_all | solution.py:203
  29.7 7.5 %subtract_convert_fusion = (bf16[256,8,4,128]{3,1,2,0:T(8,128)(2,1)S(1)}, bf16[256,8,4,128]{3,1,2,0:T(8,128)(2,1)S(1)}) fusion(s32[256,128]{1,0:T(8,128)S(1)} %bitcast.131, pred[256,4,128]{2,1,0:T(4,128)(4,1)S(1)} %iota_compare_fusion.4, bf16[256,8,128]{2,1,0:T(8,128)(2,1)S(1)} %slice.40), kind=kOutput, calls=%fused_computation.5 | convolution fusion | flops 277872640 | bytes 4980736 | tf_op jit(solution)/shard_map/ibjh,ihc->ibjc/dot_general | solution.py:144
  38.8 5.4 %collective-permute-start.1 = (f32[8,4,15,128]{3,2,1,0:T(8,128)S(1)}, f32[8,4,15,128]{3,2,1,0:T(8,128)S(1)}, u32[]{:S(2)}, u32[]{:S(2)}) collective-permute-start(f32[8,4,15,128]{3,2,1,0:T(8,128)S(1)} %get-tuple-element.12), channel_id=1, source_target_pairs={{1,0},{2,1},{3,2},{4,3},{5,4},{6,5},{7,6},{8,7},{9,8},{10,9},{11,1... | collective-permute-start | bytes 737288 | tf_op jit(solution)/shard_map/ppermute | solution.py:29
  44.2 1.9 %collective-permute-start = (f32[8,4,15,128]{3,2,1,0:T(8,128)S(1)}, f32[8,4,15,128]{3,2,1,0:T(8,128)S(1)}, u32[]{:S(2)}, u32[]{:S(2)}) collective-permute-start(f32[8,4,15,128]{3,2,1,0:T(8,128)S(1)} %get-tuple-element.11), channel_id=1, source_target_pairs={{0,1},{1,2},{2,3},{3,4},{4,5},{5,6},{6,7},{7,8},{8,9},{9,10},{10,1... | collective-permute-start | bytes 737288 | tf_op jit(solution)/shard_map/ppermute | solution.py:27
  46.1 2.1 %fusion.44.kern_ref = f32[32,31,256]{2,1,0:T(8,128)} fusion(f32[31,256,1]{1,0,2:T(8,128)S(1)} %copy-done.4, f32[32,31,31]{2,0,1:T(8,128)S(1)} %bitcast.124), kind=kOutput, calls=%fused_computation.48 | convolution fusion | flops 94470144 | bytes 1170560 | tf_op jit(solution)/shard_map/cuv,vf->cuf/dot_general | solution.py:122
  48.3 5.7 %collective-permute-done = f32[8,4,15,128]{3,2,1,0:T(8,128)S(1)} collective-permute-done((f32[8,4,15,128]{3,2,1,0:T(8,128)S(1)}, f32[8,4,15,128]{3,2,1,0:T(8,128)S(1)}, u32[]{:S(2)}, u32[]{:S(2)}) %collective-permute-start) | collective-permute-done | bytes 245792 | tf_op jit(solution)/shard_map/ppermute | solution.py:27
  54.0 2.6 %fusion.27.spec_ref = f32[32,46,256]{2,1,0:T(8,128)} fusion(f32[128,256,1]{1,0,2:T(8,128)S(1)} %copy-done.2, f32[32,15,128]{2,1,0:T(8,128)S(1)} %bitcast.129, f32[32,16,128]{2,1,0:T(8,128)S(1)} %bitcast.122, f32[32,15,128]{2,1,0:T(8,128)S(1)} %bitcast.130), kind=kOutput, calls=%fused_computation.31 | convolution fusion | flops 579190784 | bytes 2392064 | tf_op jit(solution)/shard_map/cyx,xf->cyf/dot_general | solution.py:119
  56.6 6.3 %shard_map.136 = f32[32,16,256]{2,1,0:T(8,128)} custom-call(f32[32,46,256]{2,1,0:T(8,128)} %fusion.27.spec_ref, f32[32,31,256]{2,1,0:T(8,128)} %fusion.44.kern_ref), custom_call_target="tpu_custom_call" | custom-call | tf_op jit(solution)/shard_map/pallas_call | solution.py:99
  62.9 1.9 %convolution_bitcast_fusion = f32[4,3,16,256]{3,1,2,0:T(4,128)S(1)} fusion(f32[8,4,16,256]{3,2,1,0:T(8,128)} %bitcast.126, f32[32,3]{0,1:T(4,128)S(1)} %copy-done.5, s32[]{:T(128)S(6)} %select_n.97), kind=kOutput, calls=%fused_computation.22 | convolution fusion | flops 4718592 | bytes 721284 | tf_op jit(solution)/shard_map/bsyf,bc->scyf/dot_general | solution.py:124
  65.1 4.1 %collective-permute-start.4 = (f32[3,16,128]{2,1,0:T(8,128)S(1)}, f32[3,16,128]{2,1,0:T(8,128)S(1)}, u32[]{:S(2)}, u32[]{:S(2)}) collective-permute-start(f32[3,16,128]{2,1,0:T(8,128)S(1)} %get-tuple-element.14), channel_id=1, source_target_pairs={{0,96},{32,0},{64,32},{96,64},{1,97},{33,1},{65,33},{97,65},{2,98}... | collective-permute-start | bytes 73736 | tf_op jit(solution)/shard_map/ppermute | solution.py:212
  69.2 1.3 %collective-permute-start.2 = (f32[3,16,128]{2,1,0:T(8,128)S(1)}, f32[3,16,128]{2,1,0:T(8,128)S(1)}, u32[]{:S(2)}, u32[]{:S(2)}) collective-permute-start(f32[3,16,128]{2,1,0:T(8,128)S(1)} %get-tuple-element.13), channel_id=1, source_target_pairs={{0,32},{32,64},{64,96},{96,0},{1,33},{33,65},{65,97},{97,1},{2,34}... | collective-permute-start | bytes 73736 | tf_op jit(solution)/shard_map/ppermute | solution.py:212
  70.7 3.8 %collective-permute-done.3 = f32[3,16,128]{2,1,0:T(8,128)S(1)} collective-permute-done((f32[3,16,128]{2,1,0:T(8,128)S(1)}, f32[3,16,128]{2,1,0:T(8,128)S(1)}, u32[]{:S(2)}, u32[]{:S(2)}) %collective-permute-start.3) | collective-permute-done | bytes 24608 | tf_op jit(solution)/shard_map/ppermute | solution.py:212
  74.6 1.9 %collective-permute-start.6 = (bf16[1,3,2,128]{3,2,1,0:T(2,128)(2,1)S(1)}, bf16[1,3,2,128]{3,2,1,0:T(2,128)(2,1)S(1)}, u32[]{:S(2)}, u32[]{:S(2)}) collective-permute-start(bf16[1,3,2,128]{3,2,1,0:T(2,128)(2,1)S(1)} %get-tuple-element.19), channel_id=1, source_target_pairs={{1,0},{2,1},{3,2},{4,3},{5,4},{6,5},{7,6},{8,7},{9,8},{10,9},{11,1... | collective-permute-start | bytes 4616 | tf_op jit(solution)/shard_map/ppermute | solution.py:29
  76.5 2.6 %collective-permute-start.5 = (bf16[1,3,2,128]{3,2,1,0:T(2,128)(2,1)S(1)}, bf16[1,3,2,128]{3,2,1,0:T(2,128)(2,1)S(1)}, u32[]{:S(2)}, u32[]{:S(2)}) collective-permute-start(bf16[1,3,2,128]{3,2,1,0:T(2,128)(2,1)S(1)} %get-tuple-element.18), channel_id=1, source_target_pairs={{0,1},{1,2},{2,3},{3,4},{4,5},{5,6},{6,7},{7,8},{8,9},{9,10},{10,1... | collective-permute-start | bytes 4616 | tf_op jit(solution)/shard_map/ppermute | solution.py:27
  79.1 4.4 %collective-permute-done.5 = bf16[1,3,2,128]{3,2,1,0:T(2,128)(2,1)S(1)} collective-permute-done((bf16[1,3,2,128]{3,2,1,0:T(2,128)(2,1)S(1)}, bf16[1,3,2,128]{3,2,1,0:T(2,128)(2,1)S(1)}, u32[]{:S(2)}, u32[]{:S(2)}) %collective-permute-start.5) | collective-permute-done | bytes 1568 | tf_op jit(solution)/shard_map/ppermute | solution.py:27
  84.5 1.4 %fusion.26 = bf16[18,1,8,17,64]{4,2,3,0,1:T(8,128)(2,1)S(1)} fusion(pred[18]{0:T(512)(128)(4,1)S(1)} %and_or_fusion, pred[8,17]{0,1:T(8,128)(4,1)S(1)} %copy-done.9, bf16[3,20,1,7,2]{3,0,4,1,2:T(4,128)(2,1)S(1)} %slice.46, bf16[3,20,1,8,17]{3,0,4,1,2:T(4,128)(2,1)S(1)} %copy.68, bf16[64,3,3,3]{0,3,2,1:T(4,128)(2,1)S(1)} %copy-done.7), kind=kOutput, calls=%fused_computation.30 | convolution fusion | flops 9768384 | bytes 334954 | tf_op jit(solution)/shard_map/conv_general_dilated | solution.py:37
  86.0 1.5 %convolution_convert_fusion.1 = bf16[16,8,17,64]{3,1,2,0:T(8,128)(2,1)S(1)} fusion(bf16[64,64,3,3]{1,0,3,2:T(8,128)(2,1)S(1)} %copy-done.6, bf16[18,1,7,1,64]{4,2,3,0,1:T(8,128)(2,1)S(1)} %get-tuple-element.10, bf16[18,1,7,1,64]{4,2,3,0,1:T(8,128)(2,1)S(1)} %get-tuple-element.9, bf16[18,1,8,17,64]{4,2,3,0,1:T(8,128)(2,1)S(1)} %fusion.26), kind=kOutput, calls=%fused_computation.18 | convolution fusion | flops 162322432 | bytes 697856 | tf_op jit(solution)/shard_map/conv_general_dilated | solution.py:37
  87.5 1.3 %copy.71 = bf16[1,64,16,128]{3,2,1,0:T(8,128)(2,1)} copy(bf16[1,64,16,128]{1,2,3,0:T(8,128)(2,1)S(1)} %slice_bitcast_fusion) | data formatting | bytes 524288 | tf_op jit(solution)/shard_map/convert_element_type | solution.py:224
  (56 shorter events, 8.0 us)
Async XLA Ops:
  0.0 14.6 %copy-start = (f32[64,8,961]{2,1,0:T(8,128)S(1)}, f32[64,8,961]{2,1,0:T(8,128)}, u32[]{:S(2)}) copy-start(f32[64,8,961]{2,1,0:T(8,128)} %param.20) | copy-start | bytes 5904388
  5.4 9.2 %copy-start.8 = (s32[1,4,1]{1,2,0:T(1,128)S(1)}, s32[1,4,1]{1,2,0:T(1,128)}, u32[]{:S(2)}) copy-start(s32[1,4,1]{1,2,0:T(1,128)} %param.21) | copy-start | bytes 52
  6.9 22.0 %all-to-all-start = ((bf16[256,10,128]{2,1,0:T(8,128)(2,1)}), bf16[256,10,128]{2,1,0:T(8,128)(2,1)S(1)}, u32[]{:S(2)}, u32[]{:S(2)}) async-start(bf16[256,10,128]{2,1,0:T(8,128)(2,1)} %copy.60), calls=%async_computation | async-start | bytes 2097152 | tf_op jit(solution)/shard_map/all_to_all | solution.py:203
  37.9 8.2 %copy-start.1 = (f32[8,4,31,31]{3,1,0,2:T(4,128)S(1)}, f32[8,4,31,31]{3,1,0,2:T(4,128)}, u32[]{:S(2)}) copy-start(f32[8,4,31,31]{3,1,0,2:T(4,128)} %copy.63) | copy-start | bytes 369028
  37.9 8.2 %copy-start.4 = (f32[31,256,1]{1,0,2:T(8,128)S(1)}, f32[31,256,1]{1,0,2:T(8,128)}, u32[]{:S(2)}) copy-start(f32[31,256,1]{1,0,2:T(8,128)} %constant.140) | copy-start | bytes 95236
  37.9 16.1 %copy-start.2 = (f32[128,256,1]{1,0,2:T(8,128)S(1)}, f32[128,256,1]{1,0,2:T(8,128)}, u32[]{:S(2)}) copy-start(f32[128,256,1]{1,0,2:T(8,128)} %constant.139) | copy-start | bytes 393220
  38.8 9.5 %collective-permute-start.1 = (f32[8,4,15,128]{3,2,1,0:T(8,128)S(1)}, f32[8,4,15,128]{3,2,1,0:T(8,128)S(1)}, u32[]{:S(2)}, u32[]{:S(2)}) collective-permute-start(f32[8,4,15,128]{3,2,1,0:T(8,128)S(1)} %get-tuple-element.12), channel_id=1, source_target_pairs={{1,0},{2,1},{3,2},{4,3},{5,4},{6,5},{7,6},{8,7},{9,8},{10,9},{11,1... | collective-permute-start | bytes 737288 | tf_op jit(solution)/shard_map/ppermute | solution.py:29
  44.2 9.8 %collective-permute-start = (f32[8,4,15,128]{3,2,1,0:T(8,128)S(1)}, f32[8,4,15,128]{3,2,1,0:T(8,128)S(1)}, u32[]{:S(2)}, u32[]{:S(2)}) collective-permute-start(f32[8,4,15,128]{3,2,1,0:T(8,128)S(1)} %get-tuple-element.11), channel_id=1, source_target_pairs={{0,1},{1,2},{2,3},{3,4},{4,5},{5,6},{6,7},{7,8},{8,9},{9,10},{10,1... | collective-permute-start | bytes 737288 | tf_op jit(solution)/shard_map/ppermute | solution.py:27
  56.6 6.3 %copy-start.5 = (f32[32,3]{0,1:T(4,128)S(1)}, f32[32,3]{0,1:T(4,128)}, u32[]{:S(2)}) copy-start(f32[32,3]{0,1:T(4,128)} %param.22) | copy-start | bytes 1156
  56.6 8.2 %copy-start.3 = (f32[256,128,1,1]{1,0,3,2:T(8,128)S(1)}, f32[256,128,1,1]{1,0,3,2:T(8,128)}, u32[]{:S(2)}) copy-start(f32[256,128,1,1]{1,0,3,2:T(8,128)} %constant.141) | copy-start | bytes 393220
  56.6 27.9 %copy-start.7 = (bf16[64,3,3,3]{0,3,2,1:T(4,128)(2,1)S(1)}, bf16[64,3,3,3]{0,3,2,1:T(4,128)(2,1)}, u32[]{:S(2)}) copy-start(bf16[64,3,3,3]{0,3,2,1:T(4,128)(2,1)} %param.23) | copy-start | bytes 10372
  56.6 27.9 %copy-start.9 = (pred[8,17]{0,1:T(8,128)(4,1)S(1)}, pred[8,17]{0,1:T(8,128)(4,1)}, u32[]{:S(2)}) copy-start(pred[8,17]{0,1:T(8,128)(4,1)} %constant.137) | copy-start | bytes 412
  65.1 5.6 %collective-permute-start.4 = (f32[3,16,128]{2,1,0:T(8,128)S(1)}, f32[3,16,128]{2,1,0:T(8,128)S(1)}, u32[]{:S(2)}, u32[]{:S(2)}) collective-permute-start(f32[3,16,128]{2,1,0:T(8,128)S(1)} %get-tuple-element.14), channel_id=1, source_target_pairs={{0,96},{32,0},{64,32},{96,64},{1,97},{33,1},{65,33},{97,65},{2,98}... | collective-permute-start | bytes 73736 | tf_op jit(solution)/shard_map/ppermute | solution.py:212
  69.2 5.3 %collective-permute-start.3 = (f32[3,16,128]{2,1,0:T(8,128)S(1)}, f32[3,16,128]{2,1,0:T(8,128)S(1)}, u32[]{:S(2)}, u32[]{:S(2)}) collective-permute-start(f32[3,16,128]{2,1,0:T(8,128)S(1)} %get-tuple-element.15), channel_id=1, source_target_pairs={{0,64},{32,96},{64,0},{96,32},{1,65},{33,97},{65,1},{97,33},{2,66}... | collective-permute-start | bytes 73736 | tf_op jit(solution)/shard_map/ppermute | solution.py:212
  69.2 5.3 %collective-permute-start.2 = (f32[3,16,128]{2,1,0:T(8,128)S(1)}, f32[3,16,128]{2,1,0:T(8,128)S(1)}, u32[]{:S(2)}, u32[]{:S(2)}) collective-permute-start(f32[3,16,128]{2,1,0:T(8,128)S(1)} %get-tuple-element.13), channel_id=1, source_target_pairs={{0,32},{32,64},{64,96},{96,0},{1,33},{33,65},{65,97},{97,1},{2,34}... | collective-permute-start | bytes 73736 | tf_op jit(solution)/shard_map/ppermute | solution.py:212
  74.6 4.5 %collective-permute-start.6 = (bf16[1,3,2,128]{3,2,1,0:T(2,128)(2,1)S(1)}, bf16[1,3,2,128]{3,2,1,0:T(2,128)(2,1)S(1)}, u32[]{:S(2)}, u32[]{:S(2)}) collective-permute-start(bf16[1,3,2,128]{3,2,1,0:T(2,128)(2,1)S(1)} %get-tuple-element.19), channel_id=1, source_target_pairs={{1,0},{2,1},{3,2},{4,3},{5,4},{6,5},{7,6},{8,7},{9,8},{10,9},{11,1... | collective-permute-start | bytes 4616 | tf_op jit(solution)/shard_map/ppermute | solution.py:29
  76.5 7.0 %collective-permute-start.5 = (bf16[1,3,2,128]{3,2,1,0:T(2,128)(2,1)S(1)}, bf16[1,3,2,128]{3,2,1,0:T(2,128)(2,1)S(1)}, u32[]{:S(2)}, u32[]{:S(2)}) collective-permute-start(bf16[1,3,2,128]{3,2,1,0:T(2,128)(2,1)S(1)} %get-tuple-element.18), channel_id=1, source_target_pairs={{0,1},{1,2},{2,3},{3,4},{4,5},{5,6},{6,7},{7,8},{8,9},{9,10},{10,1... | collective-permute-start | bytes 4616 | tf_op jit(solution)/shard_map/ppermute | solution.py:27
  84.5 1.5 %copy-start.6 = (bf16[64,64,3,3]{1,0,3,2:T(8,128)(2,1)S(1)}, bf16[64,64,3,3]{1,0,3,2:T(8,128)(2,1)}, u32[]{:S(2)}) copy-start(bf16[64,64,3,3]{1,0,3,2:T(8,128)(2,1)} %param.24) | copy-start | bytes 221188

commit v3 on v2

--- a/solution.py
+++ b/solution.py
@@ -108,21 +108,27 @@
     )(spec, kern)
 
 
-def patch_blur(extended, psf_bank, psf_index, response, radius):
+def kernel_spectra(psf_bank, psf_index, radius):
+    scenes = psf_index.shape[1]
+    band_dev = psf_bank.shape[1]
+    side = 2 * radius + 1
+    unused, taps, unused_too = dft_tables(W, side, radius)
+    chosen = psf_bank[psf_index[0, :, 0]].reshape(scenes, band_dev, side, side)
+    return jnp.einsum("sbuv,vf->sbuf", chosen, taps, precision=lax.Precision.HIGHEST)
+
+
+def scene_blur(extended, kern, response, scene, radius):
     band_dev, scenes, tall, width = extended.shape
     rows_dev = tall - 2 * radius
     side = 2 * radius + 1
-    forward, taps, inverse = dft_tables(width, side, radius)
+    forward, unused, inverse = dft_tables(width, side, radius)
     hi = lax.Precision.HIGHEST
-    chosen = psf_bank[psf_index[0, :, 0]].reshape(scenes, band_dev, side, side)
-    chosen = chosen.transpose(1, 0, 2, 3).reshape(band_dev * scenes, side, side)
-    spec = jnp.einsum(
-        "cyx,xf->cyf", extended.reshape(band_dev * scenes, tall, width), forward, precision=hi
-    )
-    kern = jnp.einsum("cuv,vf->cuf", chosen, taps, precision=hi)
-    out = row_taps(spec, kern, rows_dev).reshape(band_dev, scenes, rows_dev, -1)
-    color = jnp.einsum("bsyf,bc->scyf", out, response, precision=hi)
-    return jnp.einsum("scyf,fx->scyx", color, inverse, precision=hi)
+    plane = lax.dynamic_index_in_dim(extended, scene, 1, keepdims=False)
+    taps = lax.dynamic_index_in_dim(kern, scene, 0, keepdims=False)
+    spec = jnp.einsum("byx,xf->byf", plane, forward, precision=hi)
+    out = row_taps(spec, taps, rows_dev)
+    color = jnp.einsum("byf,bc->cyf", out, response, precision=hi)
+    return jnp.einsum("cyf,fx->cyx", color, inverse, precision=hi)
 
 
 def window_splat(got, scenes):
@@ -146,12 +152,7 @@
     placing = (base[:, None, None] + rows[None, :, None] == row_ids[None, None, :]).astype(
         jnp.float32
     )
-    placing = placing.astype(jnp.bfloat16)
-    upper = window.astype(jnp.bfloat16)
-    lower = (window - upper.astype(jnp.float32)).astype(jnp.bfloat16)
-    total = jnp.einsum(
-        "ibjc,ijr->brc", upper, placing, preferred_element_type=jnp.float32
-    ) + jnp.einsum("ibjc,ijr->brc", lower, placing, preferred_element_type=jnp.float32)
+    total = jnp.einsum("ibjc,ijr->brc", window, placing, precision=lax.Precision.HIGH)
     return total.reshape(band_dev, scenes, ROWS_DEV, W)
 
 
@@ -200,21 +201,26 @@
     send = jnp.einsum(
         "pi,ibh->pbh", select, payload, preferred_element_type=jnp.float32
     ).astype(hit_energy.dtype)
+    kern = kernel_spectra(psf_bank, psf_index, K // 2)
     got = lax.all_to_all(send, "tile", split_axis=0, concat_axis=0, tiled=True)
     splat = window_splat(got, scenes)
     extended = padded_2(splat, (("tile", 2),), K // 2)
     wave_index = lax.axis_index("wave")
     my_response = lax.dynamic_slice_in_dim(response, wave_index * band_dev, band_dev, 0)
-    partial = patch_blur(extended, psf_bank, psf_index, my_response, K // 2)
-    color = lax.dynamic_index_in_dim(partial, wave_index, 0, keepdims=False)
-    for step in range(1, wave_count):
-        piece = lax.dynamic_index_in_dim(partial, (wave_index + step) % wave_count, 0, keepdims=False)
-        color = color + lax.ppermute(
-            piece, "wave", [(i, (i + step) % wave_count) for i in range(wave_count)]
-        )
-    sensor = color[None].astype(jnp.bfloat16)
+    color = None
+    for step in list(range(1, wave_count)) + [0]:
+        scene = (wave_index + step) % wave_count
+        piece = scene_blur(extended, kern, my_response, scene, K // 2)
+        if step:
+            piece = lax.ppermute(
+                piece, "wave", [(i, (i + step) % wave_count) for i in range(wave_count)]
+            )
+        color = piece if color is None else color + piece
+    sensor = lax.reduce_precision(color[None], exponent_bits=8, mantissa_bits=7)
+    sensor = sensor.astype(jnp.bfloat16)
     rimmed = padded_2(sensor, (("tile", 2),), 2)
-    hidden = jax.nn.silu(conv_rows(rimmed, conv_in)).astype(jnp.bfloat16)
+    hidden = jax.nn.silu(conv_rows(rimmed, conv_in))
+    hidden = lax.reduce_precision(hidden, exponent_bits=8, mantissa_bits=7).astype(jnp.bfloat16)
     tile_index = lax.axis_index("tile")
     row_ids = lax.broadcasted_iota(jnp.int32, hidden.shape, 2)
     outside = ((tile_index == 0) & (row_ids == 0)) | (

time: 89.4 us -> 102 us (1.14)
  matrix products: 20 us -> 26.4 us
  Pallas kernels: 6.31 us -> 11.3 us
  waiting for transfers between devices: 24.4 us -> 23 us
  other arithmetic: 4.75 us -> 5.85 us
    dot_general x6 -> x14, matrix products: 8.4 us -> 14.8 us  [the longest x4 4.92 us: scene_blur(): color = jnp.einsum('byf,bc->cyf', out, response, precision=hi)]
    pallas_call x1 -> x4, Pallas kernels: 6.31 us -> 11.3 us  [row_taps(): pl.pallas_call(row_taps_kernel, out_shape=jax.ShapeDtypeStruct((channels,...]
    ppermute x3, waiting for transfers between devices: 4.07 us -> 0.01 us  [per_device(): lax.ppermute(piece, 'wave', [(i, (i + step) % wave_count) for i in range(...]
    all_to_all x1, waiting for transfers between devices: 10.1 us -> 12.4 us  [per_device(): got = lax.all_to_all(send, 'tile', split_axis=0, concat_axis=0, tiled=True)]
    transpose x1 -> x0, local copies, waits for them, and re-layouts: 2.19 us -> none  [patch_blur(): chosen = chosen.transpose(1, 0, 2, 3).reshape(band_dev * scenes, side, side)]
    concatenate x1 -> x2, other arithmetic: 0.01 us -> 1.12 us  [padded_2(): jnp.concatenate([lax.ppermute(tail, axis, [(i, (i + 1) % count) for i in...]
  transfers between devices with their start and end apart: 8 -> 8, of which waited for: 5 -> 4; matrix products, arithmetic and copies ran while one was open for 7% -> 8% of each run, Pallas kernels for 0% -> 8%
where the time goes in v3:
time: 102 us; the launch traced here: 101 us
  matrix products  26.4 us (26%)
  starting transfers between devices  25.7 us (25%)
  waiting for transfers between devices  23 us (23%)
  Pallas kernels  11.3 us (11%)
  local copies, waits for them, and re-layouts  7.78 us (8%)
  other arithmetic  5.85 us (6%)
    all_to_all x1, waiting for transfers between devices, per_device(): got = lax.all_to_all(send, 'tile', split_axis=0, concat_axis=0, tiled=True)  12.4 us
    pallas_call x4, Pallas kernels, row_taps(): pl.pallas_call(row_taps_kernel, out_shape=jax.ShapeDtypeStruct((channels,...  11.3 us
    ppermute x2, waiting for transfers between devices, padded_2(): lax.ppermute(tail, axis, [(i, (i + 1) % count) for i in range(ends)])  10.5 us
    all_to_all x1, starting transfers between devices, per_device(): got = lax.all_to_all(send, 'tile', split_axis=0, concat_axis=0, tiled=True)  7.75 us
    dot_general x1, matrix products, window_splat(): jnp.einsum('ibjh,ihc->ibjc', spread, onehot, preferred_element_type=jnp.f...  7.54 us
    ppermute x2, starting transfers between devices, padded_2(): lax.ppermute(head, axis, [((i + 1) % count, i) for i in range(ends)])  7.32 us
    ppermute x3, starting transfers between devices, per_device(): lax.ppermute(piece, 'wave', [(i, (i + step) % wave_count) for i in range(...  6.29 us
    dot_general x4, matrix products, scene_blur(): color = jnp.einsum('byf,bc->cyf', out, response, precision=hi)  4.92 us
  transfers between devices with their start and end apart: 8, of which 4 were waited for; matrix products, arithmetic and copies ran while one was open for 8% of the time, Pallas kernels for 8%

profile of v3, /device:TPU:2, one launch (start us, length us, event | category | flops | bytes accessed | tf_op | source)
XLA Modules:
  0.0 100.6 jit_solution(5762221824676191565)
XLA Ops:
  5.4 1.5 %copy.51 = bf16[256,10,128]{2,1,0:T(8,128)(2,1)} copy(bf16[256,10,128]{2,0,1:T(8,128)(2,1)S(1)} %convolution_convert_fusion) | data formatting | bytes 1310720 | tf_op jit(solution)/shard_map/convert_element_type | solution.py:203
  6.8 7.8 %all-to-all-start = ((bf16[256,10,128]{2,1,0:T(8,128)(2,1)}), bf16[256,10,128]{2,1,0:T(8,128)(2,1)S(1)}, u32[]{:S(2)}, u32[]{:S(2)}) async-start(bf16[256,10,128]{2,1,0:T(8,128)(2,1)} %copy.51), calls=%async_computation | async-start | bytes 2097152 | tf_op jit(solution)/shard_map/all_to_all | solution.py:205
  15.2 1.4 %reshape.298 = f32[4,8,31,31]{3,2,1,0:T(8,128)} reshape(f32[4,8,961]{2,1,0:T(8,128)S(1)} %gather_fusion) | data formatting | bytes 246016 | tf_op jit(solution)/shard_map/reshape | solution.py:116
  16.6 12.4 %all-to-all-done = bf16[256,10,128]{2,1,0:T(8,128)(2,1)S(1)} async-done(((bf16[256,10,128]{2,1,0:T(8,128)(2,1)}), bf16[256,10,128]{2,1,0:T(8,128)(2,1)S(1)}, u32[]{:S(2)}, u32[]{:S(2)}) %all-to-all-start) | async-done | bytes 655392 | tf_op jit(solution)/shard_map/all_to_all | solution.py:205
  29.8 7.5 %fusion.1 = f32[256,8,4,128]{3,2,1,0:T(4,128)S(1)} fusion(s32[256,128]{1,0:T(8,128)S(1)} %bitcast.121, pred[256,4,128]{2,1,0:T(4,128)(4,1)S(1)} %iota_compare_fusion.4, bf16[256,8,128]{2,1,0:T(8,128)(2,1)S(1)} %slice.40), kind=kOutput, calls=%fused_computation.3 | convolution fusion | flops 273678336 | bytes 4980736 | tf_op jit(solution)/shard_map/ibjh,ihc->ibjc/dot_general | solution.py:150
  37.3 3.2 %fusion.4 = f32[64,8,128,1]{2,0,3,1:T(8,128)S(1)} fusion(f32[256,8,4,128]{3,2,1,0:T(4,128)S(1)} %fusion.1, s32[256,4]{0,1:T(4,128)S(1)} %iota_add_fusion), kind=kOutput, calls=%fused_computation.5 | convolution fusion | flops 402718720 | bytes 4460544 | tf_op jit(solution)/shard_map/ibjc,ijr->brc/dot_general | solution.py:155
  41.3 5.4 %collective-permute-start.1 = (f32[8,4,15,128]{3,2,1,0:T(8,128)}, f32[8,4,15,128]{3,2,1,0:T(8,128)}, u32[]{:S(2)}, u32[]{:S(2)}) collective-permute-start(f32[8,4,15,128]{3,2,1,0:T(8,128)} %get-tuple-element.14), channel_id=1, source_target_pairs={{1,0},{2,1},{3,2},{4,3},{5,4},{6,5},{7,6},{8,7},{9,8},{10,9},{11,1... | collective-permute-start | bytes 737288 | tf_op jit(solution)/shard_map/ppermute | solution.py:29
  46.8 1.9 %collective-permute-start = (f32[8,4,15,128]{3,2,1,0:T(8,128)}, f32[8,4,15,128]{3,2,1,0:T(8,128)}, u32[]{:S(2)}, u32[]{:S(2)}) collective-permute-start(f32[8,4,15,128]{3,2,1,0:T(8,128)} %get-tuple-element.13), channel_id=1, source_target_pairs={{0,1},{1,2},{2,3},{3,4},{4,5},{5,6},{6,7},{7,8},{8,9},{9,10},{10,1... | collective-permute-start | bytes 737288 | tf_op jit(solution)/shard_map/ppermute | solution.py:27
  50.9 5.9 %collective-permute-done = f32[8,4,15,128]{3,2,1,0:T(8,128)} collective-permute-done((f32[8,4,15,128]{3,2,1,0:T(8,128)}, f32[8,4,15,128]{3,2,1,0:T(8,128)}, u32[]{:S(2)}, u32[]{:S(2)}) %collective-permute-start) | collective-permute-done | bytes 245792 | tf_op jit(solution)/shard_map/ppermute | solution.py:27
  62.9 2.8 %shard_map.192 = f32[8,16,256]{2,1,0:T(8,128)} custom-call(f32[8,46,256]{2,1,0:T(8,128)} %fusion.43.spec_ref, f32[8,31,256]{2,1,0:T(8,128)} %get-tuple-element.7.kern_ref), custom_call_target="tpu_custom_call" | custom-call | tf_op jit(solution)/shard_map/pallas_call | solution.py:99
  65.7 1.2 %fusion.57 = f32[3,16,256]{2,0,1:T(4,128)S(1)} fusion(f32[8,16,256]{2,1,0:T(8,128)} %shard_map.192, f32[32,3]{0,1:T(4,128)S(1)} %copy-done.4, s32[]{:T(128)S(6)} %select_n.106), kind=kOutput, calls=%fused_computation.77 | convolution fusion | flops 1179648 | bytes 180612 | tf_op jit(solution)/shard_map/byf,bc->cyf/dot_general | solution.py:130
  67.2 4.1 %collective-permute-start.4 = (f32[3,16,128]{2,1,0:T(8,128)S(1)}, f32[3,16,128]{2,1,0:T(8,128)S(1)}, u32[]{:S(2)}, u32[]{:S(2)}) collective-permute-start(f32[3,16,128]{2,1,0:T(8,128)S(1)} %fusion.74), channel_id=1, source_target_pairs={{0,96},{32,0},{64,32},{96,64},{1,97},{33,1},{65,33},{97,65},{2,98}... | collective-permute-start | bytes 73736 | tf_op jit(solution)/shard_map/ppermute | solution.py:215
  71.3 2.8 %shard_map.190 = f32[8,16,256]{2,1,0:T(8,128)} custom-call(f32[8,46,256]{2,1,0:T(8,128)} %fusion.47.spec_ref, f32[8,31,256]{2,1,0:T(8,128)} %get-tuple-element.8.kern_ref), custom_call_target="tpu_custom_call" | custom-call | tf_op jit(solution)/shard_map/pallas_call | solution.py:99
  74.1 1.2 %fusion.61 = f32[3,16,256]{2,0,1:T(4,128)S(1)} fusion(f32[8,16,256]{2,1,0:T(8,128)} %shard_map.190, f32[32,3]{0,1:T(4,128)S(1)} %copy-done.4, s32[]{:T(128)S(6)} %select_n.106), kind=kOutput, calls=%fused_computation.81 | convolution fusion | flops 1179648 | bytes 180612 | tf_op jit(solution)/shard_map/byf,bc->cyf/dot_general | solution.py:130
  75.6 2.8 %shard_map.191 = f32[8,16,256]{2,1,0:T(8,128)} custom-call(f32[8,46,256]{2,1,0:T(8,128)} %fusion.45.spec_ref, f32[8,31,256]{2,1,0:T(8,128)} %get-tuple-element.5.kern_ref), custom_call_target="tpu_custom_call" | custom-call | tf_op jit(solution)/shard_map/pallas_call | solution.py:99
  78.5 1.2 %fusion.59 = f32[3,16,256]{2,0,1:T(4,128)S(1)} fusion(f32[8,16,256]{2,1,0:T(8,128)} %shard_map.191, f32[32,3]{0,1:T(4,128)S(1)} %copy-done.4, s32[]{:T(128)S(6)} %select_n.106), kind=kOutput, calls=%fused_computation.79 | convolution fusion | flops 1179648 | bytes 180612 | tf_op jit(solution)/shard_map/byf,bc->cyf/dot_general | solution.py:130
  79.9 2.1 %collective-permute-start.3 = (f32[3,16,128]{2,1,0:T(8,128)S(1)}, f32[3,16,128]{2,1,0:T(8,128)S(1)}, u32[]{:S(2)}, u32[]{:S(2)}) collective-permute-start(f32[3,16,128]{2,1,0:T(8,128)S(1)} %fusion.76), channel_id=1, source_target_pairs={{0,64},{32,96},{64,0},{96,32},{1,65},{33,97},{65,1},{97,33},{2,66}... | collective-permute-start | bytes 73736 | tf_op jit(solution)/shard_map/ppermute | solution.py:215
  82.1 2.8 %shard_map.193 = f32[8,16,256]{2,1,0:T(8,128)} custom-call(f32[8,46,256]{2,1,0:T(8,128)} %fusion.41.spec_ref, f32[8,31,256]{2,1,0:T(8,128)} %get-tuple-element.6.kern_ref), custom_call_target="tpu_custom_call" | custom-call | tf_op jit(solution)/shard_map/pallas_call | solution.py:99
  86.4 1.9 %collective-permute-start.6 = (bf16[1,3,2,128]{3,2,1,0:T(2,128)(2,1)S(1)}, bf16[1,3,2,128]{3,2,1,0:T(2,128)(2,1)S(1)}, u32[]{:S(2)}, u32[]{:S(2)}) collective-permute-start(bf16[1,3,2,128]{3,2,1,0:T(2,128)(2,1)S(1)} %get-tuple-element.18), channel_id=1, source_target_pairs={{1,0},{2,1},{3,2},{4,3},{5,4},{6,5},{7,6},{8,7},{9,8},{10,9},{11,1... | collective-permute-start | bytes 4616 | tf_op jit(solution)/shard_map/ppermute | solution.py:29
  88.3 2.4 %collective-permute-start.5 = (bf16[1,3,2,128]{3,2,1,0:T(2,128)(2,1)S(1)}, bf16[1,3,2,128]{3,2,1,0:T(2,128)(2,1)S(1)}, u32[]{:S(2)}, u32[]{:S(2)}) collective-permute-start(bf16[1,3,2,128]{3,2,1,0:T(2,128)(2,1)S(1)} %get-tuple-element.17), channel_id=1, source_target_pairs={{0,1},{1,2},{2,3},{3,4},{4,5},{5,6},{6,7},{7,8},{8,9},{9,10},{10,1... | collective-permute-start | bytes 4616 | tf_op jit(solution)/shard_map/ppermute | solution.py:27
  90.7 4.6 %collective-permute-done.5 = bf16[1,3,2,128]{3,2,1,0:T(2,128)(2,1)S(1)} collective-permute-done((bf16[1,3,2,128]{3,2,1,0:T(2,128)(2,1)S(1)}, bf16[1,3,2,128]{3,2,1,0:T(2,128)(2,1)S(1)}, u32[]{:S(2)}, u32[]{:S(2)}) %collective-permute-start.5) | collective-permute-done | bytes 1568 | tf_op jit(solution)/shard_map/ppermute | solution.py:27
  96.3 1.4 %fusion.15 = bf16[18,1,8,17,64]{4,2,3,0,1:T(8,128)(2,1)S(1)} fusion(pred[18]{0:T(512)(128)(4,1)S(1)} %and_or_fusion, pred[8,17]{0,1:T(8,128)(4,1)S(1)} %copy-done.9, bf16[3,20,1,7,2]{3,0,4,1,2:T(4,128)(2,1)S(1)} %slice.46, bf16[3,20,1,8,17]{3,0,4,1,2:T(4,128)(2,1)S(1)} %copy.62, bf16[64,3,3,3]{0,3,2,1:T(4,128)(2,1)S(1)} %copy-done.7), kind=kOutput, calls=%fused_computation.23 | convolution fusion | flops 9925056 | bytes 334954 | tf_op jit(solution)/shard_map/conv_general_dilated | solution.py:37
  97.8 1.5 %convolution_convert_fusion.1 = bf16[16,8,17,64]{3,1,2,0:T(8,128)(2,1)S(1)} fusion(bf16[64,64,3,3]{1,0,3,2:T(8,128)(2,1)S(1)} %copy-done.6, bf16[18,1,7,1,64]{4,2,3,0,1:T(8,128)(2,1)S(1)} %get-tuple-element.12, bf16[18,1,7,1,64]{4,2,3,0,1:T(8,128)(2,1)S(1)} %get-tuple-element.11, bf16[18,1,8,17,64]{4,2,3,0,1:T(8,128)(2,1)S(1)} %fusion.15), kind=kOutput, calls=%fused_computation.15 | convolution fusion | flops 162322432 | bytes 697856 | tf_op jit(solution)/shard_map/conv_general_dilated | solution.py:37
  99.3 1.3 %copy.65 = bf16[1,64,16,128]{3,2,1,0:T(8,128)(2,1)} copy(bf16[1,64,16,128]{1,2,3,0:T(8,128)(2,1)S(1)} %slice_bitcast_fusion) | data formatting | bytes 524288 | tf_op jit(solution)/shard_map/convert_element_type | solution.py:230
  (66 shorter events, 18.8 us)
Async XLA Ops:
  0.0 14.6 %copy-start = (f32[64,8,961]{2,1,0:T(8,128)S(1)}, f32[64,8,961]{2,1,0:T(8,128)}, u32[]{:S(2)}) copy-start(f32[64,8,961]{2,1,0:T(8,128)} %param.26) | copy-start | bytes 5904388
  6.8 7.8 %copy-start.8 = (s32[1,4,1]{1,2,0:T(1,128)S(1)}, s32[1,4,1]{1,2,0:T(1,128)}, u32[]{:S(2)}) copy-start(s32[1,4,1]{1,2,0:T(1,128)} %param.27) | copy-start | bytes 52
  6.8 22.2 %all-to-all-start = ((bf16[256,10,128]{2,1,0:T(8,128)(2,1)}), bf16[256,10,128]{2,1,0:T(8,128)(2,1)S(1)}, u32[]{:S(2)}, u32[]{:S(2)}) async-start(bf16[256,10,128]{2,1,0:T(8,128)(2,1)} %copy.51), calls=%async_computation | async-start | bytes 2097152 | tf_op jit(solution)/shard_map/all_to_all | solution.py:205
  37.3 11.4 %copy-start.5 = (f32[31,256,1,1]{1,0,3,2:T(8,128)S(1)}, f32[31,256,1,1]{1,0,3,2:T(8,128)}, u32[]{:S(2)}) copy-start(f32[31,256,1,1]{1,0,3,2:T(8,128)} %constant.154) | copy-start | bytes 95236
  40.5 8.2 %copy-start.1 = (f32[4,8,31,31]{3,2,1,0:T(8,128)S(1)}, f32[4,8,31,31]{3,2,1,0:T(8,128)}, u32[]{:S(2)}) copy-start(f32[4,8,31,31]{3,2,1,0:T(8,128)} %reshape.298) | copy-start | bytes 369028
  41.3 9.6 %collective-permute-start.1 = (f32[8,4,15,128]{3,2,1,0:T(8,128)}, f32[8,4,15,128]{3,2,1,0:T(8,128)}, u32[]{:S(2)}, u32[]{:S(2)}) collective-permute-start(f32[8,4,15,128]{3,2,1,0:T(8,128)} %get-tuple-element.14), channel_id=1, source_target_pairs={{1,0},{2,1},{3,2},{4,3},{5,4},{6,5},{7,6},{8,7},{9,8},{10,9},{11,1... | collective-permute-start | bytes 737288 | tf_op jit(solution)/shard_map/ppermute | solution.py:29
  46.8 10.1 %collective-permute-start = (f32[8,4,15,128]{3,2,1,0:T(8,128)}, f32[8,4,15,128]{3,2,1,0:T(8,128)}, u32[]{:S(2)}, u32[]{:S(2)}) collective-permute-start(f32[8,4,15,128]{3,2,1,0:T(8,128)} %get-tuple-element.13), channel_id=1, source_target_pairs={{0,1},{1,2},{2,3},{3,4},{4,5},{5,6},{6,7},{7,8},{8,9},{9,10},{10,1... | collective-permute-start | bytes 737288 | tf_op jit(solution)/shard_map/ppermute | solution.py:27
  49.7 8.3 %copy-start.2 = (f32[128,256,1]{1,0,2:T(8,128)S(1)}, f32[128,256,1]{1,0,2:T(8,128)}, u32[]{:S(2)}) copy-start(f32[128,256,1]{1,0,2:T(8,128)} %constant.153) | copy-start | bytes 393220
  59.2 6.5 %copy-start.4 = (f32[32,3]{0,1:T(4,128)S(1)}, f32[32,3]{0,1:T(4,128)}, u32[]{:S(2)}) copy-start(f32[32,3]{0,1:T(4,128)} %param.28) | copy-start | bytes 1156
  59.2 7.7 %copy-start.3 = (f32[256,128,1]{1,0,2:T(8,128)S(1)}, f32[256,128,1]{1,0,2:T(8,128)}, u32[]{:S(2)}) copy-start(f32[256,128,1]{1,0,2:T(8,128)} %constant.155) | copy-start | bytes 393220
  67.2 19.0 %collective-permute-start.4 = (f32[3,16,128]{2,1,0:T(8,128)S(1)}, f32[3,16,128]{2,1,0:T(8,128)S(1)}, u32[]{:S(2)}, u32[]{:S(2)}) collective-permute-start(f32[3,16,128]{2,1,0:T(8,128)S(1)} %fusion.74), channel_id=1, source_target_pairs={{0,96},{32,0},{64,32},{96,64},{1,97},{33,1},{65,33},{97,65},{2,98}... | collective-permute-start | bytes 73736 | tf_op jit(solution)/shard_map/ppermute | solution.py:215
  75.5 10.6 %collective-permute-start.2 = (f32[3,16,128]{2,1,0:T(8,128)S(1)}, f32[3,16,128]{2,1,0:T(8,128)S(1)}, u32[]{:S(2)}, u32[]{:S(2)}) collective-permute-start(f32[3,16,128]{2,1,0:T(8,128)S(1)} %fusion.78), channel_id=1, source_target_pairs={{0,32},{32,64},{64,96},{96,0},{1,33},{33,65},{65,97},{97,1},{2,34}... | collective-permute-start | bytes 73736 | tf_op jit(solution)/shard_map/ppermute | solution.py:215
  78.5 17.8 %copy-start.7 = (bf16[64,3,3,3]{0,3,2,1:T(4,128)(2,1)S(1)}, bf16[64,3,3,3]{0,3,2,1:T(4,128)(2,1)}, u32[]{:S(2)}) copy-start(bf16[64,3,3,3]{0,3,2,1:T(4,128)(2,1)} %param.29) | copy-start | bytes 10372
  78.5 17.8 %copy-start.9 = (pred[8,17]{0,1:T(8,128)(4,1)S(1)}, pred[8,17]{0,1:T(8,128)(4,1)}, u32[]{:S(2)}) copy-start(pred[8,17]{0,1:T(8,128)(4,1)} %constant.151) | copy-start | bytes 412
  79.9 6.2 %collective-permute-start.3 = (f32[3,16,128]{2,1,0:T(8,128)S(1)}, f32[3,16,128]{2,1,0:T(8,128)S(1)}, u32[]{:S(2)}, u32[]{:S(2)}) collective-permute-start(f32[3,16,128]{2,1,0:T(8,128)S(1)} %fusion.76), channel_id=1, source_target_pairs={{0,64},{32,96},{64,0},{96,32},{1,65},{33,97},{65,1},{97,33},{2,66}... | collective-permute-start | bytes 73736 | tf_op jit(solution)/shard_map/ppermute | solution.py:215
  86.4 4.4 %collective-permute-start.6 = (bf16[1,3,2,128]{3,2,1,0:T(2,128)(2,1)S(1)}, bf16[1,3,2,128]{3,2,1,0:T(2,128)(2,1)S(1)}, u32[]{:S(2)}, u32[]{:S(2)}) collective-permute-start(bf16[1,3,2,128]{3,2,1,0:T(2,128)(2,1)S(1)} %get-tuple-element.18), channel_id=1, source_target_pairs={{1,0},{2,1},{3,2},{4,3},{5,4},{6,5},{7,6},{8,7},{9,8},{10,9},{11,1... | collective-permute-start | bytes 4616 | tf_op jit(solution)/shard_map/ppermute | solution.py:29
  88.3 7.0 %collective-permute-start.5 = (bf16[1,3,2,128]{3,2,1,0:T(2,128)(2,1)S(1)}, bf16[1,3,2,128]{3,2,1,0:T(2,128)(2,1)S(1)}, u32[]{:S(2)}, u32[]{:S(2)}) collective-permute-start(bf16[1,3,2,128]{3,2,1,0:T(2,128)(2,1)S(1)} %get-tuple-element.17), channel_id=1, source_target_pairs={{0,1},{1,2},{2,3},{3,4},{4,5},{5,6},{6,7},{7,8},{8,9},{9,10},{10,1... | collective-permute-start | bytes 4616 | tf_op jit(solution)/shard_map/ppermute | solution.py:27
  96.3 1.5 %copy-start.6 = (bf16[64,64,3,3]{1,0,3,2:T(8,128)(2,1)S(1)}, bf16[64,64,3,3]{1,0,3,2:T(8,128)(2,1)}, u32[]{:S(2)}) copy-start(bf16[64,64,3,3]{1,0,3,2:T(8,128)(2,1)} %param.30) | copy-start | bytes 221188

commit v4 on v3

--- a/solution.py
+++ b/solution.py
@@ -117,18 +117,19 @@
     return jnp.einsum("sbuv,vf->sbuf", chosen, taps, precision=lax.Precision.HIGHEST)
 
 
-def scene_blur(extended, kern, response, scene, radius):
+def patch_blur(extended, kern, response, radius):
     band_dev, scenes, tall, width = extended.shape
     rows_dev = tall - 2 * radius
     side = 2 * radius + 1
     forward, unused, inverse = dft_tables(width, side, radius)
     hi = lax.Precision.HIGHEST
-    plane = lax.dynamic_index_in_dim(extended, scene, 1, keepdims=False)
-    taps = lax.dynamic_index_in_dim(kern, scene, 0, keepdims=False)
-    spec = jnp.einsum("byx,xf->byf", plane, forward, precision=hi)
-    out = row_taps(spec, taps, rows_dev)
-    color = jnp.einsum("byf,bc->cyf", out, response, precision=hi)
-    return jnp.einsum("cyf,fx->cyx", color, inverse, precision=hi)
+    spec = jnp.einsum(
+        "cyx,xf->cyf", extended.reshape(band_dev * scenes, tall, width), forward, precision=hi
+    )
+    taps = kern.transpose(1, 0, 2, 3).reshape(band_dev * scenes, side, -1)
+    out = row_taps(spec, taps, rows_dev).reshape(band_dev, scenes, rows_dev, -1)
+    color = jnp.einsum("bsyf,bc->scyf", out, response, precision=hi)
+    return jnp.einsum("scyf,fx->scyx", color, inverse, precision=hi)
 
 
 def window_splat(got, scenes):
@@ -207,15 +208,13 @@
     extended = padded_2(splat, (("tile", 2),), K // 2)
     wave_index = lax.axis_index("wave")
     my_response = lax.dynamic_slice_in_dim(response, wave_index * band_dev, band_dev, 0)
-    color = None
-    for step in list(range(1, wave_count)) + [0]:
-        scene = (wave_index + step) % wave_count
-        piece = scene_blur(extended, kern, my_response, scene, K // 2)
-        if step:
-            piece = lax.ppermute(
-                piece, "wave", [(i, (i + step) % wave_count) for i in range(wave_count)]
-            )
-        color = piece if color is None else color + piece
+    partial = patch_blur(extended, kern, my_response, K // 2)
+    color = lax.dynamic_index_in_dim(partial, wave_index, 0, keepdims=False)
+    for step in range(1, wave_count):
+        piece = lax.dynamic_index_in_dim(partial, (wave_index + step) % wave_count, 0, keepdims=False)
+        color = color + lax.ppermute(
+            piece, "wave", [(i, (i + step) % wave_count) for i in range(wave_count)]
+        )
     sensor = lax.reduce_precision(color[None], exponent_bits=8, mantissa_bits=7)
     sensor = sensor.astype(jnp.bfloat16)
     rimmed = padded_2(sensor, (("tile", 2),), 2)

time: 102 us -> 91.3 us (0.90)
  matrix products: 26.4 us -> 20.6 us
  Pallas kernels: 11.3 us -> 6.31 us
  waiting for transfers between devices: 23 us -> 26.6 us
  other arithmetic: 5.85 us -> 4.75 us
    dot_general x12 -> x3, matrix products: 10.6 us -> 4.77 us  [the longest x1 2.56 us: patch_blur(): jnp.einsum('cyx,xf->cyf', extended.reshape(band_dev * scenes, tall, width...]
    pallas_call x4 -> x1, Pallas kernels: 11.3 us -> 6.31 us  [row_taps(): pl.pallas_call(row_taps_kernel, out_shape=jax.ShapeDtypeStruct((channels,...]
    ppermute x3, waiting for transfers between devices: 0.01 us -> 4.07 us  [per_device(): lax.ppermute(piece, 'wave', [(i, (i + step) % wave_count) for i in range(...]
    concatenate x2 -> x1, other arithmetic: 1.12 us -> 0.01 us  [padded_2(): jnp.concatenate([lax.ppermute(tail, axis, [(i, (i + 1) % count) for i in...]
    transpose x0 -> x1, local copies, waits for them, and re-layouts: none -> 1.1 us  [patch_blur(): taps = kern.transpose(1, 0, 2, 3).reshape(band_dev * scenes, side, -1)]
  transfers between devices with their start and end apart: 8 -> 8, of which waited for: 4 -> 5; matrix products, arithmetic and copies ran while one was open for 8% -> 4% of each run, Pallas kernels for 8% -> 0%
where the time goes in v4:
time: 91.3 us; the launch traced here: 90.8 us
  waiting for transfers between devices  26.6 us (29%)
  starting transfers between devices  25.1 us (27%)
  matrix products  20.6 us (23%)
  local copies, waits for them, and re-layouts  7.08 us (8%)
  Pallas kernels  6.31 us (7%)
  other arithmetic  4.75 us (5%)
    all_to_all x1, waiting for transfers between devices, per_device(): got = lax.all_to_all(send, 'tile', split_axis=0, concat_axis=0, tiled=True)  12.3 us
    ppermute x2, waiting for transfers between devices, padded_2(): lax.ppermute(tail, axis, [(i, (i + 1) % count) for i in range(ends)])  10.2 us
    all_to_all x1, starting transfers between devices, per_device(): got = lax.all_to_all(send, 'tile', split_axis=0, concat_axis=0, tiled=True)  7.75 us
    dot_general x1, matrix products, window_splat(): jnp.einsum('ibjh,ihc->ibjc', spread, onehot, preferred_element_type=jnp.f...  7.54 us
    ppermute x2, starting transfers between devices, padded_2(): lax.ppermute(head, axis, [((i + 1) % count, i) for i in range(ends)])  7.46 us
    pallas_call x1, Pallas kernels, row_taps(): pl.pallas_call(row_taps_kernel, out_shape=jax.ShapeDtypeStruct((channels,...  6.31 us
    ppermute x3, starting transfers between devices, per_device(): lax.ppermute(piece, 'wave', [(i, (i + step) % wave_count) for i in range(...  5.36 us
    ppermute x2, starting transfers between devices, padded_2(): lax.ppermute(tail, axis, [(i, (i + 1) % count) for i in range(ends)])  4.51 us
  transfers between devices with their start and end apart: 8, of which 5 were waited for; matrix products, arithmetic and copies ran while one was open for 4% of the time, Pallas kernels for 0%

profile of v4, /device:TPU:2, one launch (start us, length us, event | category | flops | bytes accessed | tf_op | source)
XLA Modules:
  0.0 90.8 jit_solution(4181568951540980101)
XLA Ops:
  4.1 1.0 %copy_select_fusion = bf16[128,8,128]{2,0,1:T(8,128)(2,1)S(1)} fusion(bf16[128,8,128]{2,1,0:T(8,128)(2,1)} %param.14, pred[128,128]{1,0:T(8,128)(4,1)S(1)} %iota_compare_fusion.7), kind=kLoop, calls=%fused_computation.56 | loop fusion | flops 131072 | bytes 540672 | tf_op jit(solution)/shard_map/jit(_where)/select_n | solution.py:180
  5.4 1.5 %copy.40 = bf16[256,10,128]{2,1,0:T(8,128)(2,1)} copy(bf16[256,10,128]{2,0,1:T(8,128)(2,1)S(1)} %convolution_convert_fusion) | data formatting | bytes 1310720 | tf_op jit(solution)/shard_map/convert_element_type | solution.py:204
  6.8 7.8 %all-to-all-start = ((bf16[256,10,128]{2,1,0:T(8,128)(2,1)}), bf16[256,10,128]{2,1,0:T(8,128)(2,1)S(1)}, u32[]{:S(2)}, u32[]{:S(2)}) async-start(bf16[256,10,128]{2,1,0:T(8,128)(2,1)} %copy.40), calls=%async_computation | async-start | bytes 2097152 | tf_op jit(solution)/shard_map/all_to_all | solution.py:206
  15.3 1.4 %reshape.309 = f32[4,8,31,31]{3,2,1,0:T(8,128)} reshape(f32[4,8,961]{2,1,0:T(8,128)S(1)} %gather_fusion) | data formatting | bytes 246016 | tf_op jit(solution)/shard_map/reshape | solution.py:116
  16.7 12.3 %all-to-all-done = bf16[256,10,128]{2,1,0:T(8,128)(2,1)S(1)} async-done(((bf16[256,10,128]{2,1,0:T(8,128)(2,1)}), bf16[256,10,128]{2,1,0:T(8,128)(2,1)S(1)}, u32[]{:S(2)}, u32[]{:S(2)}) %all-to-all-start) | async-done | bytes 655392 | tf_op jit(solution)/shard_map/all_to_all | solution.py:206
  29.8 7.5 %fusion.1 = f32[256,8,4,128]{3,2,1,0:T(4,128)S(1)} fusion(s32[256,128]{1,0:T(8,128)S(1)} %bitcast.128, pred[256,4,128]{2,1,0:T(4,128)(4,1)S(1)} %iota_compare_fusion.4, bf16[256,8,128]{2,1,0:T(8,128)(2,1)S(1)} %slice.40), kind=kOutput, calls=%fused_computation.3 | convolution fusion | flops 273678336 | bytes 4980736 | tf_op jit(solution)/shard_map/ibjh,ihc->ibjc/dot_general | solution.py:151
  37.3 3.2 %fusion.4 = f32[64,8,128,1]{2,0,3,1:T(8,128)S(1)} fusion(f32[256,8,4,128]{3,2,1,0:T(4,128)S(1)} %fusion.1, s32[256,4]{0,1:T(4,128)S(1)} %iota_add_fusion), kind=kOutput, calls=%fused_computation.5 | convolution fusion | flops 402718720 | bytes 4460544 | tf_op jit(solution)/shard_map/ibjc,ijr->brc/dot_general | solution.py:156
  40.6 5.5 %collective-permute-start.1 = (f32[8,4,15,128]{3,2,1,0:T(8,128)S(1)}, f32[8,4,15,128]{3,2,1,0:T(8,128)S(1)}, u32[]{:S(2)}, u32[]{:S(2)}) collective-permute-start(f32[8,4,15,128]{3,2,1,0:T(8,128)S(1)} %get-tuple-element.10), channel_id=1, source_target_pairs={{1,0},{2,1},{3,2},{4,3},{5,4},{6,5},{7,6},{8,7},{9,8},{10,9},{11,1... | collective-permute-start | bytes 737288 | tf_op jit(solution)/shard_map/ppermute | solution.py:29
  46.1 1.9 %collective-permute-start = (f32[8,4,15,128]{3,2,1,0:T(8,128)S(1)}, f32[8,4,15,128]{3,2,1,0:T(8,128)S(1)}, u32[]{:S(2)}, u32[]{:S(2)}) collective-permute-start(f32[8,4,15,128]{3,2,1,0:T(8,128)S(1)} %get-tuple-element.9), channel_id=1, source_target_pairs={{0,1},{1,2},{2,3},{3,4},{4,5},{5,6},{6,7},{7,8},{8,9},{9,10},{10,1... | collective-permute-start | bytes 737288 | tf_op jit(solution)/shard_map/ppermute | solution.py:27
  48.1 1.0 %convolution_bitcast_fusion = f32[8,4,31,256]{3,2,0,1:T(8,128)S(1)} fusion(f32[4,8,31,31]{3,2,1,0:T(8,128)S(1)} %copy-done.1, f32[31,256,1,1]{1,0,3,2:T(8,128)S(1)} %copy-done.4), kind=kOutput, calls=%fused_computation.14 | convolution fusion | flops 94470144 | bytes 1170560 | tf_op jit(solution)/shard_map/sbuv,vf->sbuf/dot_general | solution.py:117
  49.1 1.1 %copy.42 = f32[8,4,31,256]{3,2,1,0:T(8,128)} copy(f32[8,4,31,256]{3,2,0,1:T(8,128)S(1)} %convolution_bitcast_fusion) | data formatting | bytes 2031616 | tf_op jit(solution)/shard_map/transpose | solution.py:129
  50.2 5.8 %collective-permute-done = f32[8,4,15,128]{3,2,1,0:T(8,128)S(1)} collective-permute-done((f32[8,4,15,128]{3,2,1,0:T(8,128)S(1)}, f32[8,4,15,128]{3,2,1,0:T(8,128)S(1)}, u32[]{:S(2)}, u32[]{:S(2)}) %collective-permute-start) | collective-permute-done | bytes 245792 | tf_op jit(solution)/shard_map/ppermute | solution.py:27
  55.9 2.6 %fusion.16.spec_ref = f32[32,46,256]{2,1,0:T(8,128)} fusion(f32[128,256,1]{1,0,2:T(8,128)S(1)} %copy-done.2, f32[32,15,128]{2,1,0:T(8,128)S(1)} %bitcast.126, f32[32,16,128]{2,1,0:T(8,128)S(1)} %bitcast.121, f32[32,15,128]{2,1,0:T(8,128)S(1)} %bitcast.127), kind=kOutput, calls=%fused_computation.26 | convolution fusion | flops 579190784 | bytes 2392064 | tf_op jit(solution)/shard_map/cyx,xf->cyf/dot_general | solution.py:126
  58.5 6.3 %shard_map.136 = f32[32,16,256]{2,1,0:T(8,128)} custom-call(f32[32,46,256]{2,1,0:T(8,128)} %fusion.16.spec_ref, f32[32,31,256]{2,1,0:T(8,128)} %bitcast.119), custom_call_target="tpu_custom_call" | custom-call | tf_op jit(solution)/shard_map/pallas_call | solution.py:99
  64.8 1.9 %convolution_bitcast_fusion.1 = f32[4,3,16,256]{3,1,2,0:T(4,128)S(1)} fusion(f32[8,4,16,256]{3,2,1,0:T(8,128)} %bitcast.123, f32[32,3]{0,1:T(4,128)S(1)} %copy-done.5, s32[]{:T(128)S(6)} %select_n.97), kind=kOutput, calls=%fused_computation.18 | convolution fusion | flops 4718592 | bytes 721284 | tf_op jit(solution)/shard_map/bsyf,bc->scyf/dot_general | solution.py:131
  67.1 4.1 %collective-permute-start.4 = (f32[3,16,128]{2,1,0:T(8,128)S(1)}, f32[3,16,128]{2,1,0:T(8,128)S(1)}, u32[]{:S(2)}, u32[]{:S(2)}) collective-permute-start(f32[3,16,128]{2,1,0:T(8,128)S(1)} %get-tuple-element.12), channel_id=1, source_target_pairs={{0,96},{32,0},{64,32},{96,64},{1,97},{33,1},{65,33},{97,65},{2,98}... | collective-permute-start | bytes 73736 | tf_op jit(solution)/shard_map/ppermute | solution.py:215
  71.2 1.3 %collective-permute-start.2 = (f32[3,16,128]{2,1,0:T(8,128)S(1)}, f32[3,16,128]{2,1,0:T(8,128)S(1)}, u32[]{:S(2)}, u32[]{:S(2)}) collective-permute-start(f32[3,16,128]{2,1,0:T(8,128)S(1)} %get-tuple-element.11), channel_id=1, source_target_pairs={{0,32},{32,64},{64,96},{96,0},{1,33},{33,65},{65,97},{97,1},{2,34}... | collective-permute-start | bytes 73736 | tf_op jit(solution)/shard_map/ppermute | solution.py:215
  72.7 3.8 %collective-permute-done.3 = f32[3,16,128]{2,1,0:T(8,128)S(1)} collective-permute-done((f32[3,16,128]{2,1,0:T(8,128)S(1)}, f32[3,16,128]{2,1,0:T(8,128)S(1)}, u32[]{:S(2)}, u32[]{:S(2)}) %collective-permute-start.3) | collective-permute-done | bytes 24608 | tf_op jit(solution)/shard_map/ppermute | solution.py:215
  76.5 1.9 %collective-permute-start.6 = (bf16[1,3,2,128]{3,2,1,0:T(2,128)(2,1)S(1)}, bf16[1,3,2,128]{3,2,1,0:T(2,128)(2,1)S(1)}, u32[]{:S(2)}, u32[]{:S(2)}) collective-permute-start(bf16[1,3,2,128]{3,2,1,0:T(2,128)(2,1)S(1)} %get-tuple-element.17), channel_id=1, source_target_pairs={{1,0},{2,1},{3,2},{4,3},{5,4},{6,5},{7,6},{8,7},{9,8},{10,9},{11,1... | collective-permute-start | bytes 4616 | tf_op jit(solution)/shard_map/ppermute | solution.py:29
  78.5 2.6 %collective-permute-start.5 = (bf16[1,3,2,128]{3,2,1,0:T(2,128)(2,1)S(1)}, bf16[1,3,2,128]{3,2,1,0:T(2,128)(2,1)S(1)}, u32[]{:S(2)}, u32[]{:S(2)}) collective-permute-start(bf16[1,3,2,128]{3,2,1,0:T(2,128)(2,1)S(1)} %get-tuple-element.16), channel_id=1, source_target_pairs={{0,1},{1,2},{2,3},{3,4},{4,5},{5,6},{6,7},{7,8},{8,9},{9,10},{10,1... | collective-permute-start | bytes 4616 | tf_op jit(solution)/shard_map/ppermute | solution.py:27
  81.1 4.4 %collective-permute-done.5 = bf16[1,3,2,128]{3,2,1,0:T(2,128)(2,1)S(1)} collective-permute-done((bf16[1,3,2,128]{3,2,1,0:T(2,128)(2,1)S(1)}, bf16[1,3,2,128]{3,2,1,0:T(2,128)(2,1)S(1)}, u32[]{:S(2)}, u32[]{:S(2)}) %collective-permute-start.5) | collective-permute-done | bytes 1568 | tf_op jit(solution)/shard_map/ppermute | solution.py:27
  86.4 1.4 %fusion.15 = bf16[18,1,8,17,64]{4,2,3,0,1:T(8,128)(2,1)S(1)} fusion(pred[18]{0:T(512)(128)(4,1)S(1)} %and_or_fusion, pred[8,17]{0,1:T(8,128)(4,1)S(1)} %copy-done.9, bf16[3,20,1,7,2]{3,0,4,1,2:T(4,128)(2,1)S(1)} %slice.46, bf16[3,20,1,8,17]{3,0,4,1,2:T(4,128)(2,1)S(1)} %copy.46, bf16[64,3,3,3]{0,3,2,1:T(4,128)(2,1)S(1)} %copy-done.7), kind=kOutput, calls=%fused_computation.25 | convolution fusion | flops 9925056 | bytes 334954 | tf_op jit(solution)/shard_map/conv_general_dilated | solution.py:37
  87.9 1.5 %convolution_convert_fusion.1 = bf16[16,8,17,64]{3,1,2,0:T(8,128)(2,1)S(1)} fusion(bf16[64,64,3,3]{1,0,3,2:T(8,128)(2,1)S(1)} %copy-done.6, bf16[18,1,7,1,64]{4,2,3,0,1:T(8,128)(2,1)S(1)} %get-tuple-element.8, bf16[18,1,7,1,64]{4,2,3,0,1:T(8,128)(2,1)S(1)} %get-tuple-element.7, bf16[18,1,8,17,64]{4,2,3,0,1:T(8,128)(2,1)S(1)} %fusion.15), kind=kOutput, calls=%fused_computation.16 | convolution fusion | flops 162322432 | bytes 697856 | tf_op jit(solution)/shard_map/conv_general_dilated | solution.py:37
  89.5 1.3 %copy.49 = bf16[1,64,16,128]{3,2,1,0:T(8,128)(2,1)} copy(bf16[1,64,16,128]{1,2,3,0:T(8,128)(2,1)S(1)} %slice_bitcast_fusion) | data formatting | bytes 524288 | tf_op jit(solution)/shard_map/convert_element_type | solution.py:229
  (55 shorter events, 7.4 us)
Async XLA Ops:
  0.0 14.7 %copy-start = (f32[64,8,961]{2,1,0:T(8,128)S(1)}, f32[64,8,961]{2,1,0:T(8,128)}, u32[]{:S(2)}) copy-start(f32[64,8,961]{2,1,0:T(8,128)} %param.20) | copy-start | bytes 5904388
  6.8 7.8 %copy-start.8 = (s32[1,4,1]{1,2,0:T(1,128)S(1)}, s32[1,4,1]{1,2,0:T(1,128)}, u32[]{:S(2)}) copy-start(s32[1,4,1]{1,2,0:T(1,128)} %param.21) | copy-start | bytes 52
  6.8 22.2 %all-to-all-start = ((bf16[256,10,128]{2,1,0:T(8,128)(2,1)}), bf16[256,10,128]{2,1,0:T(8,128)(2,1)S(1)}, u32[]{:S(2)}, u32[]{:S(2)}) async-start(bf16[256,10,128]{2,1,0:T(8,128)(2,1)} %copy.40), calls=%async_computation | async-start | bytes 2097152 | tf_op jit(solution)/shard_map/all_to_all | solution.py:206
  37.3 10.7 %copy-start.4 = (f32[31,256,1,1]{1,0,3,2:T(8,128)S(1)}, f32[31,256,1,1]{1,0,3,2:T(8,128)}, u32[]{:S(2)}) copy-start(f32[31,256,1,1]{1,0,3,2:T(8,128)} %constant.140) | copy-start | bytes 95236
  40.5 7.5 %copy-start.1 = (f32[4,8,31,31]{3,2,1,0:T(8,128)S(1)}, f32[4,8,31,31]{3,2,1,0:T(8,128)}, u32[]{:S(2)}) copy-start(f32[4,8,31,31]{3,2,1,0:T(8,128)} %reshape.309) | copy-start | bytes 369028
  40.6 9.6 %collective-permute-start.1 = (f32[8,4,15,128]{3,2,1,0:T(8,128)S(1)}, f32[8,4,15,128]{3,2,1,0:T(8,128)S(1)}, u32[]{:S(2)}, u32[]{:S(2)}) collective-permute-start(f32[8,4,15,128]{3,2,1,0:T(8,128)S(1)} %get-tuple-element.10), channel_id=1, source_target_pairs={{1,0},{2,1},{3,2},{4,3},{5,4},{6,5},{7,6},{8,7},{9,8},{10,9},{11,1... | collective-permute-start | bytes 737288 | tf_op jit(solution)/shard_map/ppermute | solution.py:29
  46.1 9.8 %collective-permute-start = (f32[8,4,15,128]{3,2,1,0:T(8,128)S(1)}, f32[8,4,15,128]{3,2,1,0:T(8,128)S(1)}, u32[]{:S(2)}, u32[]{:S(2)}) collective-permute-start(f32[8,4,15,128]{3,2,1,0:T(8,128)S(1)} %get-tuple-element.9), channel_id=1, source_target_pairs={{0,1},{1,2},{2,3},{3,4},{4,5},{5,6},{6,7},{7,8},{8,9},{9,10},{10,1... | collective-permute-start | bytes 737288 | tf_op jit(solution)/shard_map/ppermute | solution.py:27
  49.0 6.9 %copy-start.2 = (f32[128,256,1]{1,0,2:T(8,128)S(1)}, f32[128,256,1]{1,0,2:T(8,128)}, u32[]{:S(2)}) copy-start(f32[128,256,1]{1,0,2:T(8,128)} %constant.139) | copy-start | bytes 393220
  58.5 6.3 %copy-start.5 = (f32[32,3]{0,1:T(4,128)S(1)}, f32[32,3]{0,1:T(4,128)}, u32[]{:S(2)}) copy-start(f32[32,3]{0,1:T(4,128)} %param.22) | copy-start | bytes 1156
  58.5 8.2 %copy-start.3 = (f32[256,128,1,1]{1,0,3,2:T(8,128)S(1)}, f32[256,128,1,1]{1,0,3,2:T(8,128)}, u32[]{:S(2)}) copy-start(f32[256,128,1,1]{1,0,3,2:T(8,128)} %constant.141) | copy-start | bytes 393220
  64.8 21.6 %copy-start.7 = (bf16[64,3,3,3]{0,3,2,1:T(4,128)(2,1)S(1)}, bf16[64,3,3,3]{0,3,2,1:T(4,128)(2,1)}, u32[]{:S(2)}) copy-start(bf16[64,3,3,3]{0,3,2,1:T(4,128)(2,1)} %param.23) | copy-start | bytes 10372
  64.8 21.6 %copy-start.9 = (pred[8,17]{0,1:T(8,128)(4,1)S(1)}, pred[8,17]{0,1:T(8,128)(4,1)}, u32[]{:S(2)}) copy-start(pred[8,17]{0,1:T(8,128)(4,1)} %constant.137) | copy-start | bytes 412
  67.1 5.6 %collective-permute-start.4 = (f32[3,16,128]{2,1,0:T(8,128)S(1)}, f32[3,16,128]{2,1,0:T(8,128)S(1)}, u32[]{:S(2)}, u32[]{:S(2)}) collective-permute-start(f32[3,16,128]{2,1,0:T(8,128)S(1)} %get-tuple-element.12), channel_id=1, source_target_pairs={{0,96},{32,0},{64,32},{96,64},{1,97},{33,1},{65,33},{97,65},{2,98}... | collective-permute-start | bytes 73736 | tf_op jit(solution)/shard_map/ppermute | solution.py:215
  71.2 5.3 %collective-permute-start.3 = (f32[3,16,128]{2,1,0:T(8,128)S(1)}, f32[3,16,128]{2,1,0:T(8,128)S(1)}, u32[]{:S(2)}, u32[]{:S(2)}) collective-permute-start(f32[3,16,128]{2,1,0:T(8,128)S(1)} %get-tuple-element.13), channel_id=1, source_target_pairs={{0,64},{32,96},{64,0},{96,32},{1,65},{33,97},{65,1},{97,33},{2,66}... | collective-permute-start | bytes 73736 | tf_op jit(solution)/shard_map/ppermute | solution.py:215
  71.2 5.3 %collective-permute-start.2 = (f32[3,16,128]{2,1,0:T(8,128)S(1)}, f32[3,16,128]{2,1,0:T(8,128)S(1)}, u32[]{:S(2)}, u32[]{:S(2)}) collective-permute-start(f32[3,16,128]{2,1,0:T(8,128)S(1)} %get-tuple-element.11), channel_id=1, source_target_pairs={{0,32},{32,64},{64,96},{96,0},{1,33},{33,65},{65,97},{97,1},{2,34}... | collective-permute-start | bytes 73736 | tf_op jit(solution)/shard_map/ppermute | solution.py:215
  76.5 4.5 %collective-permute-start.6 = (bf16[1,3,2,128]{3,2,1,0:T(2,128)(2,1)S(1)}, bf16[1,3,2,128]{3,2,1,0:T(2,128)(2,1)S(1)}, u32[]{:S(2)}, u32[]{:S(2)}) collective-permute-start(bf16[1,3,2,128]{3,2,1,0:T(2,128)(2,1)S(1)} %get-tuple-element.17), channel_id=1, source_target_pairs={{1,0},{2,1},{3,2},{4,3},{5,4},{6,5},{7,6},{8,7},{9,8},{10,9},{11,1... | collective-permute-start | bytes 4616 | tf_op jit(solution)/shard_map/ppermute | solution.py:29
  78.5 7.0 %collective-permute-start.5 = (bf16[1,3,2,128]{3,2,1,0:T(2,128)(2,1)S(1)}, bf16[1,3,2,128]{3,2,1,0:T(2,128)(2,1)S(1)}, u32[]{:S(2)}, u32[]{:S(2)}) collective-permute-start(bf16[1,3,2,128]{3,2,1,0:T(2,128)(2,1)S(1)} %get-tuple-element.16), channel_id=1, source_target_pairs={{0,1},{1,2},{2,3},{3,4},{4,5},{5,6},{6,7},{7,8},{8,9},{9,10},{10,1... | collective-permute-start | bytes 4616 | tf_op jit(solution)/shard_map/ppermute | solution.py:27
  86.4 1.5 %copy-start.6 = (bf16[64,64,3,3]{1,0,3,2:T(8,128)(2,1)S(1)}, bf16[64,64,3,3]{1,0,3,2:T(8,128)(2,1)}, u32[]{:S(2)}) copy-start(bf16[64,64,3,3]{1,0,3,2:T(8,128)(2,1)} %param.24) | copy-start | bytes 221188

commit v5 on v4

--- a/solution.py
+++ b/solution.py
@@ -132,11 +132,11 @@
     return jnp.einsum("scyf,fx->scyx", color, inverse, precision=hi)
 
 
-def window_splat(got, scenes):
-    band_dev = got.shape[1] - 2
-    energy = got[:, :band_dev]
-    field = got[:, band_dev].astype(jnp.int32)
-    column = got[:, band_dev + 1].astype(jnp.int32)
+def window_splat(got, band_dev, hit_lanes, scenes):
+    slots = got.shape[0]
+    energy = got[:, : band_dev * hit_lanes].reshape(slots, band_dev, hit_lanes)
+    field = got[:, band_dev * hit_lanes : (band_dev + 1) * hit_lanes].astype(jnp.int32)
+    column = got[:, (band_dev + 1) * hit_lanes :].astype(jnp.int32)
     offset = field % WIN
     base = field[:, 0] // WIN
     rows = jnp.arange(WIN, dtype=jnp.int32)
@@ -184,9 +184,9 @@
     column = spot % W
     payload = jnp.concatenate(
         [
-            masked,
-            field.astype(hit_energy.dtype)[:, None, :],
-            column.astype(hit_energy.dtype)[:, None, :],
+            masked.reshape(block_dev, band_dev * hit_lanes),
+            field.astype(hit_energy.dtype),
+            column.astype(hit_energy.dtype),
         ],
         axis=1,
     )
@@ -199,12 +199,10 @@
     place = target * capacity + rank
     slots = jnp.arange(tile_count * capacity, dtype=jnp.int32)
     select = (slots[:, None] == place[None, :]).astype(hit_energy.dtype)
-    send = jnp.einsum(
-        "pi,ibh->pbh", select, payload, preferred_element_type=jnp.float32
-    ).astype(hit_energy.dtype)
+    send = jnp.dot(select, payload, preferred_element_type=jnp.float32).astype(hit_energy.dtype)
     kern = kernel_spectra(psf_bank, psf_index, K // 2)
     got = lax.all_to_all(send, "tile", split_axis=0, concat_axis=0, tiled=True)
-    splat = window_splat(got, scenes)
+    splat = window_splat(got, band_dev, hit_lanes, scenes)
     extended = padded_2(splat, (("tile", 2),), K // 2)
     wave_index = lax.axis_index("wave")
     my_response = lax.dynamic_slice_in_dim(response, wave_index * band_dev, band_dev, 0)

time: 91.3 us -> 87.2 us (0.955)
  waiting for transfers between devices: 26.6 us -> 24 us
  local copies, waits for them, and re-layouts: 7.08 us -> 5.75 us
    all_to_all x1, waiting for transfers between devices: 12.3 us -> 9.55 us  [per_device(): got = lax.all_to_all(send, 'tile', split_axis=0, concat_axis=0, tiled=True)]
    convert_element_type x1 -> x0, local copies, waits for them, and re-layouts: 1.45 us -> none  [per_device(): send = jnp.einsum('pi,ibh->pbh', select, payload, preferred_element_type=...]
  transfers between devices with their start and end apart: 8 -> 8, of which waited for: 5 -> 6; matrix products, arithmetic and copies ran while one was open for 4% -> 4% of each run, Pallas kernels for 0% -> 0%
where the time goes in v5:
time: 87.2 us; the launch traced here: 86.7 us
  starting transfers between devices  24.3 us (28%)
  waiting for transfers between devices  24 us (28%)
  matrix products  21.4 us (25%)
  Pallas kernels  6.33 us (7%)
  local copies, waits for them, and re-layouts  5.75 us (7%)
  other arithmetic  4.49 us (5%)
    ppermute x2, waiting for transfers between devices, padded_2(): lax.ppermute(tail, axis, [(i, (i + 1) % count) for i in range(ends)])  10.2 us
    all_to_all x1, waiting for transfers between devices, per_device(): got = lax.all_to_all(send, 'tile', split_axis=0, concat_axis=0, tiled=True)  9.55 us
    all_to_all x1, starting transfers between devices, per_device(): got = lax.all_to_all(send, 'tile', split_axis=0, concat_axis=0, tiled=True)  7.62 us
    dot_general x1, matrix products, window_splat(): jnp.einsum('ibjh,ihc->ibjc', spread, onehot, preferred_element_type=jnp.f...  7.54 us
    ppermute x2, starting transfers between devices, padded_2(): lax.ppermute(head, axis, [((i + 1) % count, i) for i in range(ends)])  6.83 us
    pallas_call x1, Pallas kernels, row_taps(): pl.pallas_call(row_taps_kernel, out_shape=jax.ShapeDtypeStruct((channels,...  6.33 us
    ppermute x3, starting transfers between devices, per_device(): lax.ppermute(piece, 'wave', [(i, (i + step) % wave_count) for i in range(...  5.37 us
    ppermute x2, starting transfers between devices, padded_2(): lax.ppermute(tail, axis, [(i, (i + 1) % count) for i in range(ends)])  4.51 us
  transfers between devices with their start and end apart: 8, of which 6 were waited for; matrix products, arithmetic and copies ran while one was open for 4% of the time, Pallas kernels for 0%

profile of v5, /device:TPU:2, one launch (start us, length us, event | category | flops | bytes accessed | tf_op | source)
XLA Modules:
  0.0 86.7 jit_solution(11645255396731025854)
XLA Ops:
  0.9 1.0 %broadcast_select_fusion = bf16[128,8,128]{2,1,0:T(8,128)(2,1)S(1)} fusion(bf16[128,8,128]{2,1,0:T(8,128)(2,1)} %param.14, pred[128,128]{1,0:T(8,128)(4,1)S(1)} %iota_compare_fusion.8), kind=kLoop, calls=%fused_computation.61 | loop fusion | flops 131072 | bytes 540672 | tf_op jit(solution)/shard_map/jit(_where)/select_n | solution.py:180
  4.2 0.9 %fusion.55 = (bf16[128,128]{1,0:T(8,128)(2,1)S(1)}, bf16[128,128]{1,0:T(8,128)(2,1)S(1)}) fusion(s32[1,128,128]{2,1,0:T(8,128)} %param.15, s32[128]{0:T(128)S(1)} %multiply_bitcast_fusion), kind=kLoop, calls=%fused_computation.78 | loop fusion | flops 360448 | bytes 131584 | tf_op jit(solution)/shard_map/convert_element_type | solution.py:188
  5.2 1.2 %fusion.6 = bf16[32,8,1280]{2,1,0:T(8,128)(2,1)} fusion(bf16[128,128]{1,0:T(8,128)(2,1)S(1)} %get-tuple-element.15, bf16[128,128]{1,0:T(8,128)(2,1)S(1)} %get-tuple-element.14, bf16[128,1024]{1,0:T(8,128)(2,1)S(1)} %bitcast.132, s32[128]{0:T(128)S(1)} %convert_add_fusion), kind=kOutput, calls=%fused_computation.8 | convolution fusion | flops 85229568 | bytes 983552 | tf_op jit(solution)/shard_map/dot_general | solution.py:202
  6.3 7.6 %all-to-all-start = ((bf16[32,8,1280]{2,1,0:T(8,128)(2,1)}), bf16[32,8,1280]{2,1,0:T(8,128)(2,1)S(1)}, u32[]{:S(2)}, u32[]{:S(2)}) async-start(bf16[32,8,1280]{2,1,0:T(8,128)(2,1)} %fusion.6), calls=%async_computation | async-start | bytes 1310720 | tf_op jit(solution)/shard_map/all_to_all | solution.py:204
  15.2 9.6 %all-to-all-done = bf16[32,8,1280]{2,1,0:T(8,128)(2,1)S(1)} async-done(((bf16[32,8,1280]{2,1,0:T(8,128)(2,1)}), bf16[32,8,1280]{2,1,0:T(8,128)(2,1)S(1)}, u32[]{:S(2)}, u32[]{:S(2)}) %all-to-all-start) | async-done | bytes 655392 | tf_op jit(solution)/shard_map/all_to_all | solution.py:204
  25.3 7.5 %fusion.1 = f32[256,8,4,128]{3,2,1,0:T(4,128)S(1)} fusion(s32[256,128]{1,0:T(8,128)S(1)} %get-tuple-element.6, pred[256,4,128]{2,1,0:T(4,128)(4,1)S(1)} %iota_compare_fusion.4, bf16[256,8,128]{2,1,0:T(8,128)(2,1)S(1)} %bitcast.134), kind=kOutput, calls=%fused_computation.3 | convolution fusion | flops 273678336 | bytes 4980736 | tf_op jit(solution)/shard_map/ibjh,ihc->ibjc/dot_general | solution.py:151
  32.9 3.2 %fusion.4 = f32[64,8,128,1]{2,0,3,1:T(8,128)S(1)} fusion(f32[256,8,4,128]{3,2,1,0:T(4,128)S(1)} %fusion.1, s32[256,4]{0,1:T(4,128)S(1)} %iota_add_fusion), kind=kOutput, calls=%fused_computation.5 | convolution fusion | flops 402718720 | bytes 4460544 | tf_op jit(solution)/shard_map/ibjc,ijr->brc/dot_general | solution.py:156
  36.9 4.9 %collective-permute-start.1 = (f32[8,4,15,128]{3,2,1,0:T(8,128)}, f32[8,4,15,128]{3,2,1,0:T(8,128)S(1)}, u32[]{:S(2)}, u32[]{:S(2)}) collective-permute-start(f32[8,4,15,128]{3,2,1,0:T(8,128)} %get-tuple-element.10), channel_id=1, source_target_pairs={{1,0},{2,1},{3,2},{4,3},{5,4},{6,5},{7,6},{8,7},{9,8},{10,9},{11,1... | collective-permute-start | bytes 737288 | tf_op jit(solution)/shard_map/ppermute | solution.py:29
  41.8 1.9 %collective-permute-start = (f32[8,4,15,128]{3,2,1,0:T(8,128)}, f32[8,4,15,128]{3,2,1,0:T(8,128)S(1)}, u32[]{:S(2)}, u32[]{:S(2)}) collective-permute-start(f32[8,4,15,128]{3,2,1,0:T(8,128)} %get-tuple-element.9), channel_id=1, source_target_pairs={{0,1},{1,2},{2,3},{3,4},{4,5},{5,6},{6,7},{7,8},{8,9},{9,10},{10,1... | collective-permute-start | bytes 737288 | tf_op jit(solution)/shard_map/ppermute | solution.py:27
  43.8 1.0 %convolution_bitcast_fusion = f32[8,4,31,256]{3,2,0,1:T(8,128)S(1)} fusion(f32[4,8,31,31]{3,2,1,0:T(8,128)S(1)} %reshape.163, f32[31,256,1,1]{1,0,3,2:T(8,128)S(1)} %copy-done.3), kind=kOutput, calls=%fused_computation.16 | convolution fusion | flops 94470144 | bytes 1170560 | tf_op jit(solution)/shard_map/sbuv,vf->sbuf/dot_general | solution.py:117
  44.8 1.1 %copy.47 = f32[8,4,31,256]{3,2,1,0:T(8,128)} copy(f32[8,4,31,256]{3,2,0,1:T(8,128)S(1)} %convolution_bitcast_fusion) | data formatting | bytes 2031616 | tf_op jit(solution)/shard_map/transpose | solution.py:129
  46.0 5.8 %collective-permute-done = f32[8,4,15,128]{3,2,1,0:T(8,128)S(1)} collective-permute-done((f32[8,4,15,128]{3,2,1,0:T(8,128)}, f32[8,4,15,128]{3,2,1,0:T(8,128)S(1)}, u32[]{:S(2)}, u32[]{:S(2)}) %collective-permute-start) | collective-permute-done | bytes 245792 | tf_op jit(solution)/shard_map/ppermute | solution.py:27
  51.8 2.5 %fusion.17.spec_ref = f32[32,46,256]{2,1,0:T(8,128)} fusion(f32[128,256,1]{1,0,2:T(8,128)S(1)} %copy-done.1, f32[32,15,128]{2,1,0:T(8,128)S(1)} %bitcast.135, f32[32,16,128]{2,1,0:T(8,128)S(1)} %bitcast.126, f32[32,15,128]{2,1,0:T(8,128)S(1)} %bitcast.136), kind=kOutput, calls=%fused_computation.27 | convolution fusion | flops 579190784 | bytes 2392064 | tf_op jit(solution)/shard_map/cyx,xf->cyf/dot_general | solution.py:126
  54.4 6.3 %shard_map.136 = f32[32,16,256]{2,1,0:T(8,128)} custom-call(f32[32,46,256]{2,1,0:T(8,128)} %fusion.17.spec_ref, f32[32,31,256]{2,1,0:T(8,128)} %bitcast.124), custom_call_target="tpu_custom_call" | custom-call | tf_op jit(solution)/shard_map/pallas_call | solution.py:99
  60.7 1.9 %convolution_bitcast_fusion.1 = f32[4,3,16,256]{3,1,2,0:T(4,128)S(1)} fusion(f32[8,4,16,256]{3,2,1,0:T(8,128)} %bitcast.131, f32[32,3]{0,1:T(4,128)S(1)} %copy-done.4, s32[]{:T(128)S(6)} %select_n.79), kind=kOutput, calls=%fused_computation.19 | convolution fusion | flops 4718592 | bytes 721284 | tf_op jit(solution)/shard_map/bsyf,bc->scyf/dot_general | solution.py:131
  63.0 4.1 %collective-permute-start.4 = (f32[3,16,128]{2,1,0:T(8,128)S(1)}, f32[3,16,128]{2,1,0:T(8,128)S(1)}, u32[]{:S(2)}, u32[]{:S(2)}) collective-permute-start(f32[3,16,128]{2,1,0:T(8,128)S(1)} %get-tuple-element.12), channel_id=1, source_target_pairs={{0,96},{32,0},{64,32},{96,64},{1,97},{33,1},{65,33},{97,65},{2,98}... | collective-permute-start | bytes 73736 | tf_op jit(solution)/shard_map/ppermute | solution.py:213
  67.1 1.3 %collective-permute-start.2 = (f32[3,16,128]{2,1,0:T(8,128)S(1)}, f32[3,16,128]{2,1,0:T(8,128)S(1)}, u32[]{:S(2)}, u32[]{:S(2)}) collective-permute-start(f32[3,16,128]{2,1,0:T(8,128)S(1)} %get-tuple-element.11), channel_id=1, source_target_pairs={{0,32},{32,64},{64,96},{96,0},{1,33},{33,65},{65,97},{97,1},{2,34}... | collective-permute-start | bytes 73736 | tf_op jit(solution)/shard_map/ppermute | solution.py:213
  68.6 3.8 %collective-permute-done.3 = f32[3,16,128]{2,1,0:T(8,128)S(1)} collective-permute-done((f32[3,16,128]{2,1,0:T(8,128)S(1)}, f32[3,16,128]{2,1,0:T(8,128)S(1)}, u32[]{:S(2)}, u32[]{:S(2)}) %collective-permute-start.3) | collective-permute-done | bytes 24608 | tf_op jit(solution)/shard_map/ppermute | solution.py:213
  72.5 1.9 %collective-permute-start.6 = (bf16[1,3,2,128]{3,2,1,0:T(2,128)(2,1)S(1)}, bf16[1,3,2,128]{3,2,1,0:T(2,128)(2,1)S(1)}, u32[]{:S(2)}, u32[]{:S(2)}) collective-permute-start(bf16[1,3,2,128]{3,2,1,0:T(2,128)(2,1)S(1)} %get-tuple-element.17), channel_id=1, source_target_pairs={{1,0},{2,1},{3,2},{4,3},{5,4},{6,5},{7,6},{8,7},{9,8},{10,9},{11,1... | collective-permute-start | bytes 4616 | tf_op jit(solution)/shard_map/ppermute | solution.py:29
  74.4 2.6 %collective-permute-start.5 = (bf16[1,3,2,128]{3,2,1,0:T(2,128)(2,1)S(1)}, bf16[1,3,2,128]{3,2,1,0:T(2,128)(2,1)S(1)}, u32[]{:S(2)}, u32[]{:S(2)}) collective-permute-start(bf16[1,3,2,128]{3,2,1,0:T(2,128)(2,1)S(1)} %get-tuple-element.16), channel_id=1, source_target_pairs={{0,1},{1,2},{2,3},{3,4},{4,5},{5,6},{6,7},{7,8},{8,9},{9,10},{10,1... | collective-permute-start | bytes 4616 | tf_op jit(solution)/shard_map/ppermute | solution.py:27
  77.0 4.4 %collective-permute-done.5 = bf16[1,3,2,128]{3,2,1,0:T(2,128)(2,1)S(1)} collective-permute-done((bf16[1,3,2,128]{3,2,1,0:T(2,128)(2,1)S(1)}, bf16[1,3,2,128]{3,2,1,0:T(2,128)(2,1)S(1)}, u32[]{:S(2)}, u32[]{:S(2)}) %collective-permute-start.5) | collective-permute-done | bytes 1568 | tf_op jit(solution)/shard_map/ppermute | solution.py:27
  82.4 1.4 %fusion.16 = bf16[18,1,8,17,64]{4,2,3,0,1:T(8,128)(2,1)S(1)} fusion(pred[18]{0:T(512)(128)(4,1)S(1)} %and_or_fusion, pred[8,17]{0,1:T(8,128)(4,1)S(1)} %copy-done.8, bf16[3,20,1,7,2]{3,0,4,1,2:T(4,128)(2,1)S(1)} %slice.46, bf16[3,20,1,8,17]{3,0,4,1,2:T(4,128)(2,1)S(1)} %copy.51, bf16[64,3,3,3]{0,3,2,1:T(4,128)(2,1)S(1)} %copy-done.6), kind=kOutput, calls=%fused_computation.26 | convolution fusion | flops 9925056 | bytes 334954 | tf_op jit(solution)/shard_map/conv_general_dilated | solution.py:37
  83.8 1.5 %convolution_convert_fusion.1 = bf16[16,8,17,64]{3,1,2,0:T(8,128)(2,1)S(1)} fusion(bf16[64,64,3,3]{1,0,3,2:T(8,128)(2,1)S(1)} %copy-done.5, bf16[18,1,7,1,64]{4,2,3,0,1:T(8,128)(2,1)S(1)} %get-tuple-element.8, bf16[18,1,7,1,64]{4,2,3,0,1:T(8,128)(2,1)S(1)} %get-tuple-element.7, bf16[18,1,8,17,64]{4,2,3,0,1:T(8,128)(2,1)S(1)} %fusion.16), kind=kOutput, calls=%fused_computation.17 | convolution fusion | flops 162322432 | bytes 697856 | tf_op jit(solution)/shard_map/conv_general_dilated | solution.py:37
  85.4 1.3 %copy.54 = bf16[1,64,16,128]{3,2,1,0:T(8,128)(2,1)} copy(bf16[1,64,16,128]{1,2,3,0:T(8,128)(2,1)S(1)} %slice_bitcast_fusion) | data formatting | bytes 524288 | tf_op jit(solution)/shard_map/convert_element_type | solution.py:227
  (54 shorter events, 7.5 us)
Async XLA Ops:
  0.0 14.0 %copy-start = (f32[64,8,961]{2,1,0:T(8,128)S(1)}, f32[64,8,961]{2,1,0:T(8,128)}, u32[]{:S(2)}) copy-start(f32[64,8,961]{2,1,0:T(8,128)} %param.20) | copy-start | bytes 5904388
  2.0 12.0 %copy-start.7 = (s32[1,4,1]{1,2,0:T(1,128)S(1)}, s32[1,4,1]{1,2,0:T(1,128)}, u32[]{:S(2)}) copy-start(s32[1,4,1]{1,2,0:T(1,128)} %param.21) | copy-start | bytes 52
  6.3 18.4 %all-to-all-start = ((bf16[32,8,1280]{2,1,0:T(8,128)(2,1)}), bf16[32,8,1280]{2,1,0:T(8,128)(2,1)S(1)}, u32[]{:S(2)}, u32[]{:S(2)}) async-start(bf16[32,8,1280]{2,1,0:T(8,128)(2,1)} %fusion.6), calls=%async_computation | async-start | bytes 1310720 | tf_op jit(solution)/shard_map/all_to_all | solution.py:204
  32.9 10.9 %copy-start.3 = (f32[31,256,1,1]{1,0,3,2:T(8,128)S(1)}, f32[31,256,1,1]{1,0,3,2:T(8,128)}, u32[]{:S(2)}) copy-start(f32[31,256,1,1]{1,0,3,2:T(8,128)} %constant.140) | copy-start | bytes 95236
  36.9 9.1 %collective-permute-start.1 = (f32[8,4,15,128]{3,2,1,0:T(8,128)}, f32[8,4,15,128]{3,2,1,0:T(8,128)S(1)}, u32[]{:S(2)}, u32[]{:S(2)}) collective-permute-start(f32[8,4,15,128]{3,2,1,0:T(8,128)} %get-tuple-element.10), channel_id=1, source_target_pairs={{1,0},{2,1},{3,2},{4,3},{5,4},{6,5},{7,6},{8,7},{9,8},{10,9},{11,1... | collective-permute-start | bytes 737288 | tf_op jit(solution)/shard_map/ppermute | solution.py:29
  41.8 10.0 %collective-permute-start = (f32[8,4,15,128]{3,2,1,0:T(8,128)}, f32[8,4,15,128]{3,2,1,0:T(8,128)S(1)}, u32[]{:S(2)}, u32[]{:S(2)}) collective-permute-start(f32[8,4,15,128]{3,2,1,0:T(8,128)} %get-tuple-element.9), channel_id=1, source_target_pairs={{0,1},{1,2},{2,3},{3,4},{4,5},{5,6},{6,7},{7,8},{8,9},{9,10},{10,1... | collective-permute-start | bytes 737288 | tf_op jit(solution)/shard_map/ppermute | solution.py:27
  44.7 7.1 %copy-start.1 = (f32[128,256,1]{1,0,2:T(8,128)S(1)}, f32[128,256,1]{1,0,2:T(8,128)}, u32[]{:S(2)}) copy-start(f32[128,256,1]{1,0,2:T(8,128)} %constant.139) | copy-start | bytes 393220
  54.4 6.3 %copy-start.4 = (f32[32,3]{0,1:T(4,128)S(1)}, f32[32,3]{0,1:T(4,128)}, u32[]{:S(2)}) copy-start(f32[32,3]{0,1:T(4,128)} %param.22) | copy-start | bytes 1156
  54.4 8.2 %copy-start.2 = (f32[256,128,1,1]{1,0,3,2:T(8,128)S(1)}, f32[256,128,1,1]{1,0,3,2:T(8,128)}, u32[]{:S(2)}) copy-start(f32[256,128,1,1]{1,0,3,2:T(8,128)} %constant.141) | copy-start | bytes 393220
  60.7 21.6 %copy-start.6 = (bf16[64,3,3,3]{0,3,2,1:T(4,128)(2,1)S(1)}, bf16[64,3,3,3]{0,3,2,1:T(4,128)(2,1)}, u32[]{:S(2)}) copy-start(bf16[64,3,3,3]{0,3,2,1:T(4,128)(2,1)} %param.23) | copy-start | bytes 10372
  60.7 21.6 %copy-start.8 = (pred[8,17]{0,1:T(8,128)(4,1)S(1)}, pred[8,17]{0,1:T(8,128)(4,1)}, u32[]{:S(2)}) copy-start(pred[8,17]{0,1:T(8,128)(4,1)} %constant.137) | copy-start | bytes 412
  63.0 5.6 %collective-permute-start.4 = (f32[3,16,128]{2,1,0:T(8,128)S(1)}, f32[3,16,128]{2,1,0:T(8,128)S(1)}, u32[]{:S(2)}, u32[]{:S(2)}) collective-permute-start(f32[3,16,128]{2,1,0:T(8,128)S(1)} %get-tuple-element.12), channel_id=1, source_target_pairs={{0,96},{32,0},{64,32},{96,64},{1,97},{33,1},{65,33},{97,65},{2,98}... | collective-permute-start | bytes 73736 | tf_op jit(solution)/shard_map/ppermute | solution.py:213
  67.1 5.3 %collective-permute-start.3 = (f32[3,16,128]{2,1,0:T(8,128)S(1)}, f32[3,16,128]{2,1,0:T(8,128)S(1)}, u32[]{:S(2)}, u32[]{:S(2)}) collective-permute-start(f32[3,16,128]{2,1,0:T(8,128)S(1)} %get-tuple-element.13), channel_id=1, source_target_pairs={{0,64},{32,96},{64,0},{96,32},{1,65},{33,97},{65,1},{97,33},{2,66}... | collective-permute-start | bytes 73736 | tf_op jit(solution)/shard_map/ppermute | solution.py:213
  67.1 5.3 %collective-permute-start.2 = (f32[3,16,128]{2,1,0:T(8,128)S(1)}, f32[3,16,128]{2,1,0:T(8,128)S(1)}, u32[]{:S(2)}, u32[]{:S(2)}) collective-permute-start(f32[3,16,128]{2,1,0:T(8,128)S(1)} %get-tuple-element.11), channel_id=1, source_target_pairs={{0,32},{32,64},{64,96},{96,0},{1,33},{33,65},{65,97},{97,1},{2,34}... | collective-permute-start | bytes 73736 | tf_op jit(solution)/shard_map/ppermute | solution.py:213
  72.5 4.5 %collective-permute-start.6 = (bf16[1,3,2,128]{3,2,1,0:T(2,128)(2,1)S(1)}, bf16[1,3,2,128]{3,2,1,0:T(2,128)(2,1)S(1)}, u32[]{:S(2)}, u32[]{:S(2)}) collective-permute-start(bf16[1,3,2,128]{3,2,1,0:T(2,128)(2,1)S(1)} %get-tuple-element.17), channel_id=1, source_target_pairs={{1,0},{2,1},{3,2},{4,3},{5,4},{6,5},{7,6},{8,7},{9,8},{10,9},{11,1... | collective-permute-start | bytes 4616 | tf_op jit(solution)/shard_map/ppermute | solution.py:29
  74.4 7.0 %collective-permute-start.5 = (bf16[1,3,2,128]{3,2,1,0:T(2,128)(2,1)S(1)}, bf16[1,3,2,128]{3,2,1,0:T(2,128)(2,1)S(1)}, u32[]{:S(2)}, u32[]{:S(2)}) collective-permute-start(bf16[1,3,2,128]{3,2,1,0:T(2,128)(2,1)S(1)} %get-tuple-element.16), channel_id=1, source_target_pairs={{0,1},{1,2},{2,3},{3,4},{4,5},{5,6},{6,7},{7,8},{8,9},{9,10},{10,1... | collective-permute-start | bytes 4616 | tf_op jit(solution)/shard_map/ppermute | solution.py:27
  82.4 1.5 %copy-start.5 = (bf16[64,64,3,3]{1,0,3,2:T(8,128)(2,1)S(1)}, bf16[64,64,3,3]{1,0,3,2:T(8,128)(2,1)}, u32[]{:S(2)}) copy-start(bf16[64,64,3,3]{1,0,3,2:T(8,128)(2,1)} %param.24) | copy-start | bytes 221188

commit v6 on v5

--- a/solution.py
+++ b/solution.py
@@ -207,12 +207,25 @@
     wave_index = lax.axis_index("wave")
     my_response = lax.dynamic_slice_in_dim(response, wave_index * band_dev, band_dev, 0)
     partial = patch_blur(extended, kern, my_response, K // 2)
-    color = lax.dynamic_index_in_dim(partial, wave_index, 0, keepdims=False)
-    for step in range(1, wave_count):
-        piece = lax.dynamic_index_in_dim(partial, (wave_index + step) % wave_count, 0, keepdims=False)
-        color = color + lax.ppermute(
-            piece, "wave", [(i, (i + step) % wave_count) for i in range(wave_count)]
-        )
+    if wave_count == 4:
+        far = [(i, i ^ 2) for i in range(4)]
+        near = [(i, i ^ 1) for i in range(4)]
+        pairs = partial.reshape(2, 2, *partial.shape[1:])
+        mine = lax.dynamic_index_in_dim(pairs, wave_index // 2, 0, keepdims=False)
+        theirs = lax.dynamic_index_in_dim(pairs, 1 - wave_index // 2, 0, keepdims=False)
+        half = mine + lax.ppermute(theirs, "wave", far)
+        own = lax.dynamic_index_in_dim(half, wave_index % 2, 0, keepdims=False)
+        other = lax.dynamic_index_in_dim(half, 1 - wave_index % 2, 0, keepdims=False)
+        color = own + lax.ppermute(other, "wave", near)
+    else:
+        color = lax.dynamic_index_in_dim(partial, wave_index, 0, keepdims=False)
+        for step in range(1, wave_count):
+            piece = lax.dynamic_index_in_dim(
+                partial, (wave_index + step) % wave_count, 0, keepdims=False
+            )
+            color = color + lax.ppermute(
+                piece, "wave", [(i, (i + step) % wave_count) for i in range(wave_count)]
+            )
     sensor = lax.reduce_precision(color[None], exponent_bits=8, mantissa_bits=7)
     sensor = sensor.astype(jnp.bfloat16)
     rimmed = padded_2(sensor, (("tile", 2),), 2)

time: 87.2 us -> 87.9 us (level)
    ppermute x3 -> x2, waiting for transfers between devices: 4.07 us -> 4.71 us  [the longest x1 2.45 us: per_device(): color = own + lax.ppermute(other, 'wave', near)]
    ppermute x3 -> x2, starting transfers between devices: 5.37 us -> 5.41 us  [the longest x1 3.95 us: per_device(): half = mine + lax.ppermute(theirs, 'wave', far)]
  transfers between devices with their start and end apart: 8 -> 7, of which waited for: 6 -> 6; matrix products, arithmetic and copies ran while one was open for 4% -> 4% of each run, Pallas kernels for 0% -> 0%
where the time goes in v6:
time: 87.9 us; the launch traced here: 87.4 us
  waiting for transfers between devices  24.7 us (28%)
  starting transfers between devices  24.4 us (28%)
  matrix products  21.4 us (24%)
  Pallas kernels  6.32 us (7%)
  local copies, waits for them, and re-layouts  5.77 us (7%)
  other arithmetic  4.49 us (5%)
    ppermute x2, waiting for transfers between devices, padded_2(): lax.ppermute(tail, axis, [(i, (i + 1) % count) for i in range(ends)])  10.2 us
    all_to_all x1, waiting for transfers between devices, per_device(): got = lax.all_to_all(send, 'tile', split_axis=0, concat_axis=0, tiled=True)  9.59 us
    all_to_all x1, starting transfers between devices, per_device(): got = lax.all_to_all(send, 'tile', split_axis=0, concat_axis=0, tiled=True)  7.62 us
    dot_general x1, matrix products, window_splat(): jnp.einsum('ibjh,ihc->ibjc', spread, onehot, preferred_element_type=jnp.f...  7.54 us
    ppermute x2, starting transfers between devices, padded_2(): lax.ppermute(head, axis, [((i + 1) % count, i) for i in range(ends)])  6.84 us
    pallas_call x1, Pallas kernels, row_taps(): pl.pallas_call(row_taps_kernel, out_shape=jax.ShapeDtypeStruct((channels,...  6.32 us
    ppermute x2, starting transfers between devices, padded_2(): lax.ppermute(tail, axis, [(i, (i + 1) % count) for i in range(ends)])  4.51 us
    ppermute x1, starting transfers between devices, per_device(): half = mine + lax.ppermute(theirs, 'wave', far)  3.95 us
  transfers between devices with their start and end apart: 7, of which 6 were waited for; matrix products, arithmetic and copies ran while one was open for 4% of the time, Pallas kernels for 0%

profile of v6, /device:TPU:2, one launch (start us, length us, event | category | flops | bytes accessed | tf_op | source)
XLA Modules:
  0.0 87.4 jit_solution(9279831049478072529)
XLA Ops:
  0.9 1.0 %broadcast_select_fusion = bf16[128,8,128]{2,1,0:T(8,128)(2,1)S(1)} fusion(bf16[128,8,128]{2,1,0:T(8,128)(2,1)} %param.14, pred[128,128]{1,0:T(8,128)(4,1)S(1)} %iota_compare_fusion.8), kind=kLoop, calls=%fused_computation.61 | loop fusion | flops 131072 | bytes 540672 | tf_op jit(solution)/shard_map/jit(_where)/select_n | solution.py:180
  5.2 1.2 %fusion.6 = bf16[32,8,1280]{2,1,0:T(8,128)(2,1)} fusion(bf16[128,128]{1,0:T(8,128)(2,1)S(1)} %get-tuple-element.12, bf16[128,128]{1,0:T(8,128)(2,1)S(1)} %get-tuple-element.11, bf16[128,1024]{1,0:T(8,128)(2,1)S(1)} %bitcast.129, s32[128]{0:T(128)S(1)} %convert_add_fusion), kind=kOutput, calls=%fused_computation.8 | convolution fusion | flops 85229568 | bytes 983552 | tf_op jit(solution)/shard_map/dot_general | solution.py:202
  6.3 7.6 %all-to-all-start = ((bf16[32,8,1280]{2,1,0:T(8,128)(2,1)}), bf16[32,8,1280]{2,1,0:T(8,128)(2,1)S(1)}, u32[]{:S(2)}, u32[]{:S(2)}) async-start(bf16[32,8,1280]{2,1,0:T(8,128)(2,1)} %fusion.6), calls=%async_computation | async-start | bytes 1310720 | tf_op jit(solution)/shard_map/all_to_all | solution.py:204
  15.2 9.6 %all-to-all-done = bf16[32,8,1280]{2,1,0:T(8,128)(2,1)S(1)} async-done(((bf16[32,8,1280]{2,1,0:T(8,128)(2,1)}), bf16[32,8,1280]{2,1,0:T(8,128)(2,1)S(1)}, u32[]{:S(2)}, u32[]{:S(2)}) %all-to-all-start) | async-done | bytes 655392 | tf_op jit(solution)/shard_map/all_to_all | solution.py:204
  25.3 7.5 %fusion.1 = f32[256,8,4,128]{3,2,1,0:T(4,128)S(1)} fusion(s32[256,128]{1,0:T(8,128)S(1)} %get-tuple-element.6, pred[256,4,128]{2,1,0:T(4,128)(4,1)S(1)} %iota_compare_fusion.4, bf16[256,8,128]{2,1,0:T(8,128)(2,1)S(1)} %bitcast.131), kind=kOutput, calls=%fused_computation.3 | convolution fusion | flops 273678336 | bytes 4980736 | tf_op jit(solution)/shard_map/ibjh,ihc->ibjc/dot_general | solution.py:151
  32.9 3.2 %fusion.4 = f32[64,8,128,1]{2,0,3,1:T(8,128)S(1)} fusion(f32[256,8,4,128]{3,2,1,0:T(4,128)S(1)} %fusion.1, s32[256,4]{0,1:T(4,128)S(1)} %iota_add_fusion), kind=kOutput, calls=%fused_computation.5 | convolution fusion | flops 402718720 | bytes 4460544 | tf_op jit(solution)/shard_map/ibjc,ijr->brc/dot_general | solution.py:156
  36.9 4.9 %collective-permute-start.1 = (f32[8,4,15,128]{3,2,1,0:T(8,128)}, f32[8,4,15,128]{3,2,1,0:T(8,128)S(1)}, u32[]{:S(2)}, u32[]{:S(2)}) collective-permute-start(f32[8,4,15,128]{3,2,1,0:T(8,128)} %get-tuple-element.10), channel_id=1, source_target_pairs={{1,0},{2,1},{3,2},{4,3},{5,4},{6,5},{7,6},{8,7},{9,8},{10,9},{11,1... | collective-permute-start | bytes 737288 | tf_op jit(solution)/shard_map/ppermute | solution.py:29
  41.8 1.9 %collective-permute-start = (f32[8,4,15,128]{3,2,1,0:T(8,128)}, f32[8,4,15,128]{3,2,1,0:T(8,128)S(1)}, u32[]{:S(2)}, u32[]{:S(2)}) collective-permute-start(f32[8,4,15,128]{3,2,1,0:T(8,128)} %get-tuple-element.9), channel_id=1, source_target_pairs={{0,1},{1,2},{2,3},{3,4},{4,5},{5,6},{6,7},{7,8},{8,9},{9,10},{10,1... | collective-permute-start | bytes 737288 | tf_op jit(solution)/shard_map/ppermute | solution.py:27
  43.8 1.0 %convolution_bitcast_fusion = f32[8,4,31,256]{3,2,0,1:T(8,128)S(1)} fusion(f32[4,8,31,31]{3,2,1,0:T(8,128)S(1)} %reshape.166, f32[31,256,1,1]{1,0,3,2:T(8,128)S(1)} %copy-done.3), kind=kOutput, calls=%fused_computation.16 | convolution fusion | flops 94470144 | bytes 1170560 | tf_op jit(solution)/shard_map/sbuv,vf->sbuf/dot_general | solution.py:117
  44.8 1.1 %copy.47 = f32[8,4,31,256]{3,2,1,0:T(8,128)} copy(f32[8,4,31,256]{3,2,0,1:T(8,128)S(1)} %convolution_bitcast_fusion) | data formatting | bytes 2031616 | tf_op jit(solution)/shard_map/transpose | solution.py:129
  46.0 5.8 %collective-permute-done = f32[8,4,15,128]{3,2,1,0:T(8,128)S(1)} collective-permute-done((f32[8,4,15,128]{3,2,1,0:T(8,128)}, f32[8,4,15,128]{3,2,1,0:T(8,128)S(1)}, u32[]{:S(2)}, u32[]{:S(2)}) %collective-permute-start) | collective-permute-done | bytes 245792 | tf_op jit(solution)/shard_map/ppermute | solution.py:27
  51.9 2.6 %fusion.17.spec_ref = f32[32,46,256]{2,1,0:T(8,128)} fusion(f32[128,256,1]{1,0,2:T(8,128)S(1)} %copy-done.1, f32[32,15,128]{2,1,0:T(8,128)S(1)} %bitcast.134, f32[32,16,128]{2,1,0:T(8,128)S(1)} %bitcast.123, f32[32,15,128]{2,1,0:T(8,128)S(1)} %bitcast.135), kind=kOutput, calls=%fused_computation.27 | convolution fusion | flops 579190784 | bytes 2392064 | tf_op jit(solution)/shard_map/cyx,xf->cyf/dot_general | solution.py:126
  54.4 6.3 %shard_map.136 = f32[32,16,256]{2,1,0:T(8,128)} custom-call(f32[32,46,256]{2,1,0:T(8,128)} %fusion.17.spec_ref, f32[32,31,256]{2,1,0:T(8,128)} %bitcast.121), custom_call_target="tpu_custom_call" | custom-call | tf_op jit(solution)/shard_map/pallas_call | solution.py:99
  60.7 1.9 %convolution_bitcast_fusion.1 = f32[4,3,16,256]{3,1,2,0:T(4,128)S(1)} fusion(f32[8,4,16,256]{3,2,1,0:T(8,128)} %bitcast.128, f32[32,3]{0,1:T(4,128)S(1)} %copy-done.4, s32[]{:T(128)S(6)} %select_n.79), kind=kOutput, calls=%fused_computation.19 | convolution fusion | flops 4718592 | bytes 721284 | tf_op jit(solution)/shard_map/bsyf,bc->scyf/dot_general | solution.py:131
  63.0 4.0 %collective-permute-start.2 = (f32[2,3,16,128]{3,2,1,0:T(8,128)S(1)}, f32[2,3,16,128]{3,2,1,0:T(8,128)S(1)}, u32[]{:S(2)}, u32[]{:S(2)}) collective-permute-start(f32[2,3,16,128]{3,2,1,0:T(8,128)S(1)} %dynamic-slice_bitcast_fusion), channel_id=1, source_target_pairs={{0,64},{32,96},{64,0},{96,32},{1,65},{33,97},{65,1},{97,33},{2,66}... | collective-permute-start | bytes 147464 | tf_op jit(solution)/shard_map/ppermute | solution.py:216
  67.0 2.3 %collective-permute-done.2 = f32[2,3,16,128]{3,2,1,0:T(8,128)S(1)} collective-permute-done((f32[2,3,16,128]{3,2,1,0:T(8,128)S(1)}, f32[2,3,16,128]{3,2,1,0:T(8,128)S(1)}, u32[]{:S(2)}, u32[]{:S(2)}) %collective-permute-start.2) | collective-permute-done | bytes 49184 | tf_op jit(solution)/shard_map/ppermute | solution.py:216
  69.2 1.5 %collective-permute-start.3 = (f32[3,16,128]{2,1,0:T(8,128)S(1)}, f32[3,16,128]{2,1,0:T(8,128)S(1)}, u32[]{:S(2)}, u32[]{:S(2)}) collective-permute-start(f32[3,16,128]{2,1,0:T(8,128)S(1)} %dynamic-slice_bitcast_fusion.1), channel_id=1, source_target_pairs={{0,32},{32,0},{64,96},{96,64},{1,33},{33,1},{65,97},{97,65},{2,34}... | collective-permute-start | bytes 73736 | tf_op jit(solution)/shard_map/ppermute | solution.py:219
  70.7 2.5 %collective-permute-done.3 = f32[3,16,128]{2,1,0:T(8,128)S(1)} collective-permute-done((f32[3,16,128]{2,1,0:T(8,128)S(1)}, f32[3,16,128]{2,1,0:T(8,128)S(1)}, u32[]{:S(2)}, u32[]{:S(2)}) %collective-permute-start.3) | collective-permute-done | bytes 24608 | tf_op jit(solution)/shard_map/ppermute | solution.py:219
  73.2 1.9 %collective-permute-start.5 = (bf16[1,3,2,128]{3,2,1,0:T(2,128)(2,1)S(1)}, bf16[1,3,2,128]{3,2,1,0:T(2,128)(2,1)S(1)}, u32[]{:S(2)}, u32[]{:S(2)}) collective-permute-start(bf16[1,3,2,128]{3,2,1,0:T(2,128)(2,1)S(1)} %get-tuple-element.14), channel_id=1, source_target_pairs={{1,0},{2,1},{3,2},{4,3},{5,4},{6,5},{7,6},{8,7},{9,8},{10,9},{11,1... | collective-permute-start | bytes 4616 | tf_op jit(solution)/shard_map/ppermute | solution.py:29
  75.1 2.6 %collective-permute-start.4 = (bf16[1,3,2,128]{3,2,1,0:T(2,128)(2,1)S(1)}, bf16[1,3,2,128]{3,2,1,0:T(2,128)(2,1)S(1)}, u32[]{:S(2)}, u32[]{:S(2)}) collective-permute-start(bf16[1,3,2,128]{3,2,1,0:T(2,128)(2,1)S(1)} %get-tuple-element.13), channel_id=1, source_target_pairs={{0,1},{1,2},{2,3},{3,4},{4,5},{5,6},{6,7},{7,8},{8,9},{9,10},{10,1... | collective-permute-start | bytes 4616 | tf_op jit(solution)/shard_map/ppermute | solution.py:27
  77.7 4.4 %collective-permute-done.4 = bf16[1,3,2,128]{3,2,1,0:T(2,128)(2,1)S(1)} collective-permute-done((bf16[1,3,2,128]{3,2,1,0:T(2,128)(2,1)S(1)}, bf16[1,3,2,128]{3,2,1,0:T(2,128)(2,1)S(1)}, u32[]{:S(2)}, u32[]{:S(2)}) %collective-permute-start.4) | collective-permute-done | bytes 1568 | tf_op jit(solution)/shard_map/ppermute | solution.py:27
  83.1 1.4 %fusion.16 = bf16[18,1,8,17,64]{4,2,3,0,1:T(8,128)(2,1)S(1)} fusion(pred[18]{0:T(512)(128)(4,1)S(1)} %and_or_fusion, pred[8,17]{0,1:T(8,128)(4,1)S(1)} %copy-done.8, bf16[3,20,1,7,2]{3,0,4,1,2:T(4,128)(2,1)S(1)} %slice.46, bf16[3,20,1,8,17]{3,0,4,1,2:T(4,128)(2,1)S(1)} %copy.51, bf16[64,3,3,3]{0,3,2,1:T(4,128)(2,1)S(1)} %copy-done.6), kind=kOutput, calls=%fused_computation.26 | convolution fusion | flops 9925056 | bytes 334954 | tf_op jit(solution)/shard_map/conv_general_dilated | solution.py:37
  84.5 1.5 %convolution_convert_fusion.1 = bf16[16,8,17,64]{3,1,2,0:T(8,128)(2,1)S(1)} fusion(bf16[64,64,3,3]{1,0,3,2:T(8,128)(2,1)S(1)} %copy-done.5, bf16[18,1,7,1,64]{4,2,3,0,1:T(8,128)(2,1)S(1)} %get-tuple-element.8, bf16[18,1,7,1,64]{4,2,3,0,1:T(8,128)(2,1)S(1)} %get-tuple-element.7, bf16[18,1,8,17,64]{4,2,3,0,1:T(8,128)(2,1)S(1)} %fusion.16), kind=kOutput, calls=%fused_computation.17 | convolution fusion | flops 162322432 | bytes 697856 | tf_op jit(solution)/shard_map/conv_general_dilated | solution.py:37
  86.1 1.3 %copy.54 = bf16[1,64,16,128]{3,2,1,0:T(8,128)(2,1)} copy(bf16[1,64,16,128]{1,2,3,0:T(8,128)(2,1)S(1)} %slice_bitcast_fusion) | data formatting | bytes 524288 | tf_op jit(solution)/shard_map/convert_element_type | solution.py:240
  (54 shorter events, 8.2 us)
Async XLA Ops:
  0.0 14.0 %copy-start = (f32[64,8,961]{2,1,0:T(8,128)S(1)}, f32[64,8,961]{2,1,0:T(8,128)}, u32[]{:S(2)}) copy-start(f32[64,8,961]{2,1,0:T(8,128)} %param.20) | copy-start | bytes 5904388
  1.9 12.0 %copy-start.7 = (s32[1,4,1]{1,2,0:T(1,128)S(1)}, s32[1,4,1]{1,2,0:T(1,128)}, u32[]{:S(2)}) copy-start(s32[1,4,1]{1,2,0:T(1,128)} %param.21) | copy-start | bytes 52
  6.3 18.4 %all-to-all-start = ((bf16[32,8,1280]{2,1,0:T(8,128)(2,1)}), bf16[32,8,1280]{2,1,0:T(8,128)(2,1)S(1)}, u32[]{:S(2)}, u32[]{:S(2)}) async-start(bf16[32,8,1280]{2,1,0:T(8,128)(2,1)} %fusion.6), calls=%async_computation | async-start | bytes 1310720 | tf_op jit(solution)/shard_map/all_to_all | solution.py:204
  32.9 10.9 %copy-start.3 = (f32[31,256,1,1]{1,0,3,2:T(8,128)S(1)}, f32[31,256,1,1]{1,0,3,2:T(8,128)}, u32[]{:S(2)}) copy-start(f32[31,256,1,1]{1,0,3,2:T(8,128)} %constant.152) | copy-start | bytes 95236
  36.9 9.1 %collective-permute-start.1 = (f32[8,4,15,128]{3,2,1,0:T(8,128)}, f32[8,4,15,128]{3,2,1,0:T(8,128)S(1)}, u32[]{:S(2)}, u32[]{:S(2)}) collective-permute-start(f32[8,4,15,128]{3,2,1,0:T(8,128)} %get-tuple-element.10), channel_id=1, source_target_pairs={{1,0},{2,1},{3,2},{4,3},{5,4},{6,5},{7,6},{8,7},{9,8},{10,9},{11,1... | collective-permute-start | bytes 737288 | tf_op jit(solution)/shard_map/ppermute | solution.py:29
  41.8 10.0 %collective-permute-start = (f32[8,4,15,128]{3,2,1,0:T(8,128)}, f32[8,4,15,128]{3,2,1,0:T(8,128)S(1)}, u32[]{:S(2)}, u32[]{:S(2)}) collective-permute-start(f32[8,4,15,128]{3,2,1,0:T(8,128)} %get-tuple-element.9), channel_id=1, source_target_pairs={{0,1},{1,2},{2,3},{3,4},{4,5},{5,6},{6,7},{7,8},{8,9},{9,10},{10,1... | collective-permute-start | bytes 737288 | tf_op jit(solution)/shard_map/ppermute | solution.py:27
  44.8 7.1 %copy-start.1 = (f32[128,256,1]{1,0,2:T(8,128)S(1)}, f32[128,256,1]{1,0,2:T(8,128)}, u32[]{:S(2)}) copy-start(f32[128,256,1]{1,0,2:T(8,128)} %constant.151) | copy-start | bytes 393220
  54.4 6.3 %copy-start.4 = (f32[32,3]{0,1:T(4,128)S(1)}, f32[32,3]{0,1:T(4,128)}, u32[]{:S(2)}) copy-start(f32[32,3]{0,1:T(4,128)} %param.22) | copy-start | bytes 1156
  54.4 8.2 %copy-start.2 = (f32[256,128,1,1]{1,0,3,2:T(8,128)S(1)}, f32[256,128,1,1]{1,0,3,2:T(8,128)}, u32[]{:S(2)}) copy-start(f32[256,128,1,1]{1,0,3,2:T(8,128)} %constant.153) | copy-start | bytes 393220
  60.7 22.3 %copy-start.6 = (bf16[64,3,3,3]{0,3,2,1:T(4,128)(2,1)S(1)}, bf16[64,3,3,3]{0,3,2,1:T(4,128)(2,1)}, u32[]{:S(2)}) copy-start(bf16[64,3,3,3]{0,3,2,1:T(4,128)(2,1)} %param.23) | copy-start | bytes 10372
  60.7 22.3 %copy-start.8 = (pred[8,17]{0,1:T(8,128)(4,1)S(1)}, pred[8,17]{0,1:T(8,128)(4,1)}, u32[]{:S(2)}) copy-start(pred[8,17]{0,1:T(8,128)(4,1)} %constant.149) | copy-start | bytes 412
  63.0 6.2 %collective-permute-start.2 = (f32[2,3,16,128]{3,2,1,0:T(8,128)S(1)}, f32[2,3,16,128]{3,2,1,0:T(8,128)S(1)}, u32[]{:S(2)}, u32[]{:S(2)}) collective-permute-start(f32[2,3,16,128]{3,2,1,0:T(8,128)S(1)} %dynamic-slice_bitcast_fusion), channel_id=1, source_target_pairs={{0,64},{32,96},{64,0},{96,32},{1,65},{33,97},{65,1},{97,33},{2,66}... | collective-permute-start | bytes 147464 | tf_op jit(solution)/shard_map/ppermute | solution.py:216
  69.2 3.9 %collective-permute-start.3 = (f32[3,16,128]{2,1,0:T(8,128)S(1)}, f32[3,16,128]{2,1,0:T(8,128)S(1)}, u32[]{:S(2)}, u32[]{:S(2)}) collective-permute-start(f32[3,16,128]{2,1,0:T(8,128)S(1)} %dynamic-slice_bitcast_fusion.1), channel_id=1, source_target_pairs={{0,32},{32,0},{64,96},{96,64},{1,33},{33,1},{65,97},{97,65},{2,34}... | collective-permute-start | bytes 73736 | tf_op jit(solution)/shard_map/ppermute | solution.py:219
  73.2 4.5 %collective-permute-start.5 = (bf16[1,3,2,128]{3,2,1,0:T(2,128)(2,1)S(1)}, bf16[1,3,2,128]{3,2,1,0:T(2,128)(2,1)S(1)}, u32[]{:S(2)}, u32[]{:S(2)}) collective-permute-start(bf16[1,3,2,128]{3,2,1,0:T(2,128)(2,1)S(1)} %get-tuple-element.14), channel_id=1, source_target_pairs={{1,0},{2,1},{3,2},{4,3},{5,4},{6,5},{7,6},{8,7},{9,8},{10,9},{11,1... | collective-permute-start | bytes 4616 | tf_op jit(solution)/shard_map/ppermute | solution.py:29
  75.1 7.0 %collective-permute-start.4 = (bf16[1,3,2,128]{3,2,1,0:T(2,128)(2,1)S(1)}, bf16[1,3,2,128]{3,2,1,0:T(2,128)(2,1)S(1)}, u32[]{:S(2)}, u32[]{:S(2)}) collective-permute-start(bf16[1,3,2,128]{3,2,1,0:T(2,128)(2,1)S(1)} %get-tuple-element.13), channel_id=1, source_target_pairs={{0,1},{1,2},{2,3},{3,4},{4,5},{5,6},{6,7},{7,8},{8,9},{9,10},{10,1... | collective-permute-start | bytes 4616 | tf_op jit(solution)/shard_map/ppermute | solution.py:27
  83.1 1.5 %copy-start.5 = (bf16[64,64,3,3]{1,0,3,2:T(8,128)(2,1)S(1)}, bf16[64,64,3,3]{1,0,3,2:T(8,128)(2,1)}, u32[]{:S(2)}) copy-start(bf16[64,64,3,3]{1,0,3,2:T(8,128)(2,1)} %param.24) | copy-start | bytes 221188

commit v7 on v5

--- a/solution.py
+++ b/solution.py
@@ -157,6 +157,56 @@
     return total.reshape(band_dev, scenes, ROWS_DEV, W)
 
 
+def pack_kernel(capacity, energy_ref, spot_ref, tile_ref, count_ref, scene_ref, row_ref, out_ref):
+    blocks, width = energy_ref.shape
+    hits = spot_ref.shape[1]
+    slots = out_ref.shape[0]
+    tiles = slots // capacity
+    f32 = jnp.float32
+    ii = lax.broadcasted_iota(jnp.int32, (blocks, blocks), 0)
+    jj = lax.broadcasted_iota(jnp.int32, (blocks, blocks), 1)
+    eye = ii == jj
+    tile_row = tile_ref[...].astype(f32)
+    count_row = count_ref[...].astype(f32)
+    base_row = (scene_ref[...] * ROWS_DEV + row_ref[...]).astype(f32)
+    zero = jnp.zeros((blocks, blocks), f32)
+    count_col = jnp.sum(jnp.where(eye, count_row, zero), axis=1, keepdims=True)
+    base_col = jnp.sum(jnp.where(eye, base_row, zero), axis=1, keepdims=True)
+    lanes = lax.broadcasted_iota(jnp.int32, (blocks, width), 1) % hits
+    live = lanes.astype(f32) < count_col
+    energy = energy_ref[...]
+    masked = jnp.where(live, energy, jnp.zeros_like(energy))
+    spot = spot_ref[...]
+    field = base_col * WIN + lax.shift_right_logical(spot, 7).astype(f32)
+    column = jnp.bitwise_and(spot, W - 1).astype(f32)
+    tt = lax.broadcasted_iota(jnp.int32, (tiles, blocks), 0).astype(f32)
+    owners = (tt == tile_row).astype(jnp.bfloat16)
+    earlier = (ii < jj).astype(jnp.bfloat16)
+    before = jnp.dot(owners, earlier, preferred_element_type=f32)
+    rank = jnp.sum(before * owners.astype(f32), axis=0, keepdims=True)
+    place = tile_row * capacity + rank
+    pp = lax.broadcasted_iota(jnp.int32, (slots, blocks), 0).astype(f32)
+    select = (pp == place).astype(jnp.bfloat16)
+    out_ref[:, pl.ds(0, width)] = jnp.dot(select, masked, preferred_element_type=f32).astype(
+        out_ref.dtype
+    )
+    out_ref[:, pl.ds(width, hits)] = jnp.dot(
+        select, field.astype(jnp.bfloat16), preferred_element_type=f32
+    ).astype(out_ref.dtype)
+    out_ref[:, pl.ds(width + hits, hits)] = jnp.dot(
+        select, column.astype(jnp.bfloat16), preferred_element_type=f32
+    ).astype(out_ref.dtype)
+
+
+def pack(energy, spot, tile, count, scene, row, capacity, slots):
+    blocks, width = energy.shape
+    hits = spot.shape[1]
+    return pl.pallas_call(
+        functools.partial(pack_kernel, capacity),
+        out_shape=jax.ShapeDtypeStruct((slots, width + 2 * hits), energy.dtype),
+    )(energy, spot, tile, count, scene, row)
+
+
 def per_device(
     hit_energy,
     hit_spot,
@@ -175,31 +225,16 @@
     block_dev, band_dev, hit_lanes = hit_energy.shape
     capacity = 2 * block_dev // tile_count
     scenes = psf_index.shape[1]
-    lanes = lax.broadcasted_iota(jnp.int32, (block_dev, hit_lanes), 1)
-    live = lanes < block_count[0][:, None]
-    masked = jnp.where(live[:, None, :], hit_energy, jnp.zeros_like(hit_energy))
-    base_row = block_scene[0] * ROWS_DEV + block_row[0]
-    spot = hit_spot[0]
-    field = base_row[:, None] * WIN + spot // W
-    column = spot % W
-    payload = jnp.concatenate(
-        [
-            masked.reshape(block_dev, band_dev * hit_lanes),
-            field.astype(hit_energy.dtype),
-            column.astype(hit_energy.dtype),
-        ],
-        axis=1,
-    )
-    target = block_tile[0, :, 0]
-    owners = (target[:, None] == jnp.arange(tile_count, dtype=jnp.int32)[None, :]).astype(jnp.int32)
-    order = lax.broadcasted_iota(jnp.int32, (block_dev, block_dev), 0)
-    earlier = (order > order.T).astype(jnp.bfloat16)
-    before = jnp.dot(earlier, owners.astype(jnp.bfloat16), preferred_element_type=jnp.float32)
-    rank = jnp.sum(before * owners.astype(jnp.float32), axis=1).astype(jnp.int32)
-    place = target * capacity + rank
-    slots = jnp.arange(tile_count * capacity, dtype=jnp.int32)
-    select = (slots[:, None] == place[None, :]).astype(hit_energy.dtype)
-    send = jnp.dot(select, payload, preferred_element_type=jnp.float32).astype(hit_energy.dtype)
+    send = pack(
+        hit_energy.reshape(block_dev, band_dev * hit_lanes),
+        hit_spot[0],
+        block_tile[0, :, 0].reshape(1, block_dev),
+        block_count,
+        block_scene,
+        block_row,
+        capacity,
+        tile_count * capacity,
+    )
     kern = kernel_spectra(psf_bank, psf_index, K // 2)
     got = lax.all_to_all(send, "tile", split_axis=0, concat_axis=0, tiled=True)
     splat = window_splat(got, band_dev, hit_lanes, scenes)

time: 87.2 us -> 85 us (0.975)
  other arithmetic: 4.49 us -> 0.31 us
  Pallas kernels: 6.33 us -> 8.64 us
  matrix products: 21.4 us -> 19.3 us
  local copies, waits for them, and re-layouts: 5.75 us -> 7.56 us
    pallas_call x0 -> x1, Pallas kernels: none -> 2.32 us  [pack(): pl.pallas_call(functools.partial(pack_kernel, capacity), out_shape=jax.Sh...]
    dot_general x2 -> x0, matrix products: 2.05 us -> none  [the longest x1 1.17 us: per_device(): jnp.dot(select, payload, preferred_element_type=jnp.float32)]
    unnamed x21, local copies, waits for them, and re-layouts: 0.24 us -> 2.05 us
    select_n x1 -> x0, other arithmetic: 1.03 us -> none  [per_device(): masked = jnp.where(live[:, None, :], hit_energy, jnp.zeros_like(hit_energy))]
    convert_element_type x1 -> x0, other arithmetic: 0.93 us -> none  [per_device(): field.astype(hit_energy.dtype)]
    lt x1 -> x0, other arithmetic: 0.89 us -> none  [per_device(): live = lanes < block_count[0][:, None]]
where the time goes in v7:
time: 85 us; the launch traced here: 84.6 us
  starting transfers between devices  24.3 us (29%)
  waiting for transfers between devices  24 us (28%)
  matrix products  19.3 us (23%)
  Pallas kernels  8.64 us (10%)
  local copies, waits for them, and re-layouts  7.56 us (9%)
    ppermute x2, waiting for transfers between devices, padded_2(): lax.ppermute(tail, axis, [(i, (i + 1) % count) for i in range(ends)])  10.2 us
    all_to_all x1, waiting for transfers between devices, per_device(): got = lax.all_to_all(send, 'tile', split_axis=0, concat_axis=0, tiled=True)  9.55 us
    all_to_all x1, starting transfers between devices, per_device(): got = lax.all_to_all(send, 'tile', split_axis=0, concat_axis=0, tiled=True)  7.62 us
    dot_general x1, matrix products, window_splat(): jnp.einsum('ibjh,ihc->ibjc', spread, onehot, preferred_element_type=jnp.f...  7.54 us
    ppermute x2, starting transfers between devices, padded_2(): lax.ppermute(head, axis, [((i + 1) % count, i) for i in range(ends)])  6.84 us
    pallas_call x1, Pallas kernels, row_taps(): pl.pallas_call(row_taps_kernel, out_shape=jax.ShapeDtypeStruct((channels,...  6.32 us
    ppermute x3, starting transfers between devices, per_device(): lax.ppermute(piece, 'wave', [(i, (i + step) % wave_count) for i in range(...  5.36 us
    ppermute x2, starting transfers between devices, padded_2(): lax.ppermute(tail, axis, [(i, (i + 1) % count) for i in range(ends)])  4.51 us
  transfers between devices with their start and end apart: 8, of which 6 were waited for; matrix products, arithmetic and copies ran while one was open for 4% of the time, Pallas kernels for 0%

profile of v7, /device:TPU:2, one launch (start us, length us, event | category | flops | bytes accessed | tf_op | source)
XLA Modules:
  0.0 84.6 jit_solution(3725844064545817338)
XLA Ops:
  0.0 1.9 %copy.71 = bf16[16,8,8,128]{3,1,2,0:T(8,128)(2,1)} copy(bf16[16,8,8,128]{3,2,1,0:T(8,128)(2,1)} %bitcast.104) | data formatting | bytes 524288
  1.9 2.3 %shard_map.136 = bf16[256,1280]{1,0:T(8,128)(2,1)} custom-call(bf16[128,1024]{1,0:T(8,128)(2,1)} %bitcast.100, s32[128,128]{1,0:T(8,128)} %bitcast.105, s32[1,128]{1,0:T(1,128)} %bitcast.106, s32[1,128]{1,0:T(1,128)} %count_ref.1, s32[1,128]{1,0:T(1,128)} %scene_ref.1, s32[1,128]{1,0:T(1,128)} %row_ref.1), custom_call_target="tpu_custom_call" | custom-call | tf_op jit(solution)/shard_map/pallas_call | solution.py:204
  4.2 7.6 %all-to-all-start = ((bf16[32,8,1280]{2,1,0:T(8,128)(2,1)}), bf16[32,8,1280]{2,1,0:T(8,128)(2,1)S(1)}, u32[]{:S(2)}, u32[]{:S(2)}) async-start(bf16[32,8,1280]{2,1,0:T(8,128)(2,1)} %bitcast.97), calls=%async_computation | async-start | bytes 1310720 | tf_op jit(solution)/shard_map/all_to_all | solution.py:239
  13.1 9.6 %all-to-all-done = bf16[32,8,1280]{2,1,0:T(8,128)(2,1)S(1)} async-done(((bf16[32,8,1280]{2,1,0:T(8,128)(2,1)}), bf16[32,8,1280]{2,1,0:T(8,128)(2,1)S(1)}, u32[]{:S(2)}, u32[]{:S(2)}) %all-to-all-start) | async-done | bytes 655392 | tf_op jit(solution)/shard_map/all_to_all | solution.py:239
  23.2 7.5 %fusion.1 = f32[256,8,4,128]{3,2,1,0:T(4,128)S(1)} fusion(s32[256,128]{1,0:T(8,128)S(1)} %get-tuple-element.6, pred[256,4,128]{2,1,0:T(4,128)(4,1)S(1)} %iota_compare_fusion.4, bf16[256,8,128]{2,1,0:T(8,128)(2,1)S(1)} %bitcast.101), kind=kOutput, calls=%fused_computation.3 | convolution fusion | flops 273678336 | bytes 4980736 | tf_op jit(solution)/shard_map/ibjh,ihc->ibjc/dot_general | solution.py:151
  30.8 3.2 %fusion.4 = f32[64,8,128,1]{2,0,3,1:T(8,128)S(1)} fusion(f32[256,8,4,128]{3,2,1,0:T(4,128)S(1)} %fusion.1, s32[256,4]{0,1:T(4,128)S(1)} %iota_add_fusion), kind=kOutput, calls=%fused_computation.5 | convolution fusion | flops 402718720 | bytes 4460544 | tf_op jit(solution)/shard_map/ibjc,ijr->brc/dot_general | solution.py:156
  33.9 0.8 fusion.67
  34.8 4.9 %collective-permute-start.1 = (f32[8,4,15,128]{3,2,1,0:T(8,128)}, f32[8,4,15,128]{3,2,1,0:T(8,128)S(1)}, u32[]{:S(2)}, u32[]{:S(2)}) collective-permute-start(f32[8,4,15,128]{3,2,1,0:T(8,128)} %get-tuple-element.10), channel_id=1, source_target_pairs={{1,0},{2,1},{3,2},{4,3},{5,4},{6,5},{7,6},{8,7},{9,8},{10,9},{11,1... | collective-permute-start | bytes 737288 | tf_op jit(solution)/shard_map/ppermute | solution.py:29
  39.7 1.9 %collective-permute-start = (f32[8,4,15,128]{3,2,1,0:T(8,128)}, f32[8,4,15,128]{3,2,1,0:T(8,128)S(1)}, u32[]{:S(2)}, u32[]{:S(2)}) collective-permute-start(f32[8,4,15,128]{3,2,1,0:T(8,128)} %get-tuple-element.9), channel_id=1, source_target_pairs={{0,1},{1,2},{2,3},{3,4},{4,5},{5,6},{6,7},{7,8},{8,9},{9,10},{10,1... | collective-permute-start | bytes 737288 | tf_op jit(solution)/shard_map/ppermute | solution.py:27
  41.6 1.0 %convolution_bitcast_fusion = f32[8,4,31,256]{3,2,0,1:T(8,128)S(1)} fusion(f32[4,8,31,31]{3,2,1,0:T(8,128)S(1)} %reshape.118, f32[31,256,1,1]{1,0,3,2:T(8,128)S(1)} %copy-done.3), kind=kOutput, calls=%fused_computation.14 | convolution fusion | flops 94470144 | bytes 1170560 | tf_op jit(solution)/shard_map/sbuv,vf->sbuf/dot_general | solution.py:117
  42.6 1.1 %copy.47 = f32[8,4,31,256]{3,2,1,0:T(8,128)} copy(f32[8,4,31,256]{3,2,0,1:T(8,128)S(1)} %convolution_bitcast_fusion) | data formatting | bytes 2031616 | tf_op jit(solution)/shard_map/transpose | solution.py:129
  43.9 5.8 %collective-permute-done = f32[8,4,15,128]{3,2,1,0:T(8,128)S(1)} collective-permute-done((f32[8,4,15,128]{3,2,1,0:T(8,128)}, f32[8,4,15,128]{3,2,1,0:T(8,128)S(1)}, u32[]{:S(2)}, u32[]{:S(2)}) %collective-permute-start) | collective-permute-done | bytes 245792 | tf_op jit(solution)/shard_map/ppermute | solution.py:27
  49.7 2.6 %fusion.15.spec_ref = f32[32,46,256]{2,1,0:T(8,128)} fusion(f32[128,256,1]{1,0,2:T(8,128)S(1)} %copy-done.1, f32[32,15,128]{2,1,0:T(8,128)S(1)} %bitcast.102, f32[32,16,128]{2,1,0:T(8,128)S(1)} %bitcast.93, f32[32,15,128]{2,1,0:T(8,128)S(1)} %bitcast.103), kind=kOutput, calls=%fused_computation.23 | convolution fusion | flops 579190784 | bytes 2392064 | tf_op jit(solution)/shard_map/cyx,xf->cyf/dot_general | solution.py:126
  52.3 6.3 %shard_map.137 = f32[32,16,256]{2,1,0:T(8,128)} custom-call(f32[32,46,256]{2,1,0:T(8,128)} %fusion.15.spec_ref, f32[32,31,256]{2,1,0:T(8,128)} %bitcast.91), custom_call_target="tpu_custom_call" | custom-call | tf_op jit(solution)/shard_map/pallas_call | solution.py:99
  58.6 1.9 %convolution_bitcast_fusion.1 = f32[4,3,16,256]{3,1,2,0:T(4,128)S(1)} fusion(f32[8,4,16,256]{3,2,1,0:T(8,128)} %bitcast.99, f32[32,3]{0,1:T(4,128)S(1)} %copy-done.4, s32[]{:T(128)S(6)} %select_n.64), kind=kOutput, calls=%fused_computation.17 | convolution fusion | flops 4718592 | bytes 721284 | tf_op jit(solution)/shard_map/bsyf,bc->scyf/dot_general | solution.py:131
  60.9 4.1 %collective-permute-start.4 = (f32[3,16,128]{2,1,0:T(8,128)S(1)}, f32[3,16,128]{2,1,0:T(8,128)S(1)}, u32[]{:S(2)}, u32[]{:S(2)}) collective-permute-start(f32[3,16,128]{2,1,0:T(8,128)S(1)} %get-tuple-element.12), channel_id=1, source_target_pairs={{0,96},{32,0},{64,32},{96,64},{1,97},{33,1},{65,33},{97,65},{2,98}... | collective-permute-start | bytes 73736 | tf_op jit(solution)/shard_map/ppermute | solution.py:248
  65.0 1.2 %collective-permute-start.2 = (f32[3,16,128]{2,1,0:T(8,128)S(1)}, f32[3,16,128]{2,1,0:T(8,128)S(1)}, u32[]{:S(2)}, u32[]{:S(2)}) collective-permute-start(f32[3,16,128]{2,1,0:T(8,128)S(1)} %get-tuple-element.11), channel_id=1, source_target_pairs={{0,32},{32,64},{64,96},{96,0},{1,33},{33,65},{65,97},{97,1},{2,34}... | collective-permute-start | bytes 73736 | tf_op jit(solution)/shard_map/ppermute | solution.py:248
  66.5 3.8 %collective-permute-done.3 = f32[3,16,128]{2,1,0:T(8,128)S(1)} collective-permute-done((f32[3,16,128]{2,1,0:T(8,128)S(1)}, f32[3,16,128]{2,1,0:T(8,128)S(1)}, u32[]{:S(2)}, u32[]{:S(2)}) %collective-permute-start.3) | collective-permute-done | bytes 24608 | tf_op jit(solution)/shard_map/ppermute | solution.py:248
  70.3 1.9 %collective-permute-start.6 = (bf16[1,3,2,128]{3,2,1,0:T(2,128)(2,1)S(1)}, bf16[1,3,2,128]{3,2,1,0:T(2,128)(2,1)S(1)}, u32[]{:S(2)}, u32[]{:S(2)}) collective-permute-start(bf16[1,3,2,128]{3,2,1,0:T(2,128)(2,1)S(1)} %get-tuple-element.15), channel_id=1, source_target_pairs={{1,0},{2,1},{3,2},{4,3},{5,4},{6,5},{7,6},{8,7},{9,8},{10,9},{11,1... | collective-permute-start | bytes 4616 | tf_op jit(solution)/shard_map/ppermute | solution.py:29
  72.3 2.6 %collective-permute-start.5 = (bf16[1,3,2,128]{3,2,1,0:T(2,128)(2,1)S(1)}, bf16[1,3,2,128]{3,2,1,0:T(2,128)(2,1)S(1)}, u32[]{:S(2)}, u32[]{:S(2)}) collective-permute-start(bf16[1,3,2,128]{3,2,1,0:T(2,128)(2,1)S(1)} %get-tuple-element.14), channel_id=1, source_target_pairs={{0,1},{1,2},{2,3},{3,4},{4,5},{5,6},{6,7},{7,8},{8,9},{9,10},{10,1... | collective-permute-start | bytes 4616 | tf_op jit(solution)/shard_map/ppermute | solution.py:27
  74.9 4.4 %collective-permute-done.5 = bf16[1,3,2,128]{3,2,1,0:T(2,128)(2,1)S(1)} collective-permute-done((bf16[1,3,2,128]{3,2,1,0:T(2,128)(2,1)S(1)}, bf16[1,3,2,128]{3,2,1,0:T(2,128)(2,1)S(1)}, u32[]{:S(2)}, u32[]{:S(2)}) %collective-permute-start.5) | collective-permute-done | bytes 1568 | tf_op jit(solution)/shard_map/ppermute | solution.py:27
  80.2 1.4 %fusion.14 = bf16[18,1,8,17,64]{4,2,3,0,1:T(8,128)(2,1)S(1)} fusion(pred[18]{0:T(512)(128)(4,1)S(1)} %and_or_fusion, pred[8,17]{0,1:T(8,128)(4,1)S(1)} %copy-done.8, bf16[3,20,1,7,2]{3,0,4,1,2:T(4,128)(2,1)S(1)} %slice.46, bf16[3,20,1,8,17]{3,0,4,1,2:T(4,128)(2,1)S(1)} %copy.51, bf16[64,3,3,3]{0,3,2,1:T(4,128)(2,1)S(1)} %copy-done.6), kind=kOutput, calls=%fused_computation.22 | convolution fusion | flops 9925056 | bytes 334954 | tf_op jit(solution)/shard_map/conv_general_dilated | solution.py:37
  81.7 1.5 %convolution_convert_fusion = bf16[16,8,17,64]{3,1,2,0:T(8,128)(2,1)S(1)} fusion(bf16[64,64,3,3]{1,0,3,2:T(8,128)(2,1)S(1)} %copy-done.5, bf16[18,1,7,1,64]{4,2,3,0,1:T(8,128)(2,1)S(1)} %get-tuple-element.8, bf16[18,1,7,1,64]{4,2,3,0,1:T(8,128)(2,1)S(1)} %get-tuple-element.7, bf16[18,1,8,17,64]{4,2,3,0,1:T(8,128)(2,1)S(1)} %fusion.14), kind=kOutput, calls=%fused_computation.15 | convolution fusion | flops 162322432 | bytes 697856 | tf_op jit(solution)/shard_map/conv_general_dilated | solution.py:37
  83.3 1.3 %copy.54 = bf16[1,64,16,128]{3,2,1,0:T(8,128)(2,1)} copy(bf16[1,64,16,128]{1,2,3,0:T(8,128)(2,1)S(1)} %slice_bitcast_fusion) | data formatting | bytes 524288 | tf_op jit(solution)/shard_map/convert_element_type | solution.py:262
  (48 shorter events, 3.6 us)
Async XLA Ops:
  0.0 11.9 %copy-start = (f32[64,8,961]{2,1,0:T(8,128)S(1)}, f32[64,8,961]{2,1,0:T(8,128)}, u32[]{:S(2)}) copy-start(f32[64,8,961]{2,1,0:T(8,128)} %param.20) | copy-start | bytes 5904388
  0.0 11.9 %copy-start.7 = (s32[1,4,1]{1,2,0:T(1,128)S(1)}, s32[1,4,1]{1,2,0:T(1,128)}, u32[]{:S(2)}) copy-start(s32[1,4,1]{1,2,0:T(1,128)} %param.21) | copy-start | bytes 52
  4.2 18.4 %all-to-all-start = ((bf16[32,8,1280]{2,1,0:T(8,128)(2,1)}), bf16[32,8,1280]{2,1,0:T(8,128)(2,1)S(1)}, u32[]{:S(2)}, u32[]{:S(2)}) async-start(bf16[32,8,1280]{2,1,0:T(8,128)(2,1)} %bitcast.97), calls=%async_computation | async-start | bytes 1310720 | tf_op jit(solution)/shard_map/all_to_all | solution.py:239
  30.7 10.9 %copy-start.3 = (f32[31,256,1,1]{1,0,3,2:T(8,128)S(1)}, f32[31,256,1,1]{1,0,3,2:T(8,128)}, u32[]{:S(2)}) copy-start(f32[31,256,1,1]{1,0,3,2:T(8,128)} %constant.108) | copy-start | bytes 95236
  34.8 9.1 %collective-permute-start.1 = (f32[8,4,15,128]{3,2,1,0:T(8,128)}, f32[8,4,15,128]{3,2,1,0:T(8,128)S(1)}, u32[]{:S(2)}, u32[]{:S(2)}) collective-permute-start(f32[8,4,15,128]{3,2,1,0:T(8,128)} %get-tuple-element.10), channel_id=1, source_target_pairs={{1,0},{2,1},{3,2},{4,3},{5,4},{6,5},{7,6},{8,7},{9,8},{10,9},{11,1... | collective-permute-start | bytes 737288 | tf_op jit(solution)/shard_map/ppermute | solution.py:29
  39.7 10.0 %collective-permute-start = (f32[8,4,15,128]{3,2,1,0:T(8,128)}, f32[8,4,15,128]{3,2,1,0:T(8,128)S(1)}, u32[]{:S(2)}, u32[]{:S(2)}) collective-permute-start(f32[8,4,15,128]{3,2,1,0:T(8,128)} %get-tuple-element.9), channel_id=1, source_target_pairs={{0,1},{1,2},{2,3},{3,4},{4,5},{5,6},{6,7},{7,8},{8,9},{9,10},{10,1... | collective-permute-start | bytes 737288 | tf_op jit(solution)/shard_map/ppermute | solution.py:27
  42.6 7.1 %copy-start.1 = (f32[128,256,1]{1,0,2:T(8,128)S(1)}, f32[128,256,1]{1,0,2:T(8,128)}, u32[]{:S(2)}) copy-start(f32[128,256,1]{1,0,2:T(8,128)} %constant.107) | copy-start | bytes 393220
  52.3 6.3 %copy-start.4 = (f32[32,3]{0,1:T(4,128)S(1)}, f32[32,3]{0,1:T(4,128)}, u32[]{:S(2)}) copy-start(f32[32,3]{0,1:T(4,128)} %param.22) | copy-start | bytes 1156
  52.3 8.2 %copy-start.2 = (f32[256,128,1,1]{1,0,3,2:T(8,128)S(1)}, f32[256,128,1,1]{1,0,3,2:T(8,128)}, u32[]{:S(2)}) copy-start(f32[256,128,1,1]{1,0,3,2:T(8,128)} %constant.109) | copy-start | bytes 393220
  58.6 21.6 %copy-start.6 = (bf16[64,3,3,3]{0,3,2,1:T(4,128)(2,1)S(1)}, bf16[64,3,3,3]{0,3,2,1:T(4,128)(2,1)}, u32[]{:S(2)}) copy-start(bf16[64,3,3,3]{0,3,2,1:T(4,128)(2,1)} %param.23) | copy-start | bytes 10372
  58.6 21.6 %copy-start.8 = (pred[8,17]{0,1:T(8,128)(4,1)S(1)}, pred[8,17]{0,1:T(8,128)(4,1)}, u32[]{:S(2)}) copy-start(pred[8,17]{0,1:T(8,128)(4,1)} %constant.105) | copy-start | bytes 412
  60.9 5.6 %collective-permute-start.4 = (f32[3,16,128]{2,1,0:T(8,128)S(1)}, f32[3,16,128]{2,1,0:T(8,128)S(1)}, u32[]{:S(2)}, u32[]{:S(2)}) collective-permute-start(f32[3,16,128]{2,1,0:T(8,128)S(1)} %get-tuple-element.12), channel_id=1, source_target_pairs={{0,96},{32,0},{64,32},{96,64},{1,97},{33,1},{65,33},{97,65},{2,98}... | collective-permute-start | bytes 73736 | tf_op jit(solution)/shard_map/ppermute | solution.py:248
  65.0 5.3 %collective-permute-start.3 = (f32[3,16,128]{2,1,0:T(8,128)S(1)}, f32[3,16,128]{2,1,0:T(8,128)S(1)}, u32[]{:S(2)}, u32[]{:S(2)}) collective-permute-start(f32[3,16,128]{2,1,0:T(8,128)S(1)} %get-tuple-element.13), channel_id=1, source_target_pairs={{0,64},{32,96},{64,0},{96,32},{1,65},{33,97},{65,1},{97,33},{2,66}... | collective-permute-start | bytes 73736 | tf_op jit(solution)/shard_map/ppermute | solution.py:248
  65.0 5.3 %collective-permute-start.2 = (f32[3,16,128]{2,1,0:T(8,128)S(1)}, f32[3,16,128]{2,1,0:T(8,128)S(1)}, u32[]{:S(2)}, u32[]{:S(2)}) collective-permute-start(f32[3,16,128]{2,1,0:T(8,128)S(1)} %get-tuple-element.11), channel_id=1, source_target_pairs={{0,32},{32,64},{64,96},{96,0},{1,33},{33,65},{65,97},{97,1},{2,34}... | collective-permute-start | bytes 73736 | tf_op jit(solution)/shard_map/ppermute | solution.py:248
  70.3 4.5 %collective-permute-start.6 = (bf16[1,3,2,128]{3,2,1,0:T(2,128)(2,1)S(1)}, bf16[1,3,2,128]{3,2,1,0:T(2,128)(2,1)S(1)}, u32[]{:S(2)}, u32[]{:S(2)}) collective-permute-start(bf16[1,3,2,128]{3,2,1,0:T(2,128)(2,1)S(1)} %get-tuple-element.15), channel_id=1, source_target_pairs={{1,0},{2,1},{3,2},{4,3},{5,4},{6,5},{7,6},{8,7},{9,8},{10,9},{11,1... | collective-permute-start | bytes 4616 | tf_op jit(solution)/shard_map/ppermute | solution.py:29
  72.3 7.0 %collective-permute-start.5 = (bf16[1,3,2,128]{3,2,1,0:T(2,128)(2,1)S(1)}, bf16[1,3,2,128]{3,2,1,0:T(2,128)(2,1)S(1)}, u32[]{:S(2)}, u32[]{:S(2)}) collective-permute-start(bf16[1,3,2,128]{3,2,1,0:T(2,128)(2,1)S(1)} %get-tuple-element.14), channel_id=1, source_target_pairs={{0,1},{1,2},{2,3},{3,4},{4,5},{5,6},{6,7},{7,8},{8,9},{9,10},{10,1... | collective-permute-start | bytes 4616 | tf_op jit(solution)/shard_map/ppermute | solution.py:27
  80.2 1.5 %copy-start.5 = (bf16[64,64,3,3]{1,0,3,2:T(8,128)(2,1)S(1)}, bf16[64,64,3,3]{1,0,3,2:T(8,128)(2,1)}, u32[]{:S(2)}) copy-start(bf16[64,64,3,3]{1,0,3,2:T(8,128)(2,1)} %param.24) | copy-start | bytes 221188

commit v8 on v7

--- a/solution.py
+++ b/solution.py
@@ -5,6 +5,7 @@
 import numpy as np
 from jax import lax
 from jax.experimental import pallas as pl
+from jax.experimental.pallas import tpu as pltpu
 from jax.sharding import PartitionSpec as P
 
 ROWS_DEV = 16
@@ -117,19 +118,84 @@
     return jnp.einsum("sbuv,vf->sbuf", chosen, taps, precision=lax.Precision.HIGHEST)
 
 
+def blur_kernel(ext_ref, fwd_ref, kern_ref, resp_ref, inv_ref, out_ref, spec_scr, col_scr):
+    step = pl.program_id(0)
+    per = ext_ref.shape[0]
+    scenes, colors, rows = out_ref.shape[:3]
+    side = kern_ref.shape[1]
+    group = per // scenes
+    hi = lax.Precision.HIGHEST
+
+    @pl.when(step == 0)
+    def _():
+        col_scr[...] = jnp.zeros_like(col_scr)
+
+    def band(g, carry):
+        b = step * group + g
+        for s in range(scenes):
+            c = g * scenes + s
+            spec_scr[...] = jnp.dot(
+                ext_ref[c], fwd_ref[...], precision=hi, preferred_element_type=jnp.float32
+            )
+            acc_re = jnp.zeros((rows, LANE), jnp.float32)
+            acc_im = jnp.zeros((rows, LANE), jnp.float32)
+            for u in range(side):
+                xr = spec_scr[pl.ds(u, rows), pl.ds(0, LANE)]
+                xi = spec_scr[pl.ds(u, rows), pl.ds(LANE, LANE)]
+                kr = kern_ref[c, pl.ds(u, 1), pl.ds(0, LANE)]
+                ki = kern_ref[c, pl.ds(u, 1), pl.ds(LANE, LANE)]
+                acc_re = acc_re + (kr * xr - ki * xi)
+                acc_im = acc_im + (kr * xi + ki * xr)
+            for k in range(colors):
+                weight = resp_ref[b, k]
+                col_scr[s, k, :, pl.ds(0, LANE)] += weight * acc_re
+                col_scr[s, k, :, pl.ds(LANE, LANE)] += weight * acc_im
+        return carry
+
+    lax.fori_loop(0, group, band, 0)
+
+    @pl.when(step == pl.num_programs(0) - 1)
+    def _():
+        for s in range(scenes):
+            for k in range(colors):
+                out_ref[s, k] = jnp.dot(
+                    col_scr[s, k], inv_ref[...], precision=hi, preferred_element_type=jnp.float32
+                )
+
+
 def patch_blur(extended, kern, response, radius):
     band_dev, scenes, tall, width = extended.shape
     rows_dev = tall - 2 * radius
     side = 2 * radius + 1
+    colors = response.shape[1]
     forward, unused, inverse = dft_tables(width, side, radius)
-    hi = lax.Precision.HIGHEST
-    spec = jnp.einsum(
-        "cyx,xf->cyf", extended.reshape(band_dev * scenes, tall, width), forward, precision=hi
-    )
     taps = kern.transpose(1, 0, 2, 3).reshape(band_dev * scenes, side, -1)
-    out = row_taps(spec, taps, rows_dev).reshape(band_dev, scenes, rows_dev, -1)
-    color = jnp.einsum("bsyf,bc->scyf", out, response, precision=hi)
-    return jnp.einsum("scyf,fx->scyx", color, inverse, precision=hi)
+    both = taps.shape[-1]
+    group = 4 if band_dev % 4 == 0 else 1
+    per = group * scenes
+    return pl.pallas_call(
+        blur_kernel,
+        out_shape=jax.ShapeDtypeStruct((scenes, colors, rows_dev, width), jnp.float32),
+        grid=(band_dev // group,),
+        in_specs=[
+            pl.BlockSpec((per, tall, width), lambda i: (i, 0, 0)),
+            pl.BlockSpec((width, both), lambda i: (0, 0)),
+            pl.BlockSpec((per, side, both), lambda i: (i, 0, 0)),
+            pl.BlockSpec(memory_space=pltpu.SMEM),
+            pl.BlockSpec((both, width), lambda i: (0, 0)),
+        ],
+        out_specs=pl.BlockSpec((scenes, colors, rows_dev, width), lambda i: (0, 0, 0, 0)),
+        scratch_shapes=[
+            pltpu.VMEM((tall, both), jnp.float32),
+            pltpu.VMEM((scenes, colors, rows_dev, both), jnp.float32),
+        ],
+    )(
+        extended.reshape(band_dev * scenes, tall, width),
+        jnp.asarray(forward),
+        taps,
+        response,
+        jnp.asarray(inverse),
+    )
 
 
 def window_splat(got, band_dev, hit_lanes, scenes):

time: 85 us -> 86.2 us (1.014)
  matrix products: 19.3 us -> 14.5 us
  Pallas kernels: 8.64 us -> 11.4 us
  other arithmetic: 0.31 us -> 3 us
  local copies, waits for them, and re-layouts: 7.56 us -> 8.95 us
    dot_general x3 -> x0, matrix products: 4.76 us -> none  [the longest x1 2.55 us: patch_blur(): jnp.einsum('cyx,xf->cyf', extended.reshape(band_dev * scenes, tall, width...]
    pallas_call x1, Pallas kernels: 6.32 us -> 9.11 us  [patch_blur(): pl.pallas_call(blur_kernel, out_shape=jax.ShapeDtypeStruct((scenes, color...]
    concatenate x1 -> x2, other arithmetic: 0.01 us -> 1.97 us  [padded_2(): jnp.concatenate([lax.ppermute(tail, axis, [(i, (i + 1) % count) for i in...]
    unnamed x21 -> x18, local copies, waits for them, and re-layouts: 2.05 us -> 2.7 us
  transfers between devices with their start and end apart: 8 -> 8, of which waited for: 6 -> 5; matrix products, arithmetic and copies ran while one was open for 4% -> 5% of each run, Pallas kernels for 0% -> 0%
where the time goes in v8:
time: 86.2 us; the launch traced here: 85.7 us
  starting transfers between devices  24.3 us (28%)
  waiting for transfers between devices  23.2 us (27%)
  matrix products  14.5 us (17%)
  Pallas kernels  11.4 us (13%)
  local copies, waits for them, and re-layouts  8.95 us (10%)
  other arithmetic  3 us (3%)
    all_to_all x1, waiting for transfers between devices, per_device(): got = lax.all_to_all(send, 'tile', split_axis=0, concat_axis=0, tiled=True)  9.55 us
    ppermute x2, waiting for transfers between devices, padded_2(): lax.ppermute(tail, axis, [(i, (i + 1) % count) for i in range(ends)])  9.54 us
    pallas_call x1, Pallas kernels, patch_blur(): pl.pallas_call(blur_kernel, out_shape=jax.ShapeDtypeStruct((scenes, color...  9.11 us
    all_to_all x1, starting transfers between devices, per_device(): got = lax.all_to_all(send, 'tile', split_axis=0, concat_axis=0, tiled=True)  7.62 us
    dot_general x1, matrix products, window_splat(): jnp.einsum('ibjh,ihc->ibjc', spread, onehot, preferred_element_type=jnp.f...  7.54 us
    ppermute x2, starting transfers between devices, padded_2(): lax.ppermute(head, axis, [((i + 1) % count, i) for i in range(ends)])  6.84 us
    ppermute x3, starting transfers between devices, per_device(): lax.ppermute(piece, 'wave', [(i, (i + step) % wave_count) for i in range(...  5.29 us
    ppermute x2, starting transfers between devices, padded_2(): lax.ppermute(tail, axis, [(i, (i + 1) % count) for i in range(ends)])  4.51 us
  transfers between devices with their start and end apart: 8, of which 5 were waited for; matrix products, arithmetic and copies ran while one was open for 5% of the time, Pallas kernels for 0%

profile of v8, /device:TPU:2, one launch (start us, length us, event | category | flops | bytes accessed | tf_op | source)
XLA Modules:
  0.0 85.7 jit_solution(2812314244024935065)
XLA Ops:
  0.0 1.9 %copy.65 = bf16[16,8,8,128]{3,1,2,0:T(8,128)(2,1)} copy(bf16[16,8,8,128]{3,2,1,0:T(8,128)(2,1)} %bitcast.87) | data formatting | bytes 524288
  1.9 2.3 %shard_map.136 = bf16[256,1280]{1,0:T(8,128)(2,1)} custom-call(bf16[128,1024]{1,0:T(8,128)(2,1)} %bitcast.85, s32[128,128]{1,0:T(8,128)} %bitcast.89, s32[1,128]{1,0:T(1,128)} %bitcast.90, s32[1,128]{1,0:T(1,128)} %count_ref.1, s32[1,128]{1,0:T(1,128)} %scene_ref.1, s32[1,128]{1,0:T(1,128)} %row_ref.1), custom_call_target="tpu_custom_call" | custom-call | tf_op jit(solution)/shard_map/pallas_call | solution.py:270
  4.2 7.6 %all-to-all-start = ((bf16[32,8,1280]{2,1,0:T(8,128)(2,1)}), bf16[32,8,1280]{2,1,0:T(8,128)(2,1)S(1)}, u32[]{:S(2)}, u32[]{:S(2)}) async-start(bf16[32,8,1280]{2,1,0:T(8,128)(2,1)} %bitcast.83), calls=%async_computation | async-start | bytes 1310720 | tf_op jit(solution)/shard_map/all_to_all | solution.py:305
  13.1 9.6 %all-to-all-done = bf16[32,8,1280]{2,1,0:T(8,128)(2,1)S(1)} async-done(((bf16[32,8,1280]{2,1,0:T(8,128)(2,1)}), bf16[32,8,1280]{2,1,0:T(8,128)(2,1)S(1)}, u32[]{:S(2)}, u32[]{:S(2)}) %all-to-all-start) | async-done | bytes 655392 | tf_op jit(solution)/shard_map/all_to_all | solution.py:305
  23.2 7.5 %fusion.1 = f32[256,8,4,128]{3,2,1,0:T(4,128)S(1)} fusion(s32[256,128]{1,0:T(8,128)S(1)} %get-tuple-element.6, pred[256,4,128]{2,1,0:T(4,128)(4,1)S(1)} %iota_compare_fusion.4, bf16[256,8,128]{2,1,0:T(8,128)(2,1)S(1)} %bitcast.86), kind=kOutput, calls=%fused_computation.3 | convolution fusion | flops 273678336 | bytes 4980736 | tf_op jit(solution)/shard_map/ibjh,ihc->ibjc/dot_general | solution.py:217
  30.7 3.2 %fusion.4 = f32[64,8,128,1]{2,0,3,1:T(8,128)S(1)} fusion(f32[256,8,4,128]{3,2,1,0:T(4,128)S(1)} %fusion.1, s32[256,4]{0,1:T(4,128)S(1)} %iota_add_fusion), kind=kOutput, calls=%fused_computation.5 | convolution fusion | flops 402718720 | bytes 4460544 | tf_op jit(solution)/shard_map/ibjc,ijr->brc/dot_general | solution.py:222
  34.7 4.9 %collective-permute-start.1 = (f32[8,4,15,128]{3,2,1,0:T(8,128)}, f32[8,4,15,128]{3,2,1,0:T(8,128)S(1)}, u32[]{:S(2)}, u32[]{:S(2)}) collective-permute-start(f32[8,4,15,128]{3,2,1,0:T(8,128)} %get-tuple-element.10), channel_id=1, source_target_pairs={{1,0},{2,1},{3,2},{4,3},{5,4},{6,5},{7,6},{8,7},{9,8},{10,9},{11,1... | collective-permute-start | bytes 737288 | tf_op jit(solution)/shard_map/ppermute | solution.py:30
  39.6 1.9 %collective-permute-start = (f32[8,4,15,128]{3,2,1,0:T(8,128)S(1)}, f32[8,4,15,128]{3,2,1,0:T(8,128)}, u32[]{:S(2)}, u32[]{:S(2)}) collective-permute-start(f32[8,4,15,128]{3,2,1,0:T(8,128)S(1)} %get-tuple-element.9), channel_id=1, source_target_pairs={{0,1},{1,2},{2,3},{3,4},{4,5},{5,6},{6,7},{7,8},{8,9},{9,10},{10,1... | collective-permute-start | bytes 737288 | tf_op jit(solution)/shard_map/ppermute | solution.py:28
  41.5 1.0 %convolution_bitcast_fusion = f32[8,4,31,256]{3,2,0,1:T(8,128)S(1)} fusion(f32[4,8,31,31]{3,2,1,0:T(8,128)S(1)} %reshape.115, f32[31,256,1,1]{1,0,3,2:T(8,128)S(1)} %copy-done.1), kind=kOutput, calls=%fused_computation.14 | convolution fusion | flops 94470144 | bytes 1170560 | tf_op jit(solution)/shard_map/sbuv,vf->sbuf/dot_general | solution.py:118
  42.5 1.1 %copy.47 = f32[8,4,31,256]{3,2,1,0:T(8,128)} copy(f32[8,4,31,256]{3,2,0,1:T(8,128)S(1)} %convolution_bitcast_fusion) | data formatting | bytes 2031616 | tf_op jit(solution)/shard_map/transpose | solution.py:172
  44.4 5.2 %collective-permute-done = f32[8,4,15,128]{3,2,1,0:T(8,128)} collective-permute-done((f32[8,4,15,128]{3,2,1,0:T(8,128)S(1)}, f32[8,4,15,128]{3,2,1,0:T(8,128)}, u32[]{:S(2)}, u32[]{:S(2)}) %collective-permute-start) | collective-permute-done | bytes 245792 | tf_op jit(solution)/shard_map/ppermute | solution.py:28
  49.5 2.0 %pad_maximum_fusion.ext_ref = f32[32,46,128]{2,1,0:T(8,128)} fusion(f32[32,15,128]{2,1,0:T(8,128)S(1)} %bitcast.88, f32[32,16,128]{2,1,0:T(8,128)S(1)} %bitcast.79, f32[32,15,128]{2,1,0:T(8,128)} %bitcast.11), kind=kLoop, calls=%fused_computation.22 | loop fusion | flops 376832 | bytes 1507328 | tf_op jit(solution)/shard_map/concatenate | solution.py:26
  51.5 9.1 %shard_map.137 = f32[4,3,16,128]{3,2,1,0:T(8,128)} custom-call(f32[32,46,128]{2,1,0:T(8,128)} %pad_maximum_fusion.ext_ref, f32[128,256]{1,0:T(8,128)} %constant.90.clone.fwd_ref, f32[32,31,256]{2,1,0:T(8,128)} %bitcast.77, f32[8,3]{1,0:T(8,128)} %copy.57.resp_ref, f32[256,128]{1,0:T(8,128)} %constant.91.clone.inv_ref), custom_call_target="tpu_custom_call" | custom-call | tf_op jit(solution)/shard_map/pallas_call | solution.py:176
  60.6 0.8 dynamic-slice_bitcast_fusion.2
  61.4 4.0 %collective-permute-start.4 = (f32[3,16,128]{2,1,0:T(8,128)S(1)}, f32[3,16,128]{2,1,0:T(8,128)S(1)}, u32[]{:S(2)}, u32[]{:S(2)}) collective-permute-start(f32[3,16,128]{2,1,0:T(8,128)S(1)} %get-tuple-element.12), channel_id=1, source_target_pairs={{0,96},{32,0},{64,32},{96,64},{1,97},{33,1},{65,33},{97,65},{2,98}... | collective-permute-start | bytes 73736 | tf_op jit(solution)/shard_map/ppermute | solution.py:314
  65.4 1.2 %collective-permute-start.2 = (f32[3,16,128]{2,1,0:T(8,128)S(1)}, f32[3,16,128]{2,1,0:T(8,128)S(1)}, u32[]{:S(2)}, u32[]{:S(2)}) collective-permute-start(f32[3,16,128]{2,1,0:T(8,128)S(1)} %get-tuple-element.11), channel_id=1, source_target_pairs={{0,32},{32,64},{64,96},{96,0},{1,33},{33,65},{65,97},{97,1},{2,34}... | collective-permute-start | bytes 73736 | tf_op jit(solution)/shard_map/ppermute | solution.py:314
  66.9 3.8 %collective-permute-done.3 = f32[3,16,128]{2,1,0:T(8,128)S(1)} collective-permute-done((f32[3,16,128]{2,1,0:T(8,128)S(1)}, f32[3,16,128]{2,1,0:T(8,128)S(1)}, u32[]{:S(2)}, u32[]{:S(2)}) %collective-permute-start.3) | collective-permute-done | bytes 24608 | tf_op jit(solution)/shard_map/ppermute | solution.py:314
  70.7 0.7 fusion.42
  71.5 1.9 %collective-permute-start.6 = (bf16[1,3,2,128]{3,2,1,0:T(2,128)(2,1)S(1)}, bf16[1,3,2,128]{3,2,1,0:T(2,128)(2,1)S(1)}, u32[]{:S(2)}, u32[]{:S(2)}) collective-permute-start(bf16[1,3,2,128]{3,2,1,0:T(2,128)(2,1)S(1)} %get-tuple-element.15), channel_id=1, source_target_pairs={{1,0},{2,1},{3,2},{4,3},{5,4},{6,5},{7,6},{8,7},{9,8},{10,9},{11,1... | collective-permute-start | bytes 4616 | tf_op jit(solution)/shard_map/ppermute | solution.py:30
  73.4 2.6 %collective-permute-start.5 = (bf16[1,3,2,128]{3,2,1,0:T(2,128)(2,1)S(1)}, bf16[1,3,2,128]{3,2,1,0:T(2,128)(2,1)S(1)}, u32[]{:S(2)}, u32[]{:S(2)}) collective-permute-start(bf16[1,3,2,128]{3,2,1,0:T(2,128)(2,1)S(1)} %get-tuple-element.14), channel_id=1, source_target_pairs={{0,1},{1,2},{2,3},{3,4},{4,5},{5,6},{6,7},{7,8},{8,9},{9,10},{10,1... | collective-permute-start | bytes 4616 | tf_op jit(solution)/shard_map/ppermute | solution.py:28
  76.0 4.4 %collective-permute-done.5 = bf16[1,3,2,128]{3,2,1,0:T(2,128)(2,1)S(1)} collective-permute-done((bf16[1,3,2,128]{3,2,1,0:T(2,128)(2,1)S(1)}, bf16[1,3,2,128]{3,2,1,0:T(2,128)(2,1)S(1)}, u32[]{:S(2)}, u32[]{:S(2)}) %collective-permute-start.5) | collective-permute-done | bytes 1568 | tf_op jit(solution)/shard_map/ppermute | solution.py:28
  81.4 1.4 %fusion.14 = bf16[18,1,8,17,64]{4,2,3,0,1:T(8,128)(2,1)S(1)} fusion(pred[18]{0:T(512)(128)(4,1)S(1)} %and_or_fusion, pred[8,17]{0,1:T(8,128)(4,1)S(1)} %copy-done.6, bf16[3,20,1,7,2]{3,0,4,1,2:T(4,128)(2,1)S(1)} %slice.46, bf16[3,20,1,8,17]{3,0,4,1,2:T(4,128)(2,1)S(1)} %copy.50, bf16[64,3,3,3]{0,3,2,1:T(4,128)(2,1)S(1)} %copy-done.4), kind=kOutput, calls=%fused_computation.21 | convolution fusion | flops 9925056 | bytes 334954 | tf_op jit(solution)/shard_map/conv_general_dilated | solution.py:38
  82.8 1.5 %convolution_convert_fusion = bf16[16,8,17,64]{3,1,2,0:T(8,128)(2,1)S(1)} fusion(bf16[64,64,3,3]{1,0,3,2:T(8,128)(2,1)S(1)} %copy-done.3, bf16[18,1,7,1,64]{4,2,3,0,1:T(8,128)(2,1)S(1)} %get-tuple-element.8, bf16[18,1,7,1,64]{4,2,3,0,1:T(8,128)(2,1)S(1)} %get-tuple-element.7, bf16[18,1,8,17,64]{4,2,3,0,1:T(8,128)(2,1)S(1)} %fusion.14), kind=kOutput, calls=%fused_computation.15 | convolution fusion | flops 162322432 | bytes 697856 | tf_op jit(solution)/shard_map/conv_general_dilated | solution.py:38
  84.4 1.3 %copy.53 = bf16[1,64,16,128]{3,2,1,0:T(8,128)(2,1)} copy(bf16[1,64,16,128]{1,2,3,0:T(8,128)(2,1)S(1)} %slice_bitcast_fusion) | data formatting | bytes 524288 | tf_op jit(solution)/shard_map/convert_element_type | solution.py:328
  (44 shorter events, 4.5 us)
Async XLA Ops:
  0.0 11.9 %copy-start = (f32[64,8,961]{2,1,0:T(8,128)S(1)}, f32[64,8,961]{2,1,0:T(8,128)}, u32[]{:S(2)}) copy-start(f32[64,8,961]{2,1,0:T(8,128)} %param.20) | copy-start | bytes 5904388
  0.0 11.8 %copy-start.5 = (s32[1,4,1]{1,2,0:T(1,128)S(1)}, s32[1,4,1]{1,2,0:T(1,128)}, u32[]{:S(2)}) copy-start(s32[1,4,1]{1,2,0:T(1,128)} %param.21) | copy-start | bytes 52
  4.2 18.4 %all-to-all-start = ((bf16[32,8,1280]{2,1,0:T(8,128)(2,1)}), bf16[32,8,1280]{2,1,0:T(8,128)(2,1)S(1)}, u32[]{:S(2)}, u32[]{:S(2)}) async-start(bf16[32,8,1280]{2,1,0:T(8,128)(2,1)} %bitcast.83), calls=%async_computation | async-start | bytes 1310720 | tf_op jit(solution)/shard_map/all_to_all | solution.py:305
  30.7 10.8 %copy-start.1 = (f32[31,256,1,1]{1,0,3,2:T(8,128)S(1)}, f32[31,256,1,1]{1,0,3,2:T(8,128)}, u32[]{:S(2)}) copy-start(f32[31,256,1,1]{1,0,3,2:T(8,128)} %constant.107) | copy-start | bytes 95236
  34.7 9.7 %collective-permute-start.1 = (f32[8,4,15,128]{3,2,1,0:T(8,128)}, f32[8,4,15,128]{3,2,1,0:T(8,128)S(1)}, u32[]{:S(2)}, u32[]{:S(2)}) collective-permute-start(f32[8,4,15,128]{3,2,1,0:T(8,128)} %get-tuple-element.10), channel_id=1, source_target_pairs={{1,0},{2,1},{3,2},{4,3},{5,4},{6,5},{7,6},{8,7},{9,8},{10,9},{11,1... | collective-permute-start | bytes 737288 | tf_op jit(solution)/shard_map/ppermute | solution.py:30
  39.6 9.9 %collective-permute-start = (f32[8,4,15,128]{3,2,1,0:T(8,128)S(1)}, f32[8,4,15,128]{3,2,1,0:T(8,128)}, u32[]{:S(2)}, u32[]{:S(2)}) collective-permute-start(f32[8,4,15,128]{3,2,1,0:T(8,128)S(1)} %get-tuple-element.9), channel_id=1, source_target_pairs={{0,1},{1,2},{2,3},{3,4},{4,5},{5,6},{6,7},{7,8},{8,9},{9,10},{10,1... | collective-permute-start | bytes 737288 | tf_op jit(solution)/shard_map/ppermute | solution.py:28
  42.5 1.1 %copy-start.2 = (f32[32,3]{0,1:T(4,128)S(1)}, f32[32,3]{0,1:T(4,128)}, u32[]{:S(2)}) copy-start(f32[32,3]{0,1:T(4,128)} %param.22) | copy-start | bytes 1156
  51.5 29.9 %copy-start.4 = (bf16[64,3,3,3]{0,3,2,1:T(4,128)(2,1)S(1)}, bf16[64,3,3,3]{0,3,2,1:T(4,128)(2,1)}, u32[]{:S(2)}) copy-start(bf16[64,3,3,3]{0,3,2,1:T(4,128)(2,1)} %param.23) | copy-start | bytes 10372
  51.5 29.9 %copy-start.6 = (pred[8,17]{0,1:T(8,128)(4,1)S(1)}, pred[8,17]{0,1:T(8,128)(4,1)}, u32[]{:S(2)}) copy-start(pred[8,17]{0,1:T(8,128)(4,1)} %constant.105) | copy-start | bytes 412
  61.4 5.6 %collective-permute-start.4 = (f32[3,16,128]{2,1,0:T(8,128)S(1)}, f32[3,16,128]{2,1,0:T(8,128)S(1)}, u32[]{:S(2)}, u32[]{:S(2)}) collective-permute-start(f32[3,16,128]{2,1,0:T(8,128)S(1)} %get-tuple-element.12), channel_id=1, source_target_pairs={{0,96},{32,0},{64,32},{96,64},{1,97},{33,1},{65,33},{97,65},{2,98}... | collective-permute-start | bytes 73736 | tf_op jit(solution)/shard_map/ppermute | solution.py:314
  65.4 5.3 %collective-permute-start.3 = (f32[3,16,128]{2,1,0:T(8,128)S(1)}, f32[3,16,128]{2,1,0:T(8,128)S(1)}, u32[]{:S(2)}, u32[]{:S(2)}) collective-permute-start(f32[3,16,128]{2,1,0:T(8,128)S(1)} %get-tuple-element.13), channel_id=1, source_target_pairs={{0,64},{32,96},{64,0},{96,32},{1,65},{33,97},{65,1},{97,33},{2,66}... | collective-permute-start | bytes 73736 | tf_op jit(solution)/shard_map/ppermute | solution.py:314
  65.4 5.3 %collective-permute-start.2 = (f32[3,16,128]{2,1,0:T(8,128)S(1)}, f32[3,16,128]{2,1,0:T(8,128)S(1)}, u32[]{:S(2)}, u32[]{:S(2)}) collective-permute-start(f32[3,16,128]{2,1,0:T(8,128)S(1)} %get-tuple-element.11), channel_id=1, source_target_pairs={{0,32},{32,64},{64,96},{96,0},{1,33},{33,65},{65,97},{97,1},{2,34}... | collective-permute-start | bytes 73736 | tf_op jit(solution)/shard_map/ppermute | solution.py:314
  71.5 4.5 %collective-permute-start.6 = (bf16[1,3,2,128]{3,2,1,0:T(2,128)(2,1)S(1)}, bf16[1,3,2,128]{3,2,1,0:T(2,128)(2,1)S(1)}, u32[]{:S(2)}, u32[]{:S(2)}) collective-permute-start(bf16[1,3,2,128]{3,2,1,0:T(2,128)(2,1)S(1)} %get-tuple-element.15), channel_id=1, source_target_pairs={{1,0},{2,1},{3,2},{4,3},{5,4},{6,5},{7,6},{8,7},{9,8},{10,9},{11,1... | collective-permute-start | bytes 4616 | tf_op jit(solution)/shard_map/ppermute | solution.py:30
  73.4 7.0 %collective-permute-start.5 = (bf16[1,3,2,128]{3,2,1,0:T(2,128)(2,1)S(1)}, bf16[1,3,2,128]{3,2,1,0:T(2,128)(2,1)S(1)}, u32[]{:S(2)}, u32[]{:S(2)}) collective-permute-start(bf16[1,3,2,128]{3,2,1,0:T(2,128)(2,1)S(1)} %get-tuple-element.14), channel_id=1, source_target_pairs={{0,1},{1,2},{2,3},{3,4},{4,5},{5,6},{6,7},{7,8},{8,9},{9,10},{10,1... | collective-permute-start | bytes 4616 | tf_op jit(solution)/shard_map/ppermute | solution.py:28
  81.4 1.4 %copy-start.3 = (bf16[64,64,3,3]{1,0,3,2:T(8,128)(2,1)S(1)}, bf16[64,64,3,3]{1,0,3,2:T(8,128)(2,1)}, u32[]{:S(2)}) copy-start(bf16[64,64,3,3]{1,0,3,2:T(8,128)(2,1)} %param.24) | copy-start | bytes 221188

commit v9 on v7

--- a/solution.py
+++ b/solution.py
@@ -158,8 +158,8 @@
 
 
 def pack_kernel(capacity, energy_ref, spot_ref, tile_ref, count_ref, scene_ref, row_ref, out_ref):
-    blocks, width = energy_ref.shape
-    hits = spot_ref.shape[1]
+    blocks, bands, hits = energy_ref.shape
+    width = bands * hits
     slots = out_ref.shape[0]
     tiles = slots // capacity
     f32 = jnp.float32
@@ -172,10 +172,8 @@
     zero = jnp.zeros((blocks, blocks), f32)
     count_col = jnp.sum(jnp.where(eye, count_row, zero), axis=1, keepdims=True)
     base_col = jnp.sum(jnp.where(eye, base_row, zero), axis=1, keepdims=True)
-    lanes = lax.broadcasted_iota(jnp.int32, (blocks, width), 1) % hits
+    lanes = lax.broadcasted_iota(jnp.int32, (blocks, hits), 1)
     live = lanes.astype(f32) < count_col
-    energy = energy_ref[...]
-    masked = jnp.where(live, energy, jnp.zeros_like(energy))
     spot = spot_ref[...]
     field = base_col * WIN + lax.shift_right_logical(spot, 7).astype(f32)
     column = jnp.bitwise_and(spot, W - 1).astype(f32)
@@ -187,9 +185,12 @@
     place = tile_row * capacity + rank
     pp = lax.broadcasted_iota(jnp.int32, (slots, blocks), 0).astype(f32)
     select = (pp == place).astype(jnp.bfloat16)
-    out_ref[:, pl.ds(0, width)] = jnp.dot(select, masked, preferred_element_type=f32).astype(
-        out_ref.dtype
-    )
+    for band in range(bands):
+        energy = energy_ref[:, band, :]
+        masked = jnp.where(live, energy, jnp.zeros_like(energy))
+        out_ref[:, pl.ds(band * hits, hits)] = jnp.dot(
+            select, masked, preferred_element_type=f32
+        ).astype(out_ref.dtype)
     out_ref[:, pl.ds(width, hits)] = jnp.dot(
         select, field.astype(jnp.bfloat16), preferred_element_type=f32
     ).astype(out_ref.dtype)
@@ -199,8 +200,8 @@
 
 
 def pack(energy, spot, tile, count, scene, row, capacity, slots):
-    blocks, width = energy.shape
-    hits = spot.shape[1]
+    blocks, bands, hits = energy.shape
+    width = bands * hits
     return pl.pallas_call(
         functools.partial(pack_kernel, capacity),
         out_shape=jax.ShapeDtypeStruct((slots, width + 2 * hits), energy.dtype),
@@ -226,7 +227,7 @@
     capacity = 2 * block_dev // tile_count
     scenes = psf_index.shape[1]
     send = pack(
-        hit_energy.reshape(block_dev, band_dev * hit_lanes),
+        hit_energy,
         hit_spot[0],
         block_tile[0, :, 0].reshape(1, block_dev),
         block_count,

time: 85 us -> 83.5 us (0.982)
  local copies, waits for them, and re-layouts: 7.56 us -> 5.7 us
    unnamed x21 -> x20, local copies, waits for them, and re-layouts: 2.05 us -> 0.19 us
where the time goes in v9:
time: 83.5 us; the launch traced here: 83.1 us
  starting transfers between devices  24.3 us (29%)
  waiting for transfers between devices  24 us (29%)
  matrix products  19.3 us (23%)
  Pallas kernels  9.08 us (11%)
  local copies, waits for them, and re-layouts  5.7 us (7%)
    ppermute x2, waiting for transfers between devices, padded_2(): lax.ppermute(tail, axis, [(i, (i + 1) % count) for i in range(ends)])  10.2 us
    all_to_all x1, waiting for transfers between devices, per_device(): got = lax.all_to_all(send, 'tile', split_axis=0, concat_axis=0, tiled=True)  9.55 us
    all_to_all x1, starting transfers between devices, per_device(): got = lax.all_to_all(send, 'tile', split_axis=0, concat_axis=0, tiled=True)  7.62 us
    dot_general x1, matrix products, window_splat(): jnp.einsum('ibjh,ihc->ibjc', spread, onehot, preferred_element_type=jnp.f...  7.54 us
    ppermute x2, starting transfers between devices, padded_2(): lax.ppermute(head, axis, [((i + 1) % count, i) for i in range(ends)])  6.83 us
    pallas_call x1, Pallas kernels, row_taps(): pl.pallas_call(row_taps_kernel, out_shape=jax.ShapeDtypeStruct((channels,...  6.32 us
    ppermute x3, starting transfers between devices, per_device(): lax.ppermute(piece, 'wave', [(i, (i + step) % wave_count) for i in range(...  5.37 us
    ppermute x2, starting transfers between devices, padded_2(): lax.ppermute(tail, axis, [(i, (i + 1) % count) for i in range(ends)])  4.51 us
  transfers between devices with their start and end apart: 8, of which 6 were waited for; matrix products, arithmetic and copies ran while one was open for 4% of the time, Pallas kernels for 0%

profile of v9, /device:TPU:2, one launch (start us, length us, event | category | flops | bytes accessed | tf_op | source)
XLA Modules:
  0.0 83.1 jit_solution(15329734806953578734)
XLA Ops:
  0.0 2.8 %shard_map.136 = bf16[256,1280]{1,0:T(8,128)(2,1)} custom-call(bf16[128,8,128]{2,1,0:T(8,128)(2,1)} %energy_ref.1, s32[128,128]{1,0:T(8,128)} %bitcast.99, s32[1,128]{1,0:T(1,128)} %bitcast.100, s32[1,128]{1,0:T(1,128)} %count_ref.1, s32[1,128]{1,0:T(1,128)} %scene_ref.1, s32[1,128]{1,0:T(1,128)} %row_ref.1), custom_call_target="tpu_custom_call" | custom-call | tf_op jit(solution)/shard_map/pallas_call | solution.py:205
  2.8 7.6 %all-to-all-start = ((bf16[32,8,1280]{2,1,0:T(8,128)(2,1)}), bf16[32,8,1280]{2,1,0:T(8,128)(2,1)S(1)}, u32[]{:S(2)}, u32[]{:S(2)}) async-start(bf16[32,8,1280]{2,1,0:T(8,128)(2,1)} %bitcast.93), calls=%async_computation | async-start | bytes 1310720 | tf_op jit(solution)/shard_map/all_to_all | solution.py:240
  11.0 0.6 reshape.114
  11.6 9.6 %all-to-all-done = bf16[32,8,1280]{2,1,0:T(8,128)(2,1)S(1)} async-done(((bf16[32,8,1280]{2,1,0:T(8,128)(2,1)}), bf16[32,8,1280]{2,1,0:T(8,128)(2,1)S(1)}, u32[]{:S(2)}, u32[]{:S(2)}) %all-to-all-start) | async-done | bytes 655392 | tf_op jit(solution)/shard_map/all_to_all | solution.py:240
  21.8 7.5 %fusion.1 = f32[256,8,4,128]{3,2,1,0:T(4,128)S(1)} fusion(s32[256,128]{1,0:T(8,128)S(1)} %get-tuple-element.6, pred[256,4,128]{2,1,0:T(4,128)(4,1)S(1)} %iota_compare_fusion.4, bf16[256,8,128]{2,1,0:T(8,128)(2,1)S(1)} %bitcast.96), kind=kOutput, calls=%fused_computation.3 | convolution fusion | flops 273678336 | bytes 4980736 | tf_op jit(solution)/shard_map/ibjh,ihc->ibjc/dot_general | solution.py:151
  29.3 3.2 %fusion.4 = f32[64,8,128,1]{2,0,3,1:T(8,128)S(1)} fusion(f32[256,8,4,128]{3,2,1,0:T(4,128)S(1)} %fusion.1, s32[256,4]{0,1:T(4,128)S(1)} %iota_add_fusion), kind=kOutput, calls=%fused_computation.5 | convolution fusion | flops 402718720 | bytes 4460544 | tf_op jit(solution)/shard_map/ibjc,ijr->brc/dot_general | solution.py:156
  32.5 0.8 fusion.67
  33.3 4.9 %collective-permute-start.1 = (f32[8,4,15,128]{3,2,1,0:T(8,128)}, f32[8,4,15,128]{3,2,1,0:T(8,128)S(1)}, u32[]{:S(2)}, u32[]{:S(2)}) collective-permute-start(f32[8,4,15,128]{3,2,1,0:T(8,128)} %get-tuple-element.10), channel_id=1, source_target_pairs={{1,0},{2,1},{3,2},{4,3},{5,4},{6,5},{7,6},{8,7},{9,8},{10,9},{11,1... | collective-permute-start | bytes 737288 | tf_op jit(solution)/shard_map/ppermute | solution.py:29
  38.3 1.9 %collective-permute-start = (f32[8,4,15,128]{3,2,1,0:T(8,128)}, f32[8,4,15,128]{3,2,1,0:T(8,128)S(1)}, u32[]{:S(2)}, u32[]{:S(2)}) collective-permute-start(f32[8,4,15,128]{3,2,1,0:T(8,128)} %get-tuple-element.9), channel_id=1, source_target_pairs={{0,1},{1,2},{2,3},{3,4},{4,5},{5,6},{6,7},{7,8},{8,9},{9,10},{10,1... | collective-permute-start | bytes 737288 | tf_op jit(solution)/shard_map/ppermute | solution.py:27
  40.2 1.0 %convolution_bitcast_fusion = f32[8,4,31,256]{3,2,0,1:T(8,128)S(1)} fusion(f32[4,8,31,31]{3,2,1,0:T(8,128)S(1)} %reshape.114, f32[31,256,1,1]{1,0,3,2:T(8,128)S(1)} %copy-done.3), kind=kOutput, calls=%fused_computation.14 | convolution fusion | flops 94470144 | bytes 1170560 | tf_op jit(solution)/shard_map/sbuv,vf->sbuf/dot_general | solution.py:117
  41.2 1.1 %copy.47 = f32[8,4,31,256]{3,2,1,0:T(8,128)} copy(f32[8,4,31,256]{3,2,0,1:T(8,128)S(1)} %convolution_bitcast_fusion) | data formatting | bytes 2031616 | tf_op jit(solution)/shard_map/transpose | solution.py:129
  42.5 5.8 %collective-permute-done = f32[8,4,15,128]{3,2,1,0:T(8,128)S(1)} collective-permute-done((f32[8,4,15,128]{3,2,1,0:T(8,128)}, f32[8,4,15,128]{3,2,1,0:T(8,128)S(1)}, u32[]{:S(2)}, u32[]{:S(2)}) %collective-permute-start) | collective-permute-done | bytes 245792 | tf_op jit(solution)/shard_map/ppermute | solution.py:27
  48.3 2.5 %fusion.15.spec_ref = f32[32,46,256]{2,1,0:T(8,128)} fusion(f32[128,256,1]{1,0,2:T(8,128)S(1)} %copy-done.1, f32[32,15,128]{2,1,0:T(8,128)S(1)} %bitcast.97, f32[32,16,128]{2,1,0:T(8,128)S(1)} %bitcast.89, f32[32,15,128]{2,1,0:T(8,128)S(1)} %bitcast.98), kind=kOutput, calls=%fused_computation.23 | convolution fusion | flops 579190784 | bytes 2392064 | tf_op jit(solution)/shard_map/cyx,xf->cyf/dot_general | solution.py:126
  50.8 6.3 %shard_map.137 = f32[32,16,256]{2,1,0:T(8,128)} custom-call(f32[32,46,256]{2,1,0:T(8,128)} %fusion.15.spec_ref, f32[32,31,256]{2,1,0:T(8,128)} %bitcast.87), custom_call_target="tpu_custom_call" | custom-call | tf_op jit(solution)/shard_map/pallas_call | solution.py:99
  57.2 1.9 %convolution_bitcast_fusion.1 = f32[4,3,16,256]{3,1,2,0:T(4,128)S(1)} fusion(f32[8,4,16,256]{3,2,1,0:T(8,128)} %bitcast.95, f32[32,3]{0,1:T(4,128)S(1)} %copy-done.4, s32[]{:T(128)S(6)} %select_n.64), kind=kOutput, calls=%fused_computation.17 | convolution fusion | flops 4718592 | bytes 721284 | tf_op jit(solution)/shard_map/bsyf,bc->scyf/dot_general | solution.py:131
  59.4 4.1 %collective-permute-start.4 = (f32[3,16,128]{2,1,0:T(8,128)S(1)}, f32[3,16,128]{2,1,0:T(8,128)S(1)}, u32[]{:S(2)}, u32[]{:S(2)}) collective-permute-start(f32[3,16,128]{2,1,0:T(8,128)S(1)} %get-tuple-element.12), channel_id=1, source_target_pairs={{0,96},{32,0},{64,32},{96,64},{1,97},{33,1},{65,33},{97,65},{2,98}... | collective-permute-start | bytes 73736 | tf_op jit(solution)/shard_map/ppermute | solution.py:249
  63.5 1.3 %collective-permute-start.2 = (f32[3,16,128]{2,1,0:T(8,128)S(1)}, f32[3,16,128]{2,1,0:T(8,128)S(1)}, u32[]{:S(2)}, u32[]{:S(2)}) collective-permute-start(f32[3,16,128]{2,1,0:T(8,128)S(1)} %get-tuple-element.11), channel_id=1, source_target_pairs={{0,32},{32,64},{64,96},{96,0},{1,33},{33,65},{65,97},{97,1},{2,34}... | collective-permute-start | bytes 73736 | tf_op jit(solution)/shard_map/ppermute | solution.py:249
  65.1 3.8 %collective-permute-done.3 = f32[3,16,128]{2,1,0:T(8,128)S(1)} collective-permute-done((f32[3,16,128]{2,1,0:T(8,128)S(1)}, f32[3,16,128]{2,1,0:T(8,128)S(1)}, u32[]{:S(2)}, u32[]{:S(2)}) %collective-permute-start.3) | collective-permute-done | bytes 24608 | tf_op jit(solution)/shard_map/ppermute | solution.py:249
  68.9 1.9 %collective-permute-start.6 = (bf16[1,3,2,128]{3,2,1,0:T(2,128)(2,1)S(1)}, bf16[1,3,2,128]{3,2,1,0:T(2,128)(2,1)S(1)}, u32[]{:S(2)}, u32[]{:S(2)}) collective-permute-start(bf16[1,3,2,128]{3,2,1,0:T(2,128)(2,1)S(1)} %get-tuple-element.15), channel_id=1, source_target_pairs={{1,0},{2,1},{3,2},{4,3},{5,4},{6,5},{7,6},{8,7},{9,8},{10,9},{11,1... | collective-permute-start | bytes 4616 | tf_op jit(solution)/shard_map/ppermute | solution.py:29
  70.8 2.6 %collective-permute-start.5 = (bf16[1,3,2,128]{3,2,1,0:T(2,128)(2,1)S(1)}, bf16[1,3,2,128]{3,2,1,0:T(2,128)(2,1)S(1)}, u32[]{:S(2)}, u32[]{:S(2)}) collective-permute-start(bf16[1,3,2,128]{3,2,1,0:T(2,128)(2,1)S(1)} %get-tuple-element.14), channel_id=1, source_target_pairs={{0,1},{1,2},{2,3},{3,4},{4,5},{5,6},{6,7},{7,8},{8,9},{9,10},{10,1... | collective-permute-start | bytes 4616 | tf_op jit(solution)/shard_map/ppermute | solution.py:27
  73.5 4.4 %collective-permute-done.5 = bf16[1,3,2,128]{3,2,1,0:T(2,128)(2,1)S(1)} collective-permute-done((bf16[1,3,2,128]{3,2,1,0:T(2,128)(2,1)S(1)}, bf16[1,3,2,128]{3,2,1,0:T(2,128)(2,1)S(1)}, u32[]{:S(2)}, u32[]{:S(2)}) %collective-permute-start.5) | collective-permute-done | bytes 1568 | tf_op jit(solution)/shard_map/ppermute | solution.py:27
  78.8 1.4 %fusion.14 = bf16[18,1,8,17,64]{4,2,3,0,1:T(8,128)(2,1)S(1)} fusion(pred[18]{0:T(512)(128)(4,1)S(1)} %and_or_fusion, pred[8,17]{0,1:T(8,128)(4,1)S(1)} %copy-done.8, bf16[3,20,1,7,2]{3,0,4,1,2:T(4,128)(2,1)S(1)} %slice.46, bf16[3,20,1,8,17]{3,0,4,1,2:T(4,128)(2,1)S(1)} %copy.51, bf16[64,3,3,3]{0,3,2,1:T(4,128)(2,1)S(1)} %copy-done.6), kind=kOutput, calls=%fused_computation.22 | convolution fusion | flops 9925056 | bytes 334954 | tf_op jit(solution)/shard_map/conv_general_dilated | solution.py:37
  80.3 1.5 %convolution_convert_fusion = bf16[16,8,17,64]{3,1,2,0:T(8,128)(2,1)S(1)} fusion(bf16[64,64,3,3]{1,0,3,2:T(8,128)(2,1)S(1)} %copy-done.5, bf16[18,1,7,1,64]{4,2,3,0,1:T(8,128)(2,1)S(1)} %get-tuple-element.8, bf16[18,1,7,1,64]{4,2,3,0,1:T(8,128)(2,1)S(1)} %get-tuple-element.7, bf16[18,1,8,17,64]{4,2,3,0,1:T(8,128)(2,1)S(1)} %fusion.14), kind=kOutput, calls=%fused_computation.15 | convolution fusion | flops 162322432 | bytes 697856 | tf_op jit(solution)/shard_map/conv_general_dilated | solution.py:37
  81.9 1.3 %copy.54 = bf16[1,64,16,128]{3,2,1,0:T(8,128)(2,1)} copy(bf16[1,64,16,128]{1,2,3,0:T(8,128)(2,1)S(1)} %slice_bitcast_fusion) | data formatting | bytes 524288 | tf_op jit(solution)/shard_map/convert_element_type | solution.py:263
  (47 shorter events, 3.0 us)
Async XLA Ops:
  0.0 10.5 %copy-start = (f32[64,8,961]{2,1,0:T(8,128)S(1)}, f32[64,8,961]{2,1,0:T(8,128)}, u32[]{:S(2)}) copy-start(f32[64,8,961]{2,1,0:T(8,128)} %param.20) | copy-start | bytes 5904388
  0.0 10.4 %copy-start.7 = (s32[1,4,1]{1,2,0:T(1,128)S(1)}, s32[1,4,1]{1,2,0:T(1,128)}, u32[]{:S(2)}) copy-start(s32[1,4,1]{1,2,0:T(1,128)} %param.21) | copy-start | bytes 52
  2.8 18.4 %all-to-all-start = ((bf16[32,8,1280]{2,1,0:T(8,128)(2,1)}), bf16[32,8,1280]{2,1,0:T(8,128)(2,1)S(1)}, u32[]{:S(2)}, u32[]{:S(2)}) async-start(bf16[32,8,1280]{2,1,0:T(8,128)(2,1)} %bitcast.93), calls=%async_computation | async-start | bytes 1310720 | tf_op jit(solution)/shard_map/all_to_all | solution.py:240
  29.3 10.9 %copy-start.3 = (f32[31,256,1,1]{1,0,3,2:T(8,128)S(1)}, f32[31,256,1,1]{1,0,3,2:T(8,128)}, u32[]{:S(2)}) copy-start(f32[31,256,1,1]{1,0,3,2:T(8,128)} %constant.108) | copy-start | bytes 95236
  33.3 9.1 %collective-permute-start.1 = (f32[8,4,15,128]{3,2,1,0:T(8,128)}, f32[8,4,15,128]{3,2,1,0:T(8,128)S(1)}, u32[]{:S(2)}, u32[]{:S(2)}) collective-permute-start(f32[8,4,15,128]{3,2,1,0:T(8,128)} %get-tuple-element.10), channel_id=1, source_target_pairs={{1,0},{2,1},{3,2},{4,3},{5,4},{6,5},{7,6},{8,7},{9,8},{10,9},{11,1... | collective-permute-start | bytes 737288 | tf_op jit(solution)/shard_map/ppermute | solution.py:29
  38.3 10.0 %collective-permute-start = (f32[8,4,15,128]{3,2,1,0:T(8,128)}, f32[8,4,15,128]{3,2,1,0:T(8,128)S(1)}, u32[]{:S(2)}, u32[]{:S(2)}) collective-permute-start(f32[8,4,15,128]{3,2,1,0:T(8,128)} %get-tuple-element.9), channel_id=1, source_target_pairs={{0,1},{1,2},{2,3},{3,4},{4,5},{5,6},{6,7},{7,8},{8,9},{9,10},{10,1... | collective-permute-start | bytes 737288 | tf_op jit(solution)/shard_map/ppermute | solution.py:27
  41.2 7.1 %copy-start.1 = (f32[128,256,1]{1,0,2:T(8,128)S(1)}, f32[128,256,1]{1,0,2:T(8,128)}, u32[]{:S(2)}) copy-start(f32[128,256,1]{1,0,2:T(8,128)} %constant.107) | copy-start | bytes 393220
  50.8 6.3 %copy-start.4 = (f32[32,3]{0,1:T(4,128)S(1)}, f32[32,3]{0,1:T(4,128)}, u32[]{:S(2)}) copy-start(f32[32,3]{0,1:T(4,128)} %param.22) | copy-start | bytes 1156
  50.8 8.2 %copy-start.2 = (f32[256,128,1,1]{1,0,3,2:T(8,128)S(1)}, f32[256,128,1,1]{1,0,3,2:T(8,128)}, u32[]{:S(2)}) copy-start(f32[256,128,1,1]{1,0,3,2:T(8,128)} %constant.109) | copy-start | bytes 393220
  57.2 21.6 %copy-start.6 = (bf16[64,3,3,3]{0,3,2,1:T(4,128)(2,1)S(1)}, bf16[64,3,3,3]{0,3,2,1:T(4,128)(2,1)}, u32[]{:S(2)}) copy-start(bf16[64,3,3,3]{0,3,2,1:T(4,128)(2,1)} %param.23) | copy-start | bytes 10372
  57.2 21.6 %copy-start.8 = (pred[8,17]{0,1:T(8,128)(4,1)S(1)}, pred[8,17]{0,1:T(8,128)(4,1)}, u32[]{:S(2)}) copy-start(pred[8,17]{0,1:T(8,128)(4,1)} %constant.105) | copy-start | bytes 412
  59.4 5.6 %collective-permute-start.4 = (f32[3,16,128]{2,1,0:T(8,128)S(1)}, f32[3,16,128]{2,1,0:T(8,128)S(1)}, u32[]{:S(2)}, u32[]{:S(2)}) collective-permute-start(f32[3,16,128]{2,1,0:T(8,128)S(1)} %get-tuple-element.12), channel_id=1, source_target_pairs={{0,96},{32,0},{64,32},{96,64},{1,97},{33,1},{65,33},{97,65},{2,98}... | collective-permute-start | bytes 73736 | tf_op jit(solution)/shard_map/ppermute | solution.py:249
  63.5 5.3 %collective-permute-start.3 = (f32[3,16,128]{2,1,0:T(8,128)S(1)}, f32[3,16,128]{2,1,0:T(8,128)S(1)}, u32[]{:S(2)}, u32[]{:S(2)}) collective-permute-start(f32[3,16,128]{2,1,0:T(8,128)S(1)} %get-tuple-element.13), channel_id=1, source_target_pairs={{0,64},{32,96},{64,0},{96,32},{1,65},{33,97},{65,1},{97,33},{2,66}... | collective-permute-start | bytes 73736 | tf_op jit(solution)/shard_map/ppermute | solution.py:249
  63.5 5.3 %collective-permute-start.2 = (f32[3,16,128]{2,1,0:T(8,128)S(1)}, f32[3,16,128]{2,1,0:T(8,128)S(1)}, u32[]{:S(2)}, u32[]{:S(2)}) collective-permute-start(f32[3,16,128]{2,1,0:T(8,128)S(1)} %get-tuple-element.11), channel_id=1, source_target_pairs={{0,32},{32,64},{64,96},{96,0},{1,33},{33,65},{65,97},{97,1},{2,34}... | collective-permute-start | bytes 73736 | tf_op jit(solution)/shard_map/ppermute | solution.py:249
  68.9 4.5 %collective-permute-start.6 = (bf16[1,3,2,128]{3,2,1,0:T(2,128)(2,1)S(1)}, bf16[1,3,2,128]{3,2,1,0:T(2,128)(2,1)S(1)}, u32[]{:S(2)}, u32[]{:S(2)}) collective-permute-start(bf16[1,3,2,128]{3,2,1,0:T(2,128)(2,1)S(1)} %get-tuple-element.15), channel_id=1, source_target_pairs={{1,0},{2,1},{3,2},{4,3},{5,4},{6,5},{7,6},{8,7},{9,8},{10,9},{11,1... | collective-permute-start | bytes 4616 | tf_op jit(solution)/shard_map/ppermute | solution.py:29
  70.8 7.0 %collective-permute-start.5 = (bf16[1,3,2,128]{3,2,1,0:T(2,128)(2,1)S(1)}, bf16[1,3,2,128]{3,2,1,0:T(2,128)(2,1)S(1)}, u32[]{:S(2)}, u32[]{:S(2)}) collective-permute-start(bf16[1,3,2,128]{3,2,1,0:T(2,128)(2,1)S(1)} %get-tuple-element.14), channel_id=1, source_target_pairs={{0,1},{1,2},{2,3},{3,4},{4,5},{5,6},{6,7},{7,8},{8,9},{9,10},{10,1... | collective-permute-start | bytes 4616 | tf_op jit(solution)/shard_map/ppermute | solution.py:27
  78.8 1.5 %copy-start.5 = (bf16[64,64,3,3]{1,0,3,2:T(8,128)(2,1)S(1)}, bf16[64,64,3,3]{1,0,3,2:T(8,128)(2,1)}, u32[]{:S(2)}) copy-start(bf16[64,64,3,3]{1,0,3,2:T(8,128)(2,1)} %param.24) | copy-start | bytes 221188

commit v10 on v9

--- a/solution.py
+++ b/solution.py
@@ -72,9 +72,9 @@
 
 
 def row_taps_kernel(spec_ref, kern_ref, out_ref):
-    group = spec_ref.shape[0]
-    side = kern_ref.shape[1]
+    group, tall = spec_ref.shape[:2]
     rows = out_ref.shape[1]
+    side = tall - rows + 1
 
     def one(c, carry):
         acc_re = jnp.zeros((rows, LANE), jnp.float32)
@@ -114,7 +114,11 @@
     side = 2 * radius + 1
     unused, taps, unused_too = dft_tables(W, side, radius)
     chosen = psf_bank[psf_index[0, :, 0]].reshape(scenes, band_dev, side, side)
-    return jnp.einsum("sbuv,vf->sbuf", chosen, taps, precision=lax.Precision.HIGHEST)
+    chosen = jnp.pad(chosen.transpose(1, 0, 2, 3), ((0, 0), (0, 0), (0, 1), (0, 0)))
+    spectra = jnp.dot(
+        chosen.reshape(-1, side), taps, precision=lax.Precision.HIGHEST
+    )
+    return spectra.reshape(band_dev * scenes, side + 1, -1)
 
 
 def patch_blur(extended, kern, response, radius):
@@ -126,7 +130,7 @@
     spec = jnp.einsum(
         "cyx,xf->cyf", extended.reshape(band_dev * scenes, tall, width), forward, precision=hi
     )
-    taps = kern.transpose(1, 0, 2, 3).reshape(band_dev * scenes, side, -1)
+    taps = kern
     out = row_taps(spec, taps, rows_dev).reshape(band_dev, scenes, rows_dev, -1)
     color = jnp.einsum("bsyf,bc->scyf", out, response, precision=hi)
     return jnp.einsum("scyf,fx->scyx", color, inverse, precision=hi)
@@ -153,7 +157,12 @@
     placing = (base[:, None, None] + rows[None, :, None] == row_ids[None, None, :]).astype(
         jnp.float32
     )
-    total = jnp.einsum("ibjc,ijr->brc", window, placing, precision=lax.Precision.HIGH)
+    placing = placing.astype(jnp.bfloat16)
+    upper = lax.reduce_precision(window, exponent_bits=8, mantissa_bits=7)
+    lower = (window - upper).astype(jnp.bfloat16)
+    total = jnp.einsum(
+        "ibjc,ijr->brc", upper.astype(jnp.bfloat16), placing, preferred_element_type=jnp.float32
+    ) + jnp.einsum("ibjc,ijr->brc", lower, placing, preferred_element_type=jnp.float32)
     return total.reshape(band_dev, scenes, ROWS_DEV, W)
 
 

time: 83.5 us -> 80.9 us (0.969)
  waiting for transfers between devices: 24 us -> 21.9 us
    all_to_all x1, waiting for transfers between devices: 9.55 us -> 7.57 us  [per_device(): got = lax.all_to_all(send, 'tile', split_axis=0, concat_axis=0, tiled=True)]
    transpose x1 -> x0, local copies, waits for them, and re-layouts: 1.09 us -> none  [patch_blur(): taps = kern.transpose(1, 0, 2, 3).reshape(band_dev * scenes, side, -1)]
    pad x0 -> x1, local copies, waits for them, and re-layouts: none -> 1.09 us  [kernel_spectra(): jnp.pad(chosen.transpose(1, 0, 2, 3), ((0, 0), (0, 0), (0, 1), (0, 0)))]
    unnamed x20 -> x21, local copies, waits for them, and re-layouts: 0.19 us -> 1.05 us
    dot_general x2 -> x3, matrix products: 4.16 us -> 3.49 us  [the longest x1 1.95 us: kernel_spectra(): jnp.dot(chosen.reshape(-1, side), taps, precision=lax.Precision.HIGHEST)]
  transfers between devices with their start and end apart: 8 -> 8, of which waited for: 6 -> 5; matrix products, arithmetic and copies ran while one was open for 4% -> 6% of each run, Pallas kernels for 0% -> 0%
where the time goes in v10:
time: 80.9 us; the launch traced here: 80.5 us
  starting transfers between devices  24.3 us (30%)
  waiting for transfers between devices  21.9 us (27%)
  matrix products  18.6 us (23%)
  Pallas kernels  9.07 us (11%)
  local copies, waits for them, and re-layouts  5.77 us (7%)
    ppermute x2, waiting for transfers between devices, padded_2(): lax.ppermute(tail, axis, [(i, (i + 1) % count) for i in range(ends)])  10.3 us
    all_to_all x1, starting transfers between devices, per_device(): got = lax.all_to_all(send, 'tile', split_axis=0, concat_axis=0, tiled=True)  7.62 us
    all_to_all x1, waiting for transfers between devices, per_device(): got = lax.all_to_all(send, 'tile', split_axis=0, concat_axis=0, tiled=True)  7.57 us
    dot_general x1, matrix products, window_splat(): jnp.einsum('ibjh,ihc->ibjc', spread, onehot, preferred_element_type=jnp.f...  7.5 us
    ppermute x2, starting transfers between devices, padded_2(): lax.ppermute(head, axis, [((i + 1) % count, i) for i in range(ends)])  6.85 us
    pallas_call x1, Pallas kernels, row_taps(): pl.pallas_call(row_taps_kernel, out_shape=jax.ShapeDtypeStruct((channels,...  6.3 us
    ppermute x3, starting transfers between devices, per_device(): lax.ppermute(piece, 'wave', [(i, (i + step) % wave_count) for i in range(...  5.37 us
    ppermute x2, starting transfers between devices, padded_2(): lax.ppermute(tail, axis, [(i, (i + 1) % count) for i in range(ends)])  4.51 us
  transfers between devices with their start and end apart: 8, of which 5 were waited for; matrix products, arithmetic and copies ran while one was open for 6% of the time, Pallas kernels for 0%

profile of v10, /device:TPU:2, one launch (start us, length us, event | category | flops | bytes accessed | tf_op | source)
XLA Modules:
  0.0 80.5 jit_solution(17718435728250402097)
XLA Ops:
  0.0 2.8 %shard_map.136 = bf16[256,1280]{1,0:T(8,128)(2,1)} custom-call(bf16[128,8,128]{2,1,0:T(8,128)(2,1)} %energy_ref.1, s32[128,128]{1,0:T(8,128)} %bitcast.105, s32[1,128]{1,0:T(1,128)} %bitcast.106, s32[1,128]{1,0:T(1,128)} %count_ref.1, s32[1,128]{1,0:T(1,128)} %scene_ref.1, s32[1,128]{1,0:T(1,128)} %row_ref.1), custom_call_target="tpu_custom_call" | custom-call | tf_op jit(solution)/shard_map/pallas_call | solution.py:214
  2.8 7.6 %all-to-all-start = ((bf16[32,8,1280]{2,1,0:T(8,128)(2,1)}), bf16[32,8,1280]{2,1,0:T(8,128)(2,1)S(1)}, u32[]{:S(2)}, u32[]{:S(2)}) async-start(bf16[32,8,1280]{2,1,0:T(8,128)(2,1)} %bitcast.97), calls=%async_computation | async-start | bytes 1310720 | tf_op jit(solution)/shard_map/all_to_all | solution.py:249
  11.7 0.9 %copy.67 = f32[8,4,31,31]{3,2,1,0:T(8,128)} copy(f32[8,4,31,31]{3,2,0,1:T(8,128)S(1)} %bitcast.100) | data formatting | bytes 246016
  12.5 1.1 %pad.4.clone = f32[8,4,32,31]{3,2,1,0:T(8,128)S(1)} pad(f32[8,4,31,31]{3,2,1,0:T(8,128)} %copy.67, f32[]{:T(128)} %constant.89.clone.1), padding=0_0x0_0x0_1x0_0 | pad | bytes 249988 | tf_op jit(solution)/shard_map/jit(_pad)/pad | solution.py:117
  13.6 7.6 %all-to-all-done = bf16[32,8,1280]{2,1,0:T(8,128)(2,1)S(1)} async-done(((bf16[32,8,1280]{2,1,0:T(8,128)(2,1)}), bf16[32,8,1280]{2,1,0:T(8,128)(2,1)S(1)}, u32[]{:S(2)}, u32[]{:S(2)}) %all-to-all-start) | async-done | bytes 655392 | tf_op jit(solution)/shard_map/all_to_all | solution.py:249
  21.8 7.5 %fusion.4 = (bf16[256,8,4,128]{3,1,2,0:T(8,128)(2,1)S(1)}, bf16[256,8,4,128]{3,1,2,0:T(8,128)(2,1)S(1)}) fusion(s32[256,128]{1,0:T(8,128)S(1)} %get-tuple-element.8, pred[256,4,128]{2,1,0:T(4,128)(4,1)S(1)} %iota_compare_fusion.4, bf16[256,8,128]{2,1,0:T(8,128)(2,1)S(1)} %bitcast.102), kind=kOutput, calls=%fused_computation.7 | convolution fusion | flops 277872640 | bytes 4980736 | tf_op jit(solution)/shard_map/ibjh,ihc->ibjc/dot_general | solution.py:155
  29.3 0.8 fusion.13
  30.1 0.8 fusion.19
  30.9 4.9 %collective-permute-start.1 = (f32[8,4,15,128]{3,2,1,0:T(8,128)S(1)}, f32[8,4,15,128]{3,2,1,0:T(8,128)S(1)}, u32[]{:S(2)}, u32[]{:S(2)}) collective-permute-start(f32[8,4,15,128]{3,2,1,0:T(8,128)S(1)} %get-tuple-element.12), channel_id=1, source_target_pairs={{1,0},{2,1},{3,2},{4,3},{5,4},{6,5},{7,6},{8,7},{9,8},{10,9},{11,1... | collective-permute-start | bytes 737288 | tf_op jit(solution)/shard_map/ppermute | solution.py:29
  35.8 1.9 %collective-permute-start = (f32[8,4,15,128]{3,2,1,0:T(8,128)S(1)}, f32[8,4,15,128]{3,2,1,0:T(8,128)S(1)}, u32[]{:S(2)}, u32[]{:S(2)}) collective-permute-start(f32[8,4,15,128]{3,2,1,0:T(8,128)S(1)} %get-tuple-element.11), channel_id=1, source_target_pairs={{0,1},{1,2},{2,3},{3,4},{4,5},{5,6},{6,7},{7,8},{8,9},{9,10},{10,1... | collective-permute-start | bytes 737288 | tf_op jit(solution)/shard_map/ppermute | solution.py:27
  37.8 1.9 %fusion.83.kern_ref = f32[32,32,256]{2,1,0:T(8,128)} fusion(f32[32,32,31]{2,1,0:T(8,128)S(1)} %bitcast.99, f32[31,256,1]{1,0,2:T(8,128)S(1)} %copy-done.3), kind=kOutput, calls=%fused_computation.106 | convolution fusion | flops 97517568 | bytes 1207296 | tf_op jit(solution)/shard_map/dot_general | solution.py:118
  39.7 5.9 %collective-permute-done = f32[8,4,15,128]{3,2,1,0:T(8,128)S(1)} collective-permute-done((f32[8,4,15,128]{3,2,1,0:T(8,128)S(1)}, f32[8,4,15,128]{3,2,1,0:T(8,128)S(1)}, u32[]{:S(2)}, u32[]{:S(2)}) %collective-permute-start) | collective-permute-done | bytes 245792 | tf_op jit(solution)/shard_map/ppermute | solution.py:27
  45.7 2.5 %fusion.27.spec_ref = f32[32,46,256]{2,1,0:T(8,128)} fusion(f32[128,256,1]{1,0,2:T(8,128)S(1)} %copy-done.1, f32[32,15,128]{2,1,0:T(8,128)S(1)} %bitcast.103, f32[32,16,128]{2,1,0:T(8,128)S(1)} %bitcast.93, f32[32,15,128]{2,1,0:T(8,128)S(1)} %bitcast.104), kind=kOutput, calls=%fused_computation.30 | convolution fusion | flops 579190784 | bytes 2392064 | tf_op jit(solution)/shard_map/cyx,xf->cyf/dot_general | solution.py:130
  48.2 6.3 %shard_map.137 = f32[32,16,256]{2,1,0:T(8,128)} custom-call(f32[32,46,256]{2,1,0:T(8,128)} %fusion.27.spec_ref, f32[32,32,256]{2,1,0:T(8,128)} %fusion.83.kern_ref), custom_call_target="tpu_custom_call" | custom-call | tf_op jit(solution)/shard_map/pallas_call | solution.py:99
  54.5 1.9 %convolution_bitcast_fusion = f32[4,3,16,256]{3,1,2,0:T(4,128)S(1)} fusion(f32[8,4,16,256]{3,2,1,0:T(8,128)} %bitcast.101, f32[32,3]{0,1:T(4,128)S(1)} %copy-done.4, s32[]{:T(128)S(6)} %select_n.64), kind=kOutput, calls=%fused_computation.23 | convolution fusion | flops 4718592 | bytes 721284 | tf_op jit(solution)/shard_map/bsyf,bc->scyf/dot_general | solution.py:135
  56.7 4.1 %collective-permute-start.4 = (f32[3,16,128]{2,1,0:T(8,128)S(1)}, f32[3,16,128]{2,1,0:T(8,128)S(1)}, u32[]{:S(2)}, u32[]{:S(2)}) collective-permute-start(f32[3,16,128]{2,1,0:T(8,128)S(1)} %get-tuple-element.14), channel_id=1, source_target_pairs={{0,96},{32,0},{64,32},{96,64},{1,97},{33,1},{65,33},{97,65},{2,98}... | collective-permute-start | bytes 73736 | tf_op jit(solution)/shard_map/ppermute | solution.py:258
  60.9 1.3 %collective-permute-start.2 = (f32[3,16,128]{2,1,0:T(8,128)S(1)}, f32[3,16,128]{2,1,0:T(8,128)S(1)}, u32[]{:S(2)}, u32[]{:S(2)}) collective-permute-start(f32[3,16,128]{2,1,0:T(8,128)S(1)} %get-tuple-element.13), channel_id=1, source_target_pairs={{0,32},{32,64},{64,96},{96,0},{1,33},{33,65},{65,97},{97,1},{2,34}... | collective-permute-start | bytes 73736 | tf_op jit(solution)/shard_map/ppermute | solution.py:258
  62.4 3.8 %collective-permute-done.3 = f32[3,16,128]{2,1,0:T(8,128)S(1)} collective-permute-done((f32[3,16,128]{2,1,0:T(8,128)S(1)}, f32[3,16,128]{2,1,0:T(8,128)S(1)}, u32[]{:S(2)}, u32[]{:S(2)}) %collective-permute-start.3) | collective-permute-done | bytes 24608 | tf_op jit(solution)/shard_map/ppermute | solution.py:258
  66.2 1.9 %collective-permute-start.6 = (bf16[1,3,2,128]{3,2,1,0:T(2,128)(2,1)S(1)}, bf16[1,3,2,128]{3,2,1,0:T(2,128)(2,1)S(1)}, u32[]{:S(2)}, u32[]{:S(2)}) collective-permute-start(bf16[1,3,2,128]{3,2,1,0:T(2,128)(2,1)S(1)} %get-tuple-element.17), channel_id=1, source_target_pairs={{1,0},{2,1},{3,2},{4,3},{5,4},{6,5},{7,6},{8,7},{9,8},{10,9},{11,1... | collective-permute-start | bytes 4616 | tf_op jit(solution)/shard_map/ppermute | solution.py:29
  68.1 2.6 %collective-permute-start.5 = (bf16[1,3,2,128]{3,2,1,0:T(2,128)(2,1)S(1)}, bf16[1,3,2,128]{3,2,1,0:T(2,128)(2,1)S(1)}, u32[]{:S(2)}, u32[]{:S(2)}) collective-permute-start(bf16[1,3,2,128]{3,2,1,0:T(2,128)(2,1)S(1)} %get-tuple-element.16), channel_id=1, source_target_pairs={{0,1},{1,2},{2,3},{3,4},{4,5},{5,6},{6,7},{7,8},{8,9},{9,10},{10,1... | collective-permute-start | bytes 4616 | tf_op jit(solution)/shard_map/ppermute | solution.py:27
  70.8 4.4 %collective-permute-done.5 = bf16[1,3,2,128]{3,2,1,0:T(2,128)(2,1)S(1)} collective-permute-done((bf16[1,3,2,128]{3,2,1,0:T(2,128)(2,1)S(1)}, bf16[1,3,2,128]{3,2,1,0:T(2,128)(2,1)S(1)}, u32[]{:S(2)}, u32[]{:S(2)}) %collective-permute-start.5) | collective-permute-done | bytes 1568 | tf_op jit(solution)/shard_map/ppermute | solution.py:27
  76.1 1.4 %fusion.26 = bf16[18,1,8,17,64]{4,2,3,0,1:T(8,128)(2,1)S(1)} fusion(pred[18]{0:T(512)(128)(4,1)S(1)} %and_or_fusion, pred[8,17]{0,1:T(8,128)(4,1)S(1)} %copy-done.8, bf16[3,20,1,7,2]{3,0,4,1,2:T(4,128)(2,1)S(1)} %slice.46, bf16[3,20,1,8,17]{3,0,4,1,2:T(4,128)(2,1)S(1)} %copy.58, bf16[64,3,3,3]{0,3,2,1:T(4,128)(2,1)S(1)} %copy-done.6), kind=kOutput, calls=%fused_computation.29 | convolution fusion | flops 9925056 | bytes 334954 | tf_op jit(solution)/shard_map/conv_general_dilated | solution.py:37
  77.6 1.5 %convolution_convert_fusion = bf16[16,8,17,64]{3,1,2,0:T(8,128)(2,1)S(1)} fusion(bf16[64,64,3,3]{1,0,3,2:T(8,128)(2,1)S(1)} %copy-done.5, bf16[18,1,7,1,64]{4,2,3,0,1:T(8,128)(2,1)S(1)} %get-tuple-element.10, bf16[18,1,7,1,64]{4,2,3,0,1:T(8,128)(2,1)S(1)} %get-tuple-element.9, bf16[18,1,8,17,64]{4,2,3,0,1:T(8,128)(2,1)S(1)} %fusion.26), kind=kOutput, calls=%fused_computation.19 | convolution fusion | flops 162322432 | bytes 697856 | tf_op jit(solution)/shard_map/conv_general_dilated | solution.py:37
  79.2 1.3 %copy.61 = bf16[1,64,16,128]{3,2,1,0:T(8,128)(2,1)} copy(bf16[1,64,16,128]{1,2,3,0:T(8,128)(2,1)S(1)} %slice_bitcast_fusion) | data formatting | bytes 524288 | tf_op jit(solution)/shard_map/convert_element_type | solution.py:272
  (49 shorter events, 3.4 us)
Async XLA Ops:
  0.0 10.5 %copy-start = (f32[64,8,961]{2,1,0:T(8,128)S(1)}, f32[64,8,961]{2,1,0:T(8,128)}, u32[]{:S(2)}) copy-start(f32[64,8,961]{2,1,0:T(8,128)} %param.20) | copy-start | bytes 5904388
  0.0 10.4 %copy-start.7 = (s32[1,4,1]{1,2,0:T(1,128)S(1)}, s32[1,4,1]{1,2,0:T(1,128)}, u32[]{:S(2)}) copy-start(s32[1,4,1]{1,2,0:T(1,128)} %param.21) | copy-start | bytes 52
  2.8 18.4 %all-to-all-start = ((bf16[32,8,1280]{2,1,0:T(8,128)(2,1)}), bf16[32,8,1280]{2,1,0:T(8,128)(2,1)S(1)}, u32[]{:S(2)}, u32[]{:S(2)}) async-start(bf16[32,8,1280]{2,1,0:T(8,128)(2,1)} %bitcast.97), calls=%async_computation | async-start | bytes 1310720 | tf_op jit(solution)/shard_map/all_to_all | solution.py:249
  30.1 7.7 %copy-start.3 = (f32[31,256,1]{1,0,2:T(8,128)S(1)}, f32[31,256,1]{1,0,2:T(8,128)}, u32[]{:S(2)}) copy-start(f32[31,256,1]{1,0,2:T(8,128)} %constant.112) | copy-start | bytes 95236
  30.1 15.6 %copy-start.1 = (f32[128,256,1]{1,0,2:T(8,128)S(1)}, f32[128,256,1]{1,0,2:T(8,128)}, u32[]{:S(2)}) copy-start(f32[128,256,1]{1,0,2:T(8,128)} %constant.111) | copy-start | bytes 393220
  30.9 8.8 %collective-permute-start.1 = (f32[8,4,15,128]{3,2,1,0:T(8,128)S(1)}, f32[8,4,15,128]{3,2,1,0:T(8,128)S(1)}, u32[]{:S(2)}, u32[]{:S(2)}) collective-permute-start(f32[8,4,15,128]{3,2,1,0:T(8,128)S(1)} %get-tuple-element.12), channel_id=1, source_target_pairs={{1,0},{2,1},{3,2},{4,3},{5,4},{6,5},{7,6},{8,7},{9,8},{10,9},{11,1... | collective-permute-start | bytes 737288 | tf_op jit(solution)/shard_map/ppermute | solution.py:29
  35.8 9.8 %collective-permute-start = (f32[8,4,15,128]{3,2,1,0:T(8,128)S(1)}, f32[8,4,15,128]{3,2,1,0:T(8,128)S(1)}, u32[]{:S(2)}, u32[]{:S(2)}) collective-permute-start(f32[8,4,15,128]{3,2,1,0:T(8,128)S(1)} %get-tuple-element.11), channel_id=1, source_target_pairs={{0,1},{1,2},{2,3},{3,4},{4,5},{5,6},{6,7},{7,8},{8,9},{9,10},{10,1... | collective-permute-start | bytes 737288 | tf_op jit(solution)/shard_map/ppermute | solution.py:27
  48.2 6.3 %copy-start.4 = (f32[32,3]{0,1:T(4,128)S(1)}, f32[32,3]{0,1:T(4,128)}, u32[]{:S(2)}) copy-start(f32[32,3]{0,1:T(4,128)} %param.22) | copy-start | bytes 1156
  48.2 8.2 %copy-start.2 = (f32[256,128,1,1]{1,0,3,2:T(8,128)S(1)}, f32[256,128,1,1]{1,0,3,2:T(8,128)}, u32[]{:S(2)}) copy-start(f32[256,128,1,1]{1,0,3,2:T(8,128)} %constant.113) | copy-start | bytes 393220
  48.2 27.9 %copy-start.6 = (bf16[64,3,3,3]{0,3,2,1:T(4,128)(2,1)S(1)}, bf16[64,3,3,3]{0,3,2,1:T(4,128)(2,1)}, u32[]{:S(2)}) copy-start(bf16[64,3,3,3]{0,3,2,1:T(4,128)(2,1)} %param.23) | copy-start | bytes 10372
  48.2 27.9 %copy-start.8 = (pred[8,17]{0,1:T(8,128)(4,1)S(1)}, pred[8,17]{0,1:T(8,128)(4,1)}, u32[]{:S(2)}) copy-start(pred[8,17]{0,1:T(8,128)(4,1)} %constant.109) | copy-start | bytes 412
  56.7 5.6 %collective-permute-start.4 = (f32[3,16,128]{2,1,0:T(8,128)S(1)}, f32[3,16,128]{2,1,0:T(8,128)S(1)}, u32[]{:S(2)}, u32[]{:S(2)}) collective-permute-start(f32[3,16,128]{2,1,0:T(8,128)S(1)} %get-tuple-element.14), channel_id=1, source_target_pairs={{0,96},{32,0},{64,32},{96,64},{1,97},{33,1},{65,33},{97,65},{2,98}... | collective-permute-start | bytes 73736 | tf_op jit(solution)/shard_map/ppermute | solution.py:258
  60.9 5.3 %collective-permute-start.3 = (f32[3,16,128]{2,1,0:T(8,128)S(1)}, f32[3,16,128]{2,1,0:T(8,128)S(1)}, u32[]{:S(2)}, u32[]{:S(2)}) collective-permute-start(f32[3,16,128]{2,1,0:T(8,128)S(1)} %get-tuple-element.15), channel_id=1, source_target_pairs={{0,64},{32,96},{64,0},{96,32},{1,65},{33,97},{65,1},{97,33},{2,66}... | collective-permute-start | bytes 73736 | tf_op jit(solution)/shard_map/ppermute | solution.py:258
  60.9 5.3 %collective-permute-start.2 = (f32[3,16,128]{2,1,0:T(8,128)S(1)}, f32[3,16,128]{2,1,0:T(8,128)S(1)}, u32[]{:S(2)}, u32[]{:S(2)}) collective-permute-start(f32[3,16,128]{2,1,0:T(8,128)S(1)} %get-tuple-element.13), channel_id=1, source_target_pairs={{0,32},{32,64},{64,96},{96,0},{1,33},{33,65},{65,97},{97,1},{2,34}... | collective-permute-start | bytes 73736 | tf_op jit(solution)/shard_map/ppermute | solution.py:258
  66.2 4.5 %collective-permute-start.6 = (bf16[1,3,2,128]{3,2,1,0:T(2,128)(2,1)S(1)}, bf16[1,3,2,128]{3,2,1,0:T(2,128)(2,1)S(1)}, u32[]{:S(2)}, u32[]{:S(2)}) collective-permute-start(bf16[1,3,2,128]{3,2,1,0:T(2,128)(2,1)S(1)} %get-tuple-element.17), channel_id=1, source_target_pairs={{1,0},{2,1},{3,2},{4,3},{5,4},{6,5},{7,6},{8,7},{9,8},{10,9},{11,1... | collective-permute-start | bytes 4616 | tf_op jit(solution)/shard_map/ppermute | solution.py:29
  68.1 7.0 %collective-permute-start.5 = (bf16[1,3,2,128]{3,2,1,0:T(2,128)(2,1)S(1)}, bf16[1,3,2,128]{3,2,1,0:T(2,128)(2,1)S(1)}, u32[]{:S(2)}, u32[]{:S(2)}) collective-permute-start(bf16[1,3,2,128]{3,2,1,0:T(2,128)(2,1)S(1)} %get-tuple-element.16), channel_id=1, source_target_pairs={{0,1},{1,2},{2,3},{3,4},{4,5},{5,6},{6,7},{7,8},{8,9},{9,10},{10,1... | collective-permute-start | bytes 4616 | tf_op jit(solution)/shard_map/ppermute | solution.py:27
  76.1 1.5 %copy-start.5 = (bf16[64,64,3,3]{1,0,3,2:T(8,128)(2,1)S(1)}, bf16[64,64,3,3]{1,0,3,2:T(8,128)(2,1)}, u32[]{:S(2)}) copy-start(bf16[64,64,3,3]{1,0,3,2:T(8,128)(2,1)} %param.24) | copy-start | bytes 221188

commit v11 on v10

--- a/solution.py
+++ b/solution.py
@@ -247,6 +247,7 @@
     )
     kern = kernel_spectra(psf_bank, psf_index, K // 2)
     got = lax.all_to_all(send, "tile", split_axis=0, concat_axis=0, tiled=True)
+    got, kern = lax.optimization_barrier((got, kern))
     splat = window_splat(got, band_dev, hit_lanes, scenes)
     extended = padded_2(splat, (("tile", 2),), K // 2)
     wave_index = lax.axis_index("wave")

time: 80.9 us -> 79.5 us (0.983)
  the two profiles are of different devices: /device:TPU:2 before, /device:TPU:27 now
where the time goes in v11:
time: 79.5 us; the launch traced here: 79 us
  starting transfers between devices  23.7 us (30%)
  waiting for transfers between devices  23 us (29%)
  matrix products  18.6 us (23%)
  Pallas kernels  9.08 us (11%)
  local copies, waits for them, and re-layouts  3.89 us (5%)
    ppermute x2, waiting for transfers between devices, padded_2(): lax.ppermute(head, axis, [((i + 1) % count, i) for i in range(ends)])  11.4 us
    all_to_all x1, starting transfers between devices, per_device(): got = lax.all_to_all(send, 'tile', split_axis=0, concat_axis=0, tiled=True)  7.69 us
    dot_general x1, matrix products, window_splat(): jnp.einsum('ibjh,ihc->ibjc', spread, onehot, preferred_element_type=jnp.f...  7.5 us
    all_to_all x1, waiting for transfers between devices, per_device(): got = lax.all_to_all(send, 'tile', split_axis=0, concat_axis=0, tiled=True)  7.32 us
    ppermute x2, starting transfers between devices, padded_2(): lax.ppermute(tail, axis, [(i, (i + 1) % count) for i in range(ends)])  6.9 us
    pallas_call x1, Pallas kernels, row_taps(): pl.pallas_call(row_taps_kernel, out_shape=jax.ShapeDtypeStruct((channels,...  6.3 us
    ppermute x3, starting transfers between devices, per_device(): lax.ppermute(piece, 'wave', [(i, (i + step) % wave_count) for i in range(...  5.13 us
    ppermute x2, starting transfers between devices, padded_2(): lax.ppermute(head, axis, [((i + 1) % count, i) for i in range(ends)])  4.02 us
  transfers between devices with their start and end apart: 8, of which 5 were waited for; matrix products, arithmetic and copies ran while one was open for 4% of the time, Pallas kernels for 0%

profile of v11, /device:TPU:27, one launch (start us, length us, event | category | flops | bytes accessed | tf_op | source)
XLA Modules:
  0.0 79.0 jit_solution(8467767785511279436)
XLA Ops:
  0.0 2.8 %shard_map.136 = bf16[256,1280]{1,0:T(8,128)(2,1)} custom-call(bf16[128,8,128]{2,1,0:T(8,128)(2,1)} %energy_ref.1, s32[128,128]{1,0:T(8,128)} %bitcast.105, s32[1,128]{1,0:T(1,128)} %bitcast.106, s32[1,128]{1,0:T(1,128)} %count_ref.1, s32[1,128]{1,0:T(1,128)} %scene_ref.1, s32[1,128]{1,0:T(1,128)} %row_ref.1), custom_call_target="tpu_custom_call" | custom-call | tf_op jit(solution)/shard_map/pallas_call | solution.py:214
  2.8 7.7 %all-to-all-start = ((bf16[32,8,1280]{2,1,0:T(8,128)(2,1)}), bf16[32,8,1280]{2,1,0:T(8,128)(2,1)S(1)}, u32[]{:S(2)}, u32[]{:S(2)}) async-start(bf16[32,8,1280]{2,1,0:T(8,128)(2,1)} %bitcast.97), calls=%async_computation | async-start | bytes 1310720 | tf_op jit(solution)/shard_map/all_to_all | solution.py:249
  11.8 1.9 %fusion.83.kern_ref = f32[32,32,256]{2,1,0:T(8,128)} fusion(f32[32,32,31]{2,1,0:T(8,128)S(1)} %bitcast.99, f32[31,256,1]{1,0,2:T(8,128)S(1)} %copy-done.3), kind=kOutput, calls=%fused_computation.106 | convolution fusion | flops 97517568 | bytes 1207296 | tf_op jit(solution)/shard_map/dot_general | solution.py:118
  13.7 7.3 %all-to-all-done = bf16[32,8,1280]{2,1,0:T(8,128)(2,1)S(1)} async-done(((bf16[32,8,1280]{2,1,0:T(8,128)(2,1)}), bf16[32,8,1280]{2,1,0:T(8,128)(2,1)S(1)}, u32[]{:S(2)}, u32[]{:S(2)}) %all-to-all-start) | async-done | bytes 655392 | tf_op jit(solution)/shard_map/all_to_all | solution.py:249
  21.6 7.5 %fusion.4 = (bf16[256,8,4,128]{3,1,2,0:T(8,128)(2,1)S(1)}, bf16[256,8,4,128]{3,1,2,0:T(8,128)(2,1)S(1)}) fusion(s32[256,128]{1,0:T(8,128)S(1)} %get-tuple-element.12, pred[256,4,128]{2,1,0:T(4,128)(4,1)S(1)} %iota_compare_fusion.4, bf16[256,8,128]{2,1,0:T(8,128)(2,1)S(1)} %bitcast.102), kind=kOutput, calls=%fused_computation.7 | convolution fusion | flops 277872640 | bytes 4980736 | tf_op jit(solution)/shard_map/ibjh,ihc->ibjc/dot_general | solution.py:155
  29.1 0.8 fusion.13
  29.9 0.8 fusion.19
  30.8 3.7 %collective-permute-start = (f32[8,4,15,128]{3,2,1,0:T(8,128)S(1)}, f32[8,4,15,128]{3,2,1,0:T(8,128)S(1)}, u32[]{:S(2)}, u32[]{:S(2)}) collective-permute-start(f32[8,4,15,128]{3,2,1,0:T(8,128)S(1)} %get-tuple-element.15), channel_id=1, source_target_pairs={{0,1},{1,2},{2,3},{3,4},{4,5},{5,6},{6,7},{7,8},{8,9},{9,10},{10,1... | collective-permute-start | bytes 737288 | tf_op jit(solution)/shard_map/ppermute | solution.py:27
  34.5 1.9 %collective-permute-start.1 = (f32[8,4,15,128]{3,2,1,0:T(8,128)S(1)}, f32[8,4,15,128]{3,2,1,0:T(8,128)S(1)}, u32[]{:S(2)}, u32[]{:S(2)}) collective-permute-start(f32[8,4,15,128]{3,2,1,0:T(8,128)S(1)} %get-tuple-element.16), channel_id=1, source_target_pairs={{1,0},{2,1},{3,2},{4,3},{5,4},{6,5},{7,6},{8,7},{9,8},{10,9},{11,1... | collective-permute-start | bytes 737288 | tf_op jit(solution)/shard_map/ppermute | solution.py:29
  36.5 1.3 %collective-permute-done = f32[8,4,15,128]{3,2,1,0:T(8,128)S(1)} collective-permute-done((f32[8,4,15,128]{3,2,1,0:T(8,128)S(1)}, f32[8,4,15,128]{3,2,1,0:T(8,128)S(1)}, u32[]{:S(2)}, u32[]{:S(2)}) %collective-permute-start) | collective-permute-done | bytes 245792 | tf_op jit(solution)/shard_map/ppermute | solution.py:27
  37.8 6.5 %collective-permute-done.1 = f32[8,4,15,128]{3,2,1,0:T(8,128)S(1)} collective-permute-done((f32[8,4,15,128]{3,2,1,0:T(8,128)S(1)}, f32[8,4,15,128]{3,2,1,0:T(8,128)S(1)}, u32[]{:S(2)}, u32[]{:S(2)}) %collective-permute-start.1) | collective-permute-done | bytes 245792 | tf_op jit(solution)/shard_map/ppermute | solution.py:29
  44.3 2.5 %fusion.27.spec_ref = f32[32,46,256]{2,1,0:T(8,128)} fusion(f32[128,256,1]{1,0,2:T(8,128)S(1)} %copy-done.1, f32[32,15,128]{2,1,0:T(8,128)S(1)} %bitcast.104, f32[32,16,128]{2,1,0:T(8,128)S(1)} %bitcast.93, f32[32,15,128]{2,1,0:T(8,128)S(1)} %bitcast.103), kind=kOutput, calls=%fused_computation.30 | convolution fusion | flops 579190784 | bytes 2392064 | tf_op jit(solution)/shard_map/cyx,xf->cyf/dot_general | solution.py:130
  46.8 6.3 %shard_map.137 = f32[32,16,256]{2,1,0:T(8,128)} custom-call(f32[32,46,256]{2,1,0:T(8,128)} %fusion.27.spec_ref, f32[32,32,256]{2,1,0:T(8,128)} %fusion.83.kern_ref), custom_call_target="tpu_custom_call" | custom-call | tf_op jit(solution)/shard_map/pallas_call | solution.py:99
  53.2 1.9 %convolution_bitcast_fusion = f32[4,3,16,256]{3,1,2,0:T(4,128)S(1)} fusion(f32[8,4,16,256]{3,2,1,0:T(8,128)} %bitcast.101, f32[32,3]{0,1:T(4,128)S(1)} %copy-done.4, s32[]{:T(128)S(6)} %select_n.64), kind=kOutput, calls=%fused_computation.23 | convolution fusion | flops 4718592 | bytes 721284 | tf_op jit(solution)/shard_map/bsyf,bc->scyf/dot_general | solution.py:135
  55.4 1.7 %collective-permute-start.2 = (f32[3,16,128]{2,1,0:T(8,128)S(1)}, f32[3,16,128]{2,1,0:T(8,128)S(1)}, u32[]{:S(2)}, u32[]{:S(2)}) collective-permute-start(f32[3,16,128]{2,1,0:T(8,128)S(1)} %get-tuple-element.17), channel_id=1, source_target_pairs={{0,32},{32,64},{64,96},{96,0},{1,33},{33,65},{65,97},{97,1},{2,34}... | collective-permute-start | bytes 73736 | tf_op jit(solution)/shard_map/ppermute | solution.py:259
  57.1 2.2 %collective-permute-start.4 = (f32[3,16,128]{2,1,0:T(8,128)S(1)}, f32[3,16,128]{2,1,0:T(8,128)S(1)}, u32[]{:S(2)}, u32[]{:S(2)}) collective-permute-start(f32[3,16,128]{2,1,0:T(8,128)S(1)} %get-tuple-element.18), channel_id=1, source_target_pairs={{0,96},{32,0},{64,32},{96,64},{1,97},{33,1},{65,33},{97,65},{2,98}... | collective-permute-start | bytes 73736 | tf_op jit(solution)/shard_map/ppermute | solution.py:259
  59.3 1.2 %collective-permute-start.3 = (f32[3,16,128]{2,1,0:T(8,128)S(1)}, f32[3,16,128]{2,1,0:T(8,128)S(1)}, u32[]{:S(2)}, u32[]{:S(2)}) collective-permute-start(f32[3,16,128]{2,1,0:T(8,128)S(1)} %get-tuple-element.19), channel_id=1, source_target_pairs={{0,64},{32,96},{64,0},{96,32},{1,65},{33,97},{65,1},{97,33},{2,66}... | collective-permute-start | bytes 73736 | tf_op jit(solution)/shard_map/ppermute | solution.py:259
  60.5 3.0 %collective-permute-done.3 = f32[3,16,128]{2,1,0:T(8,128)S(1)} collective-permute-done((f32[3,16,128]{2,1,0:T(8,128)S(1)}, f32[3,16,128]{2,1,0:T(8,128)S(1)}, u32[]{:S(2)}, u32[]{:S(2)}) %collective-permute-start.3) | collective-permute-done | bytes 24608 | tf_op jit(solution)/shard_map/ppermute | solution.py:259
  63.5 3.2 %collective-permute-start.5 = (bf16[1,3,2,128]{3,2,1,0:T(2,128)(2,1)S(1)}, bf16[1,3,2,128]{3,2,1,0:T(2,128)(2,1)S(1)}, u32[]{:S(2)}, u32[]{:S(2)}) collective-permute-start(bf16[1,3,2,128]{3,2,1,0:T(2,128)(2,1)S(1)} %get-tuple-element.20), channel_id=1, source_target_pairs={{0,1},{1,2},{2,3},{3,4},{4,5},{5,6},{6,7},{7,8},{8,9},{9,10},{10,1... | collective-permute-start | bytes 4616 | tf_op jit(solution)/shard_map/ppermute | solution.py:27
  66.7 2.1 %collective-permute-start.6 = (bf16[1,3,2,128]{3,2,1,0:T(2,128)(2,1)S(1)}, bf16[1,3,2,128]{3,2,1,0:T(2,128)(2,1)S(1)}, u32[]{:S(2)}, u32[]{:S(2)}) collective-permute-start(bf16[1,3,2,128]{3,2,1,0:T(2,128)(2,1)S(1)} %get-tuple-element.21), channel_id=1, source_target_pairs={{1,0},{2,1},{3,2},{4,3},{5,4},{6,5},{7,6},{8,7},{9,8},{10,9},{11,1... | collective-permute-start | bytes 4616 | tf_op jit(solution)/shard_map/ppermute | solution.py:29
  68.8 4.9 %collective-permute-done.6 = bf16[1,3,2,128]{3,2,1,0:T(2,128)(2,1)S(1)} collective-permute-done((bf16[1,3,2,128]{3,2,1,0:T(2,128)(2,1)S(1)}, bf16[1,3,2,128]{3,2,1,0:T(2,128)(2,1)S(1)}, u32[]{:S(2)}, u32[]{:S(2)}) %collective-permute-start.6) | collective-permute-done | bytes 1568 | tf_op jit(solution)/shard_map/ppermute | solution.py:29
  74.7 1.4 %fusion.26 = bf16[18,1,8,17,64]{4,2,3,0,1:T(8,128)(2,1)S(1)} fusion(pred[18]{0:T(512)(128)(4,1)S(1)} %and_or_fusion, pred[8,17]{0,1:T(8,128)(4,1)S(1)} %copy-done.8, bf16[3,20,1,7,2]{3,0,4,1,2:T(4,128)(2,1)S(1)} %slice.43, bf16[3,20,1,8,17]{3,0,4,1,2:T(4,128)(2,1)S(1)} %copy.58, bf16[64,3,3,3]{0,3,2,1:T(4,128)(2,1)S(1)} %copy-done.6), kind=kOutput, calls=%fused_computation.29 | convolution fusion | flops 9925056 | bytes 334954 | tf_op jit(solution)/shard_map/conv_general_dilated | solution.py:37
  76.1 1.5 %convolution_convert_fusion = bf16[16,8,17,64]{3,1,2,0:T(8,128)(2,1)S(1)} fusion(bf16[64,64,3,3]{1,0,3,2:T(8,128)(2,1)S(1)} %copy-done.5, bf16[18,1,7,1,64]{4,2,3,0,1:T(8,128)(2,1)S(1)} %get-tuple-element.14, bf16[18,1,7,1,64]{4,2,3,0,1:T(8,128)(2,1)S(1)} %get-tuple-element.13, bf16[18,1,8,17,64]{4,2,3,0,1:T(8,128)(2,1)S(1)} %fusion.26), kind=kOutput, calls=%fused_computation.19 | convolution fusion | flops 162322432 | bytes 697856 | tf_op jit(solution)/shard_map/conv_general_dilated | solution.py:37
  77.7 1.3 %copy.61 = bf16[1,64,16,128]{3,2,1,0:T(8,128)(2,1)} copy(bf16[1,64,16,128]{1,2,3,0:T(8,128)(2,1)S(1)} %slice_bitcast_fusion) | data formatting | bytes 524288 | tf_op jit(solution)/shard_map/convert_element_type | solution.py:273
  (49 shorter events, 3.3 us)
Async XLA Ops:
  0.0 10.5 %copy-start = (f32[64,8,961]{2,1,0:T(8,128)S(1)}, f32[64,8,961]{2,1,0:T(8,128)}, u32[]{:S(2)}) copy-start(f32[64,8,961]{2,1,0:T(8,128)} %param.20) | copy-start | bytes 5904388
  0.0 10.5 %copy-start.7 = (s32[1,4,1]{1,2,0:T(1,128)S(1)}, s32[1,4,1]{1,2,0:T(1,128)}, u32[]{:S(2)}) copy-start(s32[1,4,1]{1,2,0:T(1,128)} %param.21) | copy-start | bytes 52
  2.8 9.0 %copy-start.3 = (f32[31,256,1]{1,0,2:T(8,128)S(1)}, f32[31,256,1]{1,0,2:T(8,128)}, u32[]{:S(2)}) copy-start(f32[31,256,1]{1,0,2:T(8,128)} %constant.111) | copy-start | bytes 95236
  2.8 18.3 %all-to-all-start = ((bf16[32,8,1280]{2,1,0:T(8,128)(2,1)}), bf16[32,8,1280]{2,1,0:T(8,128)(2,1)S(1)}, u32[]{:S(2)}, u32[]{:S(2)}) async-start(bf16[32,8,1280]{2,1,0:T(8,128)(2,1)} %bitcast.97), calls=%async_computation | async-start | bytes 1310720 | tf_op jit(solution)/shard_map/all_to_all | solution.py:249
  29.9 14.4 %copy-start.1 = (f32[128,256,1]{1,0,2:T(8,128)S(1)}, f32[128,256,1]{1,0,2:T(8,128)}, u32[]{:S(2)}) copy-start(f32[128,256,1]{1,0,2:T(8,128)} %constant.112) | copy-start | bytes 393220
  30.8 7.0 %collective-permute-start = (f32[8,4,15,128]{3,2,1,0:T(8,128)S(1)}, f32[8,4,15,128]{3,2,1,0:T(8,128)S(1)}, u32[]{:S(2)}, u32[]{:S(2)}) collective-permute-start(f32[8,4,15,128]{3,2,1,0:T(8,128)S(1)} %get-tuple-element.15), channel_id=1, source_target_pairs={{0,1},{1,2},{2,3},{3,4},{4,5},{5,6},{6,7},{7,8},{8,9},{9,10},{10,1... | collective-permute-start | bytes 737288 | tf_op jit(solution)/shard_map/ppermute | solution.py:27
  34.5 9.8 %collective-permute-start.1 = (f32[8,4,15,128]{3,2,1,0:T(8,128)S(1)}, f32[8,4,15,128]{3,2,1,0:T(8,128)S(1)}, u32[]{:S(2)}, u32[]{:S(2)}) collective-permute-start(f32[8,4,15,128]{3,2,1,0:T(8,128)S(1)} %get-tuple-element.16), channel_id=1, source_target_pairs={{1,0},{2,1},{3,2},{4,3},{5,4},{6,5},{7,6},{8,7},{9,8},{10,9},{11,1... | collective-permute-start | bytes 737288 | tf_op jit(solution)/shard_map/ppermute | solution.py:29
  46.8 6.3 %copy-start.4 = (f32[32,3]{0,1:T(4,128)S(1)}, f32[32,3]{0,1:T(4,128)}, u32[]{:S(2)}) copy-start(f32[32,3]{0,1:T(4,128)} %param.22) | copy-start | bytes 1156
  46.8 8.2 %copy-start.2 = (f32[256,128,1,1]{1,0,3,2:T(8,128)S(1)}, f32[256,128,1,1]{1,0,3,2:T(8,128)}, u32[]{:S(2)}) copy-start(f32[256,128,1,1]{1,0,3,2:T(8,128)} %constant.113) | copy-start | bytes 393220
  46.8 27.8 %copy-start.6 = (bf16[64,3,3,3]{0,3,2,1:T(4,128)(2,1)S(1)}, bf16[64,3,3,3]{0,3,2,1:T(4,128)(2,1)}, u32[]{:S(2)}) copy-start(bf16[64,3,3,3]{0,3,2,1:T(4,128)(2,1)} %param.23) | copy-start | bytes 10372
  46.8 27.8 %copy-start.8 = (pred[8,17]{0,1:T(8,128)(4,1)S(1)}, pred[8,17]{0,1:T(8,128)(4,1)}, u32[]{:S(2)}) copy-start(pred[8,17]{0,1:T(8,128)(4,1)} %constant.109) | copy-start | bytes 412
  55.4 5.1 %collective-permute-start.2 = (f32[3,16,128]{2,1,0:T(8,128)S(1)}, f32[3,16,128]{2,1,0:T(8,128)S(1)}, u32[]{:S(2)}, u32[]{:S(2)}) collective-permute-start(f32[3,16,128]{2,1,0:T(8,128)S(1)} %get-tuple-element.17), channel_id=1, source_target_pairs={{0,32},{32,64},{64,96},{96,0},{1,33},{33,65},{65,97},{97,1},{2,34}... | collective-permute-start | bytes 73736 | tf_op jit(solution)/shard_map/ppermute | solution.py:259
  57.1 3.4 %collective-permute-start.4 = (f32[3,16,128]{2,1,0:T(8,128)S(1)}, f32[3,16,128]{2,1,0:T(8,128)S(1)}, u32[]{:S(2)}, u32[]{:S(2)}) collective-permute-start(f32[3,16,128]{2,1,0:T(8,128)S(1)} %get-tuple-element.18), channel_id=1, source_target_pairs={{0,96},{32,0},{64,32},{96,64},{1,97},{33,1},{65,33},{97,65},{2,98}... | collective-permute-start | bytes 73736 | tf_op jit(solution)/shard_map/ppermute | solution.py:259
  59.3 4.2 %collective-permute-start.3 = (f32[3,16,128]{2,1,0:T(8,128)S(1)}, f32[3,16,128]{2,1,0:T(8,128)S(1)}, u32[]{:S(2)}, u32[]{:S(2)}) collective-permute-start(f32[3,16,128]{2,1,0:T(8,128)S(1)} %get-tuple-element.19), channel_id=1, source_target_pairs={{0,64},{32,96},{64,0},{96,32},{1,65},{33,97},{65,1},{97,33},{2,66}... | collective-permute-start | bytes 73736 | tf_op jit(solution)/shard_map/ppermute | solution.py:259
  63.5 5.3 %collective-permute-start.5 = (bf16[1,3,2,128]{3,2,1,0:T(2,128)(2,1)S(1)}, bf16[1,3,2,128]{3,2,1,0:T(2,128)(2,1)S(1)}, u32[]{:S(2)}, u32[]{:S(2)}) collective-permute-start(bf16[1,3,2,128]{3,2,1,0:T(2,128)(2,1)S(1)} %get-tuple-element.20), channel_id=1, source_target_pairs={{0,1},{1,2},{2,3},{3,4},{4,5},{5,6},{6,7},{7,8},{8,9},{9,10},{10,1... | collective-permute-start | bytes 4616 | tf_op jit(solution)/shard_map/ppermute | solution.py:27
  66.7 7.0 %collective-permute-start.6 = (bf16[1,3,2,128]{3,2,1,0:T(2,128)(2,1)S(1)}, bf16[1,3,2,128]{3,2,1,0:T(2,128)(2,1)S(1)}, u32[]{:S(2)}, u32[]{:S(2)}) collective-permute-start(bf16[1,3,2,128]{3,2,1,0:T(2,128)(2,1)S(1)} %get-tuple-element.21), channel_id=1, source_target_pairs={{1,0},{2,1},{3,2},{4,3},{5,4},{6,5},{7,6},{8,7},{9,8},{10,9},{11,1... | collective-permute-start | bytes 4616 | tf_op jit(solution)/shard_map/ppermute | solution.py:29
  74.7 1.5 %copy-start.5 = (bf16[64,64,3,3]{1,0,3,2:T(8,128)(2,1)S(1)}, bf16[64,64,3,3]{1,0,3,2:T(8,128)(2,1)}, u32[]{:S(2)}) copy-start(bf16[64,64,3,3]{1,0,3,2:T(8,128)(2,1)} %param.24) | copy-start | bytes 221188

commit v12 on v11

--- a/solution.py
+++ b/solution.py
@@ -126,7 +126,7 @@
     rows_dev = tall - 2 * radius
     side = 2 * radius + 1
     forward, unused, inverse = dft_tables(width, side, radius)
-    hi = lax.Precision.HIGHEST
+    hi = lax.Precision.HIGH
     spec = jnp.einsum(
         "cyx,xf->cyf", extended.reshape(band_dev * scenes, tall, width), forward, precision=hi
     )

time: 79.5 us -> 78.6 us (0.989)
  matrix products: 18.6 us -> 17.7 us
where the time goes in v12:
time: 78.6 us; the launch traced here: 78.1 us
  starting transfers between devices  23.6 us (30%)
  waiting for transfers between devices  23.2 us (30%)
  matrix products  17.7 us (23%)
  Pallas kernels  9.07 us (12%)
  local copies, waits for them, and re-layouts  3.89 us (5%)
    ppermute x2, waiting for transfers between devices, padded_2(): lax.ppermute(head, axis, [((i + 1) % count, i) for i in range(ends)])  11.6 us
    all_to_all x1, starting transfers between devices, per_device(): got = lax.all_to_all(send, 'tile', split_axis=0, concat_axis=0, tiled=True)  7.7 us
    dot_general x1, matrix products, window_splat(): jnp.einsum('ibjh,ihc->ibjc', spread, onehot, preferred_element_type=jnp.f...  7.5 us
    all_to_all x1, waiting for transfers between devices, per_device(): got = lax.all_to_all(send, 'tile', split_axis=0, concat_axis=0, tiled=True)  7.32 us
    ppermute x2, starting transfers between devices, padded_2(): lax.ppermute(tail, axis, [(i, (i + 1) % count) for i in range(ends)])  6.9 us
    pallas_call x1, Pallas kernels, row_taps(): pl.pallas_call(row_taps_kernel, out_shape=jax.ShapeDtypeStruct((channels,...  6.3 us
    ppermute x3, starting transfers between devices, per_device(): lax.ppermute(piece, 'wave', [(i, (i + step) % wave_count) for i in range(...  5.13 us
    ppermute x2, starting transfers between devices, padded_2(): lax.ppermute(head, axis, [((i + 1) % count, i) for i in range(ends)])  3.84 us
  transfers between devices with their start and end apart: 8, of which 5 were waited for; matrix products, arithmetic and copies ran while one was open for 4% of the time, Pallas kernels for 0%

profile of v12, /device:TPU:27, one launch (start us, length us, event | category | flops | bytes accessed | tf_op | source)
XLA Modules:
  0.0 78.1 jit_solution(17296346901408300580)
XLA Ops:
  0.0 2.8 %shard_map.136 = bf16[256,1280]{1,0:T(8,128)(2,1)} custom-call(bf16[128,8,128]{2,1,0:T(8,128)(2,1)} %energy_ref.1, s32[128,128]{1,0:T(8,128)} %bitcast.105, s32[1,128]{1,0:T(1,128)} %bitcast.106, s32[1,128]{1,0:T(1,128)} %count_ref.1, s32[1,128]{1,0:T(1,128)} %scene_ref.1, s32[1,128]{1,0:T(1,128)} %row_ref.1), custom_call_target="tpu_custom_call" | custom-call | tf_op jit(solution)/shard_map/pallas_call | solution.py:214
  2.8 7.7 %all-to-all-start = ((bf16[32,8,1280]{2,1,0:T(8,128)(2,1)}), bf16[32,8,1280]{2,1,0:T(8,128)(2,1)S(1)}, u32[]{:S(2)}, u32[]{:S(2)}) async-start(bf16[32,8,1280]{2,1,0:T(8,128)(2,1)} %bitcast.97), calls=%async_computation | async-start | bytes 1310720 | tf_op jit(solution)/shard_map/all_to_all | solution.py:249
  11.8 1.9 %fusion.83.kern_ref = f32[32,32,256]{2,1,0:T(8,128)} fusion(f32[32,32,31]{2,1,0:T(8,128)S(1)} %bitcast.99, f32[31,256,1]{1,0,2:T(8,128)S(1)} %copy-done.3), kind=kOutput, calls=%fused_computation.106 | convolution fusion | flops 97517568 | bytes 1207296 | tf_op jit(solution)/shard_map/dot_general | solution.py:118
  13.8 7.3 %all-to-all-done = bf16[32,8,1280]{2,1,0:T(8,128)(2,1)S(1)} async-done(((bf16[32,8,1280]{2,1,0:T(8,128)(2,1)}), bf16[32,8,1280]{2,1,0:T(8,128)(2,1)S(1)}, u32[]{:S(2)}, u32[]{:S(2)}) %all-to-all-start) | async-done | bytes 655392 | tf_op jit(solution)/shard_map/all_to_all | solution.py:249
  21.6 7.5 %fusion.4 = (bf16[256,8,4,128]{3,1,2,0:T(8,128)(2,1)S(1)}, bf16[256,8,4,128]{3,1,2,0:T(8,128)(2,1)S(1)}) fusion(s32[256,128]{1,0:T(8,128)S(1)} %get-tuple-element.12, pred[256,4,128]{2,1,0:T(4,128)(4,1)S(1)} %iota_compare_fusion.4, bf16[256,8,128]{2,1,0:T(8,128)(2,1)S(1)} %bitcast.102), kind=kOutput, calls=%fused_computation.7 | convolution fusion | flops 277872640 | bytes 4980736 | tf_op jit(solution)/shard_map/ibjh,ihc->ibjc/dot_general | solution.py:155
  29.1 0.8 fusion.13
  29.9 0.8 fusion.19
  30.8 3.7 %collective-permute-start = (f32[8,4,15,128]{3,2,1,0:T(8,128)S(1)}, f32[8,4,15,128]{3,2,1,0:T(8,128)S(1)}, u32[]{:S(2)}, u32[]{:S(2)}) collective-permute-start(f32[8,4,15,128]{3,2,1,0:T(8,128)S(1)} %get-tuple-element.15), channel_id=1, source_target_pairs={{0,1},{1,2},{2,3},{3,4},{4,5},{5,6},{6,7},{7,8},{8,9},{9,10},{10,1... | collective-permute-start | bytes 737288 | tf_op jit(solution)/shard_map/ppermute | solution.py:27
  34.5 1.9 %collective-permute-start.1 = (f32[8,4,15,128]{3,2,1,0:T(8,128)S(1)}, f32[8,4,15,128]{3,2,1,0:T(8,128)S(1)}, u32[]{:S(2)}, u32[]{:S(2)}) collective-permute-start(f32[8,4,15,128]{3,2,1,0:T(8,128)S(1)} %get-tuple-element.16), channel_id=1, source_target_pairs={{1,0},{2,1},{3,2},{4,3},{5,4},{6,5},{7,6},{8,7},{9,8},{10,9},{11,1... | collective-permute-start | bytes 737288 | tf_op jit(solution)/shard_map/ppermute | solution.py:29
  36.5 1.3 %collective-permute-done = f32[8,4,15,128]{3,2,1,0:T(8,128)S(1)} collective-permute-done((f32[8,4,15,128]{3,2,1,0:T(8,128)S(1)}, f32[8,4,15,128]{3,2,1,0:T(8,128)S(1)}, u32[]{:S(2)}, u32[]{:S(2)}) %collective-permute-start) | collective-permute-done | bytes 245792 | tf_op jit(solution)/shard_map/ppermute | solution.py:27
  37.8 6.5 %collective-permute-done.1 = f32[8,4,15,128]{3,2,1,0:T(8,128)S(1)} collective-permute-done((f32[8,4,15,128]{3,2,1,0:T(8,128)S(1)}, f32[8,4,15,128]{3,2,1,0:T(8,128)S(1)}, u32[]{:S(2)}, u32[]{:S(2)}) %collective-permute-start.1) | collective-permute-done | bytes 245792 | tf_op jit(solution)/shard_map/ppermute | solution.py:29
  44.3 1.9 %fusion.27.spec_ref = f32[32,46,256]{2,1,0:T(8,128)} fusion(f32[128,256,1]{1,0,2:T(8,128)S(1)} %copy-done.1, f32[32,15,128]{2,1,0:T(8,128)S(1)} %bitcast.104, f32[32,16,128]{2,1,0:T(8,128)S(1)} %bitcast.93, f32[32,15,128]{2,1,0:T(8,128)S(1)} %bitcast.103), kind=kOutput, calls=%fused_computation.30 | convolution fusion | flops 289783808 | bytes 2392064 | tf_op jit(solution)/shard_map/cyx,xf->cyf/dot_general | solution.py:130
  46.2 6.3 %shard_map.137 = f32[32,16,256]{2,1,0:T(8,128)} custom-call(f32[32,46,256]{2,1,0:T(8,128)} %fusion.27.spec_ref, f32[32,32,256]{2,1,0:T(8,128)} %fusion.83.kern_ref), custom_call_target="tpu_custom_call" | custom-call | tf_op jit(solution)/shard_map/pallas_call | solution.py:99
  52.6 1.7 %convolution_bitcast_fusion = f32[4,3,16,256]{3,1,2,0:T(4,128)S(1)} fusion(f32[8,4,16,256]{3,2,1,0:T(8,128)} %bitcast.101, f32[32,3]{0,1:T(4,128)S(1)} %copy-done.4, s32[]{:T(128)S(6)} %select_n.64), kind=kOutput, calls=%fused_computation.23 | convolution fusion | flops 2359296 | bytes 721284 | tf_op jit(solution)/shard_map/bsyf,bc->scyf/dot_general | solution.py:135
  54.5 1.7 %collective-permute-start.2 = (f32[3,16,128]{2,1,0:T(8,128)S(1)}, f32[3,16,128]{2,1,0:T(8,128)S(1)}, u32[]{:S(2)}, u32[]{:S(2)}) collective-permute-start(f32[3,16,128]{2,1,0:T(8,128)S(1)} %get-tuple-element.17), channel_id=1, source_target_pairs={{0,32},{32,64},{64,96},{96,0},{1,33},{33,65},{65,97},{97,1},{2,34}... | collective-permute-start | bytes 73736 | tf_op jit(solution)/shard_map/ppermute | solution.py:259
  56.2 2.2 %collective-permute-start.4 = (f32[3,16,128]{2,1,0:T(8,128)S(1)}, f32[3,16,128]{2,1,0:T(8,128)S(1)}, u32[]{:S(2)}, u32[]{:S(2)}) collective-permute-start(f32[3,16,128]{2,1,0:T(8,128)S(1)} %get-tuple-element.18), channel_id=1, source_target_pairs={{0,96},{32,0},{64,32},{96,64},{1,97},{33,1},{65,33},{97,65},{2,98}... | collective-permute-start | bytes 73736 | tf_op jit(solution)/shard_map/ppermute | solution.py:259
  58.4 1.2 %collective-permute-start.3 = (f32[3,16,128]{2,1,0:T(8,128)S(1)}, f32[3,16,128]{2,1,0:T(8,128)S(1)}, u32[]{:S(2)}, u32[]{:S(2)}) collective-permute-start(f32[3,16,128]{2,1,0:T(8,128)S(1)} %get-tuple-element.19), channel_id=1, source_target_pairs={{0,64},{32,96},{64,0},{96,32},{1,65},{33,97},{65,1},{97,33},{2,66}... | collective-permute-start | bytes 73736 | tf_op jit(solution)/shard_map/ppermute | solution.py:259
  59.6 2.9 %collective-permute-done.3 = f32[3,16,128]{2,1,0:T(8,128)S(1)} collective-permute-done((f32[3,16,128]{2,1,0:T(8,128)S(1)}, f32[3,16,128]{2,1,0:T(8,128)S(1)}, u32[]{:S(2)}, u32[]{:S(2)}) %collective-permute-start.3) | collective-permute-done | bytes 24608 | tf_op jit(solution)/shard_map/ppermute | solution.py:259
  62.6 3.2 %collective-permute-start.5 = (bf16[1,3,2,128]{3,2,1,0:T(2,128)(2,1)S(1)}, bf16[1,3,2,128]{3,2,1,0:T(2,128)(2,1)S(1)}, u32[]{:S(2)}, u32[]{:S(2)}) collective-permute-start(bf16[1,3,2,128]{3,2,1,0:T(2,128)(2,1)S(1)} %get-tuple-element.20), channel_id=1, source_target_pairs={{0,1},{1,2},{2,3},{3,4},{4,5},{5,6},{6,7},{7,8},{8,9},{9,10},{10,1... | collective-permute-start | bytes 4616 | tf_op jit(solution)/shard_map/ppermute | solution.py:27
  65.8 1.9 %collective-permute-start.6 = (bf16[1,3,2,128]{3,2,1,0:T(2,128)(2,1)S(1)}, bf16[1,3,2,128]{3,2,1,0:T(2,128)(2,1)S(1)}, u32[]{:S(2)}, u32[]{:S(2)}) collective-permute-start(bf16[1,3,2,128]{3,2,1,0:T(2,128)(2,1)S(1)} %get-tuple-element.21), channel_id=1, source_target_pairs={{1,0},{2,1},{3,2},{4,3},{5,4},{6,5},{7,6},{8,7},{9,8},{10,9},{11,1... | collective-permute-start | bytes 4616 | tf_op jit(solution)/shard_map/ppermute | solution.py:29
  67.8 5.1 %collective-permute-done.6 = bf16[1,3,2,128]{3,2,1,0:T(2,128)(2,1)S(1)} collective-permute-done((bf16[1,3,2,128]{3,2,1,0:T(2,128)(2,1)S(1)}, bf16[1,3,2,128]{3,2,1,0:T(2,128)(2,1)S(1)}, u32[]{:S(2)}, u32[]{:S(2)}) %collective-permute-start.6) | collective-permute-done | bytes 1568 | tf_op jit(solution)/shard_map/ppermute | solution.py:29
  73.8 1.4 %fusion.26 = bf16[18,1,8,17,64]{4,2,3,0,1:T(8,128)(2,1)S(1)} fusion(pred[18]{0:T(512)(128)(4,1)S(1)} %and_or_fusion, pred[8,17]{0,1:T(8,128)(4,1)S(1)} %copy-done.8, bf16[3,20,1,7,2]{3,0,4,1,2:T(4,128)(2,1)S(1)} %slice.43, bf16[3,20,1,8,17]{3,0,4,1,2:T(4,128)(2,1)S(1)} %copy.58, bf16[64,3,3,3]{0,3,2,1:T(4,128)(2,1)S(1)} %copy-done.6), kind=kOutput, calls=%fused_computation.29 | convolution fusion | flops 9925056 | bytes 334954 | tf_op jit(solution)/shard_map/conv_general_dilated | solution.py:37
  75.2 1.5 %convolution_convert_fusion = bf16[16,8,17,64]{3,1,2,0:T(8,128)(2,1)S(1)} fusion(bf16[64,64,3,3]{1,0,3,2:T(8,128)(2,1)S(1)} %copy-done.5, bf16[18,1,7,1,64]{4,2,3,0,1:T(8,128)(2,1)S(1)} %get-tuple-element.14, bf16[18,1,7,1,64]{4,2,3,0,1:T(8,128)(2,1)S(1)} %get-tuple-element.13, bf16[18,1,8,17,64]{4,2,3,0,1:T(8,128)(2,1)S(1)} %fusion.26), kind=kOutput, calls=%fused_computation.19 | convolution fusion | flops 162322432 | bytes 697856 | tf_op jit(solution)/shard_map/conv_general_dilated | solution.py:37
  76.8 1.3 %copy.61 = bf16[1,64,16,128]{3,2,1,0:T(8,128)(2,1)} copy(bf16[1,64,16,128]{1,2,3,0:T(8,128)(2,1)S(1)} %slice_bitcast_fusion) | data formatting | bytes 524288 | tf_op jit(solution)/shard_map/convert_element_type | solution.py:273
  (49 shorter events, 3.2 us)
Async XLA Ops:
  0.0 10.5 %copy-start = (f32[64,8,961]{2,1,0:T(8,128)S(1)}, f32[64,8,961]{2,1,0:T(8,128)}, u32[]{:S(2)}) copy-start(f32[64,8,961]{2,1,0:T(8,128)} %param.20) | copy-start | bytes 5904388
  0.0 10.5 %copy-start.7 = (s32[1,4,1]{1,2,0:T(1,128)S(1)}, s32[1,4,1]{1,2,0:T(1,128)}, u32[]{:S(2)}) copy-start(s32[1,4,1]{1,2,0:T(1,128)} %param.21) | copy-start | bytes 52
  2.8 9.0 %copy-start.3 = (f32[31,256,1]{1,0,2:T(8,128)S(1)}, f32[31,256,1]{1,0,2:T(8,128)}, u32[]{:S(2)}) copy-start(f32[31,256,1]{1,0,2:T(8,128)} %constant.111) | copy-start | bytes 95236
  2.8 18.3 %all-to-all-start = ((bf16[32,8,1280]{2,1,0:T(8,128)(2,1)}), bf16[32,8,1280]{2,1,0:T(8,128)(2,1)S(1)}, u32[]{:S(2)}, u32[]{:S(2)}) async-start(bf16[32,8,1280]{2,1,0:T(8,128)(2,1)} %bitcast.97), calls=%async_computation | async-start | bytes 1310720 | tf_op jit(solution)/shard_map/all_to_all | solution.py:249
  29.9 14.4 %copy-start.1 = (f32[128,256,1]{1,0,2:T(8,128)S(1)}, f32[128,256,1]{1,0,2:T(8,128)}, u32[]{:S(2)}) copy-start(f32[128,256,1]{1,0,2:T(8,128)} %constant.112) | copy-start | bytes 393220
  30.8 7.0 %collective-permute-start = (f32[8,4,15,128]{3,2,1,0:T(8,128)S(1)}, f32[8,4,15,128]{3,2,1,0:T(8,128)S(1)}, u32[]{:S(2)}, u32[]{:S(2)}) collective-permute-start(f32[8,4,15,128]{3,2,1,0:T(8,128)S(1)} %get-tuple-element.15), channel_id=1, source_target_pairs={{0,1},{1,2},{2,3},{3,4},{4,5},{5,6},{6,7},{7,8},{8,9},{9,10},{10,1... | collective-permute-start | bytes 737288 | tf_op jit(solution)/shard_map/ppermute | solution.py:27
  34.5 9.8 %collective-permute-start.1 = (f32[8,4,15,128]{3,2,1,0:T(8,128)S(1)}, f32[8,4,15,128]{3,2,1,0:T(8,128)S(1)}, u32[]{:S(2)}, u32[]{:S(2)}) collective-permute-start(f32[8,4,15,128]{3,2,1,0:T(8,128)S(1)} %get-tuple-element.16), channel_id=1, source_target_pairs={{1,0},{2,1},{3,2},{4,3},{5,4},{6,5},{7,6},{8,7},{9,8},{10,9},{11,1... | collective-permute-start | bytes 737288 | tf_op jit(solution)/shard_map/ppermute | solution.py:29
  46.2 6.3 %copy-start.4 = (f32[32,3]{0,1:T(4,128)S(1)}, f32[32,3]{0,1:T(4,128)}, u32[]{:S(2)}) copy-start(f32[32,3]{0,1:T(4,128)} %param.22) | copy-start | bytes 1156
  46.2 8.0 %copy-start.2 = (f32[256,128,1,1]{1,0,3,2:T(8,128)S(1)}, f32[256,128,1,1]{1,0,3,2:T(8,128)}, u32[]{:S(2)}) copy-start(f32[256,128,1,1]{1,0,3,2:T(8,128)} %constant.113) | copy-start | bytes 393220
  46.2 27.5 %copy-start.6 = (bf16[64,3,3,3]{0,3,2,1:T(4,128)(2,1)S(1)}, bf16[64,3,3,3]{0,3,2,1:T(4,128)(2,1)}, u32[]{:S(2)}) copy-start(bf16[64,3,3,3]{0,3,2,1:T(4,128)(2,1)} %param.23) | copy-start | bytes 10372
  46.2 27.5 %copy-start.8 = (pred[8,17]{0,1:T(8,128)(4,1)S(1)}, pred[8,17]{0,1:T(8,128)(4,1)}, u32[]{:S(2)}) copy-start(pred[8,17]{0,1:T(8,128)(4,1)} %constant.109) | copy-start | bytes 412
  54.5 5.1 %collective-permute-start.2 = (f32[3,16,128]{2,1,0:T(8,128)S(1)}, f32[3,16,128]{2,1,0:T(8,128)S(1)}, u32[]{:S(2)}, u32[]{:S(2)}) collective-permute-start(f32[3,16,128]{2,1,0:T(8,128)S(1)} %get-tuple-element.17), channel_id=1, source_target_pairs={{0,32},{32,64},{64,96},{96,0},{1,33},{33,65},{65,97},{97,1},{2,34}... | collective-permute-start | bytes 73736 | tf_op jit(solution)/shard_map/ppermute | solution.py:259
  56.2 3.4 %collective-permute-start.4 = (f32[3,16,128]{2,1,0:T(8,128)S(1)}, f32[3,16,128]{2,1,0:T(8,128)S(1)}, u32[]{:S(2)}, u32[]{:S(2)}) collective-permute-start(f32[3,16,128]{2,1,0:T(8,128)S(1)} %get-tuple-element.18), channel_id=1, source_target_pairs={{0,96},{32,0},{64,32},{96,64},{1,97},{33,1},{65,33},{97,65},{2,98}... | collective-permute-start | bytes 73736 | tf_op jit(solution)/shard_map/ppermute | solution.py:259
  58.4 4.2 %collective-permute-start.3 = (f32[3,16,128]{2,1,0:T(8,128)S(1)}, f32[3,16,128]{2,1,0:T(8,128)S(1)}, u32[]{:S(2)}, u32[]{:S(2)}) collective-permute-start(f32[3,16,128]{2,1,0:T(8,128)S(1)} %get-tuple-element.19), channel_id=1, source_target_pairs={{0,64},{32,96},{64,0},{96,32},{1,65},{33,97},{65,1},{97,33},{2,66}... | collective-permute-start | bytes 73736 | tf_op jit(solution)/shard_map/ppermute | solution.py:259
  62.6 5.1 %collective-permute-start.5 = (bf16[1,3,2,128]{3,2,1,0:T(2,128)(2,1)S(1)}, bf16[1,3,2,128]{3,2,1,0:T(2,128)(2,1)S(1)}, u32[]{:S(2)}, u32[]{:S(2)}) collective-permute-start(bf16[1,3,2,128]{3,2,1,0:T(2,128)(2,1)S(1)} %get-tuple-element.20), channel_id=1, source_target_pairs={{0,1},{1,2},{2,3},{3,4},{4,5},{5,6},{6,7},{7,8},{8,9},{9,10},{10,1... | collective-permute-start | bytes 4616 | tf_op jit(solution)/shard_map/ppermute | solution.py:27
  65.8 7.0 %collective-permute-start.6 = (bf16[1,3,2,128]{3,2,1,0:T(2,128)(2,1)S(1)}, bf16[1,3,2,128]{3,2,1,0:T(2,128)(2,1)S(1)}, u32[]{:S(2)}, u32[]{:S(2)}) collective-permute-start(bf16[1,3,2,128]{3,2,1,0:T(2,128)(2,1)S(1)} %get-tuple-element.21), channel_id=1, source_target_pairs={{1,0},{2,1},{3,2},{4,3},{5,4},{6,5},{7,6},{8,7},{9,8},{10,9},{11,1... | collective-permute-start | bytes 4616 | tf_op jit(solution)/shard_map/ppermute | solution.py:29
  73.8 1.5 %copy-start.5 = (bf16[64,64,3,3]{1,0,3,2:T(8,128)(2,1)S(1)}, bf16[64,64,3,3]{1,0,3,2:T(8,128)(2,1)}, u32[]{:S(2)}) copy-start(bf16[64,64,3,3]{1,0,3,2:T(8,128)(2,1)} %param.24) | copy-start | bytes 221188

commit v13 on v12

--- a/solution.py
+++ b/solution.py
@@ -13,7 +13,7 @@
 K = 31
 DFT_N = 144
 LANE = 128
-GROUP = 8
+GROUP = 16
 
 
 def padded_2(cells, sides, width):

time: 78.6 us -> 78.8 us (level)
  no operation moved by 1% of the time
where the time goes in v13:
time: 78.8 us; the launch traced here: 78.3 us
  starting transfers between devices  23.6 us (30%)
  waiting for transfers between devices  23.2 us (29%)
  matrix products  17.7 us (22%)
  Pallas kernels  9.3 us (12%)
  local copies, waits for them, and re-layouts  3.89 us (5%)
    ppermute x2, waiting for transfers between devices, padded_2(): lax.ppermute(head, axis, [((i + 1) % count, i) for i in range(ends)])  11.6 us
    all_to_all x1, starting transfers between devices, per_device(): got = lax.all_to_all(send, 'tile', split_axis=0, concat_axis=0, tiled=True)  7.7 us
    dot_general x1, matrix products, window_splat(): jnp.einsum('ibjh,ihc->ibjc', spread, onehot, preferred_element_type=jnp.f...  7.5 us
    all_to_all x1, waiting for transfers between devices, per_device(): got = lax.all_to_all(send, 'tile', split_axis=0, concat_axis=0, tiled=True)  7.32 us
    ppermute x2, starting transfers between devices, padded_2(): lax.ppermute(tail, axis, [(i, (i + 1) % count) for i in range(ends)])  6.9 us
    pallas_call x1, Pallas kernels, row_taps(): pl.pallas_call(row_taps_kernel, out_shape=jax.ShapeDtypeStruct((channels,...  6.53 us
    ppermute x3, starting transfers between devices, per_device(): lax.ppermute(piece, 'wave', [(i, (i + step) % wave_count) for i in range(...  5.13 us
    ppermute x2, starting transfers between devices, padded_2(): lax.ppermute(head, axis, [((i + 1) % count, i) for i in range(ends)])  3.84 us
  transfers between devices with their start and end apart: 8, of which 5 were waited for; matrix products, arithmetic and copies ran while one was open for 4% of the time, Pallas kernels for 0%

profile of v13, /device:TPU:27, one launch (start us, length us, event | category | flops | bytes accessed | tf_op | source)
XLA Modules:
  0.0 78.3 jit_solution(12032250500336803294)
XLA Ops:
  0.0 2.8 %shard_map.136 = bf16[256,1280]{1,0:T(8,128)(2,1)} custom-call(bf16[128,8,128]{2,1,0:T(8,128)(2,1)} %energy_ref.1, s32[128,128]{1,0:T(8,128)} %bitcast.105, s32[1,128]{1,0:T(1,128)} %bitcast.106, s32[1,128]{1,0:T(1,128)} %count_ref.1, s32[1,128]{1,0:T(1,128)} %scene_ref.1, s32[1,128]{1,0:T(1,128)} %row_ref.1), custom_call_target="tpu_custom_call" | custom-call | tf_op jit(solution)/shard_map/pallas_call | solution.py:214
  2.8 7.7 %all-to-all-start = ((bf16[32,8,1280]{2,1,0:T(8,128)(2,1)}), bf16[32,8,1280]{2,1,0:T(8,128)(2,1)S(1)}, u32[]{:S(2)}, u32[]{:S(2)}) async-start(bf16[32,8,1280]{2,1,0:T(8,128)(2,1)} %bitcast.97), calls=%async_computation | async-start | bytes 1310720 | tf_op jit(solution)/shard_map/all_to_all | solution.py:249
  11.8 1.9 %fusion.83.kern_ref = f32[32,32,256]{2,1,0:T(8,128)} fusion(f32[32,32,31]{2,1,0:T(8,128)S(1)} %bitcast.99, f32[31,256,1]{1,0,2:T(8,128)S(1)} %copy-done.3), kind=kOutput, calls=%fused_computation.106 | convolution fusion | flops 97517568 | bytes 1207296 | tf_op jit(solution)/shard_map/dot_general | solution.py:118
  13.8 7.3 %all-to-all-done = bf16[32,8,1280]{2,1,0:T(8,128)(2,1)S(1)} async-done(((bf16[32,8,1280]{2,1,0:T(8,128)(2,1)}), bf16[32,8,1280]{2,1,0:T(8,128)(2,1)S(1)}, u32[]{:S(2)}, u32[]{:S(2)}) %all-to-all-start) | async-done | bytes 655392 | tf_op jit(solution)/shard_map/all_to_all | solution.py:249
  21.6 7.5 %fusion.4 = (bf16[256,8,4,128]{3,1,2,0:T(8,128)(2,1)S(1)}, bf16[256,8,4,128]{3,1,2,0:T(8,128)(2,1)S(1)}) fusion(s32[256,128]{1,0:T(8,128)S(1)} %get-tuple-element.12, pred[256,4,128]{2,1,0:T(4,128)(4,1)S(1)} %iota_compare_fusion.4, bf16[256,8,128]{2,1,0:T(8,128)(2,1)S(1)} %bitcast.102), kind=kOutput, calls=%fused_computation.7 | convolution fusion | flops 277872640 | bytes 4980736 | tf_op jit(solution)/shard_map/ibjh,ihc->ibjc/dot_general | solution.py:155
  29.1 0.8 fusion.13
  29.9 0.8 fusion.19
  30.8 3.7 %collective-permute-start = (f32[8,4,15,128]{3,2,1,0:T(8,128)S(1)}, f32[8,4,15,128]{3,2,1,0:T(8,128)S(1)}, u32[]{:S(2)}, u32[]{:S(2)}) collective-permute-start(f32[8,4,15,128]{3,2,1,0:T(8,128)S(1)} %get-tuple-element.15), channel_id=1, source_target_pairs={{0,1},{1,2},{2,3},{3,4},{4,5},{5,6},{6,7},{7,8},{8,9},{9,10},{10,1... | collective-permute-start | bytes 737288 | tf_op jit(solution)/shard_map/ppermute | solution.py:27
  34.5 1.9 %collective-permute-start.1 = (f32[8,4,15,128]{3,2,1,0:T(8,128)S(1)}, f32[8,4,15,128]{3,2,1,0:T(8,128)S(1)}, u32[]{:S(2)}, u32[]{:S(2)}) collective-permute-start(f32[8,4,15,128]{3,2,1,0:T(8,128)S(1)} %get-tuple-element.16), channel_id=1, source_target_pairs={{1,0},{2,1},{3,2},{4,3},{5,4},{6,5},{7,6},{8,7},{9,8},{10,9},{11,1... | collective-permute-start | bytes 737288 | tf_op jit(solution)/shard_map/ppermute | solution.py:29
  36.5 1.3 %collective-permute-done = f32[8,4,15,128]{3,2,1,0:T(8,128)S(1)} collective-permute-done((f32[8,4,15,128]{3,2,1,0:T(8,128)S(1)}, f32[8,4,15,128]{3,2,1,0:T(8,128)S(1)}, u32[]{:S(2)}, u32[]{:S(2)}) %collective-permute-start) | collective-permute-done | bytes 245792 | tf_op jit(solution)/shard_map/ppermute | solution.py:27
  37.8 6.5 %collective-permute-done.1 = f32[8,4,15,128]{3,2,1,0:T(8,128)S(1)} collective-permute-done((f32[8,4,15,128]{3,2,1,0:T(8,128)S(1)}, f32[8,4,15,128]{3,2,1,0:T(8,128)S(1)}, u32[]{:S(2)}, u32[]{:S(2)}) %collective-permute-start.1) | collective-permute-done | bytes 245792 | tf_op jit(solution)/shard_map/ppermute | solution.py:29
  44.3 1.9 %fusion.27.spec_ref = f32[32,46,256]{2,1,0:T(8,128)} fusion(f32[128,256,1]{1,0,2:T(8,128)S(1)} %copy-done.1, f32[32,15,128]{2,1,0:T(8,128)S(1)} %bitcast.104, f32[32,16,128]{2,1,0:T(8,128)S(1)} %bitcast.93, f32[32,15,128]{2,1,0:T(8,128)S(1)} %bitcast.103), kind=kOutput, calls=%fused_computation.30 | convolution fusion | flops 289783808 | bytes 2392064 | tf_op jit(solution)/shard_map/cyx,xf->cyf/dot_general | solution.py:130
  46.2 6.5 %shard_map.137 = f32[32,16,256]{2,1,0:T(8,128)} custom-call(f32[32,46,256]{2,1,0:T(8,128)} %fusion.27.spec_ref, f32[32,32,256]{2,1,0:T(8,128)} %fusion.83.kern_ref), custom_call_target="tpu_custom_call" | custom-call | tf_op jit(solution)/shard_map/pallas_call | solution.py:99
  52.8 1.7 %convolution_bitcast_fusion = f32[4,3,16,256]{3,1,2,0:T(4,128)S(1)} fusion(f32[8,4,16,256]{3,2,1,0:T(8,128)} %bitcast.101, f32[32,3]{0,1:T(4,128)S(1)} %copy-done.4, s32[]{:T(128)S(6)} %select_n.64), kind=kOutput, calls=%fused_computation.23 | convolution fusion | flops 2359296 | bytes 721284 | tf_op jit(solution)/shard_map/bsyf,bc->scyf/dot_general | solution.py:135
  54.7 1.7 %collective-permute-start.2 = (f32[3,16,128]{2,1,0:T(8,128)S(1)}, f32[3,16,128]{2,1,0:T(8,128)S(1)}, u32[]{:S(2)}, u32[]{:S(2)}) collective-permute-start(f32[3,16,128]{2,1,0:T(8,128)S(1)} %get-tuple-element.17), channel_id=1, source_target_pairs={{0,32},{32,64},{64,96},{96,0},{1,33},{33,65},{65,97},{97,1},{2,34}... | collective-permute-start | bytes 73736 | tf_op jit(solution)/shard_map/ppermute | solution.py:259
  56.4 2.2 %collective-permute-start.4 = (f32[3,16,128]{2,1,0:T(8,128)S(1)}, f32[3,16,128]{2,1,0:T(8,128)S(1)}, u32[]{:S(2)}, u32[]{:S(2)}) collective-permute-start(f32[3,16,128]{2,1,0:T(8,128)S(1)} %get-tuple-element.18), channel_id=1, source_target_pairs={{0,96},{32,0},{64,32},{96,64},{1,97},{33,1},{65,33},{97,65},{2,98}... | collective-permute-start | bytes 73736 | tf_op jit(solution)/shard_map/ppermute | solution.py:259
  58.6 1.2 %collective-permute-start.3 = (f32[3,16,128]{2,1,0:T(8,128)S(1)}, f32[3,16,128]{2,1,0:T(8,128)S(1)}, u32[]{:S(2)}, u32[]{:S(2)}) collective-permute-start(f32[3,16,128]{2,1,0:T(8,128)S(1)} %get-tuple-element.19), channel_id=1, source_target_pairs={{0,64},{32,96},{64,0},{96,32},{1,65},{33,97},{65,1},{97,33},{2,66}... | collective-permute-start | bytes 73736 | tf_op jit(solution)/shard_map/ppermute | solution.py:259
  59.9 2.9 %collective-permute-done.3 = f32[3,16,128]{2,1,0:T(8,128)S(1)} collective-permute-done((f32[3,16,128]{2,1,0:T(8,128)S(1)}, f32[3,16,128]{2,1,0:T(8,128)S(1)}, u32[]{:S(2)}, u32[]{:S(2)}) %collective-permute-start.3) | collective-permute-done | bytes 24608 | tf_op jit(solution)/shard_map/ppermute | solution.py:259
  62.8 3.2 %collective-permute-start.5 = (bf16[1,3,2,128]{3,2,1,0:T(2,128)(2,1)S(1)}, bf16[1,3,2,128]{3,2,1,0:T(2,128)(2,1)S(1)}, u32[]{:S(2)}, u32[]{:S(2)}) collective-permute-start(bf16[1,3,2,128]{3,2,1,0:T(2,128)(2,1)S(1)} %get-tuple-element.20), channel_id=1, source_target_pairs={{0,1},{1,2},{2,3},{3,4},{4,5},{5,6},{6,7},{7,8},{8,9},{9,10},{10,1... | collective-permute-start | bytes 4616 | tf_op jit(solution)/shard_map/ppermute | solution.py:27
  66.0 1.9 %collective-permute-start.6 = (bf16[1,3,2,128]{3,2,1,0:T(2,128)(2,1)S(1)}, bf16[1,3,2,128]{3,2,1,0:T(2,128)(2,1)S(1)}, u32[]{:S(2)}, u32[]{:S(2)}) collective-permute-start(bf16[1,3,2,128]{3,2,1,0:T(2,128)(2,1)S(1)} %get-tuple-element.21), channel_id=1, source_target_pairs={{1,0},{2,1},{3,2},{4,3},{5,4},{6,5},{7,6},{8,7},{9,8},{10,9},{11,1... | collective-permute-start | bytes 4616 | tf_op jit(solution)/shard_map/ppermute | solution.py:29
  68.0 5.1 %collective-permute-done.6 = bf16[1,3,2,128]{3,2,1,0:T(2,128)(2,1)S(1)} collective-permute-done((bf16[1,3,2,128]{3,2,1,0:T(2,128)(2,1)S(1)}, bf16[1,3,2,128]{3,2,1,0:T(2,128)(2,1)S(1)}, u32[]{:S(2)}, u32[]{:S(2)}) %collective-permute-start.6) | collective-permute-done | bytes 1568 | tf_op jit(solution)/shard_map/ppermute | solution.py:29
  74.0 1.4 %fusion.26 = bf16[18,1,8,17,64]{4,2,3,0,1:T(8,128)(2,1)S(1)} fusion(pred[18]{0:T(512)(128)(4,1)S(1)} %and_or_fusion, pred[8,17]{0,1:T(8,128)(4,1)S(1)} %copy-done.8, bf16[3,20,1,7,2]{3,0,4,1,2:T(4,128)(2,1)S(1)} %slice.43, bf16[3,20,1,8,17]{3,0,4,1,2:T(4,128)(2,1)S(1)} %copy.58, bf16[64,3,3,3]{0,3,2,1:T(4,128)(2,1)S(1)} %copy-done.6), kind=kOutput, calls=%fused_computation.29 | convolution fusion | flops 9925056 | bytes 334954 | tf_op jit(solution)/shard_map/conv_general_dilated | solution.py:37
  75.5 1.5 %convolution_convert_fusion = bf16[16,8,17,64]{3,1,2,0:T(8,128)(2,1)S(1)} fusion(bf16[64,64,3,3]{1,0,3,2:T(8,128)(2,1)S(1)} %copy-done.5, bf16[18,1,7,1,64]{4,2,3,0,1:T(8,128)(2,1)S(1)} %get-tuple-element.14, bf16[18,1,7,1,64]{4,2,3,0,1:T(8,128)(2,1)S(1)} %get-tuple-element.13, bf16[18,1,8,17,64]{4,2,3,0,1:T(8,128)(2,1)S(1)} %fusion.26), kind=kOutput, calls=%fused_computation.19 | convolution fusion | flops 162322432 | bytes 697856 | tf_op jit(solution)/shard_map/conv_general_dilated | solution.py:37
  77.1 1.3 %copy.61 = bf16[1,64,16,128]{3,2,1,0:T(8,128)(2,1)} copy(bf16[1,64,16,128]{1,2,3,0:T(8,128)(2,1)S(1)} %slice_bitcast_fusion) | data formatting | bytes 524288 | tf_op jit(solution)/shard_map/convert_element_type | solution.py:273
  (49 shorter events, 3.2 us)
Async XLA Ops:
  0.0 10.5 %copy-start = (f32[64,8,961]{2,1,0:T(8,128)S(1)}, f32[64,8,961]{2,1,0:T(8,128)}, u32[]{:S(2)}) copy-start(f32[64,8,961]{2,1,0:T(8,128)} %param.20) | copy-start | bytes 5904388
  0.0 10.5 %copy-start.7 = (s32[1,4,1]{1,2,0:T(1,128)S(1)}, s32[1,4,1]{1,2,0:T(1,128)}, u32[]{:S(2)}) copy-start(s32[1,4,1]{1,2,0:T(1,128)} %param.21) | copy-start | bytes 52
  2.8 9.0 %copy-start.3 = (f32[31,256,1]{1,0,2:T(8,128)S(1)}, f32[31,256,1]{1,0,2:T(8,128)}, u32[]{:S(2)}) copy-start(f32[31,256,1]{1,0,2:T(8,128)} %constant.111) | copy-start | bytes 95236
  2.8 18.3 %all-to-all-start = ((bf16[32,8,1280]{2,1,0:T(8,128)(2,1)}), bf16[32,8,1280]{2,1,0:T(8,128)(2,1)S(1)}, u32[]{:S(2)}, u32[]{:S(2)}) async-start(bf16[32,8,1280]{2,1,0:T(8,128)(2,1)} %bitcast.97), calls=%async_computation | async-start | bytes 1310720 | tf_op jit(solution)/shard_map/all_to_all | solution.py:249
  29.9 14.4 %copy-start.1 = (f32[128,256,1]{1,0,2:T(8,128)S(1)}, f32[128,256,1]{1,0,2:T(8,128)}, u32[]{:S(2)}) copy-start(f32[128,256,1]{1,0,2:T(8,128)} %constant.112) | copy-start | bytes 393220
  30.8 7.0 %collective-permute-start = (f32[8,4,15,128]{3,2,1,0:T(8,128)S(1)}, f32[8,4,15,128]{3,2,1,0:T(8,128)S(1)}, u32[]{:S(2)}, u32[]{:S(2)}) collective-permute-start(f32[8,4,15,128]{3,2,1,0:T(8,128)S(1)} %get-tuple-element.15), channel_id=1, source_target_pairs={{0,1},{1,2},{2,3},{3,4},{4,5},{5,6},{6,7},{7,8},{8,9},{9,10},{10,1... | collective-permute-start | bytes 737288 | tf_op jit(solution)/shard_map/ppermute | solution.py:27
  34.5 9.8 %collective-permute-start.1 = (f32[8,4,15,128]{3,2,1,0:T(8,128)S(1)}, f32[8,4,15,128]{3,2,1,0:T(8,128)S(1)}, u32[]{:S(2)}, u32[]{:S(2)}) collective-permute-start(f32[8,4,15,128]{3,2,1,0:T(8,128)S(1)} %get-tuple-element.16), channel_id=1, source_target_pairs={{1,0},{2,1},{3,2},{4,3},{5,4},{6,5},{7,6},{8,7},{9,8},{10,9},{11,1... | collective-permute-start | bytes 737288 | tf_op jit(solution)/shard_map/ppermute | solution.py:29
  46.2 6.5 %copy-start.4 = (f32[32,3]{0,1:T(4,128)S(1)}, f32[32,3]{0,1:T(4,128)}, u32[]{:S(2)}) copy-start(f32[32,3]{0,1:T(4,128)} %param.22) | copy-start | bytes 1156
  46.2 8.2 %copy-start.2 = (f32[256,128,1,1]{1,0,3,2:T(8,128)S(1)}, f32[256,128,1,1]{1,0,3,2:T(8,128)}, u32[]{:S(2)}) copy-start(f32[256,128,1,1]{1,0,3,2:T(8,128)} %constant.113) | copy-start | bytes 393220
  46.2 27.7 %copy-start.6 = (bf16[64,3,3,3]{0,3,2,1:T(4,128)(2,1)S(1)}, bf16[64,3,3,3]{0,3,2,1:T(4,128)(2,1)}, u32[]{:S(2)}) copy-start(bf16[64,3,3,3]{0,3,2,1:T(4,128)(2,1)} %param.23) | copy-start | bytes 10372
  46.2 27.7 %copy-start.8 = (pred[8,17]{0,1:T(8,128)(4,1)S(1)}, pred[8,17]{0,1:T(8,128)(4,1)}, u32[]{:S(2)}) copy-start(pred[8,17]{0,1:T(8,128)(4,1)} %constant.109) | copy-start | bytes 412
  54.7 5.1 %collective-permute-start.2 = (f32[3,16,128]{2,1,0:T(8,128)S(1)}, f32[3,16,128]{2,1,0:T(8,128)S(1)}, u32[]{:S(2)}, u32[]{:S(2)}) collective-permute-start(f32[3,16,128]{2,1,0:T(8,128)S(1)} %get-tuple-element.17), channel_id=1, source_target_pairs={{0,32},{32,64},{64,96},{96,0},{1,33},{33,65},{65,97},{97,1},{2,34}... | collective-permute-start | bytes 73736 | tf_op jit(solution)/shard_map/ppermute | solution.py:259
  56.4 3.4 %collective-permute-start.4 = (f32[3,16,128]{2,1,0:T(8,128)S(1)}, f32[3,16,128]{2,1,0:T(8,128)S(1)}, u32[]{:S(2)}, u32[]{:S(2)}) collective-permute-start(f32[3,16,128]{2,1,0:T(8,128)S(1)} %get-tuple-element.18), channel_id=1, source_target_pairs={{0,96},{32,0},{64,32},{96,64},{1,97},{33,1},{65,33},{97,65},{2,98}... | collective-permute-start | bytes 73736 | tf_op jit(solution)/shard_map/ppermute | solution.py:259
  58.6 4.2 %collective-permute-start.3 = (f32[3,16,128]{2,1,0:T(8,128)S(1)}, f32[3,16,128]{2,1,0:T(8,128)S(1)}, u32[]{:S(2)}, u32[]{:S(2)}) collective-permute-start(f32[3,16,128]{2,1,0:T(8,128)S(1)} %get-tuple-element.19), channel_id=1, source_target_pairs={{0,64},{32,96},{64,0},{96,32},{1,65},{33,97},{65,1},{97,33},{2,66}... | collective-permute-start | bytes 73736 | tf_op jit(solution)/shard_map/ppermute | solution.py:259
  62.8 5.1 %collective-permute-start.5 = (bf16[1,3,2,128]{3,2,1,0:T(2,128)(2,1)S(1)}, bf16[1,3,2,128]{3,2,1,0:T(2,128)(2,1)S(1)}, u32[]{:S(2)}, u32[]{:S(2)}) collective-permute-start(bf16[1,3,2,128]{3,2,1,0:T(2,128)(2,1)S(1)} %get-tuple-element.20), channel_id=1, source_target_pairs={{0,1},{1,2},{2,3},{3,4},{4,5},{5,6},{6,7},{7,8},{8,9},{9,10},{10,1... | collective-permute-start | bytes 4616 | tf_op jit(solution)/shard_map/ppermute | solution.py:27
  66.0 7.0 %collective-permute-start.6 = (bf16[1,3,2,128]{3,2,1,0:T(2,128)(2,1)S(1)}, bf16[1,3,2,128]{3,2,1,0:T(2,128)(2,1)S(1)}, u32[]{:S(2)}, u32[]{:S(2)}) collective-permute-start(bf16[1,3,2,128]{3,2,1,0:T(2,128)(2,1)S(1)} %get-tuple-element.21), channel_id=1, source_target_pairs={{1,0},{2,1},{3,2},{4,3},{5,4},{6,5},{7,6},{8,7},{9,8},{10,9},{11,1... | collective-permute-start | bytes 4616 | tf_op jit(solution)/shard_map/ppermute | solution.py:29
  74.0 1.5 %copy-start.5 = (bf16[64,64,3,3]{1,0,3,2:T(8,128)(2,1)S(1)}, bf16[64,64,3,3]{1,0,3,2:T(8,128)(2,1)}, u32[]{:S(2)}) copy-start(bf16[64,64,3,3]{1,0,3,2:T(8,128)(2,1)} %param.24) | copy-start | bytes 221188

commit v14 on v13

--- a/solution.py
+++ b/solution.py
@@ -160,9 +160,11 @@
     placing = placing.astype(jnp.bfloat16)
     upper = lax.reduce_precision(window, exponent_bits=8, mantissa_bits=7)
     lower = (window - upper).astype(jnp.bfloat16)
+    parts = jnp.concatenate([upper.astype(jnp.bfloat16), lower], axis=2)
     total = jnp.einsum(
-        "ibjc,ijr->brc", upper.astype(jnp.bfloat16), placing, preferred_element_type=jnp.float32
-    ) + jnp.einsum("ibjc,ijr->brc", lower, placing, preferred_element_type=jnp.float32)
+        "ibjc,ijr->brc", parts, jnp.concatenate([placing, placing], axis=1),
+        preferred_element_type=jnp.float32,
+    )
     return total.reshape(band_dev, scenes, ROWS_DEV, W)
 
 

time: 78.8 us -> 81.6 us (1.036)
  the two profiles are of different devices: /device:TPU:27 before, /device:TPU:2 now
where the time goes in v14:
time: 81.6 us; the launch traced here: 81.2 us
  starting transfers between devices  24.5 us (30%)
  waiting for transfers between devices  23.8 us (29%)
  matrix products  18.6 us (23%)
  Pallas kernels  9.3 us (11%)
  local copies, waits for them, and re-layouts  3.9 us (5%)
    ppermute x2, waiting for transfers between devices, padded_2(): lax.ppermute(tail, axis, [(i, (i + 1) % count) for i in range(ends)])  10.3 us
    all_to_all x1, starting transfers between devices, per_device(): got = lax.all_to_all(send, 'tile', split_axis=0, concat_axis=0, tiled=True)  7.75 us
    all_to_all x1, waiting for transfers between devices, per_device(): got = lax.all_to_all(send, 'tile', split_axis=0, concat_axis=0, tiled=True)  7.55 us
    dot_general x1, matrix products, window_splat(): jnp.einsum('ibjh,ihc->ibjc', spread, onehot, preferred_element_type=jnp.f...  7.5 us
    ppermute x2, starting transfers between devices, padded_2(): lax.ppermute(head, axis, [((i + 1) % count, i) for i in range(ends)])  6.85 us
    pallas_call x1, Pallas kernels, row_taps(): pl.pallas_call(row_taps_kernel, out_shape=jax.ShapeDtypeStruct((channels,...  6.53 us
    ppermute x3, starting transfers between devices, per_device(): lax.ppermute(piece, 'wave', [(i, (i + step) % wave_count) for i in range(...  5.37 us
    ppermute x2, starting transfers between devices, padded_2(): lax.ppermute(tail, axis, [(i, (i + 1) % count) for i in range(ends)])  4.51 us
  transfers between devices with their start and end apart: 8, of which 6 were waited for; matrix products, arithmetic and copies ran while one was open for 4% of the time, Pallas kernels for 0%

profile of v14, /device:TPU:2, one launch (start us, length us, event | category | flops | bytes accessed | tf_op | source)
XLA Modules:
  0.0 81.2 jit_solution(17062593022773499622)
XLA Ops:
  0.0 2.8 %shard_map.136 = bf16[256,1280]{1,0:T(8,128)(2,1)} custom-call(bf16[128,8,128]{2,1,0:T(8,128)(2,1)} %energy_ref.1, s32[128,128]{1,0:T(8,128)} %bitcast.99, s32[1,128]{1,0:T(1,128)} %bitcast.100, s32[1,128]{1,0:T(1,128)} %count_ref.1, s32[1,128]{1,0:T(1,128)} %scene_ref.1, s32[1,128]{1,0:T(1,128)} %row_ref.1), custom_call_target="tpu_custom_call" | custom-call | tf_op jit(solution)/shard_map/pallas_call | solution.py:216
  2.8 7.8 %all-to-all-start = ((bf16[32,8,1280]{2,1,0:T(8,128)(2,1)}), bf16[32,8,1280]{2,1,0:T(8,128)(2,1)S(1)}, u32[]{:S(2)}, u32[]{:S(2)}) async-start(bf16[32,8,1280]{2,1,0:T(8,128)(2,1)} %bitcast.89), calls=%async_computation | async-start | bytes 1310720 | tf_op jit(solution)/shard_map/all_to_all | solution.py:251
  11.1 0.6 reshape.114
  11.9 1.9 %fusion.70.kern_ref = f32[32,32,256]{2,1,0:T(8,128)} fusion(f32[32,32,31]{2,1,0:T(8,128)S(1)} %bitcast.93, f32[31,256,1]{1,0,2:T(8,128)S(1)} %copy-done.3), kind=kOutput, calls=%fused_computation.103 | convolution fusion | flops 97517568 | bytes 1207296 | tf_op jit(solution)/shard_map/dot_general | solution.py:118
  13.8 7.5 %all-to-all-done = bf16[32,8,1280]{2,1,0:T(8,128)(2,1)S(1)} async-done(((bf16[32,8,1280]{2,1,0:T(8,128)(2,1)}), bf16[32,8,1280]{2,1,0:T(8,128)(2,1)S(1)}, u32[]{:S(2)}, u32[]{:S(2)}) %all-to-all-start) | async-done | bytes 655392 | tf_op jit(solution)/shard_map/all_to_all | solution.py:251
  21.9 7.5 %reduce-precision_convert_fusion = (bf16[256,8,4,128]{3,1,2,0:T(8,128)(2,1)S(1)}, bf16[256,8,4,128]{3,1,2,0:T(8,128)(2,1)S(1)}) fusion(s32[256,128]{1,0:T(8,128)S(1)} %get-tuple-element.12, pred[256,4,128]{2,1,0:T(4,128)(4,1)S(1)} %iota_compare_fusion.4, bf16[256,8,128]{2,1,0:T(8,128)(2,1)S(1)} %bitcast.96), kind=kOutput, calls=%fused_computation.6 | convolution fusion | flops 277872640 | bytes 4980736 | tf_op jit(solution)/shard_map/ibjh,ihc->ibjc/dot_general | solution.py:155
  29.9 2.4 %fusion.5 = f32[64,8,128,1]{2,0,3,1:T(8,128)S(1)} fusion(bf16[256,8,8,128]{3,1,2,0:T(8,128)(2,1)S(1)} %pad_maximum_fusion, bf16[256,4,64]{0,2,1:T(8,128)(2,1)S(1)} %convert_convert_fusion), kind=kOutput, calls=%fused_computation.9 | convolution fusion | flops 268959744 | bytes 4587520 | tf_op jit(solution)/shard_map/ibjc,ijr->brc/dot_general | solution.py:164
  32.3 4.9 %collective-permute-start.1 = (f32[8,4,15,128]{3,2,1,0:T(8,128)S(1)}, f32[8,4,15,128]{3,2,1,0:T(8,128)S(1)}, u32[]{:S(2)}, u32[]{:S(2)}) collective-permute-start(f32[8,4,15,128]{3,2,1,0:T(8,128)S(1)} %get-tuple-element.16), channel_id=1, source_target_pairs={{1,0},{2,1},{3,2},{4,3},{5,4},{6,5},{7,6},{8,7},{9,8},{10,9},{11,1... | collective-permute-start | bytes 737288 | tf_op jit(solution)/shard_map/ppermute | solution.py:29
  37.3 1.9 %collective-permute-start = (f32[8,4,15,128]{3,2,1,0:T(8,128)S(1)}, f32[8,4,15,128]{3,2,1,0:T(8,128)S(1)}, u32[]{:S(2)}, u32[]{:S(2)}) collective-permute-start(f32[8,4,15,128]{3,2,1,0:T(8,128)S(1)} %get-tuple-element.15), channel_id=1, source_target_pairs={{0,1},{1,2},{2,3},{3,4},{4,5},{5,6},{6,7},{7,8},{8,9},{9,10},{10,1... | collective-permute-start | bytes 737288 | tf_op jit(solution)/shard_map/ppermute | solution.py:27
  39.2 1.9 %collective-permute-done.1 = f32[8,4,15,128]{3,2,1,0:T(8,128)S(1)} collective-permute-done((f32[8,4,15,128]{3,2,1,0:T(8,128)S(1)}, f32[8,4,15,128]{3,2,1,0:T(8,128)S(1)}, u32[]{:S(2)}, u32[]{:S(2)}) %collective-permute-start.1) | collective-permute-done | bytes 245792 | tf_op jit(solution)/shard_map/ppermute | solution.py:29
  41.1 5.9 %collective-permute-done = f32[8,4,15,128]{3,2,1,0:T(8,128)S(1)} collective-permute-done((f32[8,4,15,128]{3,2,1,0:T(8,128)S(1)}, f32[8,4,15,128]{3,2,1,0:T(8,128)S(1)}, u32[]{:S(2)}, u32[]{:S(2)}) %collective-permute-start) | collective-permute-done | bytes 245792 | tf_op jit(solution)/shard_map/ppermute | solution.py:27
  47.1 1.9 %fusion.16.spec_ref = f32[32,46,256]{2,1,0:T(8,128)} fusion(f32[128,256,1]{1,0,2:T(8,128)S(1)} %copy-done.1, f32[32,15,128]{2,1,0:T(8,128)S(1)} %bitcast.97, f32[32,16,128]{2,1,0:T(8,128)S(1)} %bitcast.91, f32[32,15,128]{2,1,0:T(8,128)S(1)} %bitcast.98), kind=kOutput, calls=%fused_computation.26 | convolution fusion | flops 289783808 | bytes 2392064 | tf_op jit(solution)/shard_map/cyx,xf->cyf/dot_general | solution.py:130
  49.0 6.5 %shard_map.137 = f32[32,16,256]{2,1,0:T(8,128)} custom-call(f32[32,46,256]{2,1,0:T(8,128)} %fusion.16.spec_ref, f32[32,32,256]{2,1,0:T(8,128)} %fusion.70.kern_ref), custom_call_target="tpu_custom_call" | custom-call | tf_op jit(solution)/shard_map/pallas_call | solution.py:99
  55.6 1.7 %convolution_bitcast_fusion = f32[4,3,16,256]{3,1,2,0:T(4,128)S(1)} fusion(f32[8,4,16,256]{3,2,1,0:T(8,128)} %bitcast.95, f32[32,3]{0,1:T(4,128)S(1)} %copy-done.4, s32[]{:T(128)S(6)} %select_n.64), kind=kOutput, calls=%fused_computation.20 | convolution fusion | flops 2359296 | bytes 721284 | tf_op jit(solution)/shard_map/bsyf,bc->scyf/dot_general | solution.py:135
  57.5 4.1 %collective-permute-start.4 = (f32[3,16,128]{2,1,0:T(8,128)S(1)}, f32[3,16,128]{2,1,0:T(8,128)S(1)}, u32[]{:S(2)}, u32[]{:S(2)}) collective-permute-start(f32[3,16,128]{2,1,0:T(8,128)S(1)} %get-tuple-element.18), channel_id=1, source_target_pairs={{0,96},{32,0},{64,32},{96,64},{1,97},{33,1},{65,33},{97,65},{2,98}... | collective-permute-start | bytes 73736 | tf_op jit(solution)/shard_map/ppermute | solution.py:261
  61.6 1.3 %collective-permute-start.2 = (f32[3,16,128]{2,1,0:T(8,128)S(1)}, f32[3,16,128]{2,1,0:T(8,128)S(1)}, u32[]{:S(2)}, u32[]{:S(2)}) collective-permute-start(f32[3,16,128]{2,1,0:T(8,128)S(1)} %get-tuple-element.17), channel_id=1, source_target_pairs={{0,32},{32,64},{64,96},{96,0},{1,33},{33,65},{65,97},{97,1},{2,34}... | collective-permute-start | bytes 73736 | tf_op jit(solution)/shard_map/ppermute | solution.py:261
  63.1 3.8 %collective-permute-done.3 = f32[3,16,128]{2,1,0:T(8,128)S(1)} collective-permute-done((f32[3,16,128]{2,1,0:T(8,128)S(1)}, f32[3,16,128]{2,1,0:T(8,128)S(1)}, u32[]{:S(2)}, u32[]{:S(2)}) %collective-permute-start.3) | collective-permute-done | bytes 24608 | tf_op jit(solution)/shard_map/ppermute | solution.py:261
  67.0 1.9 %collective-permute-start.6 = (bf16[1,3,2,128]{3,2,1,0:T(2,128)(2,1)S(1)}, bf16[1,3,2,128]{3,2,1,0:T(2,128)(2,1)S(1)}, u32[]{:S(2)}, u32[]{:S(2)}) collective-permute-start(bf16[1,3,2,128]{3,2,1,0:T(2,128)(2,1)S(1)} %get-tuple-element.21), channel_id=1, source_target_pairs={{1,0},{2,1},{3,2},{4,3},{5,4},{6,5},{7,6},{8,7},{9,8},{10,9},{11,1... | collective-permute-start | bytes 4616 | tf_op jit(solution)/shard_map/ppermute | solution.py:29
  68.9 2.6 %collective-permute-start.5 = (bf16[1,3,2,128]{3,2,1,0:T(2,128)(2,1)S(1)}, bf16[1,3,2,128]{3,2,1,0:T(2,128)(2,1)S(1)}, u32[]{:S(2)}, u32[]{:S(2)}) collective-permute-start(bf16[1,3,2,128]{3,2,1,0:T(2,128)(2,1)S(1)} %get-tuple-element.20), channel_id=1, source_target_pairs={{0,1},{1,2},{2,3},{3,4},{4,5},{5,6},{6,7},{7,8},{8,9},{9,10},{10,1... | collective-permute-start | bytes 4616 | tf_op jit(solution)/shard_map/ppermute | solution.py:27
  71.5 4.4 %collective-permute-done.5 = bf16[1,3,2,128]{3,2,1,0:T(2,128)(2,1)S(1)} collective-permute-done((bf16[1,3,2,128]{3,2,1,0:T(2,128)(2,1)S(1)}, bf16[1,3,2,128]{3,2,1,0:T(2,128)(2,1)S(1)}, u32[]{:S(2)}, u32[]{:S(2)}) %collective-permute-start.5) | collective-permute-done | bytes 1568 | tf_op jit(solution)/shard_map/ppermute | solution.py:27
  76.2 0.6 copy.53
  76.9 1.4 %fusion.15 = bf16[18,1,8,17,64]{4,2,3,0,1:T(8,128)(2,1)S(1)} fusion(pred[18]{0:T(512)(128)(4,1)S(1)} %and_or_fusion, pred[8,17]{0,1:T(8,128)(4,1)S(1)} %copy-done.8, bf16[3,20,1,7,2]{3,0,4,1,2:T(4,128)(2,1)S(1)} %slice.43, bf16[3,20,1,8,17]{3,0,4,1,2:T(4,128)(2,1)S(1)} %copy.53, bf16[64,3,3,3]{0,3,2,1:T(4,128)(2,1)S(1)} %copy-done.6), kind=kOutput, calls=%fused_computation.25 | convolution fusion | flops 9925056 | bytes 334954 | tf_op jit(solution)/shard_map/conv_general_dilated | solution.py:37
  78.3 1.5 %convolution_convert_fusion = bf16[16,8,17,64]{3,1,2,0:T(8,128)(2,1)S(1)} fusion(bf16[64,64,3,3]{1,0,3,2:T(8,128)(2,1)S(1)} %copy-done.5, bf16[18,1,7,1,64]{4,2,3,0,1:T(8,128)(2,1)S(1)} %get-tuple-element.14, bf16[18,1,7,1,64]{4,2,3,0,1:T(8,128)(2,1)S(1)} %get-tuple-element.13, bf16[18,1,8,17,64]{4,2,3,0,1:T(8,128)(2,1)S(1)} %fusion.15), kind=kOutput, calls=%fused_computation.18 | convolution fusion | flops 162322432 | bytes 697856 | tf_op jit(solution)/shard_map/conv_general_dilated | solution.py:37
  79.9 1.3 %copy.56 = bf16[1,64,16,128]{3,2,1,0:T(8,128)(2,1)} copy(bf16[1,64,16,128]{1,2,3,0:T(8,128)(2,1)S(1)} %slice_bitcast_fusion) | data formatting | bytes 524288 | tf_op jit(solution)/shard_map/convert_element_type | solution.py:275
  (50 shorter events, 2.7 us)
Async XLA Ops:
  0.0 10.6 %copy-start = (f32[64,8,961]{2,1,0:T(8,128)S(1)}, f32[64,8,961]{2,1,0:T(8,128)}, u32[]{:S(2)}) copy-start(f32[64,8,961]{2,1,0:T(8,128)} %param.20) | copy-start | bytes 5904388
  0.0 10.5 %copy-start.7 = (s32[1,4,1]{1,2,0:T(1,128)S(1)}, s32[1,4,1]{1,2,0:T(1,128)}, u32[]{:S(2)}) copy-start(s32[1,4,1]{1,2,0:T(1,128)} %param.21) | copy-start | bytes 52
  2.8 9.1 %copy-start.3 = (f32[31,256,1]{1,0,2:T(8,128)S(1)}, f32[31,256,1]{1,0,2:T(8,128)}, u32[]{:S(2)}) copy-start(f32[31,256,1]{1,0,2:T(8,128)} %constant.111) | copy-start | bytes 95236
  2.8 18.6 %all-to-all-start = ((bf16[32,8,1280]{2,1,0:T(8,128)(2,1)}), bf16[32,8,1280]{2,1,0:T(8,128)(2,1)S(1)}, u32[]{:S(2)}, u32[]{:S(2)}) async-start(bf16[32,8,1280]{2,1,0:T(8,128)(2,1)} %bitcast.89), calls=%async_computation | async-start | bytes 1310720 | tf_op jit(solution)/shard_map/all_to_all | solution.py:251
  29.8 17.2 %copy-start.1 = (f32[128,256,1]{1,0,2:T(8,128)S(1)}, f32[128,256,1]{1,0,2:T(8,128)}, u32[]{:S(2)}) copy-start(f32[128,256,1]{1,0,2:T(8,128)} %constant.112) | copy-start | bytes 393220
  32.3 8.8 %collective-permute-start.1 = (f32[8,4,15,128]{3,2,1,0:T(8,128)S(1)}, f32[8,4,15,128]{3,2,1,0:T(8,128)S(1)}, u32[]{:S(2)}, u32[]{:S(2)}) collective-permute-start(f32[8,4,15,128]{3,2,1,0:T(8,128)S(1)} %get-tuple-element.16), channel_id=1, source_target_pairs={{1,0},{2,1},{3,2},{4,3},{5,4},{6,5},{7,6},{8,7},{9,8},{10,9},{11,1... | collective-permute-start | bytes 737288 | tf_op jit(solution)/shard_map/ppermute | solution.py:29
  37.3 9.8 %collective-permute-start = (f32[8,4,15,128]{3,2,1,0:T(8,128)S(1)}, f32[8,4,15,128]{3,2,1,0:T(8,128)S(1)}, u32[]{:S(2)}, u32[]{:S(2)}) collective-permute-start(f32[8,4,15,128]{3,2,1,0:T(8,128)S(1)} %get-tuple-element.15), channel_id=1, source_target_pairs={{0,1},{1,2},{2,3},{3,4},{4,5},{5,6},{6,7},{7,8},{8,9},{9,10},{10,1... | collective-permute-start | bytes 737288 | tf_op jit(solution)/shard_map/ppermute | solution.py:27
  49.0 6.5 %copy-start.4 = (f32[32,3]{0,1:T(4,128)S(1)}, f32[32,3]{0,1:T(4,128)}, u32[]{:S(2)}) copy-start(f32[32,3]{0,1:T(4,128)} %param.22) | copy-start | bytes 1156
  49.0 8.2 %copy-start.2 = (f32[256,128,1,1]{1,0,3,2:T(8,128)S(1)}, f32[256,128,1,1]{1,0,3,2:T(8,128)}, u32[]{:S(2)}) copy-start(f32[256,128,1,1]{1,0,3,2:T(8,128)} %constant.113) | copy-start | bytes 393220
  49.0 27.8 %copy-start.6 = (bf16[64,3,3,3]{0,3,2,1:T(4,128)(2,1)S(1)}, bf16[64,3,3,3]{0,3,2,1:T(4,128)(2,1)}, u32[]{:S(2)}) copy-start(bf16[64,3,3,3]{0,3,2,1:T(4,128)(2,1)} %param.23) | copy-start | bytes 10372
  49.0 27.8 %copy-start.8 = (pred[8,17]{0,1:T(8,128)(4,1)S(1)}, pred[8,17]{0,1:T(8,128)(4,1)}, u32[]{:S(2)}) copy-start(pred[8,17]{0,1:T(8,128)(4,1)} %constant.109) | copy-start | bytes 412
  57.5 5.6 %collective-permute-start.4 = (f32[3,16,128]{2,1,0:T(8,128)S(1)}, f32[3,16,128]{2,1,0:T(8,128)S(1)}, u32[]{:S(2)}, u32[]{:S(2)}) collective-permute-start(f32[3,16,128]{2,1,0:T(8,128)S(1)} %get-tuple-element.18), channel_id=1, source_target_pairs={{0,96},{32,0},{64,32},{96,64},{1,97},{33,1},{65,33},{97,65},{2,98}... | collective-permute-start | bytes 73736 | tf_op jit(solution)/shard_map/ppermute | solution.py:261
  61.6 5.3 %collective-permute-start.3 = (f32[3,16,128]{2,1,0:T(8,128)S(1)}, f32[3,16,128]{2,1,0:T(8,128)S(1)}, u32[]{:S(2)}, u32[]{:S(2)}) collective-permute-start(f32[3,16,128]{2,1,0:T(8,128)S(1)} %get-tuple-element.19), channel_id=1, source_target_pairs={{0,64},{32,96},{64,0},{96,32},{1,65},{33,97},{65,1},{97,33},{2,66}... | collective-permute-start | bytes 73736 | tf_op jit(solution)/shard_map/ppermute | solution.py:261
  61.6 5.3 %collective-permute-start.2 = (f32[3,16,128]{2,1,0:T(8,128)S(1)}, f32[3,16,128]{2,1,0:T(8,128)S(1)}, u32[]{:S(2)}, u32[]{:S(2)}) collective-permute-start(f32[3,16,128]{2,1,0:T(8,128)S(1)} %get-tuple-element.17), channel_id=1, source_target_pairs={{0,32},{32,64},{64,96},{96,0},{1,33},{33,65},{65,97},{97,1},{2,34}... | collective-permute-start | bytes 73736 | tf_op jit(solution)/shard_map/ppermute | solution.py:261
  67.0 4.5 %collective-permute-start.6 = (bf16[1,3,2,128]{3,2,1,0:T(2,128)(2,1)S(1)}, bf16[1,3,2,128]{3,2,1,0:T(2,128)(2,1)S(1)}, u32[]{:S(2)}, u32[]{:S(2)}) collective-permute-start(bf16[1,3,2,128]{3,2,1,0:T(2,128)(2,1)S(1)} %get-tuple-element.21), channel_id=1, source_target_pairs={{1,0},{2,1},{3,2},{4,3},{5,4},{6,5},{7,6},{8,7},{9,8},{10,9},{11,1... | collective-permute-start | bytes 4616 | tf_op jit(solution)/shard_map/ppermute | solution.py:29
  68.9 7.0 %collective-permute-start.5 = (bf16[1,3,2,128]{3,2,1,0:T(2,128)(2,1)S(1)}, bf16[1,3,2,128]{3,2,1,0:T(2,128)(2,1)S(1)}, u32[]{:S(2)}, u32[]{:S(2)}) collective-permute-start(bf16[1,3,2,128]{3,2,1,0:T(2,128)(2,1)S(1)} %get-tuple-element.20), channel_id=1, source_target_pairs={{0,1},{1,2},{2,3},{3,4},{4,5},{5,6},{6,7},{7,8},{8,9},{9,10},{10,1... | collective-permute-start | bytes 4616 | tf_op jit(solution)/shard_map/ppermute | solution.py:27
  76.9 1.5 %copy-start.5 = (bf16[64,64,3,3]{1,0,3,2:T(8,128)(2,1)S(1)}, bf16[64,64,3,3]{1,0,3,2:T(8,128)(2,1)}, u32[]{:S(2)}) copy-start(bf16[64,64,3,3]{1,0,3,2:T(8,128)(2,1)} %param.24) | copy-start | bytes 221188

commit v15 on v13

--- a/solution.py
+++ b/solution.py
@@ -249,7 +249,13 @@
     got = lax.all_to_all(send, "tile", split_axis=0, concat_axis=0, tiled=True)
     got, kern = lax.optimization_barrier((got, kern))
     splat = window_splat(got, band_dev, hit_lanes, scenes)
-    extended = padded_2(splat, (("tile", 2),), K // 2)
+    count = tile_count
+    radius = K // 2
+    above = lax.ppermute(splat, "tile", [(i, i + 1) for i in range(count - 1)])
+    below = lax.ppermute(splat, "tile", [(i + 1, i) for i in range(count - 1)])
+    extended = jnp.concatenate(
+        [above[:, :, ROWS_DEV - radius :], splat, below[:, :, :radius]], axis=2
+    )
     wave_index = lax.axis_index("wave")
     my_response = lax.dynamic_slice_in_dim(response, wave_index * band_dev, band_dev, 0)
     partial = patch_blur(extended, kern, my_response, K // 2)

time: 78.8 us -> 78.7 us (level)
    ppermute x0 -> x2, waiting for transfers between devices: none -> 7.8 us  [the longest x1 6.48 us: per_device(): below = lax.ppermute(splat, 'tile', [(i + 1, i) for i in range(count - 1)])]
    ppermute x2 -> x1, waiting for transfers between devices: 11.6 us -> 5.05 us  [padded_2(): lax.ppermute(head, axis, [((i + 1) % count, i) for i in range(ends)])]
    ppermute x0 -> x2, starting transfers between devices: none -> 5.64 us  [the longest x1 3.72 us: per_device(): above = lax.ppermute(splat, 'tile', [(i, i + 1) for i in range(count - 1)])]
    ppermute x2 -> x1, starting transfers between devices: 6.9 us -> 3.18 us  [padded_2(): lax.ppermute(tail, axis, [(i, (i + 1) % count) for i in range(ends)])]
    ppermute x2 -> x1, starting transfers between devices: 3.84 us -> 1.92 us  [padded_2(): lax.ppermute(head, axis, [((i + 1) % count, i) for i in range(ends)])]
    ppermute x2 -> x1, waiting for transfers between devices: 1.32 us -> 0.01 us  [padded_2(): lax.ppermute(tail, axis, [(i, (i + 1) % count) for i in range(ends)])]
where the time goes in v15:
time: 78.7 us; the launch traced here: 78.3 us
  starting transfers between devices  23.6 us (30%)
  waiting for transfers between devices  23.1 us (29%)
  matrix products  17.7 us (22%)
  Pallas kernels  9.29 us (12%)
  local copies, waits for them, and re-layouts  3.88 us (5%)
    all_to_all x1, starting transfers between devices, per_device(): got = lax.all_to_all(send, 'tile', split_axis=0, concat_axis=0, tiled=True)  7.7 us
    dot_general x1, matrix products, window_splat(): jnp.einsum('ibjh,ihc->ibjc', spread, onehot, preferred_element_type=jnp.f...  7.5 us
    all_to_all x1, waiting for transfers between devices, per_device(): got = lax.all_to_all(send, 'tile', split_axis=0, concat_axis=0, tiled=True)  7.32 us
    pallas_call x1, Pallas kernels, row_taps(): pl.pallas_call(row_taps_kernel, out_shape=jax.ShapeDtypeStruct((channels,...  6.54 us
    ppermute x1, waiting for transfers between devices, per_device(): below = lax.ppermute(splat, 'tile', [(i + 1, i) for i in range(count - 1)])  6.48 us
    ppermute x3, starting transfers between devices, per_device(): lax.ppermute(piece, 'wave', [(i, (i + step) % wave_count) for i in range(...  5.13 us
    ppermute x1, waiting for transfers between devices, padded_2(): lax.ppermute(head, axis, [((i + 1) % count, i) for i in range(ends)])  5.05 us
    ppermute x1, starting transfers between devices, per_device(): above = lax.ppermute(splat, 'tile', [(i, i + 1) for i in range(count - 1)])  3.72 us
  transfers between devices with their start and end apart: 8, of which 5 were waited for; matrix products, arithmetic and copies ran while one was open for 4% of the time, Pallas kernels for 0%

profile of v15, /device:TPU:27, one launch (start us, length us, event | category | flops | bytes accessed | tf_op | source)
XLA Modules:
  0.0 78.3 jit_solution(9453542300361153497)
XLA Ops:
  0.0 2.8 %shard_map.136 = bf16[256,1280]{1,0:T(8,128)(2,1)} custom-call(bf16[128,8,128]{2,1,0:T(8,128)(2,1)} %energy_ref.1, s32[128,128]{1,0:T(8,128)} %bitcast.107, s32[1,128]{1,0:T(1,128)} %bitcast.108, s32[1,128]{1,0:T(1,128)} %count_ref.1, s32[1,128]{1,0:T(1,128)} %scene_ref.1, s32[1,128]{1,0:T(1,128)} %row_ref.1), custom_call_target="tpu_custom_call" | custom-call | tf_op jit(solution)/shard_map/pallas_call | solution.py:214
  2.8 7.7 %all-to-all-start = ((bf16[32,8,1280]{2,1,0:T(8,128)(2,1)}), bf16[32,8,1280]{2,1,0:T(8,128)(2,1)S(1)}, u32[]{:S(2)}, u32[]{:S(2)}) async-start(bf16[32,8,1280]{2,1,0:T(8,128)(2,1)} %bitcast.96), calls=%async_computation | async-start | bytes 1310720 | tf_op jit(solution)/shard_map/all_to_all | solution.py:249
  11.8 1.9 %fusion.82.kern_ref = f32[32,32,256]{2,1,0:T(8,128)} fusion(f32[32,32,31]{2,1,0:T(8,128)S(1)} %bitcast.98, f32[31,256,1]{1,0,2:T(8,128)S(1)} %copy-done.3), kind=kOutput, calls=%fused_computation.105 | convolution fusion | flops 97517568 | bytes 1207296 | tf_op jit(solution)/shard_map/dot_general | solution.py:118
  13.7 7.3 %all-to-all-done = bf16[32,8,1280]{2,1,0:T(8,128)(2,1)S(1)} async-done(((bf16[32,8,1280]{2,1,0:T(8,128)(2,1)}), bf16[32,8,1280]{2,1,0:T(8,128)(2,1)S(1)}, u32[]{:S(2)}, u32[]{:S(2)}) %all-to-all-start) | async-done | bytes 655392 | tf_op jit(solution)/shard_map/all_to_all | solution.py:249
  21.6 7.5 %fusion.4 = (bf16[256,8,4,128]{3,1,2,0:T(8,128)(2,1)S(1)}, bf16[256,8,4,128]{3,1,2,0:T(8,128)(2,1)S(1)}) fusion(s32[256,128]{1,0:T(8,128)S(1)} %get-tuple-element.12, pred[256,4,128]{2,1,0:T(4,128)(4,1)S(1)} %iota_compare_fusion.4, bf16[256,8,128]{2,1,0:T(8,128)(2,1)S(1)} %bitcast.105), kind=kOutput, calls=%fused_computation.7 | convolution fusion | flops 277872640 | bytes 4980736 | tf_op jit(solution)/shard_map/ibjh,ihc->ibjc/dot_general | solution.py:155
  29.1 0.8 fusion.13
  29.9 0.8 %fusion.19 = f32[64,8,128]{2,0,1:T(8,128)S(1)} fusion(f32[64,8,128]{2,0,1:T(8,128)S(1)} %fusion.13, bf16[256,8,4,128]{3,1,2,0:T(8,128)(2,1)S(1)} %get-tuple-element.9, s32[256,4]{0,1:T(4,128)S(1)} %iota_add_fusion), kind=kOutput, calls=%fused_computation.24 | convolution fusion | flops 134479872 | bytes 2625536 | tf_op jit(solution)/shard_map/ibjc,ijr->brc/dot_general | solution.py:165
  30.7 3.7 %collective-permute-start = (f32[8,4,16,128]{3,2,1,0:T(8,128)S(1)}, f32[8,4,16,128]{3,2,1,0:T(8,128)S(1)}, u32[]{:S(2)}, u32[]{:S(2)}) collective-permute-start(f32[8,4,16,128]{3,2,1,0:T(8,128)S(1)} %bitcast.101), channel_id=1, source_target_pairs={{0,1},{1,2},{2,3},{3,4},{4,5},{5,6},{6,7},{7,8},{8,9},{9,10},{10,1... | collective-permute-start | bytes 786440 | tf_op jit(solution)/shard_map/ppermute | solution.py:254
  34.4 1.9 %collective-permute-start.1 = (f32[8,4,16,128]{3,2,1,0:T(8,128)S(1)}, f32[8,4,16,128]{3,2,1,0:T(8,128)S(1)}, u32[]{:S(2)}, u32[]{:S(2)}) collective-permute-start(f32[8,4,16,128]{3,2,1,0:T(8,128)S(1)} %bitcast.102), channel_id=1, source_target_pairs={{1,0},{2,1},{3,2},{4,3},{5,4},{6,5},{7,6},{8,7},{9,8},{10,9},{11,1... | collective-permute-start | bytes 786440 | tf_op jit(solution)/shard_map/ppermute | solution.py:255
  36.4 1.3 %collective-permute-done = f32[8,4,16,128]{3,2,1,0:T(8,128)S(1)} collective-permute-done((f32[8,4,16,128]{3,2,1,0:T(8,128)S(1)}, f32[8,4,16,128]{3,2,1,0:T(8,128)S(1)}, u32[]{:S(2)}, u32[]{:S(2)}) %collective-permute-start) | collective-permute-done | bytes 262176 | tf_op jit(solution)/shard_map/ppermute | solution.py:254
  37.8 6.5 %collective-permute-done.1 = f32[8,4,16,128]{3,2,1,0:T(8,128)S(1)} collective-permute-done((f32[8,4,16,128]{3,2,1,0:T(8,128)S(1)}, f32[8,4,16,128]{3,2,1,0:T(8,128)S(1)}, u32[]{:S(2)}, u32[]{:S(2)}) %collective-permute-start.1) | collective-permute-done | bytes 262176 | tf_op jit(solution)/shard_map/ppermute | solution.py:255
  44.2 2.0 %fusion.27.spec_ref = f32[32,46,256]{2,1,0:T(8,128)} fusion(f32[128,256,1]{1,0,2:T(8,128)S(1)} %copy-done.1, f32[32,15,128]{2,1,0:T(8,128)S(1)} %bitcast.106, f32[32,16,128]{2,1,0:T(8,128)S(1)} %bitcast.103, f32[32,15,128]{2,1,0:T(8,128)S(1)} %bitcast.104), kind=kOutput, calls=%fused_computation.30 | convolution fusion | flops 289783808 | bytes 2392064 | tf_op jit(solution)/shard_map/cyx,xf->cyf/dot_general | solution.py:130
  46.2 6.5 %shard_map.137 = f32[32,16,256]{2,1,0:T(8,128)} custom-call(f32[32,46,256]{2,1,0:T(8,128)} %fusion.27.spec_ref, f32[32,32,256]{2,1,0:T(8,128)} %fusion.82.kern_ref), custom_call_target="tpu_custom_call" | custom-call | tf_op jit(solution)/shard_map/pallas_call | solution.py:99
  52.7 1.7 %convolution_bitcast_fusion = f32[4,3,16,256]{3,1,2,0:T(4,128)S(1)} fusion(f32[8,4,16,256]{3,2,1,0:T(8,128)} %bitcast.100, f32[32,3]{0,1:T(4,128)S(1)} %copy-done.4, s32[]{:T(128)S(6)} %select_n.64), kind=kOutput, calls=%fused_computation.23 | convolution fusion | flops 2359296 | bytes 721284 | tf_op jit(solution)/shard_map/bsyf,bc->scyf/dot_general | solution.py:135
  54.7 1.7 %collective-permute-start.2 = (f32[3,16,128]{2,1,0:T(8,128)S(1)}, f32[3,16,128]{2,1,0:T(8,128)S(1)}, u32[]{:S(2)}, u32[]{:S(2)}) collective-permute-start(f32[3,16,128]{2,1,0:T(8,128)S(1)} %get-tuple-element.15), channel_id=1, source_target_pairs={{0,32},{32,64},{64,96},{96,0},{1,33},{33,65},{65,97},{97,1},{2,34}... | collective-permute-start | bytes 73736 | tf_op jit(solution)/shard_map/ppermute | solution.py:265
  56.4 2.2 %collective-permute-start.4 = (f32[3,16,128]{2,1,0:T(8,128)S(1)}, f32[3,16,128]{2,1,0:T(8,128)S(1)}, u32[]{:S(2)}, u32[]{:S(2)}) collective-permute-start(f32[3,16,128]{2,1,0:T(8,128)S(1)} %get-tuple-element.16), channel_id=1, source_target_pairs={{0,96},{32,0},{64,32},{96,64},{1,97},{33,1},{65,33},{97,65},{2,98}... | collective-permute-start | bytes 73736 | tf_op jit(solution)/shard_map/ppermute | solution.py:265
  58.6 1.2 %collective-permute-start.3 = (f32[3,16,128]{2,1,0:T(8,128)S(1)}, f32[3,16,128]{2,1,0:T(8,128)S(1)}, u32[]{:S(2)}, u32[]{:S(2)}) collective-permute-start(f32[3,16,128]{2,1,0:T(8,128)S(1)} %get-tuple-element.17), channel_id=1, source_target_pairs={{0,64},{32,96},{64,0},{96,32},{1,65},{33,97},{65,1},{97,33},{2,66}... | collective-permute-start | bytes 73736 | tf_op jit(solution)/shard_map/ppermute | solution.py:265
  59.8 2.9 %collective-permute-done.3 = f32[3,16,128]{2,1,0:T(8,128)S(1)} collective-permute-done((f32[3,16,128]{2,1,0:T(8,128)S(1)}, f32[3,16,128]{2,1,0:T(8,128)S(1)}, u32[]{:S(2)}, u32[]{:S(2)}) %collective-permute-start.3) | collective-permute-done | bytes 24608 | tf_op jit(solution)/shard_map/ppermute | solution.py:265
  62.8 3.2 %collective-permute-start.5 = (bf16[1,3,2,128]{3,2,1,0:T(2,128)(2,1)S(1)}, bf16[1,3,2,128]{3,2,1,0:T(2,128)(2,1)S(1)}, u32[]{:S(2)}, u32[]{:S(2)}) collective-permute-start(bf16[1,3,2,128]{3,2,1,0:T(2,128)(2,1)S(1)} %get-tuple-element.18), channel_id=1, source_target_pairs={{0,1},{1,2},{2,3},{3,4},{4,5},{5,6},{6,7},{7,8},{8,9},{9,10},{10,1... | collective-permute-start | bytes 4616 | tf_op jit(solution)/shard_map/ppermute | solution.py:27
  66.0 1.9 %collective-permute-start.6 = (bf16[1,3,2,128]{3,2,1,0:T(2,128)(2,1)S(1)}, bf16[1,3,2,128]{3,2,1,0:T(2,128)(2,1)S(1)}, u32[]{:S(2)}, u32[]{:S(2)}) collective-permute-start(bf16[1,3,2,128]{3,2,1,0:T(2,128)(2,1)S(1)} %get-tuple-element.19), channel_id=1, source_target_pairs={{1,0},{2,1},{3,2},{4,3},{5,4},{6,5},{7,6},{8,7},{9,8},{10,9},{11,1... | collective-permute-start | bytes 4616 | tf_op jit(solution)/shard_map/ppermute | solution.py:29
  67.9 5.1 %collective-permute-done.6 = bf16[1,3,2,128]{3,2,1,0:T(2,128)(2,1)S(1)} collective-permute-done((bf16[1,3,2,128]{3,2,1,0:T(2,128)(2,1)S(1)}, bf16[1,3,2,128]{3,2,1,0:T(2,128)(2,1)S(1)}, u32[]{:S(2)}, u32[]{:S(2)}) %collective-permute-start.6) | collective-permute-done | bytes 1568 | tf_op jit(solution)/shard_map/ppermute | solution.py:29
  74.0 1.4 %fusion.26 = bf16[18,1,8,17,64]{4,2,3,0,1:T(8,128)(2,1)S(1)} fusion(pred[18]{0:T(512)(128)(4,1)S(1)} %and_or_fusion, pred[8,17]{0,1:T(8,128)(4,1)S(1)} %copy-done.8, bf16[3,20,1,7,2]{3,0,4,1,2:T(4,128)(2,1)S(1)} %slice.43, bf16[3,20,1,8,17]{3,0,4,1,2:T(4,128)(2,1)S(1)} %copy.58, bf16[64,3,3,3]{0,3,2,1:T(4,128)(2,1)S(1)} %copy-done.6), kind=kOutput, calls=%fused_computation.29 | convolution fusion | flops 9925056 | bytes 334954 | tf_op jit(solution)/shard_map/conv_general_dilated | solution.py:37
  75.4 1.5 %convolution_convert_fusion = bf16[16,8,17,64]{3,1,2,0:T(8,128)(2,1)S(1)} fusion(bf16[64,64,3,3]{1,0,3,2:T(8,128)(2,1)S(1)} %copy-done.5, bf16[18,1,7,1,64]{4,2,3,0,1:T(8,128)(2,1)S(1)} %get-tuple-element.14, bf16[18,1,7,1,64]{4,2,3,0,1:T(8,128)(2,1)S(1)} %get-tuple-element.13, bf16[18,1,8,17,64]{4,2,3,0,1:T(8,128)(2,1)S(1)} %fusion.26), kind=kOutput, calls=%fused_computation.19 | convolution fusion | flops 162322432 | bytes 697856 | tf_op jit(solution)/shard_map/conv_general_dilated | solution.py:37
  77.0 1.3 %copy.61 = bf16[1,64,16,128]{3,2,1,0:T(8,128)(2,1)} copy(bf16[1,64,16,128]{1,2,3,0:T(8,128)(2,1)S(1)} %slice_bitcast_fusion) | data formatting | bytes 524288 | tf_op jit(solution)/shard_map/convert_element_type | solution.py:279
  (49 shorter events, 3.2 us)
Async XLA Ops:
  0.0 10.5 %copy-start = (f32[64,8,961]{2,1,0:T(8,128)S(1)}, f32[64,8,961]{2,1,0:T(8,128)}, u32[]{:S(2)}) copy-start(f32[64,8,961]{2,1,0:T(8,128)} %param.20) | copy-start | bytes 5904388
  0.0 10.5 %copy-start.7 = (s32[1,4,1]{1,2,0:T(1,128)S(1)}, s32[1,4,1]{1,2,0:T(1,128)}, u32[]{:S(2)}) copy-start(s32[1,4,1]{1,2,0:T(1,128)} %param.21) | copy-start | bytes 52
  2.8 9.0 %copy-start.3 = (f32[31,256,1]{1,0,2:T(8,128)S(1)}, f32[31,256,1]{1,0,2:T(8,128)}, u32[]{:S(2)}) copy-start(f32[31,256,1]{1,0,2:T(8,128)} %constant.111) | copy-start | bytes 95236
  2.8 18.3 %all-to-all-start = ((bf16[32,8,1280]{2,1,0:T(8,128)(2,1)}), bf16[32,8,1280]{2,1,0:T(8,128)(2,1)S(1)}, u32[]{:S(2)}, u32[]{:S(2)}) async-start(bf16[32,8,1280]{2,1,0:T(8,128)(2,1)} %bitcast.96), calls=%async_computation | async-start | bytes 1310720 | tf_op jit(solution)/shard_map/all_to_all | solution.py:249
  29.9 14.3 %copy-start.1 = (f32[128,256,1]{1,0,2:T(8,128)S(1)}, f32[128,256,1]{1,0,2:T(8,128)}, u32[]{:S(2)}) copy-start(f32[128,256,1]{1,0,2:T(8,128)} %constant.112) | copy-start | bytes 393220
  30.7 7.0 %collective-permute-start = (f32[8,4,16,128]{3,2,1,0:T(8,128)S(1)}, f32[8,4,16,128]{3,2,1,0:T(8,128)S(1)}, u32[]{:S(2)}, u32[]{:S(2)}) collective-permute-start(f32[8,4,16,128]{3,2,1,0:T(8,128)S(1)} %bitcast.101), channel_id=1, source_target_pairs={{0,1},{1,2},{2,3},{3,4},{4,5},{5,6},{6,7},{7,8},{8,9},{9,10},{10,1... | collective-permute-start | bytes 786440 | tf_op jit(solution)/shard_map/ppermute | solution.py:254
  34.4 9.8 %collective-permute-start.1 = (f32[8,4,16,128]{3,2,1,0:T(8,128)S(1)}, f32[8,4,16,128]{3,2,1,0:T(8,128)S(1)}, u32[]{:S(2)}, u32[]{:S(2)}) collective-permute-start(f32[8,4,16,128]{3,2,1,0:T(8,128)S(1)} %bitcast.102), channel_id=1, source_target_pairs={{1,0},{2,1},{3,2},{4,3},{5,4},{6,5},{7,6},{8,7},{9,8},{10,9},{11,1... | collective-permute-start | bytes 786440 | tf_op jit(solution)/shard_map/ppermute | solution.py:255
  46.2 6.6 %copy-start.4 = (f32[32,3]{0,1:T(4,128)S(1)}, f32[32,3]{0,1:T(4,128)}, u32[]{:S(2)}) copy-start(f32[32,3]{0,1:T(4,128)} %param.22) | copy-start | bytes 1156
  46.2 8.2 %copy-start.2 = (f32[256,128,1,1]{1,0,3,2:T(8,128)S(1)}, f32[256,128,1,1]{1,0,3,2:T(8,128)}, u32[]{:S(2)}) copy-start(f32[256,128,1,1]{1,0,3,2:T(8,128)} %constant.113) | copy-start | bytes 393220
  46.2 27.7 %copy-start.6 = (bf16[64,3,3,3]{0,3,2,1:T(4,128)(2,1)S(1)}, bf16[64,3,3,3]{0,3,2,1:T(4,128)(2,1)}, u32[]{:S(2)}) copy-start(bf16[64,3,3,3]{0,3,2,1:T(4,128)(2,1)} %param.23) | copy-start | bytes 10372
  46.2 27.8 %copy-start.8 = (pred[8,17]{0,1:T(8,128)(4,1)S(1)}, pred[8,17]{0,1:T(8,128)(4,1)}, u32[]{:S(2)}) copy-start(pred[8,17]{0,1:T(8,128)(4,1)} %constant.109) | copy-start | bytes 412
  54.7 5.1 %collective-permute-start.2 = (f32[3,16,128]{2,1,0:T(8,128)S(1)}, f32[3,16,128]{2,1,0:T(8,128)S(1)}, u32[]{:S(2)}, u32[]{:S(2)}) collective-permute-start(f32[3,16,128]{2,1,0:T(8,128)S(1)} %get-tuple-element.15), channel_id=1, source_target_pairs={{0,32},{32,64},{64,96},{96,0},{1,33},{33,65},{65,97},{97,1},{2,34}... | collective-permute-start | bytes 73736 | tf_op jit(solution)/shard_map/ppermute | solution.py:265
  56.4 3.4 %collective-permute-start.4 = (f32[3,16,128]{2,1,0:T(8,128)S(1)}, f32[3,16,128]{2,1,0:T(8,128)S(1)}, u32[]{:S(2)}, u32[]{:S(2)}) collective-permute-start(f32[3,16,128]{2,1,0:T(8,128)S(1)} %get-tuple-element.16), channel_id=1, source_target_pairs={{0,96},{32,0},{64,32},{96,64},{1,97},{33,1},{65,33},{97,65},{2,98}... | collective-permute-start | bytes 73736 | tf_op jit(solution)/shard_map/ppermute | solution.py:265
  58.6 4.2 %collective-permute-start.3 = (f32[3,16,128]{2,1,0:T(8,128)S(1)}, f32[3,16,128]{2,1,0:T(8,128)S(1)}, u32[]{:S(2)}, u32[]{:S(2)}) collective-permute-start(f32[3,16,128]{2,1,0:T(8,128)S(1)} %get-tuple-element.17), channel_id=1, source_target_pairs={{0,64},{32,96},{64,0},{96,32},{1,65},{33,97},{65,1},{97,33},{2,66}... | collective-permute-start | bytes 73736 | tf_op jit(solution)/shard_map/ppermute | solution.py:265
  62.8 5.1 %collective-permute-start.5 = (bf16[1,3,2,128]{3,2,1,0:T(2,128)(2,1)S(1)}, bf16[1,3,2,128]{3,2,1,0:T(2,128)(2,1)S(1)}, u32[]{:S(2)}, u32[]{:S(2)}) collective-permute-start(bf16[1,3,2,128]{3,2,1,0:T(2,128)(2,1)S(1)} %get-tuple-element.18), channel_id=1, source_target_pairs={{0,1},{1,2},{2,3},{3,4},{4,5},{5,6},{6,7},{7,8},{8,9},{9,10},{10,1... | collective-permute-start | bytes 4616 | tf_op jit(solution)/shard_map/ppermute | solution.py:27
  66.0 7.0 %collective-permute-start.6 = (bf16[1,3,2,128]{3,2,1,0:T(2,128)(2,1)S(1)}, bf16[1,3,2,128]{3,2,1,0:T(2,128)(2,1)S(1)}, u32[]{:S(2)}, u32[]{:S(2)}) collective-permute-start(bf16[1,3,2,128]{3,2,1,0:T(2,128)(2,1)S(1)} %get-tuple-element.19), channel_id=1, source_target_pairs={{1,0},{2,1},{3,2},{4,3},{5,4},{6,5},{7,6},{8,7},{9,8},{10,9},{11,1... | collective-permute-start | bytes 4616 | tf_op jit(solution)/shard_map/ppermute | solution.py:29
  73.9 1.5 %copy-start.5 = (bf16[64,64,3,3]{1,0,3,2:T(8,128)(2,1)S(1)}, bf16[64,64,3,3]{1,0,3,2:T(8,128)(2,1)}, u32[]{:S(2)}) copy-start(bf16[64,64,3,3]{1,0,3,2:T(8,128)(2,1)} %param.24) | copy-start | bytes 221188
